TPU v7x, 128 devices: a whole 4x4x4 slice. The times are simulated.
128 devices in a mesh: region: 128 (over y, z, x, core).
Axes of the slice: x: 4, y: 4, z: 4, core: 2. Of those that a mesh axis runs over, the one named last changes fastest.
Arguments:
- mixing_ratio: bfloat16 [150, 1048576], P(None, 'region'), may hold values from 0.049804688 to 5
- send_rows: int32 [128, 8, 128], P('region'), may hold values from 0 to 8191, as said below
- migrant_count: int32 [128, 8], P('region'), may hold values from 1 to 128, as said below
- arrival_slot: int32 [128, 8, 128], P('region'), may hold values from 0 to 8191, as said below
- halo_blocks: int32 [128, 2, 16], P('region'), may hold values from 0 to 63
- neighbour_block: int32 [8192, 3], P('region'), may hold values from 0 to 95
- mix_weight: bfloat16 [8192, 4, 128, 128], P('region'), may hold values from 0 to 0.0078125
- inverse_temp: float32 [1048576], P('region'), may hold values from -1 to 1
- reactant_order: float32 [256, 150], replicated, may hold values from 0 to 0.05
- log_prefactor: float32 [256], replicated, may hold values from -1 to 1
- activation_energy: float32 [256], replicated, may hold values from 0.2 to 1.5
- production: float32 [150, 256], replicated, may hold values from 0 to 0.0078125
- loss_coefficient: float32 [150, 256], replicated, may hold values from 0 to 0.0078125
Outputs:
- updated_ratio: float32 [150, 1048576], P(None, 'region')
Inputs may be any that keep to these rules, and one draw needn't show every extreme that they name: `migrant_count`: entry j of a region counts the parcels it sends to the region at offset o_j along the loop of regions; it equals the count that region sends back at offset -o_j. Some pair of regions reaches 128; regions near a few busy ones send far more. `send_rows`: the first migrant_count entries of each peer slot are distinct local parcels of the region, disjoint over all slots; the remaining entries are 0. `arrival_slot`: over all peer slots, the first migrant_count entries name each parcel that the same region lists in send_rows exactly once; the remaining entries are 0.
All inputs are finite; a program needn't handle non-finite values.
Results may differ from a plain program's by a relative error of at most 0.0003.
Values may be sent and summed in bfloat16 or wider, within the bound.
No kernel may reach another device: no remote copies, remote signals or barrier semaphores. Data moves between devices by JAX's collectives and lax.ppermute only.
A program may use at most 128 MiB of HBM per device.

v0:
```python
import functools

import jax
import jax.numpy as jnp
from jax import lax
from jax.experimental import pallas as pl
from jax.experimental.pallas import tpu as pltpu
from jax.sharding import PartitionSpec as P

HOP = 4
TILE_BLOCKS = 4


def from_behind(block, axis, distance):
    devices = range(lax.axis_size(axis))
    route = [((i - distance) % len(devices), i) for i in devices]
    return lax.ppermute(block, axis, route)


def peer_offsets():
    return [column - HOP if column < HOP else column - HOP + 1 for column in range(2 * HOP)]


def migrate(mixing_ratio, send_rows, migrant_count, arrival_slot):
    species, parcels = mixing_ratio.shape
    capacity = send_rows.shape[-1]
    offsets = peer_offsets()
    peer_count = len(offsets)
    outgoing = jnp.take(mixing_ratio, send_rows[0].reshape(-1), axis=1).reshape(
        species, peer_count, capacity
    )
    arrived = []
    for column in range(peer_count):
        opposite = peer_count - 1 - column
        arrived.append(from_behind(outgoing[:, opposite, :], "region", -offsets[column]))
    received = jnp.stack(arrived, axis=1)
    lane_index = jnp.arange(capacity, dtype=jnp.int32)
    live_lane = lane_index[None, :] < migrant_count[0][:, None]
    target_slot = jnp.where(live_lane, arrival_slot[0], parcels)
    return mixing_ratio.at[:, target_slot.reshape(-1)].set(
        received.reshape(species, -1), mode="drop"
    )


def block_table(migrated, halo_blocks, block_size):
    species, parcels = migrated.shape
    blocks = migrated.reshape(species, parcels // block_size, block_size)
    to_lower = jnp.take(blocks, halo_blocks[0, 0], axis=1)
    to_upper = jnp.take(blocks, halo_blocks[0, 1], axis=1)
    from_lower = from_behind(to_upper, "region", 1)
    from_upper = from_behind(to_lower, "region", -1)
    return jnp.concatenate(
        [
            migrated,
            from_lower.reshape(species, -1),
            from_upper.reshape(species, -1),
        ],
        axis=1,
    )


def split3(x):
    high = x.astype(jnp.bfloat16)
    low = (x - high.astype(jnp.float32)).astype(jnp.bfloat16)
    return high, low


def dot3(a_high, a_low, b_high, b_low):
    f32 = jnp.float32
    total = jnp.dot(a_high, b_high, preferred_element_type=f32)
    total = total + jnp.dot(a_high, b_low, preferred_element_type=f32)
    return total + jnp.dot(a_low, b_high, preferred_element_type=f32)


def mix_react_kernel(tile_blocks, neighbours, block_size, nb_ref, own_ref, *refs):
    count = tile_blocks * neighbours
    picked = refs[:count]
    (
        weight_ref,
        temp_ref,
        order_high,
        order_low,
        prefactor_ref,
        energy_ref,
        prod_high,
        prod_low,
        loss_high,
        loss_low,
        out_ref,
        mixed_ref,
    ) = refs[count:]
    f32 = jnp.float32
    for t in range(tile_blocks):
        lanes = slice(t * block_size, (t + 1) * block_size)
        acc = jnp.dot(own_ref[:, lanes], weight_ref[t, 0], preferred_element_type=f32)
        for k in range(neighbours):
            acc = acc + jnp.dot(
                picked[t * neighbours + k][...], weight_ref[t, k + 1], preferred_element_type=f32
            )
        mixed_ref[:, lanes] = acc
    mixed = mixed_ref[...]
    log_high, log_low = split3(jnp.log(mixed))
    exponent = dot3(order_high[...], order_low[...], log_high, log_low)
    rate = jnp.exp(prefactor_ref[...] - energy_ref[...] * temp_ref[...] + exponent)
    rate_high, rate_low = split3(rate)
    gained = dot3(prod_high[...], prod_low[...], rate_high, rate_low)
    lost_mass = dot3(loss_high[...], loss_low[...], rate_high, rate_low)
    out_ref[...] = (mixed + gained) / (1.0 + lost_mass / mixed)


def mix_react(
    table,
    neighbour_block,
    mix_weight,
    inverse_temp,
    reactant_order,
    log_prefactor,
    activation_energy,
    production,
    loss_coefficient,
):
    species = table.shape[0]
    count_blocks, _, block_size, _ = mix_weight.shape
    neighbours = neighbour_block.shape[1]
    reactions = reactant_order.shape[0]
    tile_blocks = TILE_BLOCKS
    width = tile_blocks * block_size
    steps = count_blocks // tile_blocks

    def picked_spec(t, k):
        return pl.BlockSpec(
            (species, block_size),
            lambda i, nb: (0, nb[(i * tile_blocks + t) * neighbours + k]),
        )

    def whole(shape):
        return pl.BlockSpec(shape, lambda i, nb: (0,) * len(shape))

    order_high, order_low = split3(reactant_order)
    prod_high, prod_low = split3(production)
    loss_high, loss_low = split3(loss_coefficient)
    in_specs = (
        [pl.BlockSpec((species, width), lambda i, nb: (0, i))]
        + [picked_spec(t, k) for t in range(tile_blocks) for k in range(neighbours)]
        + [
            pl.BlockSpec((tile_blocks,) + mix_weight.shape[1:], lambda i, nb: (i, 0, 0, 0)),
            pl.BlockSpec((1, width), lambda i, nb: (0, i)),
            whole(reactant_order.shape),
            whole(reactant_order.shape),
            whole((reactions, 1)),
            whole((reactions, 1)),
            whole(production.shape),
            whole(production.shape),
            whole(loss_coefficient.shape),
            whole(loss_coefficient.shape),
        ]
    )
    grid_spec = pltpu.PrefetchScalarGridSpec(
        num_scalar_prefetch=1,
        grid=(steps,),
        in_specs=in_specs,
        out_specs=pl.BlockSpec((species, width), lambda i, nb: (0, i)),
        scratch_shapes=[pltpu.VMEM((species, width), jnp.float32)],
    )
    kernel = functools.partial(mix_react_kernel, tile_blocks, neighbours, block_size)
    return pl.pallas_call(
        kernel,
        grid_spec=grid_spec,
        out_shape=jax.ShapeDtypeStruct((species, count_blocks * block_size), jnp.float32),
        compiler_params=pltpu.CompilerParams(dimension_semantics=("arbitrary",)),
    )(
        neighbour_block.reshape(-1),
        table,
        *([table] * (tile_blocks * neighbours)),
        mix_weight,
        inverse_temp.reshape(1, -1),
        order_high,
        order_low,
        log_prefactor.reshape(-1, 1),
        activation_energy.reshape(-1, 1),
        prod_high,
        prod_low,
        loss_high,
        loss_low,
    )


def shards(
    mixing_ratio,
    send_rows,
    migrant_count,
    arrival_slot,
    halo_blocks,
    neighbour_block,
    mix_weight,
    inverse_temp,
    reactant_order,
    log_prefactor,
    activation_energy,
    production,
    loss_coefficient,
):
    migrated = migrate(mixing_ratio, send_rows, migrant_count, arrival_slot)
    table = block_table(migrated, halo_blocks, mix_weight.shape[-1])
    return mix_react(
        table,
        neighbour_block,
        mix_weight,
        inverse_temp,
        reactant_order,
        log_prefactor,
        activation_energy,
        production,
        loss_coefficient,
    )


def solution(mesh):
    placed = (
        P(None, "region"),
        P("region", None, None),
        P("region", None),
        P("region", None, None),
        P("region", None, None),
        P("region", None),
        P("region", None, None, None),
        P("region"),
        P(),
        P(),
        P(),
        P(),
        P(),
    )
    return jax.shard_map(
        shards, mesh=mesh, in_specs=placed, out_specs=P(None, "region"), check_vma=False
    )
```

profile of v0, /device:TPU:0, one launch (start us, length us, event | category | flops | bytes accessed | tf_op | source)
XLA Modules:
  0.0 99.9 jit_solution(12219696124682431671)
XLA Ops:
  0.0 5.7 %copy.45 = bf16[150,8192]{0,1:T(8,128)(2,1)} copy(bf16[150,8192]{1,0:T(8,128)(2,1)} %param.15) | data formatting | bytes 4915200 | tf_op args[0]
  5.7 0.0 copy-done.4
  5.7 6.2 %gather_fusion = bf16[1024,150]{1,0:T(8,128)(2,1)S(1)} fusion(bf16[150,8192]{0,1:T(8,128)(2,1)} %copy.45, s32[1024]{0:T(1024)S(1)} %broadcast_clamp_fusion), kind=kCustom, calls=%fused_computation.2 | custom fusion | bytes 618496 | tf_op jit(solution)/shard_map/jit(_take)/gather | solution.py:29
  11.9 0.2 broadcast_select_fusion
  12.2 3.2 %collective-permute-start = (bf16[150,128]{0,1:T(8,128)(2,1)S(1)}, bf16[150,128]{0,1:T(8,128)(2,1)S(1)}, u32[]{:S(2)}, u32[]{:S(2)}) collective-permute-start(bf16[150,128]{0,1:T(8,128)(2,1)S(1)} %get-tuple-element.21), channel_id=1, source_target_pairs={{124,0},{125,1},{126,2},{127,3},{0,4},{1,5},{2,6},{3,7},{4,8},{5,9... | collective-permute-start | bytes 115208 | tf_op jit(solution)/shard_map/ppermute | solution.py:17
  15.4 0.0 collective-permute-start.1
  15.4 1.0 collective-permute-start.2
  16.4 2.2 %collective-permute-start.3 = (bf16[150,128]{0,1:T(8,128)(2,1)S(1)}, bf16[150,128]{0,1:T(8,128)(2,1)S(1)}, u32[]{:S(2)}, u32[]{:S(2)}) collective-permute-start(bf16[150,128]{0,1:T(8,128)(2,1)S(1)} %get-tuple-element.18), channel_id=1, source_target_pairs={{127,0},{0,1},{1,2},{2,3},{3,4},{4,5},{5,6},{6,7},{7,8},{8,9},{9,1... | collective-permute-start | bytes 115208 | tf_op jit(solution)/shard_map/ppermute | solution.py:17
  18.6 5.6 %collective-permute-start.4 = (bf16[150,128]{0,1:T(8,128)(2,1)S(1)}, bf16[150,128]{0,1:T(8,128)(2,1)S(1)}, u32[]{:S(2)}, u32[]{:S(2)}) collective-permute-start(bf16[150,128]{0,1:T(8,128)(2,1)S(1)} %get-tuple-element.17), channel_id=1, source_target_pairs={{1,0},{2,1},{3,2},{4,3},{5,4},{6,5},{7,6},{8,7},{9,8},{10,9},{11,1... | collective-permute-start | bytes 115208 | tf_op jit(solution)/shard_map/ppermute | solution.py:17
  24.1 0.0 copy-done.10
  24.1 0.1 fusion
  24.2 0.0 copy-done.9
  24.2 0.0 copy-done.5
  24.3 0.0 collective-permute-done
  24.3 2.8 %collective-permute-start.5 = (bf16[150,128]{0,1:T(8,128)(2,1)S(1)}, bf16[150,128]{0,1:T(8,128)(2,1)S(1)}, u32[]{:S(2)}, u32[]{:S(2)}) collective-permute-start(bf16[150,128]{0,1:T(8,128)(2,1)S(1)} %get-tuple-element.16), channel_id=1, source_target_pairs={{2,0},{3,1},{4,2},{5,3},{6,4},{7,5},{8,6},{9,7},{10,8},{11,9},{12,... | collective-permute-start | bytes 115208 | tf_op jit(solution)/shard_map/ppermute | solution.py:17
  27.1 0.0 collective-permute-done.1
  27.1 1.1 %collective-permute-start.6 = (bf16[150,128]{0,1:T(8,128)(2,1)S(1)}, bf16[150,128]{0,1:T(8,128)(2,1)S(1)}, u32[]{:S(2)}, u32[]{:S(2)}) collective-permute-start(bf16[150,128]{0,1:T(8,128)(2,1)S(1)} %get-tuple-element.15), channel_id=1, source_target_pairs={{3,0},{4,1},{5,2},{6,3},{7,4},{8,5},{9,6},{10,7},{11,8},{12,9},{13... | collective-permute-start | bytes 115208 | tf_op jit(solution)/shard_map/ppermute | solution.py:17
  28.1 0.0 collective-permute-done.2
  28.1 2.8 %collective-permute-start.7 = (bf16[150,128]{0,1:T(8,128)(2,1)S(1)}, bf16[150,128]{0,1:T(8,128)(2,1)S(1)}, u32[]{:S(2)}, u32[]{:S(2)}) collective-permute-start(bf16[150,128]{0,1:T(8,128)(2,1)S(1)} %get-tuple-element.14), channel_id=1, source_target_pairs={{4,0},{5,1},{6,2},{7,3},{8,4},{9,5},{10,6},{11,7},{12,8},{13,9},{1... | collective-permute-start | bytes 115208 | tf_op jit(solution)/shard_map/ppermute | solution.py:17
  31.0 0.0 collective-permute-done.3
  31.0 0.0 collective-permute-done.4
  31.0 0.0 collective-permute-done.5
  31.0 0.0 collective-permute-done.6
  31.1 3.1 %collective-permute-done.7 = bf16[150,128]{0,1:T(8,128)(2,1)S(1)} collective-permute-done((bf16[150,128]{0,1:T(8,128)(2,1)S(1)}, bf16[150,128]{0,1:T(8,128)(2,1)S(1)}, u32[]{:S(2)}, u32[]{:S(2)}) %collective-permute-start.7) | collective-permute-done | bytes 38432 | tf_op jit(solution)/shard_map/ppermute | solution.py:17
  34.1 9.9 %scatter_fusion = bf16[150,8192]{0,1:T(8,128)(2,1)} fusion(bf16[150,8192]{0,1:T(8,128)(2,1)} %copy.45, s32[1024]{0:T(1024)S(1)} %bitcast.85, bf16[1024,150]{1,0:T(8,128)(2,1)S(1)} %bitcast.81), kind=kCustom, calls=%fused_computation.3 | custom fusion | bytes 925696 | tf_op jit(solution)/shard_map/scatter | solution.py:40
  44.1 5.4 %copy.46 = bf16[150,64,128]{2,0,1:T(8,128)(2,1)S(1)} copy(bf16[150,64,128]{0,2,1:T(8,128)(2,1)} %bitcast.75) | data formatting | bytes 4915200 | tf_op jit(solution)/shard_map/reshape | solution.py:47
  49.5 0.0 copy-start.1
  49.5 0.0 copy-start.7
  49.6 0.0 copy-start.8
  49.6 0.0 copy-start.6
  49.6 0.7 gather_fusion.1
  50.3 0.0 copy-start.2
  50.3 0.1 select_bitcast_fusion.1
  50.4 0.9 copy.47
  51.3 0.0 collective-permute-start.8
  51.3 0.7 gather_fusion.2
  52.0 0.0 copy-start.3
  52.0 0.1 select_bitcast_fusion
  52.1 0.9 copy.49
  53.1 7.2 %collective-permute-start.9 = (bf16[150,16,128]{2,1,0:T(8,128)(2,1)}, bf16[150,16,128]{2,1,0:T(8,128)(2,1)}, u32[]{:S(2)}, u32[]{:S(2)}) collective-permute-start(bf16[150,16,128]{2,1,0:T(8,128)(2,1)} %copy.49), channel_id=1, source_target_pairs={{1,0},{2,1},{3,2},{4,3},{5,4},{6,5},{7,6},{8,7},{9,8},{10,9},{11,1... | collective-permute-start | bytes 1843208 | tf_op jit(solution)/shard_map/ppermute | solution.py:17
  60.2 0.0 copy-done.1
  60.2 0.1 copy.52
  60.4 0.1 copy.53.refs_14_
  60.5 0.0 copy-start
  60.5 0.0 copy-done.7
  60.5 0.8 copy.54.refs_16_
  61.3 0.0 copy-done.8
  61.3 0.8 copy.55.refs_17_
  62.1 0.0 copy-done.6
  62.1 0.1 copy.43
  62.2 0.7 reshape.112.nb_ref
  62.9 0.7 subtract_convert_fusion.refs_15_
  63.6 0.0 copy-done.2
  63.6 0.7 subtract_convert_fusion.1
  64.3 4.5 %copy.50 = bf16[150,8192]{1,0:T(8,128)(2,1)S(1)} copy(bf16[150,8192]{0,1:T(8,128)(2,1)} %scatter_fusion) | data formatting | bytes 4915200 | tf_op jit(solution)/shard_map/scatter | solution.py:40
  68.8 0.0 collective-permute-done.8
  68.9 1.2 %pad.6 = bf16[152,16,128]{2,1,0:T(8,128)(2,1)S(1)} pad(bf16[150,16,128]{2,1,0:T(8,128)(2,1)} %collective-permute-done.8, bf16[]{:T(256)} %constant.53), padding=0_2x0_0x0_0 | pad | bytes 1236994
  70.0 0.0 copy-done
  70.0 0.2 copy.57
  70.2 0.0 collective-permute-done.9
  70.2 1.2 %pad.7 = bf16[152,16,128]{2,1,0:T(8,128)(2,1)S(1)} pad(bf16[150,16,128]{2,1,0:T(8,128)(2,1)} %collective-permute-done.9, bf16[]{:T(256)} %constant.53), padding=0_2x0_0x0_0 | pad | bytes 1236994
  71.4 0.2 copy.58
  71.6 3.7 %pad_maximum_fusion.own_ref.refs_0_.refs_1_.refs_2_.refs_3_.refs_4_.refs_5_.refs_6_.refs_7_.refs_8_.refs_9_.refs_10_.refs_11_ = bf16[150,12288]{1,0:T(8,128)(2,1)} fusion(bf16[150,2048]{1,0:T(8,128)(2,1)S(1)} %bitcast.77, bf16[150,2048]{1,0:T(8,128)(2,1)S(1)} %bitcast.76, bf16[150,8192]{1,0:T(8,128)(2,1)S(1)} %copy.50), kind=kLoop, calls=%fused_computation.4 | loop fusion | flops 11059200 | bytes 7372800 | tf_op jit(solution)/shard_map/concatenate | solution.py:52
  75.3 24.5 %shard_map.127 = f32[150,8192]{1,0:T(8,128)} custom-call(s32[192]{0:T(256)} %reshape.112.nb_ref, bf16[150,12288]{1,0:T(8,128)(2,1)} %pad_maximum_fusion.own_ref.refs_0_.refs_1_.refs_2_.refs_3_.refs_4_.refs_5_.refs_6_.refs_7_.refs_8_.refs_9_.refs_10_.refs_11_, ...), custom_call_target="tpu_custom_call" | custom-call | tf_op jit(solution)/shard_map/pallas_call | solution.py:166
  (22 shorter events, 0.2 us)
Async XLA Ops:
  0.0 5.7 %copy-start.4 = (s32[1,8,128]{2,1,0:T(8,128)S(1)}, s32[1,8,128]{2,1,0:T(8,128)}, u32[]{:S(2)}) copy-start(s32[1,8,128]{2,1,0:T(8,128)} %param.16) | copy-start | bytes 12292
  0.0 24.1 %copy-start.10 = (s32[1,8]{1,0:T(1,128)S(1)}, s32[1,8]{1,0:T(1,128)}, u32[]{:S(2)}) copy-start(s32[1,8]{1,0:T(1,128)} %param.17) | copy-start | bytes 100
  0.0 24.2 %copy-start.9 = (s32[1,2,16]{2,1,0:T(2,128)S(1)}, s32[1,2,16]{2,1,0:T(2,128)}, u32[]{:S(2)}) copy-start(s32[1,2,16]{2,1,0:T(2,128)} %param.19) | copy-start | bytes 388
  0.0 24.2 %copy-start.5 = (s32[1,8,128]{2,1,0:T(8,128)S(1)}, s32[1,8,128]{2,1,0:T(8,128)}, u32[]{:S(2)}) copy-start(s32[1,8,128]{2,1,0:T(8,128)} %param.18) | copy-start | bytes 12292
  12.2 12.1 %collective-permute-start = (bf16[150,128]{0,1:T(8,128)(2,1)S(1)}, bf16[150,128]{0,1:T(8,128)(2,1)S(1)}, u32[]{:S(2)}, u32[]{:S(2)}) collective-permute-start(bf16[150,128]{0,1:T(8,128)(2,1)S(1)} %get-tuple-element.21), channel_id=1, source_target_pairs={{124,0},{125,1},{126,2},{127,3},{0,4},{1,5},{2,6},{3,7},{4,8},{5,9... | collective-permute-start | bytes 115208 | tf_op jit(solution)/shard_map/ppermute | solution.py:17
  15.4 11.7 %collective-permute-start.1 = (bf16[150,128]{0,1:T(8,128)(2,1)S(1)}, bf16[150,128]{0,1:T(8,128)(2,1)S(1)}, u32[]{:S(2)}, u32[]{:S(2)}) collective-permute-start(bf16[150,128]{0,1:T(8,128)(2,1)S(1)} %get-tuple-element.20), channel_id=1, source_target_pairs={{125,0},{126,1},{127,2},{0,3},{1,4},{2,5},{3,6},{4,7},{5,8},{6,9},... | collective-permute-start | bytes 115208 | tf_op jit(solution)/shard_map/ppermute | solution.py:17
  15.4 12.8 %collective-permute-start.2 = (bf16[150,128]{0,1:T(8,128)(2,1)S(1)}, bf16[150,128]{0,1:T(8,128)(2,1)S(1)}, u32[]{:S(2)}, u32[]{:S(2)}) collective-permute-start(bf16[150,128]{0,1:T(8,128)(2,1)S(1)} %get-tuple-element.19), channel_id=1, source_target_pairs={{126,0},{127,1},{0,2},{1,3},{2,4},{3,5},{4,6},{5,7},{6,8},{7,9},{8... | collective-permute-start | bytes 115208 | tf_op jit(solution)/shard_map/ppermute | solution.py:17
  16.4 14.6 %collective-permute-start.3 = (bf16[150,128]{0,1:T(8,128)(2,1)S(1)}, bf16[150,128]{0,1:T(8,128)(2,1)S(1)}, u32[]{:S(2)}, u32[]{:S(2)}) collective-permute-start(bf16[150,128]{0,1:T(8,128)(2,1)S(1)} %get-tuple-element.18), channel_id=1, source_target_pairs={{127,0},{0,1},{1,2},{2,3},{3,4},{4,5},{5,6},{6,7},{7,8},{8,9},{9,1... | collective-permute-start | bytes 115208 | tf_op jit(solution)/shard_map/ppermute | solution.py:17
  18.6 12.4 %collective-permute-start.4 = (bf16[150,128]{0,1:T(8,128)(2,1)S(1)}, bf16[150,128]{0,1:T(8,128)(2,1)S(1)}, u32[]{:S(2)}, u32[]{:S(2)}) collective-permute-start(bf16[150,128]{0,1:T(8,128)(2,1)S(1)} %get-tuple-element.17), channel_id=1, source_target_pairs={{1,0},{2,1},{3,2},{4,3},{5,4},{6,5},{7,6},{8,7},{9,8},{10,9},{11,1... | collective-permute-start | bytes 115208 | tf_op jit(solution)/shard_map/ppermute | solution.py:17
  24.3 6.7 %collective-permute-start.5 = (bf16[150,128]{0,1:T(8,128)(2,1)S(1)}, bf16[150,128]{0,1:T(8,128)(2,1)S(1)}, u32[]{:S(2)}, u32[]{:S(2)}) collective-permute-start(bf16[150,128]{0,1:T(8,128)(2,1)S(1)} %get-tuple-element.16), channel_id=1, source_target_pairs={{2,0},{3,1},{4,2},{5,3},{6,4},{7,5},{8,6},{9,7},{10,8},{11,9},{12,... | collective-permute-start | bytes 115208 | tf_op jit(solution)/shard_map/ppermute | solution.py:17
  27.1 4.0 %collective-permute-start.6 = (bf16[150,128]{0,1:T(8,128)(2,1)S(1)}, bf16[150,128]{0,1:T(8,128)(2,1)S(1)}, u32[]{:S(2)}, u32[]{:S(2)}) collective-permute-start(bf16[150,128]{0,1:T(8,128)(2,1)S(1)} %get-tuple-element.15), channel_id=1, source_target_pairs={{3,0},{4,1},{5,2},{6,3},{7,4},{8,5},{9,6},{10,7},{11,8},{12,9},{13... | collective-permute-start | bytes 115208 | tf_op jit(solution)/shard_map/ppermute | solution.py:17
  28.1 6.0 %collective-permute-start.7 = (bf16[150,128]{0,1:T(8,128)(2,1)S(1)}, bf16[150,128]{0,1:T(8,128)(2,1)S(1)}, u32[]{:S(2)}, u32[]{:S(2)}) collective-permute-start(bf16[150,128]{0,1:T(8,128)(2,1)S(1)} %get-tuple-element.14), channel_id=1, source_target_pairs={{4,0},{5,1},{6,2},{7,3},{8,4},{9,5},{10,6},{11,7},{12,8},{13,9},{1... | collective-permute-start | bytes 115208 | tf_op jit(solution)/shard_map/ppermute | solution.py:17
  49.5 10.7 %copy-start.1 = (f32[256,150]{0,1:T(8,128)S(1)}, f32[256,150]{0,1:T(8,128)}, u32[]{:S(2)}) copy-start(f32[256,150]{0,1:T(8,128)} %param.23) | copy-start | bytes 460804
  49.5 11.0 %copy-start.7 = (f32[256]{0:T(256)S(1)}, f32[256]{0:T(256)}, u32[]{:S(2)}) copy-start(f32[256]{0:T(256)} %param.24) | copy-start | bytes 3076
  49.6 11.7 %copy-start.8 = (f32[256]{0:T(256)S(1)}, f32[256]{0:T(256)}, u32[]{:S(2)}) copy-start(f32[256]{0:T(256)} %param.25) | copy-start | bytes 3076
  49.6 12.5 %copy-start.6 = (s32[64,3]{0,1:T(4,128)S(1)}, s32[64,3]{0,1:T(4,128)}, u32[]{:S(2)}) copy-start(s32[64,3]{0,1:T(4,128)} %param.20) | copy-start | bytes 2308
  50.3 13.3 %copy-start.2 = (f32[150,256]{1,0:T(8,128)S(1)}, f32[150,256]{1,0:T(8,128)}, u32[]{:S(2)}) copy-start(f32[150,256]{1,0:T(8,128)} %param.27) | copy-start | bytes 460804
  51.3 17.5 %collective-permute-start.8 = (bf16[150,16,128]{2,1,0:T(8,128)(2,1)}, bf16[150,16,128]{2,1,0:T(8,128)(2,1)}, u32[]{:S(2)}, u32[]{:S(2)}) collective-permute-start(bf16[150,16,128]{2,1,0:T(8,128)(2,1)} %copy.47), channel_id=1, source_target_pairs={{127,0},{0,1},{1,2},{2,3},{3,4},{4,5},{5,6},{6,7},{7,8},{8,9},{9,1... | collective-permute-start | bytes 1843208 | tf_op jit(solution)/shard_map/ppermute | solution.py:17
  52.0 11.6 %copy-start.3 = (f32[150,256]{1,0:T(8,128)S(1)}, f32[150,256]{1,0:T(8,128)}, u32[]{:S(2)}) copy-start(f32[150,256]{1,0:T(8,128)} %param.26) | copy-start | bytes 460804
  53.1 17.2 %collective-permute-start.9 = (bf16[150,16,128]{2,1,0:T(8,128)(2,1)}, bf16[150,16,128]{2,1,0:T(8,128)(2,1)}, u32[]{:S(2)}, u32[]{:S(2)}) collective-permute-start(bf16[150,16,128]{2,1,0:T(8,128)(2,1)} %copy.49), channel_id=1, source_target_pairs={{1,0},{2,1},{3,2},{4,3},{5,4},{6,5},{7,6},{8,7},{9,8},{10,9},{11,1... | collective-permute-start | bytes 1843208 | tf_op jit(solution)/shard_map/ppermute | solution.py:17
  60.5 9.5 %copy-start = (bf16[256,150]{1,0:T(8,128)(2,1)}, bf16[256,150]{1,0:T(8,128)(2,1)S(1)}, u32[]{:S(2)}) copy-start(bf16[256,150]{1,0:T(8,128)(2,1)S(1)} %copy.53.refs_14_) | copy-start | bytes 230404
where the time goes:
time: 101 us; the launch traced here: 99.9 us
  local copies, waits for them, and re-layouts  40.4 us (40%)
  starting transfers between devices  25.8 us (26%)
  Pallas kernels  24.5 us (24%)
  other arithmetic  5.74 us (6%)
  waiting for transfers between devices  3.1 us (3%)
    ppermute x10, starting transfers between devices, from_behind(): return lax.ppermute(block, axis, route)  25.8 us
    pallas_call x1, Pallas kernels, mix_react(): pl.pallas_call(kernel, grid_spec=grid_spec, out_shape=jax.ShapeDtypeStruc...  24.5 us
    scatter x2, local copies, waits for them, and re-layouts, migrate(): mixing_ratio.at[:, target_slot.reshape(-1)]  14.4 us
    unnamed x36, local copies, waits for them, and re-layouts  8.71 us
    gather x1, local copies, waits for them, and re-layouts, migrate(): jnp.take(mixing_ratio, send_rows[0].reshape(-1), axis=1)  6.19 us
    reshape x1, local copies, waits for them, and re-layouts, block_table(): blocks = migrated.reshape(species, parcels // block_size, block_size)  5.43 us
    concatenate x1, other arithmetic, block_table(): jnp.concatenate([migrated, from_lower.reshape(species, -1), from_upper.re...  3.74 us
    ppermute x10, waiting for transfers between devices, from_behind(): return lax.ppermute(block, axis, route)  3.1 us
  transfers between devices with their start and end apart: 10, of which 1 were waited for; matrix products, arithmetic and copies ran while one was open for 12% of the time, Pallas kernels for 0%

commit v1 on v0

--- a/solution.py
+++ b/solution.py
@@ -21,25 +21,35 @@
     return [column - HOP if column < HOP else column - HOP + 1 for column in range(2 * HOP)]
 
 
+def one_hot(rows, size, axis):
+    positions = lax.broadcasted_iota(jnp.int32, (size, rows.shape[0]), 0)
+    if axis == 0:
+        return (positions == rows[None, :]).astype(jnp.bfloat16)
+    return (positions.T == rows[:, None]).astype(jnp.bfloat16)
+
+
 def migrate(mixing_ratio, send_rows, migrant_count, arrival_slot):
     species, parcels = mixing_ratio.shape
     capacity = send_rows.shape[-1]
     offsets = peer_offsets()
     peer_count = len(offsets)
-    outgoing = jnp.take(mixing_ratio, send_rows[0].reshape(-1), axis=1).reshape(
-        species, peer_count, capacity
-    )
+    f32 = jnp.float32
+    pick = one_hot(send_rows[0].reshape(-1), parcels, 0)
+    outgoing = jnp.dot(mixing_ratio, pick, preferred_element_type=f32).astype(jnp.bfloat16)
+    outgoing = outgoing.reshape(species, peer_count, capacity)
     arrived = []
     for column in range(peer_count):
         opposite = peer_count - 1 - column
         arrived.append(from_behind(outgoing[:, opposite, :], "region", -offsets[column]))
-    received = jnp.stack(arrived, axis=1)
+    received = jnp.stack(arrived, axis=1).reshape(species, -1)
     lane_index = jnp.arange(capacity, dtype=jnp.int32)
     live_lane = lane_index[None, :] < migrant_count[0][:, None]
-    target_slot = jnp.where(live_lane, arrival_slot[0], parcels)
-    return mixing_ratio.at[:, target_slot.reshape(-1)].set(
-        received.reshape(species, -1), mode="drop"
-    )
+    target_slot = jnp.where(live_lane, arrival_slot[0], parcels).reshape(-1)
+    place = one_hot(target_slot, parcels, 1)
+    marked = jnp.concatenate([received, jnp.ones((1, received.shape[1]), received.dtype)], axis=0)
+    placed = jnp.dot(marked, place, preferred_element_type=f32)
+    hit = placed[species:] > 0.5
+    return jnp.where(hit, placed[:species].astype(jnp.bfloat16), mixing_ratio)
 
 
 def block_table(migrated, halo_blocks, block_size):
@@ -78,18 +88,25 @@
     (
         weight_ref,
         temp_ref,
-        order_high,
-        order_low,
-        prefactor_ref,
-        energy_ref,
-        prod_high,
-        prod_low,
-        loss_high,
-        loss_low,
+        order_ref,
+        rate_terms_ref,
+        prod_ref,
+        loss_ref,
         out_ref,
         mixed_ref,
+        order_split,
+        prod_split,
+        loss_split,
     ) = refs[count:]
     f32 = jnp.float32
+
+    @pl.when(pl.program_id(0) == 0)
+    def _():
+        for source, target in ((order_ref, order_split), (prod_ref, prod_split), (loss_ref, loss_split)):
+            high, low = split3(source[...])
+            target[0] = high
+            target[1] = low
+
     for t in range(tile_blocks):
         lanes = slice(t * block_size, (t + 1) * block_size)
         acc = jnp.dot(own_ref[:, lanes], weight_ref[t, 0], preferred_element_type=f32)
@@ -100,11 +117,13 @@
         mixed_ref[:, lanes] = acc
     mixed = mixed_ref[...]
     log_high, log_low = split3(jnp.log(mixed))
-    exponent = dot3(order_high[...], order_low[...], log_high, log_low)
-    rate = jnp.exp(prefactor_ref[...] - energy_ref[...] * temp_ref[...] + exponent)
+    exponent = dot3(order_split[0], order_split[1], log_high, log_low)
+    prefactor = rate_terms_ref[:, 0:1]
+    energy = rate_terms_ref[:, 1:2]
+    rate = jnp.exp(prefactor - energy * temp_ref[...] + exponent)
     rate_high, rate_low = split3(rate)
-    gained = dot3(prod_high[...], prod_low[...], rate_high, rate_low)
-    lost_mass = dot3(loss_high[...], loss_low[...], rate_high, rate_low)
+    gained = dot3(prod_split[0], prod_split[1], rate_high, rate_low)
+    lost_mass = dot3(loss_split[0], loss_split[1], rate_high, rate_low)
     out_ref[...] = (mixed + gained) / (1.0 + lost_mass / mixed)
 
 
@@ -130,15 +149,12 @@
     def picked_spec(t, k):
         return pl.BlockSpec(
             (species, block_size),
-            lambda i, nb: (0, nb[(i * tile_blocks + t) * neighbours + k]),
+            lambda i, nb: (0, nb[i * tile_blocks + t, k]),
         )
 
     def whole(shape):
         return pl.BlockSpec(shape, lambda i, nb: (0,) * len(shape))
 
-    order_high, order_low = split3(reactant_order)
-    prod_high, prod_low = split3(production)
-    loss_high, loss_low = split3(loss_coefficient)
     in_specs = (
         [pl.BlockSpec((species, width), lambda i, nb: (0, i))]
         + [picked_spec(t, k) for t in range(tile_blocks) for k in range(neighbours)]
@@ -146,21 +162,23 @@
             pl.BlockSpec((tile_blocks,) + mix_weight.shape[1:], lambda i, nb: (i, 0, 0, 0)),
             pl.BlockSpec((1, width), lambda i, nb: (0, i)),
             whole(reactant_order.shape),
-            whole(reactant_order.shape),
-            whole((reactions, 1)),
-            whole((reactions, 1)),
-            whole(production.shape),
+            whole((reactions, 2)),
             whole(production.shape),
             whole(loss_coefficient.shape),
-            whole(loss_coefficient.shape),
         ]
     )
+    bf16 = jnp.bfloat16
     grid_spec = pltpu.PrefetchScalarGridSpec(
         num_scalar_prefetch=1,
         grid=(steps,),
         in_specs=in_specs,
         out_specs=pl.BlockSpec((species, width), lambda i, nb: (0, i)),
-        scratch_shapes=[pltpu.VMEM((species, width), jnp.float32)],
+        scratch_shapes=[
+            pltpu.VMEM((species, width), jnp.float32),
+            pltpu.VMEM((2,) + reactant_order.shape, bf16),
+            pltpu.VMEM((2,) + production.shape, bf16),
+            pltpu.VMEM((2,) + loss_coefficient.shape, bf16),
+        ],
     )
     kernel = functools.partial(mix_react_kernel, tile_blocks, neighbours, block_size)
     return pl.pallas_call(
@@ -169,19 +187,15 @@
         out_shape=jax.ShapeDtypeStruct((species, count_blocks * block_size), jnp.float32),
         compiler_params=pltpu.CompilerParams(dimension_semantics=("arbitrary",)),
     )(
-        neighbour_block.reshape(-1),
+        neighbour_block,
         table,
         *([table] * (tile_blocks * neighbours)),
         mix_weight,
         inverse_temp.reshape(1, -1),
-        order_high,
-        order_low,
-        log_prefactor.reshape(-1, 1),
-        activation_energy.reshape(-1, 1),
-        prod_high,
-        prod_low,
-        loss_high,
-        loss_low,
+        reactant_order,
+        jnp.stack([log_prefactor, activation_energy], axis=1),
+        production,
+        loss_coefficient,
     )
 
 

time: 101 us -> 98.4 us (0.974)
  local copies, waits for them, and re-layouts: 40.4 us -> 16.4 us
  matrix products: 0 us -> 14.3 us
  waiting for transfers between devices: 3.1 us -> 14 us
  starting transfers between devices: 25.8 us -> 22.3 us
    scatter x2 -> x0, local copies, waits for them, and re-layouts: 14.4 us -> none  [migrate(): mixing_ratio.at[:, target_slot.reshape(-1)]]
    dot_general x0 -> x2, matrix products: none -> 14.3 us  [the longest x1 7.35 us: migrate(): jnp.dot(mixing_ratio, pick, preferred_element_type=f32).astype(jnp.bfloat16)]
    ppermute x10, waiting for transfers between devices: 3.1 us -> 14 us  [from_behind(): return lax.ppermute(block, axis, route)]
    gather x1 -> x0, local copies, waits for them, and re-layouts: 6.19 us -> none  [migrate(): jnp.take(mixing_ratio, send_rows[0].reshape(-1), axis=1)]
    unnamed x36 -> x41, local copies, waits for them, and re-layouts: 8.71 us -> 4.1 us
    ppermute x10, starting transfers between devices: 25.8 us -> 22.3 us  [from_behind(): return lax.ppermute(block, axis, route)]
    gather x1, local copies, waits for them, and re-layouts: 0.67 us -> 3.22 us  [block_table(): to_lower = jnp.take(blocks, halo_blocks[0, 0], axis=1)]
    reshape x3 -> x0, local copies, waits for them, and re-layouts: 2.31 us -> none  [the longest x1 0.81 us: mix_react(): activation_energy.reshape(-1, 1)]
  transfers between devices with their start and end apart: 10 -> 10, of which waited for: 1 -> 3; matrix products, arithmetic and copies ran while one was open for 12% -> 5% of each run, Pallas kernels for 0% -> 0%
where the time goes in v1:
time: 98.4 us; the launch traced here: 97.9 us
  Pallas kernels  24.9 us (25%)
  starting transfers between devices  22.3 us (23%)
  local copies, waits for them, and re-layouts  16.4 us (17%)
  matrix products  14.3 us (15%)
  waiting for transfers between devices  14 us (14%)
  other arithmetic  5.58 us (6%)
    pallas_call x1, Pallas kernels, mix_react(): pl.pallas_call(kernel, grid_spec=grid_spec, out_shape=jax.ShapeDtypeStruc...  24.9 us
    ppermute x10, starting transfers between devices, from_behind(): return lax.ppermute(block, axis, route)  22.3 us
    ppermute x10, waiting for transfers between devices, from_behind(): return lax.ppermute(block, axis, route)  14 us
    dot_general x1, matrix products, migrate(): jnp.dot(mixing_ratio, pick, preferred_element_type=f32).astype(jnp.bfloat16)  7.35 us
    dot_general x1, matrix products, migrate(): placed = jnp.dot(marked, place, preferred_element_type=f32)  6.96 us
    unnamed x41, local copies, waits for them, and re-layouts  4.1 us
    concatenate x1, other arithmetic, block_table(): jnp.concatenate([migrated, from_lower.reshape(species, -1), from_upper.re...  3.7 us
    reshape x2, local copies, waits for them, and re-layouts, block_table(): blocks = migrated.reshape(species, parcels // block_size, block_size)  3.55 us
  transfers between devices with their start and end apart: 10, of which 3 were waited for; matrix products, arithmetic and copies ran while one was open for 5% of the time, Pallas kernels for 0%

profile of v1, /device:TPU:0, one launch (start us, length us, event | category | flops | bytes accessed | tf_op | source)
XLA Modules:
  0.0 97.9 jit_solution(14288445898705984591)
XLA Ops:
  0.0 0.0 copy-start.4
  0.0 0.0 copy-start.2
  0.0 0.0 copy-start.7
  0.0 7.3 %fusion.5 = bf16[1024,150]{0,1:T(8,128)(2,1)S(1)} fusion(bf16[150,8192]{1,0:T(8,128)(2,1)} %param.15, s32[1024]{0:T(1024)} %bitcast.100), kind=kOutput, calls=%fused_computation.11 | convolution fusion | flops 2525124608 | bytes 2768896 | tf_op jit(solution)/shard_map/dot_general | solution.py:38
  7.4 0.1 copy.64
  7.4 0.5 fusion.9
  8.0 3.2 %collective-permute-start = (bf16[150,128]{1,0:T(8,128)(2,1)S(1)}, bf16[150,128]{1,0:T(8,128)(2,1)S(1)}, u32[]{:S(2)}, u32[]{:S(2)}) collective-permute-start(bf16[150,128]{1,0:T(8,128)(2,1)S(1)} %bitcast.95), channel_id=1, source_target_pairs={{124,0},{125,1},{126,2},{127,3},{0,4},{1,5},{2,6},{3,7},{4,8},{5,9... | collective-permute-start | bytes 115208 | tf_op jit(solution)/shard_map/ppermute | solution.py:17
  11.1 0.1 collective-permute-start.1
  11.2 1.0 %collective-permute-start.2 = (bf16[150,128]{1,0:T(8,128)(2,1)S(1)}, bf16[150,128]{1,0:T(8,128)(2,1)S(1)}, u32[]{:S(2)}, u32[]{:S(2)}) collective-permute-start(bf16[150,128]{1,0:T(8,128)(2,1)S(1)} %bitcast.92), channel_id=1, source_target_pairs={{126,0},{127,1},{0,2},{1,3},{2,4},{3,5},{4,6},{5,7},{6,8},{7,9},{8... | collective-permute-start | bytes 115208 | tf_op jit(solution)/shard_map/ppermute | solution.py:17
  12.3 2.3 %collective-permute-start.3 = (bf16[150,128]{1,0:T(8,128)(2,1)S(1)}, bf16[150,128]{1,0:T(8,128)(2,1)S(1)}, u32[]{:S(2)}, u32[]{:S(2)}) collective-permute-start(bf16[150,128]{1,0:T(8,128)(2,1)S(1)} %bitcast.90), channel_id=1, source_target_pairs={{127,0},{0,1},{1,2},{2,3},{3,4},{4,5},{5,6},{6,7},{7,8},{8,9},{9,1... | collective-permute-start | bytes 115208 | tf_op jit(solution)/shard_map/ppermute | solution.py:17
  14.6 5.7 %collective-permute-start.4 = (bf16[150,128]{1,0:T(8,128)(2,1)S(1)}, bf16[150,128]{1,0:T(8,128)(2,1)S(1)}, u32[]{:S(2)}, u32[]{:S(2)}) collective-permute-start(bf16[150,128]{1,0:T(8,128)(2,1)S(1)} %bitcast.89), channel_id=1, source_target_pairs={{1,0},{2,1},{3,2},{4,3},{5,4},{6,5},{7,6},{8,7},{9,8},{10,9},{11,1... | collective-permute-start | bytes 115208 | tf_op jit(solution)/shard_map/ppermute | solution.py:17
  20.2 0.0 copy-done.4
  20.3 0.0 copy-done.2
  20.3 0.0 copy-done.7
  20.3 0.1 bitcast_select_fusion
  20.4 0.0 collective-permute-done
  20.4 1.9 %collective-permute-start.5 = (bf16[150,128]{1,0:T(8,128)(2,1)S(1)}, bf16[150,128]{1,0:T(8,128)(2,1)S(1)}, u32[]{:S(2)}, u32[]{:S(2)}) collective-permute-start(bf16[150,128]{1,0:T(8,128)(2,1)S(1)} %bitcast.94), channel_id=1, source_target_pairs={{2,0},{3,1},{4,2},{5,3},{6,4},{7,5},{8,6},{9,7},{10,8},{11,9},{12,... | collective-permute-start | bytes 115208 | tf_op jit(solution)/shard_map/ppermute | solution.py:17
  22.3 0.0 collective-permute-done.1
  22.3 0.2 collective-permute-start.6
  22.5 0.0 collective-permute-done.2
  22.5 3.5 %collective-permute-start.7 = (bf16[150,128]{1,0:T(8,128)(2,1)S(1)}, bf16[150,128]{1,0:T(8,128)(2,1)S(1)}, u32[]{:S(2)}, u32[]{:S(2)}) collective-permute-start(bf16[150,128]{1,0:T(8,128)(2,1)S(1)} %bitcast.88), channel_id=1, source_target_pairs={{4,0},{5,1},{6,2},{7,3},{8,4},{9,5},{10,6},{11,7},{12,8},{13,9},{1... | collective-permute-start | bytes 115208 | tf_op jit(solution)/shard_map/ppermute | solution.py:17
  26.0 0.0 collective-permute-done.3
  26.0 0.0 collective-permute-done.4
  26.1 0.0 collective-permute-done.5
  26.1 0.0 collective-permute-done.6
  26.1 2.4 %collective-permute-done.7 = bf16[150,128]{1,0:T(8,128)(2,1)S(1)} collective-permute-done((bf16[150,128]{1,0:T(8,128)(2,1)S(1)}, bf16[150,128]{1,0:T(8,128)(2,1)S(1)}, u32[]{:S(2)}, u32[]{:S(2)}) %collective-permute-start.7) | collective-permute-done | bytes 38432 | tf_op jit(solution)/shard_map/ppermute | solution.py:17
  28.7 0.0 copy-start
  28.7 7.0 %fusion = f32[151,8192]{1,0:T(8,128)S(1)} fusion(s32[1024]{0:T(1024)S(1)} %bitcast_select_fusion, bf16[150,1024]{1,0:T(8,128)(2,1)S(1)} %bitcast.86), kind=kOutput, calls=%fused_computation.4 | convolution fusion | flops 2541748224 | bytes 5259264 | tf_op jit(solution)/shard_map/dot_general | solution.py:50
  35.7 0.1 compare_reduce_fusion
  35.8 0.0 copy-done
  35.8 0.3 fusion.4
  36.2 0.7 copy.66
  36.8 0.5 slice.64
  37.4 3.0 %copy.49 = bf16[150,64,128]{2,0,1:T(8,128)(2,1)} copy(bf16[150,64,128]{2,1,0:T(8,128)(2,1)S(1)} %slice.64) | data formatting | bytes 4915200 | tf_op jit(solution)/shard_map/reshape | solution.py:57
  40.4 0.0 copy-start.3
  40.4 0.0 copy-start.5
  40.4 0.0 copy-start.6
  40.4 0.0 copy-start.1
  40.4 3.2 %gather_fusion.1 = bf16[16,150,128]{2,1,0:T(8,128)(2,1)} fusion(bf16[150,64,128]{2,0,1:T(8,128)(2,1)} %copy.49, s32[1024]{0:T(1024)S(1)} %pad_clamp_fusion), kind=kCustom, calls=%fused_computation.1.clone | custom fusion | bytes 1228864 | tf_op jit(solution)/shard_map/jit(_take)/gather | solution.py:58
  43.6 2.4 %gather_fusion = bf16[16,150,128]{2,1,0:T(8,128)(2,1)S(1)} fusion(bf16[150,64,128]{2,0,1:T(8,128)(2,1)} %copy.49, s32[1024]{0:T(1024)S(1)} %pad_clamp_fusion.1), kind=kCustom, calls=%fused_computation.clone | custom fusion | bytes 1228864 | tf_op jit(solution)/shard_map/jit(_take)/gather | solution.py:59
  46.0 1.2 %select_bitcast_fusion = bf16[150,16,128]{2,0,1:T(8,128)(2,1)S(1)} fusion(bf16[16,150,128]{2,1,0:T(8,128)(2,1)} %gather_fusion.1, pred[16]{0:T(512)(128)(4,1)S(1)} %get-tuple-element.18), kind=kLoop, calls=%fused_computation.12 | loop fusion | flops 307200 | bytes 1228816 | tf_op jit(solution)/shard_map/jit(_take)/select_n | solution.py:58
  47.2 0.9 copy.52
  48.1 4.5 %collective-permute-start.9 = (bf16[150,16,128]{2,1,0:T(8,128)(2,1)}, bf16[150,16,128]{2,1,0:T(8,128)(2,1)}, u32[]{:S(2)}, u32[]{:S(2)}) collective-permute-start(bf16[150,16,128]{2,1,0:T(8,128)(2,1)} %copy.52), channel_id=1, source_target_pairs={{1,0},{2,1},{3,2},{4,3},{5,4},{6,5},{7,6},{8,7},{9,8},{10,9},{11,1... | collective-permute-start | bytes 1843208 | tf_op jit(solution)/shard_map/ppermute | solution.py:17
  52.7 0.1 select_bitcast_fusion.1
  52.8 0.9 copy.50
  53.7 0.0 collective-permute-start.8
  53.7 0.0 copy-done.3
  53.7 0.7 copy.53.nb_ref
  54.4 0.0 copy-done.5
  54.4 0.0 copy-done.6
  54.4 0.8 copy.55.refs_15_
  55.2 0.0 copy-done.1
  55.2 0.8 copy.54.refs_14_
  56.1 4.6 %collective-permute-done.9 = bf16[150,16,128]{2,1,0:T(8,128)(2,1)} collective-permute-done((bf16[150,16,128]{2,1,0:T(8,128)(2,1)}, bf16[150,16,128]{2,1,0:T(8,128)(2,1)}, u32[]{:S(2)}, u32[]{:S(2)}) %collective-permute-start.9) | collective-permute-done | bytes 614432 | tf_op jit(solution)/shard_map/ppermute | solution.py:17
  60.6 1.2 %pad.10 = bf16[152,16,128]{2,1,0:T(8,128)(2,1)S(1)} pad(bf16[150,16,128]{2,1,0:T(8,128)(2,1)} %collective-permute-done.9, bf16[]{:T(256)} %constant.41), padding=0_2x0_0x0_0 | pad | bytes 1236994
  61.8 0.2 copy.68
  62.0 6.9 %collective-permute-done.8 = bf16[150,16,128]{2,1,0:T(8,128)(2,1)S(1)} collective-permute-done((bf16[150,16,128]{2,1,0:T(8,128)(2,1)}, bf16[150,16,128]{2,1,0:T(8,128)(2,1)S(1)}, u32[]{:S(2)}, u32[]{:S(2)}) %collective-permute-start.8) | collective-permute-done | bytes 614432 | tf_op jit(solution)/shard_map/ppermute | solution.py:17
  68.9 0.1 pad.9
  69.0 0.2 copy.67
  69.2 3.7 %pad_maximum_fusion.own_ref.refs_0_.refs_1_.refs_2_.refs_3_.refs_4_.refs_5_.refs_6_.refs_7_.refs_8_.refs_9_.refs_10_.refs_11_ = bf16[150,12288]{1,0:T(8,128)(2,1)} fusion(bf16[150,2048]{1,0:T(8,128)(2,1)S(1)} %bitcast.81, bf16[150,2048]{1,0:T(8,128)(2,1)S(1)} %bitcast.82, bf16[150,8192]{1,0:T(8,128)(2,1)S(1)} %fusion.4), kind=kLoop, calls=%fused_computation.9 | loop fusion | flops 11059200 | bytes 7372800 | tf_op jit(solution)/shard_map/concatenate | solution.py:62
  72.9 24.9 %shard_map.127 = f32[150,8192]{1,0:T(8,128)} custom-call(s32[64,3]{1,0:T(8,128)} %copy.53.nb_ref, bf16[150,12288]{1,0:T(8,128)(2,1)} %pad_maximum_fusion.own_ref.refs_0_.refs_1_.refs_2_.refs_3_.refs_4_.refs_5_.refs_6_.refs_7_.refs_8_.refs_9_.refs_10_.refs_11_, ...), custom_call_target="tpu_custom_call" | custom-call | tf_op jit(solution)/shard_map/pallas_call | solution.py:184
  (23 shorter events, 0.3 us)
Async XLA Ops:
  0.0 20.2 %copy-start.4 = (s32[1,2,16]{2,1,0:T(2,128)S(1)}, s32[1,2,16]{2,1,0:T(2,128)}, u32[]{:S(2)}) copy-start(s32[1,2,16]{2,1,0:T(2,128)} %param.19) | copy-start | bytes 388
  0.0 20.3 %copy-start.2 = (s32[1,8,128]{2,1,0:T(8,128)S(1)}, s32[1,8,128]{2,1,0:T(8,128)}, u32[]{:S(2)}) copy-start(s32[1,8,128]{2,1,0:T(8,128)} %param.18) | copy-start | bytes 12292
  0.0 20.3 %copy-start.7 = (s32[1,8]{1,0:T(1,128)S(1)}, s32[1,8]{1,0:T(1,128)}, u32[]{:S(2)}) copy-start(s32[1,8]{1,0:T(1,128)} %param.17) | copy-start | bytes 100
  8.0 12.4 %collective-permute-start = (bf16[150,128]{1,0:T(8,128)(2,1)S(1)}, bf16[150,128]{1,0:T(8,128)(2,1)S(1)}, u32[]{:S(2)}, u32[]{:S(2)}) collective-permute-start(bf16[150,128]{1,0:T(8,128)(2,1)S(1)} %bitcast.95), channel_id=1, source_target_pairs={{124,0},{125,1},{126,2},{127,3},{0,4},{1,5},{2,6},{3,7},{4,8},{5,9... | collective-permute-start | bytes 115208 | tf_op jit(solution)/shard_map/ppermute | solution.py:17
  11.1 11.1 %collective-permute-start.1 = (bf16[150,128]{1,0:T(8,128)(2,1)S(1)}, bf16[150,128]{1,0:T(8,128)(2,1)S(1)}, u32[]{:S(2)}, u32[]{:S(2)}) collective-permute-start(bf16[150,128]{1,0:T(8,128)(2,1)S(1)} %bitcast.93), channel_id=1, source_target_pairs={{125,0},{126,1},{127,2},{0,3},{1,4},{2,5},{3,6},{4,7},{5,8},{6,9},... | collective-permute-start | bytes 115208 | tf_op jit(solution)/shard_map/ppermute | solution.py:17
  11.2 11.3 %collective-permute-start.2 = (bf16[150,128]{1,0:T(8,128)(2,1)S(1)}, bf16[150,128]{1,0:T(8,128)(2,1)S(1)}, u32[]{:S(2)}, u32[]{:S(2)}) collective-permute-start(bf16[150,128]{1,0:T(8,128)(2,1)S(1)} %bitcast.92), channel_id=1, source_target_pairs={{126,0},{127,1},{0,2},{1,3},{2,4},{3,5},{4,6},{5,7},{6,8},{7,9},{8... | collective-permute-start | bytes 115208 | tf_op jit(solution)/shard_map/ppermute | solution.py:17
  12.3 13.8 %collective-permute-start.3 = (bf16[150,128]{1,0:T(8,128)(2,1)S(1)}, bf16[150,128]{1,0:T(8,128)(2,1)S(1)}, u32[]{:S(2)}, u32[]{:S(2)}) collective-permute-start(bf16[150,128]{1,0:T(8,128)(2,1)S(1)} %bitcast.90), channel_id=1, source_target_pairs={{127,0},{0,1},{1,2},{2,3},{3,4},{4,5},{5,6},{6,7},{7,8},{8,9},{9,1... | collective-permute-start | bytes 115208 | tf_op jit(solution)/shard_map/ppermute | solution.py:17
  14.6 11.5 %collective-permute-start.4 = (bf16[150,128]{1,0:T(8,128)(2,1)S(1)}, bf16[150,128]{1,0:T(8,128)(2,1)S(1)}, u32[]{:S(2)}, u32[]{:S(2)}) collective-permute-start(bf16[150,128]{1,0:T(8,128)(2,1)S(1)} %bitcast.89), channel_id=1, source_target_pairs={{1,0},{2,1},{3,2},{4,3},{5,4},{6,5},{7,6},{8,7},{9,8},{10,9},{11,1... | collective-permute-start | bytes 115208 | tf_op jit(solution)/shard_map/ppermute | solution.py:17
  20.4 5.7 %collective-permute-start.5 = (bf16[150,128]{1,0:T(8,128)(2,1)S(1)}, bf16[150,128]{1,0:T(8,128)(2,1)S(1)}, u32[]{:S(2)}, u32[]{:S(2)}) collective-permute-start(bf16[150,128]{1,0:T(8,128)(2,1)S(1)} %bitcast.94), channel_id=1, source_target_pairs={{2,0},{3,1},{4,2},{5,3},{6,4},{7,5},{8,6},{9,7},{10,8},{11,9},{12,... | collective-permute-start | bytes 115208 | tf_op jit(solution)/shard_map/ppermute | solution.py:17
  22.3 3.8 %collective-permute-start.6 = (bf16[150,128]{1,0:T(8,128)(2,1)S(1)}, bf16[150,128]{1,0:T(8,128)(2,1)S(1)}, u32[]{:S(2)}, u32[]{:S(2)}) collective-permute-start(bf16[150,128]{1,0:T(8,128)(2,1)S(1)} %bitcast.91), channel_id=1, source_target_pairs={{3,0},{4,1},{5,2},{6,3},{7,4},{8,5},{9,6},{10,7},{11,8},{12,9},{13... | collective-permute-start | bytes 115208 | tf_op jit(solution)/shard_map/ppermute | solution.py:17
  22.5 6.0 %collective-permute-start.7 = (bf16[150,128]{1,0:T(8,128)(2,1)S(1)}, bf16[150,128]{1,0:T(8,128)(2,1)S(1)}, u32[]{:S(2)}, u32[]{:S(2)}) collective-permute-start(bf16[150,128]{1,0:T(8,128)(2,1)S(1)} %bitcast.88), channel_id=1, source_target_pairs={{4,0},{5,1},{6,2},{7,3},{8,4},{9,5},{10,6},{11,7},{12,8},{13,9},{1... | collective-permute-start | bytes 115208 | tf_op jit(solution)/shard_map/ppermute | solution.py:17
  28.7 7.1 %copy-start = (bf16[150,8192]{1,0:T(8,128)(2,1)S(1)}, bf16[150,8192]{1,0:T(8,128)(2,1)}, u32[]{:S(2)}) copy-start(bf16[150,8192]{1,0:T(8,128)(2,1)} %param.15) | copy-start | bytes 7372804
  40.4 13.3 %copy-start.3 = (s32[64,3]{0,1:T(4,128)S(1)}, s32[64,3]{0,1:T(4,128)}, u32[]{:S(2)}) copy-start(s32[64,3]{0,1:T(4,128)} %param.20) | copy-start | bytes 2308
  40.4 14.0 %copy-start.5 = (f32[256]{0:T(256)S(1)}, f32[256]{0:T(256)}, u32[]{:S(2)}) copy-start(f32[256]{0:T(256)} %param.25) | copy-start | bytes 3076
  40.4 14.0 %copy-start.6 = (f32[256]{0:T(256)S(1)}, f32[256]{0:T(256)}, u32[]{:S(2)}) copy-start(f32[256]{0:T(256)} %param.24) | copy-start | bytes 3076
  40.4 14.8 %copy-start.1 = (f32[256,150]{0,1:T(8,128)S(1)}, f32[256,150]{0,1:T(8,128)}, u32[]{:S(2)}) copy-start(f32[256,150]{0,1:T(8,128)} %param.23) | copy-start | bytes 460804
  48.1 12.5 %collective-permute-start.9 = (bf16[150,16,128]{2,1,0:T(8,128)(2,1)}, bf16[150,16,128]{2,1,0:T(8,128)(2,1)}, u32[]{:S(2)}, u32[]{:S(2)}) collective-permute-start(bf16[150,16,128]{2,1,0:T(8,128)(2,1)} %copy.52), channel_id=1, source_target_pairs={{1,0},{2,1},{3,2},{4,3},{5,4},{6,5},{7,6},{8,7},{9,8},{10,9},{11,1... | collective-permute-start | bytes 1843208 | tf_op jit(solution)/shard_map/ppermute | solution.py:17
  53.7 15.2 %collective-permute-start.8 = (bf16[150,16,128]{2,1,0:T(8,128)(2,1)}, bf16[150,16,128]{2,1,0:T(8,128)(2,1)S(1)}, u32[]{:S(2)}, u32[]{:S(2)}) collective-permute-start(bf16[150,16,128]{2,1,0:T(8,128)(2,1)} %copy.50), channel_id=1, source_target_pairs={{127,0},{0,1},{1,2},{2,3},{3,4},{4,5},{5,6},{6,7},{7,8},{8,9},{9,1... | collective-permute-start | bytes 1843208 | tf_op jit(solution)/shard_map/ppermute | solution.py:17

commit v2 on v1

--- a/solution.py
+++ b/solution.py
@@ -52,21 +52,41 @@
     return jnp.where(hit, placed[:species].astype(jnp.bfloat16), mixing_ratio)
 
 
-def block_table(migrated, halo_blocks, block_size):
-    species, parcels = migrated.shape
-    blocks = migrated.reshape(species, parcels // block_size, block_size)
-    to_lower = jnp.take(blocks, halo_blocks[0, 0], axis=1)
-    to_upper = jnp.take(blocks, halo_blocks[0, 1], axis=1)
-    from_lower = from_behind(to_upper, "region", 1)
-    from_upper = from_behind(to_lower, "region", -1)
-    return jnp.concatenate(
-        [
-            migrated,
-            from_lower.reshape(species, -1),
-            from_upper.reshape(species, -1),
-        ],
-        axis=1,
-    )
+def halo_kernel(block_size, halo_ref, migrated_hbm, out_hbm, sems):
+    sides, listed = halo_ref.shape
+    copies = []
+    for side in range(sides):
+        for j in range(listed):
+            start = pl.multiple_of(halo_ref[side, j] * block_size, block_size)
+            copy = pltpu.make_async_copy(
+                migrated_hbm.at[:, pl.ds(start, block_size)],
+                out_hbm.at[side, :, pl.ds(j * block_size, block_size)],
+                sems.at[side, j],
+            )
+            copy.start()
+            copies.append(copy)
+    for copy in copies:
+        copy.wait()
+
+
+def halo_exchange(migrated, halo_blocks, block_size):
+    species = migrated.shape[0]
+    sides, listed = halo_blocks.shape[1:]
+    grid_spec = pltpu.PrefetchScalarGridSpec(
+        num_scalar_prefetch=1,
+        grid=(1,),
+        in_specs=[pl.BlockSpec(memory_space=pl.ANY)],
+        out_specs=pl.BlockSpec(memory_space=pl.ANY),
+        scratch_shapes=[pltpu.SemaphoreType.DMA((sides, listed))],
+    )
+    listed_blocks = pl.pallas_call(
+        functools.partial(halo_kernel, block_size),
+        grid_spec=grid_spec,
+        out_shape=jax.ShapeDtypeStruct((sides, species, listed * block_size), migrated.dtype),
+    )(halo_blocks[0], migrated)
+    from_lower = from_behind(listed_blocks[1], "region", 1)
+    from_upper = from_behind(listed_blocks[0], "region", -1)
+    return from_lower, from_upper
 
 
 def split3(x):
@@ -82,37 +102,86 @@
     return total + jnp.dot(a_low, b_high, preferred_element_type=f32)
 
 
-def mix_react_kernel(tile_blocks, neighbours, block_size, nb_ref, own_ref, *refs):
-    count = tile_blocks * neighbours
-    picked = refs[:count]
-    (
-        weight_ref,
-        temp_ref,
-        order_ref,
-        rate_terms_ref,
-        prod_ref,
-        loss_ref,
-        out_ref,
-        mixed_ref,
-        order_split,
-        prod_split,
-        loss_split,
-    ) = refs[count:]
+def mix_react_kernel(
+    tile_blocks,
+    neighbours,
+    block_size,
+    nb_ref,
+    own_ref,
+    weight_ref,
+    temp_ref,
+    order_ref,
+    rate_terms_ref,
+    prod_ref,
+    loss_ref,
+    migrated_hbm,
+    lower_hbm,
+    upper_hbm,
+    out_ref,
+    picked,
+    sems,
+    mixed_ref,
+    order_split,
+    prod_split,
+    loss_split,
+):
     f32 = jnp.float32
-
-    @pl.when(pl.program_id(0) == 0)
+    step = pl.program_id(0)
+    steps = pl.num_programs(0)
+    own_count = migrated_hbm.shape[1] // block_size
+    halo_count = lower_hbm.shape[1] // block_size
+
+    def fetch(at, slot, start):
+        for t in range(tile_blocks):
+            for k in range(neighbours):
+                index = nb_ref[at * tile_blocks + t, k]
+                target = picked.at[slot, t * neighbours + k]
+                sem = sems.at[slot, t * neighbours + k]
+                if not start:
+                    pltpu.make_async_copy(
+                        migrated_hbm.at[:, pl.ds(0, block_size)], target, sem
+                    ).wait()
+                    continue
+                sources = (
+                    (migrated_hbm, index, index < own_count),
+                    (lower_hbm, index - own_count,
+                     (index >= own_count) & (index < own_count + halo_count)),
+                    (upper_hbm, index - own_count - halo_count,
+                     index >= own_count + halo_count),
+                )
+                for source, local, chosen in sources:
+                    limit = source.shape[1] // block_size - 1
+                    local = jnp.minimum(jnp.maximum(local, 0), limit)
+
+                    @pl.when(chosen)
+                    def _():
+                        begin = pl.multiple_of(local * block_size, block_size)
+                        pltpu.make_async_copy(
+                            source.at[:, pl.ds(begin, block_size)], target, sem
+                        ).start()
+
+    @pl.when(step == 0)
     def _():
+        fetch(0, 0, True)
         for source, target in ((order_ref, order_split), (prod_ref, prod_split), (loss_ref, loss_split)):
             high, low = split3(source[...])
             target[0] = high
             target[1] = low
+
+    slot = step % 2
+
+    @pl.when(step + 1 < steps)
+    def _():
+        fetch(step + 1, 1 - slot, True)
+
+    fetch(step, slot, False)
 
     for t in range(tile_blocks):
         lanes = slice(t * block_size, (t + 1) * block_size)
         acc = jnp.dot(own_ref[:, lanes], weight_ref[t, 0], preferred_element_type=f32)
         for k in range(neighbours):
             acc = acc + jnp.dot(
-                picked[t * neighbours + k][...], weight_ref[t, k + 1], preferred_element_type=f32
+                picked[slot, t * neighbours + k], weight_ref[t, k + 1], preferred_element_type=f32
             )
         mixed_ref[:, lanes] = acc
     mixed = mixed_ref[...]
@@ -128,7 +197,9 @@
 
 
 def mix_react(
-    table,
+    migrated,
+    from_lower,
+    from_upper,
     neighbour_block,
     mix_weight,
     inverse_temp,
@@ -138,7 +209,7 @@
     production,
     loss_coefficient,
 ):
-    species = table.shape[0]
+    species = migrated.shape[0]
     count_blocks, _, block_size, _ = mix_weight.shape
     neighbours = neighbour_block.shape[1]
     reactions = reactant_order.shape[0]
@@ -146,27 +217,21 @@
     width = tile_blocks * block_size
     steps = count_blocks // tile_blocks
 
-    def picked_spec(t, k):
-        return pl.BlockSpec(
-            (species, block_size),
-            lambda i, nb: (0, nb[i * tile_blocks + t, k]),
-        )
-
     def whole(shape):
         return pl.BlockSpec(shape, lambda i, nb: (0,) * len(shape))
 
-    in_specs = (
-        [pl.BlockSpec((species, width), lambda i, nb: (0, i))]
-        + [picked_spec(t, k) for t in range(tile_blocks) for k in range(neighbours)]
-        + [
-            pl.BlockSpec((tile_blocks,) + mix_weight.shape[1:], lambda i, nb: (i, 0, 0, 0)),
-            pl.BlockSpec((1, width), lambda i, nb: (0, i)),
-            whole(reactant_order.shape),
-            whole((reactions, 2)),
-            whole(production.shape),
-            whole(loss_coefficient.shape),
-        ]
-    )
+    in_specs = [
+        pl.BlockSpec((species, width), lambda i, nb: (0, i)),
+        pl.BlockSpec((tile_blocks,) + mix_weight.shape[1:], lambda i, nb: (i, 0, 0, 0)),
+        pl.BlockSpec((1, width), lambda i, nb: (0, i)),
+        whole(reactant_order.shape),
+        whole((reactions, 2)),
+        whole(production.shape),
+        whole(loss_coefficient.shape),
+        pl.BlockSpec(memory_space=pl.ANY),
+        pl.BlockSpec(memory_space=pl.ANY),
+        pl.BlockSpec(memory_space=pl.ANY),
+    ]
     bf16 = jnp.bfloat16
     grid_spec = pltpu.PrefetchScalarGridSpec(
         num_scalar_prefetch=1,
@@ -174,6 +239,8 @@
         in_specs=in_specs,
         out_specs=pl.BlockSpec((species, width), lambda i, nb: (0, i)),
         scratch_shapes=[
+            pltpu.VMEM((2, tile_blocks * neighbours, species, block_size), bf16),
+            pltpu.SemaphoreType.DMA((2, tile_blocks * neighbours)),
             pltpu.VMEM((species, width), jnp.float32),
             pltpu.VMEM((2,) + reactant_order.shape, bf16),
             pltpu.VMEM((2,) + production.shape, bf16),
@@ -188,14 +255,16 @@
         compiler_params=pltpu.CompilerParams(dimension_semantics=("arbitrary",)),
     )(
         neighbour_block,
-        table,
-        *([table] * (tile_blocks * neighbours)),
+        migrated,
         mix_weight,
         inverse_temp.reshape(1, -1),
         reactant_order,
         jnp.stack([log_prefactor, activation_energy], axis=1),
         production,
         loss_coefficient,
+        migrated,
+        from_lower,
+        from_upper,
     )
 
 
@@ -215,9 +284,11 @@
     loss_coefficient,
 ):
     migrated = migrate(mixing_ratio, send_rows, migrant_count, arrival_slot)
-    table = block_table(migrated, halo_blocks, mix_weight.shape[-1])
+    from_lower, from_upper = halo_exchange(migrated, halo_blocks, mix_weight.shape[-1])
     return mix_react(
-        table,
+        migrated,
+        from_lower,
+        from_upper,
         neighbour_block,
         mix_weight,
         inverse_temp,

time: 98.4 us -> 125 us (1.27)
  Pallas kernels: 24.9 us -> 64.6 us
  local copies, waits for them, and re-layouts: 16.4 us -> 5.35 us
  other arithmetic: 5.58 us -> 2.02 us
    pallas_call x0 -> x1, Pallas kernels: none -> 39.9 us  [halo_exchange(): pl.pallas_call(functools.partial(halo_kernel, block_size), grid_spec=grid...]
    gather x2 -> x0, local copies, waits for them, and re-layouts: 5.59 us -> none  [the longest x1 3.22 us: block_table(): to_lower = jnp.take(blocks, halo_blocks[0, 0], axis=1)]
    concatenate x1 -> x0, other arithmetic: 3.7 us -> none  [block_table(): jnp.concatenate([migrated, from_lower.reshape(species, -1), from_upper.re...]
    reshape x2 -> x0, local copies, waits for them, and re-layouts: 3.55 us -> none  [block_table(): blocks = migrated.reshape(species, parcels // block_size, block_size)]
    select_n x2 -> x0, local copies, waits for them, and re-layouts: 1.83 us -> none  [the longest x1 0.93 us: block_table(): to_upper = jnp.take(blocks, halo_blocks[0, 1], axis=1)]
    select_n x1, other arithmetic: 0.34 us -> 1.83 us  [migrate(): return jnp.where(hit, placed[:species].astype(jnp.bfloat16), mixing_ratio)]
    unnamed x41 -> x38, local copies, waits for them, and re-layouts: 4.1 us -> 2.65 us
    squeeze x0 -> x1, local copies, waits for them, and re-layouts: none -> 1.35 us  [halo_exchange(): from_upper = from_behind(listed_blocks[0], 'region', -1)]
  transfers between devices with their start and end apart: 10 -> 10, of which waited for: 3 -> 3; matrix products, arithmetic and copies ran while one was open for 5% -> 2% of each run, Pallas kernels for 0% -> 0%
where the time goes in v2:
time: 125 us; the launch traced here: 124 us
  Pallas kernels  64.6 us (52%)
  starting transfers between devices  22.5 us (18%)
  waiting for transfers between devices  15.1 us (12%)
  matrix products  14.3 us (11%)
  local copies, waits for them, and re-layouts  5.35 us (4%)
  other arithmetic  2.02 us (2%)
    pallas_call x1, Pallas kernels, halo_exchange(): pl.pallas_call(functools.partial(halo_kernel, block_size), grid_spec=grid...  39.9 us
    pallas_call x1, Pallas kernels, mix_react(): pl.pallas_call(kernel, grid_spec=grid_spec, out_shape=jax.ShapeDtypeStruc...  24.7 us
    ppermute x10, starting transfers between devices, from_behind(): return lax.ppermute(block, axis, route)  22.5 us
    ppermute x10, waiting for transfers between devices, from_behind(): return lax.ppermute(block, axis, route)  15.1 us
    dot_general x1, matrix products, migrate(): jnp.dot(mixing_ratio, pick, preferred_element_type=f32).astype(jnp.bfloat16)  7.33 us
    dot_general x1, matrix products, migrate(): placed = jnp.dot(marked, place, preferred_element_type=f32)  6.97 us
    unnamed x38, local copies, waits for them, and re-layouts  2.65 us
  transfers between devices with their start and end apart: 10, of which 3 were waited for; matrix products, arithmetic and copies ran while one was open for 2% of the time, Pallas kernels for 0%

profile of v2, /device:TPU:0, one launch (start us, length us, event | category | flops | bytes accessed | tf_op | source)
XLA Modules:
  0.0 124.3 jit_solution(14538971551630577003)
XLA Ops:
  0.0 0.0 copy-start.4
  0.0 0.0 copy-start.8
  0.0 7.3 %fusion.5 = bf16[1024,150]{0,1:T(8,128)(2,1)S(1)} fusion(bf16[150,8192]{1,0:T(8,128)(2,1)} %param.13, s32[1024]{0:T(1024)} %bitcast.81), kind=kOutput, calls=%fused_computation.8 | convolution fusion | flops 2525124608 | bytes 2768896 | tf_op jit(solution)/shard_map/dot_general | solution.py:38
  7.3 0.1 copy.56
  7.4 0.5 fusion.9
  7.9 3.2 %collective-permute-start = (bf16[150,128]{1,0:T(8,128)(2,1)S(1)}, bf16[150,128]{1,0:T(8,128)(2,1)S(1)}, u32[]{:S(2)}, u32[]{:S(2)}) collective-permute-start(bf16[150,128]{1,0:T(8,128)(2,1)S(1)} %bitcast.75), channel_id=1, source_target_pairs={{124,0},{125,1},{126,2},{127,3},{0,4},{1,5},{2,6},{3,7},{4,8},{5,9... | collective-permute-start | bytes 115208 | tf_op jit(solution)/shard_map/ppermute | solution.py:17
  11.1 0.1 collective-permute-start.1
  11.2 1.0 collective-permute-start.2
  12.3 2.3 %collective-permute-start.3 = (bf16[150,128]{1,0:T(8,128)(2,1)S(1)}, bf16[150,128]{1,0:T(8,128)(2,1)S(1)}, u32[]{:S(2)}, u32[]{:S(2)}) collective-permute-start(bf16[150,128]{1,0:T(8,128)(2,1)S(1)} %bitcast.71), channel_id=1, source_target_pairs={{127,0},{0,1},{1,2},{2,3},{3,4},{4,5},{5,6},{6,7},{7,8},{8,9},{9,1... | collective-permute-start | bytes 115208 | tf_op jit(solution)/shard_map/ppermute | solution.py:17
  14.6 5.7 %collective-permute-start.4 = (bf16[150,128]{1,0:T(8,128)(2,1)S(1)}, bf16[150,128]{1,0:T(8,128)(2,1)S(1)}, u32[]{:S(2)}, u32[]{:S(2)}) collective-permute-start(bf16[150,128]{1,0:T(8,128)(2,1)S(1)} %bitcast.70), channel_id=1, source_target_pairs={{1,0},{2,1},{3,2},{4,3},{5,4},{6,5},{7,6},{8,7},{9,8},{10,9},{11,1... | collective-permute-start | bytes 115208 | tf_op jit(solution)/shard_map/ppermute | solution.py:17
  20.2 0.0 copy-done.4
  20.2 0.0 copy-done.8
  20.2 0.1 bitcast_select_fusion
  20.3 0.0 collective-permute-done
  20.3 1.9 %collective-permute-start.5 = (bf16[150,128]{1,0:T(8,128)(2,1)S(1)}, bf16[150,128]{1,0:T(8,128)(2,1)S(1)}, u32[]{:S(2)}, u32[]{:S(2)}) collective-permute-start(bf16[150,128]{1,0:T(8,128)(2,1)S(1)} %bitcast.72), channel_id=1, source_target_pairs={{2,0},{3,1},{4,2},{5,3},{6,4},{7,5},{8,6},{9,7},{10,8},{11,9},{12,... | collective-permute-start | bytes 115208 | tf_op jit(solution)/shard_map/ppermute | solution.py:17
  22.3 0.0 collective-permute-done.1
  22.3 0.2 collective-permute-start.6
  22.5 0.0 collective-permute-done.2
  22.5 3.5 %collective-permute-start.7 = (bf16[150,128]{1,0:T(8,128)(2,1)S(1)}, bf16[150,128]{1,0:T(8,128)(2,1)S(1)}, u32[]{:S(2)}, u32[]{:S(2)}) collective-permute-start(bf16[150,128]{1,0:T(8,128)(2,1)S(1)} %bitcast.68), channel_id=1, source_target_pairs={{4,0},{5,1},{6,2},{7,3},{8,4},{9,5},{10,6},{11,7},{12,8},{13,9},{1... | collective-permute-start | bytes 115208 | tf_op jit(solution)/shard_map/ppermute | solution.py:17
  26.0 0.0 collective-permute-done.3
  26.0 0.0 collective-permute-done.4
  26.1 0.0 collective-permute-done.5
  26.1 0.0 collective-permute-done.6
  26.1 2.4 %collective-permute-done.7 = bf16[150,128]{1,0:T(8,128)(2,1)S(1)} collective-permute-done((bf16[150,128]{1,0:T(8,128)(2,1)S(1)}, bf16[150,128]{1,0:T(8,128)(2,1)S(1)}, u32[]{:S(2)}, u32[]{:S(2)}) %collective-permute-start.7) | collective-permute-done | bytes 38432 | tf_op jit(solution)/shard_map/ppermute | solution.py:17
  28.6 0.0 copy-start
  28.7 7.0 %fusion = f32[151,8192]{1,0:T(8,128)S(1)} fusion(s32[1024]{0:T(1024)S(1)} %bitcast_select_fusion, bf16[150,1024]{1,0:T(8,128)(2,1)S(1)} %bitcast.66), kind=kOutput, calls=%fused_computation.2 | convolution fusion | flops 2541748224 | bytes 5259264 | tf_op jit(solution)/shard_map/dot_general | solution.py:50
  35.6 0.1 compare_reduce_fusion
  35.8 0.0 copy-done
  35.8 1.8 %fusion.4.migrated_hbm.own_ref = bf16[150,8192]{1,0:T(8,128)(2,1)} fusion(bf16[150,8192]{1,0:T(8,128)(2,1)S(1)} %copy-done, f32[151,8192]{1,0:T(8,128)S(1)} %fusion, pred[8192]{0:T(1024)(128)(4,1)S(1)} %compare_reduce_fusion), kind=kLoop, calls=%fused_computation.7 | loop fusion | flops 1228800 | bytes 7380992 | tf_op jit(solution)/shard_map/jit(_where)/select_n | solution.py:52
  37.6 0.0 copy-start.5
  37.6 0.0 copy-start.6
  37.6 0.0 copy-start.7
  37.6 0.0 copy-start.3
  37.6 39.9 %shard_map.127 = bf16[2,150,2048]{2,1,0:T(8,128)(2,1)} custom-call(s32[2,16]{1,0:T(2,128)} %bitcast.79, bf16[150,8192]{1,0:T(8,128)(2,1)} %fusion.4.migrated_hbm.own_ref), custom_call_target="tpu_custom_call" | custom-call | tf_op jit(solution)/shard_map/pallas_call | solution.py:82
  77.5 1.3 %slice_bitcast_fusion = (bf16[150,2048]{1,0:T(8,128)(2,1)S(1)}, bf16[150,2048]{1,0:T(8,128)(2,1)S(1)}) fusion(bf16[2,150,2048]{2,1,0:T(8,128)(2,1)} %shard_map.127), kind=kLoop, calls=%fused_computation.9 | loop fusion | bytes 2457600 | tf_op jit(solution)/shard_map/squeeze | solution.py:88
  78.9 4.6 %collective-permute-start.9 = (bf16[150,2048]{1,0:T(8,128)(2,1)S(1)}, bf16[150,2048]{1,0:T(8,128)(2,1)S(1)}, u32[]{:S(2)}, u32[]{:S(2)}) collective-permute-start(bf16[150,2048]{1,0:T(8,128)(2,1)S(1)} %get-tuple-element.5), channel_id=1, source_target_pairs={{1,0},{2,1},{3,2},{4,3},{5,4},{6,5},{7,6},{8,7},{9,8},{10,9},{11,1... | collective-permute-start | bytes 1843208 | tf_op jit(solution)/shard_map/ppermute | solution.py:17
  83.5 0.0 collective-permute-start.8
  83.5 0.0 copy-done.5
  83.5 0.7 copy.45.nb_ref
  84.2 0.0 copy-done.6
  84.2 0.0 copy-done.7
  84.3 0.8 copy.47.rate_terms_ref
  85.1 0.0 copy-done.3
  85.1 0.8 copy.46.order_ref
  85.9 5.4 %collective-permute-done.9.upper_hbm = bf16[150,2048]{1,0:T(8,128)(2,1)S(1)} collective-permute-done((bf16[150,2048]{1,0:T(8,128)(2,1)S(1)}, bf16[150,2048]{1,0:T(8,128)(2,1)S(1)}, u32[]{:S(2)}, u32[]{:S(2)}) %collective-permute-start.9) | collective-permute-done | bytes 614432 | tf_op jit(solution)/shard_map/ppermute | solution.py:17
  91.3 0.0 copy-start.1
  91.3 7.3 %collective-permute-done.8.lower_hbm = bf16[150,2048]{1,0:T(8,128)(2,1)S(1)} collective-permute-done((bf16[150,2048]{1,0:T(8,128)(2,1)S(1)}, bf16[150,2048]{1,0:T(8,128)(2,1)S(1)}, u32[]{:S(2)}, u32[]{:S(2)}) %collective-permute-start.8) | collective-permute-done | bytes 614432 | tf_op jit(solution)/shard_map/ppermute | solution.py:17
  98.6 0.0 copy-start.2
  98.6 0.0 copy-done.1
  98.6 0.8 copy-done.2
  99.5 24.7 %shard_map.128 = f32[150,8192]{1,0:T(8,128)} custom-call(s32[64,3]{1,0:T(8,128)} %copy.45.nb_ref, bf16[150,8192]{1,0:T(8,128)(2,1)} %fusion.4.migrated_hbm.own_ref, bf16[64,4,128,128]{3,2,1,0:T(8,128)(2,1)} %weight_ref.1, f32[1,8192]{1,0:T(1,128)} %bitcast.76, f32[256,150]{1,0:T(8,128)} %copy.46.order_ref, f32[256,2]{1,0:T(8,128)} %copy.47.rate_terms_ref, ...), custom_call_target="tpu_custom_call" | custom-call | tf_op jit(solution)/shard_map/pallas_call | solution.py:251
  (20 shorter events, 0.3 us)
Async XLA Ops:
  0.0 20.2 %copy-start.4 = (s32[1,8,128]{2,1,0:T(8,128)S(1)}, s32[1,8,128]{2,1,0:T(8,128)}, u32[]{:S(2)}) copy-start(s32[1,8,128]{2,1,0:T(8,128)} %param.16) | copy-start | bytes 12292
  0.0 20.2 %copy-start.8 = (s32[1,8]{1,0:T(1,128)S(1)}, s32[1,8]{1,0:T(1,128)}, u32[]{:S(2)}) copy-start(s32[1,8]{1,0:T(1,128)} %param.15) | copy-start | bytes 100
  7.9 12.4 %collective-permute-start = (bf16[150,128]{1,0:T(8,128)(2,1)S(1)}, bf16[150,128]{1,0:T(8,128)(2,1)S(1)}, u32[]{:S(2)}, u32[]{:S(2)}) collective-permute-start(bf16[150,128]{1,0:T(8,128)(2,1)S(1)} %bitcast.75), channel_id=1, source_target_pairs={{124,0},{125,1},{126,2},{127,3},{0,4},{1,5},{2,6},{3,7},{4,8},{5,9... | collective-permute-start | bytes 115208 | tf_op jit(solution)/shard_map/ppermute | solution.py:17
  11.1 11.1 %collective-permute-start.1 = (bf16[150,128]{1,0:T(8,128)(2,1)S(1)}, bf16[150,128]{1,0:T(8,128)(2,1)S(1)}, u32[]{:S(2)}, u32[]{:S(2)}) collective-permute-start(bf16[150,128]{1,0:T(8,128)(2,1)S(1)} %bitcast.74), channel_id=1, source_target_pairs={{125,0},{126,1},{127,2},{0,3},{1,4},{2,5},{3,6},{4,7},{5,8},{6,9},... | collective-permute-start | bytes 115208 | tf_op jit(solution)/shard_map/ppermute | solution.py:17
  11.2 11.2 %collective-permute-start.2 = (bf16[150,128]{1,0:T(8,128)(2,1)S(1)}, bf16[150,128]{1,0:T(8,128)(2,1)S(1)}, u32[]{:S(2)}, u32[]{:S(2)}) collective-permute-start(bf16[150,128]{1,0:T(8,128)(2,1)S(1)} %bitcast.73), channel_id=1, source_target_pairs={{126,0},{127,1},{0,2},{1,3},{2,4},{3,5},{4,6},{5,7},{6,8},{7,9},{8... | collective-permute-start | bytes 115208 | tf_op jit(solution)/shard_map/ppermute | solution.py:17
  12.3 13.7 %collective-permute-start.3 = (bf16[150,128]{1,0:T(8,128)(2,1)S(1)}, bf16[150,128]{1,0:T(8,128)(2,1)S(1)}, u32[]{:S(2)}, u32[]{:S(2)}) collective-permute-start(bf16[150,128]{1,0:T(8,128)(2,1)S(1)} %bitcast.71), channel_id=1, source_target_pairs={{127,0},{0,1},{1,2},{2,3},{3,4},{4,5},{5,6},{6,7},{7,8},{8,9},{9,1... | collective-permute-start | bytes 115208 | tf_op jit(solution)/shard_map/ppermute | solution.py:17
  14.6 11.5 %collective-permute-start.4 = (bf16[150,128]{1,0:T(8,128)(2,1)S(1)}, bf16[150,128]{1,0:T(8,128)(2,1)S(1)}, u32[]{:S(2)}, u32[]{:S(2)}) collective-permute-start(bf16[150,128]{1,0:T(8,128)(2,1)S(1)} %bitcast.70), channel_id=1, source_target_pairs={{1,0},{2,1},{3,2},{4,3},{5,4},{6,5},{7,6},{8,7},{9,8},{10,9},{11,1... | collective-permute-start | bytes 115208 | tf_op jit(solution)/shard_map/ppermute | solution.py:17
  20.3 5.7 %collective-permute-start.5 = (bf16[150,128]{1,0:T(8,128)(2,1)S(1)}, bf16[150,128]{1,0:T(8,128)(2,1)S(1)}, u32[]{:S(2)}, u32[]{:S(2)}) collective-permute-start(bf16[150,128]{1,0:T(8,128)(2,1)S(1)} %bitcast.72), channel_id=1, source_target_pairs={{2,0},{3,1},{4,2},{5,3},{6,4},{7,5},{8,6},{9,7},{10,8},{11,9},{12,... | collective-permute-start | bytes 115208 | tf_op jit(solution)/shard_map/ppermute | solution.py:17
  22.3 3.8 %collective-permute-start.6 = (bf16[150,128]{1,0:T(8,128)(2,1)S(1)}, bf16[150,128]{1,0:T(8,128)(2,1)S(1)}, u32[]{:S(2)}, u32[]{:S(2)}) collective-permute-start(bf16[150,128]{1,0:T(8,128)(2,1)S(1)} %bitcast.69), channel_id=1, source_target_pairs={{3,0},{4,1},{5,2},{6,3},{7,4},{8,5},{9,6},{10,7},{11,8},{12,9},{13... | collective-permute-start | bytes 115208 | tf_op jit(solution)/shard_map/ppermute | solution.py:17
  22.5 6.0 %collective-permute-start.7 = (bf16[150,128]{1,0:T(8,128)(2,1)S(1)}, bf16[150,128]{1,0:T(8,128)(2,1)S(1)}, u32[]{:S(2)}, u32[]{:S(2)}) collective-permute-start(bf16[150,128]{1,0:T(8,128)(2,1)S(1)} %bitcast.68), channel_id=1, source_target_pairs={{4,0},{5,1},{6,2},{7,3},{8,4},{9,5},{10,6},{11,7},{12,8},{13,9},{1... | collective-permute-start | bytes 115208 | tf_op jit(solution)/shard_map/ppermute | solution.py:17
  28.6 7.1 %copy-start = (bf16[150,8192]{1,0:T(8,128)(2,1)S(1)}, bf16[150,8192]{1,0:T(8,128)(2,1)}, u32[]{:S(2)}) copy-start(bf16[150,8192]{1,0:T(8,128)(2,1)} %param.13) | copy-start | bytes 7372804
  37.6 46.0 %copy-start.5 = (s32[64,3]{0,1:T(4,128)S(1)}, s32[64,3]{0,1:T(4,128)}, u32[]{:S(2)}) copy-start(s32[64,3]{0,1:T(4,128)} %param.18) | copy-start | bytes 2308
  37.6 46.7 %copy-start.6 = (f32[256]{0:T(256)S(1)}, f32[256]{0:T(256)}, u32[]{:S(2)}) copy-start(f32[256]{0:T(256)} %param.23) | copy-start | bytes 3076
  37.6 46.7 %copy-start.7 = (f32[256]{0:T(256)S(1)}, f32[256]{0:T(256)}, u32[]{:S(2)}) copy-start(f32[256]{0:T(256)} %param.22) | copy-start | bytes 3076
  37.6 47.5 %copy-start.3 = (f32[256,150]{0,1:T(8,128)S(1)}, f32[256,150]{0,1:T(8,128)}, u32[]{:S(2)}) copy-start(f32[256,150]{0,1:T(8,128)} %param.21) | copy-start | bytes 460804
  78.9 12.4 %collective-permute-start.9 = (bf16[150,2048]{1,0:T(8,128)(2,1)S(1)}, bf16[150,2048]{1,0:T(8,128)(2,1)S(1)}, u32[]{:S(2)}, u32[]{:S(2)}) collective-permute-start(bf16[150,2048]{1,0:T(8,128)(2,1)S(1)} %get-tuple-element.5), channel_id=1, source_target_pairs={{1,0},{2,1},{3,2},{4,3},{5,4},{6,5},{7,6},{8,7},{9,8},{10,9},{11,1... | collective-permute-start | bytes 1843208 | tf_op jit(solution)/shard_map/ppermute | solution.py:17
  83.5 15.1 %collective-permute-start.8 = (bf16[150,2048]{1,0:T(8,128)(2,1)S(1)}, bf16[150,2048]{1,0:T(8,128)(2,1)S(1)}, u32[]{:S(2)}, u32[]{:S(2)}) collective-permute-start(bf16[150,2048]{1,0:T(8,128)(2,1)S(1)} %get-tuple-element.6), channel_id=1, source_target_pairs={{127,0},{0,1},{1,2},{2,3},{3,4},{4,5},{5,6},{6,7},{7,8},{8,9},{9,1... | collective-permute-start | bytes 1843208 | tf_op jit(solution)/shard_map/ppermute | solution.py:17
  91.3 7.3 %copy-start.1 = (bf16[150,2048]{1,0:T(8,128)(2,1)}, bf16[150,2048]{1,0:T(8,128)(2,1)S(1)}, u32[]{:S(2)}) copy-start(bf16[150,2048]{1,0:T(8,128)(2,1)S(1)} %collective-permute-done.9.upper_hbm) | copy-start | bytes 1843204
  98.6 0.8 copy-start.2

commit v3 on v2

--- a/solution.py
+++ b/solution.py
@@ -76,7 +76,9 @@
         num_scalar_prefetch=1,
         grid=(1,),
         in_specs=[pl.BlockSpec(memory_space=pl.ANY)],
-        out_specs=pl.BlockSpec(memory_space=pl.ANY),
+        out_specs=pl.BlockSpec(
+            (sides, species, listed * block_size), lambda i, halo: (0, 0, 0)
+        ),
         scratch_shapes=[pltpu.SemaphoreType.DMA((sides, listed))],
     )
     listed_blocks = pl.pallas_call(

time: 125 us -> 88.4 us (0.71)
  Pallas kernels: 64.6 us -> 28.1 us
    pallas_call x1, Pallas kernels: 39.9 us -> 3.43 us  [halo_exchange(): pl.pallas_call(functools.partial(halo_kernel, block_size), grid_spec=grid...]
  transfers between devices with their start and end apart: 10 -> 10, of which waited for: 3 -> 3; matrix products, arithmetic and copies ran while one was open for 2% -> 3% of each run, Pallas kernels for 0% -> 0%
where the time goes in v3:
time: 88.4 us; the launch traced here: 87.8 us
  Pallas kernels  28.1 us (32%)
  starting transfers between devices  22.5 us (25%)
  waiting for transfers between devices  15.1 us (17%)
  matrix products  14.3 us (16%)
  local copies, waits for them, and re-layouts  5.35 us (6%)
  other arithmetic  2.02 us (2%)
    pallas_call x1, Pallas kernels, mix_react(): pl.pallas_call(kernel, grid_spec=grid_spec, out_shape=jax.ShapeDtypeStruc...  24.7 us
    ppermute x10, starting transfers between devices, from_behind(): return lax.ppermute(block, axis, route)  22.5 us
    ppermute x10, waiting for transfers between devices, from_behind(): return lax.ppermute(block, axis, route)  15.1 us
    dot_general x1, matrix products, migrate(): jnp.dot(mixing_ratio, pick, preferred_element_type=f32).astype(jnp.bfloat16)  7.33 us
    dot_general x1, matrix products, migrate(): placed = jnp.dot(marked, place, preferred_element_type=f32)  6.97 us
    pallas_call x1, Pallas kernels, halo_exchange(): pl.pallas_call(functools.partial(halo_kernel, block_size), grid_spec=grid...  3.43 us
    unnamed x38, local copies, waits for them, and re-layouts  2.65 us
    select_n x1, other arithmetic, migrate(): return jnp.where(hit, placed[:species].astype(jnp.bfloat16), mixing_ratio)  1.83 us
  transfers between devices with their start and end apart: 10, of which 3 were waited for; matrix products, arithmetic and copies ran while one was open for 3% of the time, Pallas kernels for 0%

profile of v3, /device:TPU:0, one launch (start us, length us, event | category | flops | bytes accessed | tf_op | source)
XLA Modules:
  0.0 87.8 jit_solution(13771030472539580907)
XLA Ops:
  0.0 0.0 copy-start.4
  0.0 0.0 copy-start.8
  0.0 7.3 %fusion.5 = bf16[1024,150]{0,1:T(8,128)(2,1)S(1)} fusion(bf16[150,8192]{1,0:T(8,128)(2,1)} %param.13, s32[1024]{0:T(1024)} %bitcast.81), kind=kOutput, calls=%fused_computation.8 | convolution fusion | flops 2525124608 | bytes 2768896 | tf_op jit(solution)/shard_map/dot_general | solution.py:38
  7.3 0.1 copy.56
  7.4 0.5 fusion.9
  7.9 3.2 %collective-permute-start = (bf16[150,128]{1,0:T(8,128)(2,1)S(1)}, bf16[150,128]{1,0:T(8,128)(2,1)S(1)}, u32[]{:S(2)}, u32[]{:S(2)}) collective-permute-start(bf16[150,128]{1,0:T(8,128)(2,1)S(1)} %bitcast.75), channel_id=1, source_target_pairs={{124,0},{125,1},{126,2},{127,3},{0,4},{1,5},{2,6},{3,7},{4,8},{5,9... | collective-permute-start | bytes 115208 | tf_op jit(solution)/shard_map/ppermute | solution.py:17
  11.1 0.1 collective-permute-start.1
  11.2 1.0 %collective-permute-start.2 = (bf16[150,128]{1,0:T(8,128)(2,1)S(1)}, bf16[150,128]{1,0:T(8,128)(2,1)S(1)}, u32[]{:S(2)}, u32[]{:S(2)}) collective-permute-start(bf16[150,128]{1,0:T(8,128)(2,1)S(1)} %bitcast.73), channel_id=1, source_target_pairs={{126,0},{127,1},{0,2},{1,3},{2,4},{3,5},{4,6},{5,7},{6,8},{7,9},{8... | collective-permute-start | bytes 115208 | tf_op jit(solution)/shard_map/ppermute | solution.py:17
  12.3 2.3 %collective-permute-start.3 = (bf16[150,128]{1,0:T(8,128)(2,1)S(1)}, bf16[150,128]{1,0:T(8,128)(2,1)S(1)}, u32[]{:S(2)}, u32[]{:S(2)}) collective-permute-start(bf16[150,128]{1,0:T(8,128)(2,1)S(1)} %bitcast.71), channel_id=1, source_target_pairs={{127,0},{0,1},{1,2},{2,3},{3,4},{4,5},{5,6},{6,7},{7,8},{8,9},{9,1... | collective-permute-start | bytes 115208 | tf_op jit(solution)/shard_map/ppermute | solution.py:17
  14.6 5.7 %collective-permute-start.4 = (bf16[150,128]{1,0:T(8,128)(2,1)S(1)}, bf16[150,128]{1,0:T(8,128)(2,1)S(1)}, u32[]{:S(2)}, u32[]{:S(2)}) collective-permute-start(bf16[150,128]{1,0:T(8,128)(2,1)S(1)} %bitcast.70), channel_id=1, source_target_pairs={{1,0},{2,1},{3,2},{4,3},{5,4},{6,5},{7,6},{8,7},{9,8},{10,9},{11,1... | collective-permute-start | bytes 115208 | tf_op jit(solution)/shard_map/ppermute | solution.py:17
  20.2 0.0 copy-done.4
  20.2 0.0 copy-done.8
  20.2 0.1 bitcast_select_fusion
  20.3 0.0 collective-permute-done
  20.3 1.9 %collective-permute-start.5 = (bf16[150,128]{1,0:T(8,128)(2,1)S(1)}, bf16[150,128]{1,0:T(8,128)(2,1)S(1)}, u32[]{:S(2)}, u32[]{:S(2)}) collective-permute-start(bf16[150,128]{1,0:T(8,128)(2,1)S(1)} %bitcast.72), channel_id=1, source_target_pairs={{2,0},{3,1},{4,2},{5,3},{6,4},{7,5},{8,6},{9,7},{10,8},{11,9},{12,... | collective-permute-start | bytes 115208 | tf_op jit(solution)/shard_map/ppermute | solution.py:17
  22.3 0.0 collective-permute-done.1
  22.3 0.2 collective-permute-start.6
  22.5 0.0 collective-permute-done.2
  22.5 3.5 %collective-permute-start.7 = (bf16[150,128]{1,0:T(8,128)(2,1)S(1)}, bf16[150,128]{1,0:T(8,128)(2,1)S(1)}, u32[]{:S(2)}, u32[]{:S(2)}) collective-permute-start(bf16[150,128]{1,0:T(8,128)(2,1)S(1)} %bitcast.68), channel_id=1, source_target_pairs={{4,0},{5,1},{6,2},{7,3},{8,4},{9,5},{10,6},{11,7},{12,8},{13,9},{1... | collective-permute-start | bytes 115208 | tf_op jit(solution)/shard_map/ppermute | solution.py:17
  26.0 0.0 collective-permute-done.3
  26.0 0.0 collective-permute-done.4
  26.1 0.0 collective-permute-done.5
  26.1 0.0 collective-permute-done.6
  26.1 2.4 %collective-permute-done.7 = bf16[150,128]{1,0:T(8,128)(2,1)S(1)} collective-permute-done((bf16[150,128]{1,0:T(8,128)(2,1)S(1)}, bf16[150,128]{1,0:T(8,128)(2,1)S(1)}, u32[]{:S(2)}, u32[]{:S(2)}) %collective-permute-start.7) | collective-permute-done | bytes 38432 | tf_op jit(solution)/shard_map/ppermute | solution.py:17
  28.6 0.0 copy-start
  28.7 7.0 %fusion = f32[151,8192]{1,0:T(8,128)S(1)} fusion(s32[1024]{0:T(1024)S(1)} %bitcast_select_fusion, bf16[150,1024]{1,0:T(8,128)(2,1)S(1)} %bitcast.66), kind=kOutput, calls=%fused_computation.2 | convolution fusion | flops 2541748224 | bytes 5259264 | tf_op jit(solution)/shard_map/dot_general | solution.py:50
  35.6 0.1 compare_reduce_fusion
  35.8 0.0 copy-done
  35.8 1.8 %fusion.4.migrated_hbm.own_ref = bf16[150,8192]{1,0:T(8,128)(2,1)} fusion(bf16[150,8192]{1,0:T(8,128)(2,1)S(1)} %copy-done, f32[151,8192]{1,0:T(8,128)S(1)} %fusion, pred[8192]{0:T(1024)(128)(4,1)S(1)} %compare_reduce_fusion), kind=kLoop, calls=%fused_computation.7 | loop fusion | flops 1228800 | bytes 7380992 | tf_op jit(solution)/shard_map/jit(_where)/select_n | solution.py:52
  37.6 0.0 copy-start.5
  37.6 0.0 copy-start.6
  37.6 0.0 copy-start.7
  37.6 0.0 copy-start.3
  37.6 3.4 %shard_map.127 = bf16[2,150,2048]{2,1,0:T(8,128)(2,1)} custom-call(s32[2,16]{1,0:T(2,128)} %bitcast.79, bf16[150,8192]{1,0:T(8,128)(2,1)} %fusion.4.migrated_hbm.own_ref), custom_call_target="tpu_custom_call" | custom-call | tf_op jit(solution)/shard_map/pallas_call | solution.py:84
  41.0 1.3 %slice_bitcast_fusion = (bf16[150,2048]{1,0:T(8,128)(2,1)S(1)}, bf16[150,2048]{1,0:T(8,128)(2,1)S(1)}) fusion(bf16[2,150,2048]{2,1,0:T(8,128)(2,1)} %shard_map.127), kind=kLoop, calls=%fused_computation.9 | loop fusion | bytes 2457600 | tf_op jit(solution)/shard_map/squeeze | solution.py:90
  42.4 4.7 %collective-permute-start.9 = (bf16[150,2048]{1,0:T(8,128)(2,1)S(1)}, bf16[150,2048]{1,0:T(8,128)(2,1)S(1)}, u32[]{:S(2)}, u32[]{:S(2)}) collective-permute-start(bf16[150,2048]{1,0:T(8,128)(2,1)S(1)} %get-tuple-element.5), channel_id=1, source_target_pairs={{1,0},{2,1},{3,2},{4,3},{5,4},{6,5},{7,6},{8,7},{9,8},{10,9},{11,1... | collective-permute-start | bytes 1843208 | tf_op jit(solution)/shard_map/ppermute | solution.py:17
  47.0 0.0 collective-permute-start.8
  47.0 0.0 copy-done.5
  47.0 0.7 copy.45.nb_ref
  47.8 0.0 copy-done.6
  47.8 0.0 copy-done.7
  47.8 0.8 copy.47.rate_terms_ref
  48.6 0.0 copy-done.3
  48.6 0.8 copy.46.order_ref
  49.4 5.4 %collective-permute-done.9.upper_hbm = bf16[150,2048]{1,0:T(8,128)(2,1)S(1)} collective-permute-done((bf16[150,2048]{1,0:T(8,128)(2,1)S(1)}, bf16[150,2048]{1,0:T(8,128)(2,1)S(1)}, u32[]{:S(2)}, u32[]{:S(2)}) %collective-permute-start.9) | collective-permute-done | bytes 614432 | tf_op jit(solution)/shard_map/ppermute | solution.py:17
  54.8 0.0 copy-start.1
  54.8 7.3 %collective-permute-done.8.lower_hbm = bf16[150,2048]{1,0:T(8,128)(2,1)S(1)} collective-permute-done((bf16[150,2048]{1,0:T(8,128)(2,1)S(1)}, bf16[150,2048]{1,0:T(8,128)(2,1)S(1)}, u32[]{:S(2)}, u32[]{:S(2)}) %collective-permute-start.8) | collective-permute-done | bytes 614432 | tf_op jit(solution)/shard_map/ppermute | solution.py:17
  62.1 0.0 copy-start.2
  62.1 0.0 copy-done.1
  62.1 0.8 copy-done.2
  63.0 24.7 %shard_map.128 = f32[150,8192]{1,0:T(8,128)} custom-call(s32[64,3]{1,0:T(8,128)} %copy.45.nb_ref, bf16[150,8192]{1,0:T(8,128)(2,1)} %fusion.4.migrated_hbm.own_ref, bf16[64,4,128,128]{3,2,1,0:T(8,128)(2,1)} %weight_ref.1, f32[1,8192]{1,0:T(1,128)} %bitcast.76, f32[256,150]{1,0:T(8,128)} %copy.46.order_ref, f32[256,2]{1,0:T(8,128)} %copy.47.rate_terms_ref, ...), custom_call_target="tpu_custom_call" | custom-call | tf_op jit(solution)/shard_map/pallas_call | solution.py:253
  (20 shorter events, 0.3 us)
Async XLA Ops:
  0.0 20.2 %copy-start.4 = (s32[1,8,128]{2,1,0:T(8,128)S(1)}, s32[1,8,128]{2,1,0:T(8,128)}, u32[]{:S(2)}) copy-start(s32[1,8,128]{2,1,0:T(8,128)} %param.16) | copy-start | bytes 12292
  0.0 20.2 %copy-start.8 = (s32[1,8]{1,0:T(1,128)S(1)}, s32[1,8]{1,0:T(1,128)}, u32[]{:S(2)}) copy-start(s32[1,8]{1,0:T(1,128)} %param.15) | copy-start | bytes 100
  7.9 12.4 %collective-permute-start = (bf16[150,128]{1,0:T(8,128)(2,1)S(1)}, bf16[150,128]{1,0:T(8,128)(2,1)S(1)}, u32[]{:S(2)}, u32[]{:S(2)}) collective-permute-start(bf16[150,128]{1,0:T(8,128)(2,1)S(1)} %bitcast.75), channel_id=1, source_target_pairs={{124,0},{125,1},{126,2},{127,3},{0,4},{1,5},{2,6},{3,7},{4,8},{5,9... | collective-permute-start | bytes 115208 | tf_op jit(solution)/shard_map/ppermute | solution.py:17
  11.1 11.1 %collective-permute-start.1 = (bf16[150,128]{1,0:T(8,128)(2,1)S(1)}, bf16[150,128]{1,0:T(8,128)(2,1)S(1)}, u32[]{:S(2)}, u32[]{:S(2)}) collective-permute-start(bf16[150,128]{1,0:T(8,128)(2,1)S(1)} %bitcast.74), channel_id=1, source_target_pairs={{125,0},{126,1},{127,2},{0,3},{1,4},{2,5},{3,6},{4,7},{5,8},{6,9},... | collective-permute-start | bytes 115208 | tf_op jit(solution)/shard_map/ppermute | solution.py:17
  11.2 11.2 %collective-permute-start.2 = (bf16[150,128]{1,0:T(8,128)(2,1)S(1)}, bf16[150,128]{1,0:T(8,128)(2,1)S(1)}, u32[]{:S(2)}, u32[]{:S(2)}) collective-permute-start(bf16[150,128]{1,0:T(8,128)(2,1)S(1)} %bitcast.73), channel_id=1, source_target_pairs={{126,0},{127,1},{0,2},{1,3},{2,4},{3,5},{4,6},{5,7},{6,8},{7,9},{8... | collective-permute-start | bytes 115208 | tf_op jit(solution)/shard_map/ppermute | solution.py:17
  12.3 13.7 %collective-permute-start.3 = (bf16[150,128]{1,0:T(8,128)(2,1)S(1)}, bf16[150,128]{1,0:T(8,128)(2,1)S(1)}, u32[]{:S(2)}, u32[]{:S(2)}) collective-permute-start(bf16[150,128]{1,0:T(8,128)(2,1)S(1)} %bitcast.71), channel_id=1, source_target_pairs={{127,0},{0,1},{1,2},{2,3},{3,4},{4,5},{5,6},{6,7},{7,8},{8,9},{9,1... | collective-permute-start | bytes 115208 | tf_op jit(solution)/shard_map/ppermute | solution.py:17
  14.6 11.5 %collective-permute-start.4 = (bf16[150,128]{1,0:T(8,128)(2,1)S(1)}, bf16[150,128]{1,0:T(8,128)(2,1)S(1)}, u32[]{:S(2)}, u32[]{:S(2)}) collective-permute-start(bf16[150,128]{1,0:T(8,128)(2,1)S(1)} %bitcast.70), channel_id=1, source_target_pairs={{1,0},{2,1},{3,2},{4,3},{5,4},{6,5},{7,6},{8,7},{9,8},{10,9},{11,1... | collective-permute-start | bytes 115208 | tf_op jit(solution)/shard_map/ppermute | solution.py:17
  20.3 5.7 %collective-permute-start.5 = (bf16[150,128]{1,0:T(8,128)(2,1)S(1)}, bf16[150,128]{1,0:T(8,128)(2,1)S(1)}, u32[]{:S(2)}, u32[]{:S(2)}) collective-permute-start(bf16[150,128]{1,0:T(8,128)(2,1)S(1)} %bitcast.72), channel_id=1, source_target_pairs={{2,0},{3,1},{4,2},{5,3},{6,4},{7,5},{8,6},{9,7},{10,8},{11,9},{12,... | collective-permute-start | bytes 115208 | tf_op jit(solution)/shard_map/ppermute | solution.py:17
  22.3 3.8 %collective-permute-start.6 = (bf16[150,128]{1,0:T(8,128)(2,1)S(1)}, bf16[150,128]{1,0:T(8,128)(2,1)S(1)}, u32[]{:S(2)}, u32[]{:S(2)}) collective-permute-start(bf16[150,128]{1,0:T(8,128)(2,1)S(1)} %bitcast.69), channel_id=1, source_target_pairs={{3,0},{4,1},{5,2},{6,3},{7,4},{8,5},{9,6},{10,7},{11,8},{12,9},{13... | collective-permute-start | bytes 115208 | tf_op jit(solution)/shard_map/ppermute | solution.py:17
  22.5 6.0 %collective-permute-start.7 = (bf16[150,128]{1,0:T(8,128)(2,1)S(1)}, bf16[150,128]{1,0:T(8,128)(2,1)S(1)}, u32[]{:S(2)}, u32[]{:S(2)}) collective-permute-start(bf16[150,128]{1,0:T(8,128)(2,1)S(1)} %bitcast.68), channel_id=1, source_target_pairs={{4,0},{5,1},{6,2},{7,3},{8,4},{9,5},{10,6},{11,7},{12,8},{13,9},{1... | collective-permute-start | bytes 115208 | tf_op jit(solution)/shard_map/ppermute | solution.py:17
  28.6 7.1 %copy-start = (bf16[150,8192]{1,0:T(8,128)(2,1)S(1)}, bf16[150,8192]{1,0:T(8,128)(2,1)}, u32[]{:S(2)}) copy-start(bf16[150,8192]{1,0:T(8,128)(2,1)} %param.13) | copy-start | bytes 7372804
  37.6 9.5 %copy-start.5 = (s32[64,3]{0,1:T(4,128)S(1)}, s32[64,3]{0,1:T(4,128)}, u32[]{:S(2)}) copy-start(s32[64,3]{0,1:T(4,128)} %param.18) | copy-start | bytes 2308
  37.6 10.2 %copy-start.6 = (f32[256]{0:T(256)S(1)}, f32[256]{0:T(256)}, u32[]{:S(2)}) copy-start(f32[256]{0:T(256)} %param.23) | copy-start | bytes 3076
  37.6 10.2 %copy-start.7 = (f32[256]{0:T(256)S(1)}, f32[256]{0:T(256)}, u32[]{:S(2)}) copy-start(f32[256]{0:T(256)} %param.22) | copy-start | bytes 3076
  37.6 11.0 %copy-start.3 = (f32[256,150]{0,1:T(8,128)S(1)}, f32[256,150]{0,1:T(8,128)}, u32[]{:S(2)}) copy-start(f32[256,150]{0,1:T(8,128)} %param.21) | copy-start | bytes 460804
  42.4 12.4 %collective-permute-start.9 = (bf16[150,2048]{1,0:T(8,128)(2,1)S(1)}, bf16[150,2048]{1,0:T(8,128)(2,1)S(1)}, u32[]{:S(2)}, u32[]{:S(2)}) collective-permute-start(bf16[150,2048]{1,0:T(8,128)(2,1)S(1)} %get-tuple-element.5), channel_id=1, source_target_pairs={{1,0},{2,1},{3,2},{4,3},{5,4},{6,5},{7,6},{8,7},{9,8},{10,9},{11,1... | collective-permute-start | bytes 1843208 | tf_op jit(solution)/shard_map/ppermute | solution.py:17
  47.0 15.1 %collective-permute-start.8 = (bf16[150,2048]{1,0:T(8,128)(2,1)S(1)}, bf16[150,2048]{1,0:T(8,128)(2,1)S(1)}, u32[]{:S(2)}, u32[]{:S(2)}) collective-permute-start(bf16[150,2048]{1,0:T(8,128)(2,1)S(1)} %get-tuple-element.6), channel_id=1, source_target_pairs={{127,0},{0,1},{1,2},{2,3},{3,4},{4,5},{5,6},{6,7},{7,8},{8,9},{9,1... | collective-permute-start | bytes 1843208 | tf_op jit(solution)/shard_map/ppermute | solution.py:17
  54.8 7.3 %copy-start.1 = (bf16[150,2048]{1,0:T(8,128)(2,1)}, bf16[150,2048]{1,0:T(8,128)(2,1)S(1)}, u32[]{:S(2)}) copy-start(bf16[150,2048]{1,0:T(8,128)(2,1)S(1)} %collective-permute-done.9.upper_hbm) | copy-start | bytes 1843204
  62.1 0.8 copy-start.2

commit v4 on v2

--- a/solution.py
+++ b/solution.py
@@ -8,7 +8,8 @@
 from jax.sharding import PartitionSpec as P
 
 HOP = 4
-TILE_BLOCKS = 4
+TILE_BLOCKS = 8
+PAD_ROWS = 160
 
 
 def from_behind(block, axis, distance):
@@ -52,15 +53,16 @@
     return jnp.where(hit, placed[:species].astype(jnp.bfloat16), mixing_ratio)
 
 
-def halo_kernel(block_size, halo_ref, migrated_hbm, out_hbm, sems):
+def halo_kernel(block_size, halo_ref, migrated_hbm, lower_ref, upper_ref, sems):
     sides, listed = halo_ref.shape
+    outs = (lower_ref, upper_ref)
     copies = []
     for side in range(sides):
         for j in range(listed):
             start = pl.multiple_of(halo_ref[side, j] * block_size, block_size)
             copy = pltpu.make_async_copy(
                 migrated_hbm.at[:, pl.ds(start, block_size)],
-                out_hbm.at[side, :, pl.ds(j * block_size, block_size)],
+                outs[side].at[:, pl.ds(j * block_size, block_size)],
                 sems.at[side, j],
             )
             copy.start()
@@ -76,13 +78,15 @@
         num_scalar_prefetch=1,
         grid=(1,),
         in_specs=[pl.BlockSpec(memory_space=pl.ANY)],
-        out_specs=pl.BlockSpec(memory_space=pl.ANY),
+        out_specs=[
+            pl.BlockSpec((species, listed * block_size), lambda i, halo: (0, 0))
+        ] * sides,
         scratch_shapes=[pltpu.SemaphoreType.DMA((sides, listed))],
     )
     listed_blocks = pl.pallas_call(
         functools.partial(halo_kernel, block_size),
         grid_spec=grid_spec,
-        out_shape=jax.ShapeDtypeStruct((sides, species, listed * block_size), migrated.dtype),
+        out_shape=[jax.ShapeDtypeStruct((species, listed * block_size), migrated.dtype)] * sides,
     )(halo_blocks[0], migrated)
     from_lower = from_behind(listed_blocks[1], "region", 1)
     from_upper = from_behind(listed_blocks[0], "region", -1)
@@ -122,8 +126,8 @@
     sems,
     mixed_ref,
     order_split,
-    prod_split,
-    loss_split,
+    gain_split,
+    gain_high,
 ):
     f32 = jnp.float32
     step = pl.program_id(0)
@@ -163,10 +167,22 @@
     @pl.when(step == 0)
     def _():
         fetch(0, 0, True)
-        for source, target in ((order_ref, order_split), (prod_ref, prod_split), (loss_ref, loss_split)):
+        order_high, order_low = split3(order_ref[...])
+        reactions = order_high.shape[0]
+        order_split[0:reactions] = order_high
+        order_split[reactions:] = order_low
+        gain_split[...] = jnp.zeros_like(gain_split)
+        rows = prod_ref.shape[0]
+        for part, source in enumerate((prod_ref, loss_ref)):
             high, low = split3(source[...])
-            target[0] = high
-            target[1] = low
+            gain_split[pl.ds(2 * part * PAD_ROWS, rows)] = high
+            gain_split[pl.ds((2 * part + 1) * PAD_ROWS, rows)] = low
+            gain_high[pl.ds(part * PAD_ROWS, rows)] = high
+        gain_high[...] = jnp.where(
+            lax.broadcasted_iota(jnp.int32, gain_high.shape, 0) % PAD_ROWS < rows,
+            gain_high[...],
+            jnp.zeros_like(gain_high),
+        )
 
     slot = step % 2
 
@@ -178,21 +194,31 @@
 
     for t in range(tile_blocks):
         lanes = slice(t * block_size, (t + 1) * block_size)
-        acc = jnp.dot(own_ref[:, lanes], weight_ref[t, 0], preferred_element_type=f32)
-        for k in range(neighbours):
-            acc = acc + jnp.dot(
-                picked[slot, t * neighbours + k], weight_ref[t, k + 1], preferred_element_type=f32
-            )
-        mixed_ref[:, lanes] = acc
+        stacked = jnp.concatenate(
+            [own_ref[:, lanes]] + [picked[slot, t * neighbours + k] for k in range(neighbours)],
+            axis=1,
+        )
+        weight = weight_ref[t].reshape((neighbours + 1) * block_size, block_size)
+        mixed_ref[:, lanes] = jnp.dot(stacked, weight, preferred_element_type=f32)
     mixed = mixed_ref[...]
+    species = mixed.shape[0]
     log_high, log_low = split3(jnp.log(mixed))
-    exponent = dot3(order_split[0], order_split[1], log_high, log_low)
+    reactions = order_split.shape[0] // 2
+    both = jnp.dot(order_split[...], log_high, preferred_element_type=f32)
+    exponent = both[:reactions] + both[reactions:]
+    exponent = exponent + jnp.dot(order_split[0:reactions], log_low, preferred_element_type=f32)
     prefactor = rate_terms_ref[:, 0:1]
     energy = rate_terms_ref[:, 1:2]
     rate = jnp.exp(prefactor - energy * temp_ref[...] + exponent)
     rate_high, rate_low = split3(rate)
-    gained = dot3(prod_split[0], prod_split[1], rate_high, rate_low)
-    lost_mass = dot3(loss_split[0], loss_split[1], rate_high, rate_low)
+    by_high = jnp.dot(gain_split[...], rate_high, preferred_element_type=f32)
+    by_low = jnp.dot(gain_high[...], rate_low, preferred_element_type=f32)
+    gained = by_high[0:species] + by_high[PAD_ROWS:PAD_ROWS + species] + by_low[0:species]
+    lost_mass = (
+        by_high[2 * PAD_ROWS:2 * PAD_ROWS + species]
+        + by_high[3 * PAD_ROWS:3 * PAD_ROWS + species]
+        + by_low[PAD_ROWS:PAD_ROWS + species]
+    )
     out_ref[...] = (mixed + gained) / (1.0 + lost_mass / mixed)
 
 
@@ -242,9 +268,9 @@
             pltpu.VMEM((2, tile_blocks * neighbours, species, block_size), bf16),
             pltpu.SemaphoreType.DMA((2, tile_blocks * neighbours)),
             pltpu.VMEM((species, width), jnp.float32),
-            pltpu.VMEM((2,) + reactant_order.shape, bf16),
-            pltpu.VMEM((2,) + production.shape, bf16),
-            pltpu.VMEM((2,) + loss_coefficient.shape, bf16),
+            pltpu.VMEM((2 * reactions, species), bf16),
+            pltpu.VMEM((4 * PAD_ROWS, reactions), bf16),
+            pltpu.VMEM((2 * PAD_ROWS, reactions), bf16),
         ],
     )
     kernel = functools.partial(mix_react_kernel, tile_blocks, neighbours, block_size)

time: 125 us -> 78.2 us (0.63)
  Pallas kernels: 64.6 us -> 23.5 us
  waiting for transfers between devices: 15.1 us -> 8.19 us
  starting transfers between devices: 22.5 us -> 25.1 us
    pallas_call x1, Pallas kernels: 39.9 us -> 3.31 us  [halo_exchange(): pl.pallas_call(functools.partial(halo_kernel, block_size), grid_spec=grid...]
    ppermute x10, waiting for transfers between devices: 15.1 us -> 8.19 us  [from_behind(): return lax.ppermute(block, axis, route)]
    pallas_call x1, Pallas kernels: 24.7 us -> 20.2 us  [mix_react(): pl.pallas_call(kernel, grid_spec=grid_spec, out_shape=jax.ShapeDtypeStruc...]
    ppermute x10, starting transfers between devices: 22.5 us -> 25.1 us  [from_behind(): return lax.ppermute(block, axis, route)]
    squeeze x1 -> x0, local copies, waits for them, and re-layouts: 1.35 us -> none  [halo_exchange(): from_upper = from_behind(listed_blocks[0], 'region', -1)]
  transfers between devices with their start and end apart: 10 -> 10, of which waited for: 3 -> 2; matrix products, arithmetic and copies ran while one was open for 2% -> 3% of each run, Pallas kernels for 0% -> 0%
where the time goes in v4:
time: 78.2 us; the launch traced here: 77.7 us
  starting transfers between devices  25.1 us (32%)
  Pallas kernels  23.5 us (30%)
  matrix products  14.3 us (18%)
  waiting for transfers between devices  8.19 us (10%)
  local copies, waits for them, and re-layouts  4.21 us (5%)
  other arithmetic  2.02 us (3%)
    ppermute x10, starting transfers between devices, from_behind(): return lax.ppermute(block, axis, route)  25.1 us
    pallas_call x1, Pallas kernels, mix_react(): pl.pallas_call(kernel, grid_spec=grid_spec, out_shape=jax.ShapeDtypeStruc...  20.2 us
    ppermute x10, waiting for transfers between devices, from_behind(): return lax.ppermute(block, axis, route)  8.19 us
    dot_general x1, matrix products, migrate(): jnp.dot(mixing_ratio, pick, preferred_element_type=f32).astype(jnp.bfloat16)  7.33 us
    dot_general x1, matrix products, migrate(): placed = jnp.dot(marked, place, preferred_element_type=f32)  6.97 us
    pallas_call x1, Pallas kernels, halo_exchange(): pl.pallas_call(functools.partial(halo_kernel, block_size), grid_spec=grid...  3.31 us
    unnamed x38, local copies, waits for them, and re-layouts  2.86 us
    select_n x1, other arithmetic, migrate(): return jnp.where(hit, placed[:species].astype(jnp.bfloat16), mixing_ratio)  1.83 us
  transfers between devices with their start and end apart: 10, of which 2 were waited for; matrix products, arithmetic and copies ran while one was open for 3% of the time, Pallas kernels for 0%

profile of v4, /device:TPU:0, one launch (start us, length us, event | category | flops | bytes accessed | tf_op | source)
XLA Modules:
  0.0 77.7 jit_solution(4314814947550874748)
XLA Ops:
  0.0 0.0 copy-start.4
  0.0 0.0 copy-start.8
  0.0 7.3 %fusion.5 = bf16[1024,150]{0,1:T(8,128)(2,1)S(1)} fusion(bf16[150,8192]{1,0:T(8,128)(2,1)} %param.13, s32[1024]{0:T(1024)} %bitcast.77), kind=kOutput, calls=%fused_computation.8 | convolution fusion | flops 2525124608 | bytes 2768896 | tf_op jit(solution)/shard_map/dot_general | solution.py:39
  7.3 0.1 copy.56
  7.4 0.5 fusion.9
  7.9 3.2 %collective-permute-start = (bf16[150,128]{1,0:T(8,128)(2,1)S(1)}, bf16[150,128]{1,0:T(8,128)(2,1)S(1)}, u32[]{:S(2)}, u32[]{:S(2)}) collective-permute-start(bf16[150,128]{1,0:T(8,128)(2,1)S(1)} %bitcast.71), channel_id=1, source_target_pairs={{124,0},{125,1},{126,2},{127,3},{0,4},{1,5},{2,6},{3,7},{4,8},{5,9... | collective-permute-start | bytes 115208 | tf_op jit(solution)/shard_map/ppermute | solution.py:18
  11.1 0.1 collective-permute-start.1
  11.2 1.0 %collective-permute-start.2 = (bf16[150,128]{1,0:T(8,128)(2,1)S(1)}, bf16[150,128]{1,0:T(8,128)(2,1)S(1)}, u32[]{:S(2)}, u32[]{:S(2)}) collective-permute-start(bf16[150,128]{1,0:T(8,128)(2,1)S(1)} %bitcast.69), channel_id=1, source_target_pairs={{126,0},{127,1},{0,2},{1,3},{2,4},{3,5},{4,6},{5,7},{6,8},{7,9},{8... | collective-permute-start | bytes 115208 | tf_op jit(solution)/shard_map/ppermute | solution.py:18
  12.3 2.3 %collective-permute-start.3 = (bf16[150,128]{1,0:T(8,128)(2,1)S(1)}, bf16[150,128]{1,0:T(8,128)(2,1)S(1)}, u32[]{:S(2)}, u32[]{:S(2)}) collective-permute-start(bf16[150,128]{1,0:T(8,128)(2,1)S(1)} %bitcast.67), channel_id=1, source_target_pairs={{127,0},{0,1},{1,2},{2,3},{3,4},{4,5},{5,6},{6,7},{7,8},{8,9},{9,1... | collective-permute-start | bytes 115208 | tf_op jit(solution)/shard_map/ppermute | solution.py:18
  14.6 5.7 %collective-permute-start.4 = (bf16[150,128]{1,0:T(8,128)(2,1)S(1)}, bf16[150,128]{1,0:T(8,128)(2,1)S(1)}, u32[]{:S(2)}, u32[]{:S(2)}) collective-permute-start(bf16[150,128]{1,0:T(8,128)(2,1)S(1)} %bitcast.66), channel_id=1, source_target_pairs={{1,0},{2,1},{3,2},{4,3},{5,4},{6,5},{7,6},{8,7},{9,8},{10,9},{11,1... | collective-permute-start | bytes 115208 | tf_op jit(solution)/shard_map/ppermute | solution.py:18
  20.2 0.0 copy-done.4
  20.2 0.0 copy-done.8
  20.2 0.1 bitcast_select_fusion
  20.3 0.0 collective-permute-done
  20.3 1.9 %collective-permute-start.5 = (bf16[150,128]{1,0:T(8,128)(2,1)S(1)}, bf16[150,128]{1,0:T(8,128)(2,1)S(1)}, u32[]{:S(2)}, u32[]{:S(2)}) collective-permute-start(bf16[150,128]{1,0:T(8,128)(2,1)S(1)} %bitcast.68), channel_id=1, source_target_pairs={{2,0},{3,1},{4,2},{5,3},{6,4},{7,5},{8,6},{9,7},{10,8},{11,9},{12,... | collective-permute-start | bytes 115208 | tf_op jit(solution)/shard_map/ppermute | solution.py:18
  22.3 0.0 collective-permute-done.1
  22.3 0.2 collective-permute-start.6
  22.5 0.0 collective-permute-done.2
  22.5 3.5 %collective-permute-start.7 = (bf16[150,128]{1,0:T(8,128)(2,1)S(1)}, bf16[150,128]{1,0:T(8,128)(2,1)S(1)}, u32[]{:S(2)}, u32[]{:S(2)}) collective-permute-start(bf16[150,128]{1,0:T(8,128)(2,1)S(1)} %bitcast.64), channel_id=1, source_target_pairs={{4,0},{5,1},{6,2},{7,3},{8,4},{9,5},{10,6},{11,7},{12,8},{13,9},{1... | collective-permute-start | bytes 115208 | tf_op jit(solution)/shard_map/ppermute | solution.py:18
  26.0 0.0 collective-permute-done.3
  26.0 0.0 collective-permute-done.4
  26.1 0.0 collective-permute-done.5
  26.1 0.0 collective-permute-done.6
  26.1 2.4 %collective-permute-done.7 = bf16[150,128]{1,0:T(8,128)(2,1)S(1)} collective-permute-done((bf16[150,128]{1,0:T(8,128)(2,1)S(1)}, bf16[150,128]{1,0:T(8,128)(2,1)S(1)}, u32[]{:S(2)}, u32[]{:S(2)}) %collective-permute-start.7) | collective-permute-done | bytes 38432 | tf_op jit(solution)/shard_map/ppermute | solution.py:18
  28.6 0.0 copy-start
  28.7 7.0 %fusion = f32[151,8192]{1,0:T(8,128)S(1)} fusion(s32[1024]{0:T(1024)S(1)} %bitcast_select_fusion, bf16[150,1024]{1,0:T(8,128)(2,1)S(1)} %bitcast.62), kind=kOutput, calls=%fused_computation.2 | convolution fusion | flops 2541748224 | bytes 5259264 | tf_op jit(solution)/shard_map/dot_general | solution.py:51
  35.6 0.1 compare_reduce_fusion
  35.8 0.0 copy-done
  35.8 0.0 copy-start.5
  35.8 0.0 copy-start.6
  35.8 0.0 copy-start.7
  35.8 0.0 copy-start.3
  35.8 1.8 %fusion.4.migrated_hbm.own_ref = bf16[150,8192]{1,0:T(8,128)(2,1)} fusion(bf16[150,8192]{1,0:T(8,128)(2,1)S(1)} %copy-done, f32[151,8192]{1,0:T(8,128)S(1)} %fusion, pred[8192]{0:T(1024)(128)(4,1)S(1)} %compare_reduce_fusion), kind=kLoop, calls=%fused_computation.7 | loop fusion | flops 1228800 | bytes 7380992 | tf_op jit(solution)/shard_map/jit(_where)/select_n | solution.py:53
  37.6 3.3 %shard_map.127 = (bf16[150,2048]{1,0:T(8,128)(2,1)}, bf16[150,2048]{1,0:T(8,128)(2,1)}) custom-call(s32[2,16]{1,0:T(2,128)} %bitcast.73, bf16[150,8192]{1,0:T(8,128)(2,1)} %fusion.4.migrated_hbm.own_ref), custom_call_target="tpu_custom_call" | custom-call | tf_op jit(solution)/shard_map/pallas_call | solution.py:86
  41.0 0.2 collective-permute-start.8
  41.1 7.1 %collective-permute-start.9 = (bf16[150,2048]{1,0:T(8,128)(2,1)}, bf16[150,2048]{1,0:T(8,128)(2,1)S(1)}, u32[]{:S(2)}, u32[]{:S(2)}) collective-permute-start(bf16[150,2048]{1,0:T(8,128)(2,1)} %get-tuple-element.8), channel_id=1, source_target_pairs={{1,0},{2,1},{3,2},{4,3},{5,4},{6,5},{7,6},{8,7},{9,8},{10,9},{11,1... | collective-permute-start | bytes 1843208 | tf_op jit(solution)/shard_map/ppermute | solution.py:18
  48.2 0.0 copy-done.5
  48.2 0.7 copy.45.nb_ref
  48.9 0.0 copy-done.6
  48.9 0.0 copy-done.7
  48.9 0.8 %copy.47.rate_terms_ref = f32[256,2]{1,0:T(8,128)} copy(f32[256,2]{0,1:T(2,128)S(1)} %pad_maximum_fusion) | data formatting | bytes 4096 | tf_op jit(solution)/shard_map/stack | solution.py:288
  49.7 0.0 copy-done.3
  49.7 0.8 %copy.46.order_ref = f32[256,150]{1,0:T(8,128)} copy(f32[256,150]{0,1:T(8,128)S(1)} %copy-done.3) | data formatting | bytes 307200 | tf_op args[8]
  50.5 5.8 %collective-permute-done.8.lower_hbm = bf16[150,2048]{1,0:T(8,128)(2,1)S(1)} collective-permute-done((bf16[150,2048]{1,0:T(8,128)(2,1)}, bf16[150,2048]{1,0:T(8,128)(2,1)S(1)}, u32[]{:S(2)}, u32[]{:S(2)}) %collective-permute-start.8) | collective-permute-done | bytes 614432 | tf_op jit(solution)/shard_map/ppermute | solution.py:18
  56.3 0.0 copy-start.1
  56.3 0.0 collective-permute-done.9.upper_hbm
  56.3 0.0 copy-start.2
  56.3 0.8 %copy-done.1 = bf16[150,2048]{1,0:T(8,128)(2,1)} copy-done((bf16[150,2048]{1,0:T(8,128)(2,1)}, bf16[150,2048]{1,0:T(8,128)(2,1)S(1)}, u32[]{:S(2)}) %copy-start.1) | copy-done | bytes 614424
  57.2 0.2 copy-done.2
  57.4 20.2 %shard_map.128 = f32[150,8192]{1,0:T(8,128)} custom-call(s32[64,3]{1,0:T(8,128)} %copy.45.nb_ref, bf16[150,8192]{1,0:T(8,128)(2,1)} %fusion.4.migrated_hbm.own_ref, bf16[64,4,128,128]{3,2,1,0:T(8,128)(2,1)} %weight_ref.1, f32[1,8192]{1,0:T(1,128)} %bitcast.72, f32[256,150]{1,0:T(8,128)} %copy.46.order_ref, f32[256,2]{1,0:T(8,128)} %copy.47.rate_terms_ref, ...), custom_call_target="tpu_custom_call" | custom-call | tf_op jit(solution)/shard_map/pallas_call | solution.py:277
  (20 shorter events, 0.3 us)
Async XLA Ops:
  0.0 20.2 %copy-start.4 = (s32[1,8,128]{2,1,0:T(8,128)S(1)}, s32[1,8,128]{2,1,0:T(8,128)}, u32[]{:S(2)}) copy-start(s32[1,8,128]{2,1,0:T(8,128)} %param.16) | copy-start | bytes 12292
  0.0 20.2 %copy-start.8 = (s32[1,8]{1,0:T(1,128)S(1)}, s32[1,8]{1,0:T(1,128)}, u32[]{:S(2)}) copy-start(s32[1,8]{1,0:T(1,128)} %param.15) | copy-start | bytes 100
  7.9 12.4 %collective-permute-start = (bf16[150,128]{1,0:T(8,128)(2,1)S(1)}, bf16[150,128]{1,0:T(8,128)(2,1)S(1)}, u32[]{:S(2)}, u32[]{:S(2)}) collective-permute-start(bf16[150,128]{1,0:T(8,128)(2,1)S(1)} %bitcast.71), channel_id=1, source_target_pairs={{124,0},{125,1},{126,2},{127,3},{0,4},{1,5},{2,6},{3,7},{4,8},{5,9... | collective-permute-start | bytes 115208 | tf_op jit(solution)/shard_map/ppermute | solution.py:18
  11.1 11.1 %collective-permute-start.1 = (bf16[150,128]{1,0:T(8,128)(2,1)S(1)}, bf16[150,128]{1,0:T(8,128)(2,1)S(1)}, u32[]{:S(2)}, u32[]{:S(2)}) collective-permute-start(bf16[150,128]{1,0:T(8,128)(2,1)S(1)} %bitcast.70), channel_id=1, source_target_pairs={{125,0},{126,1},{127,2},{0,3},{1,4},{2,5},{3,6},{4,7},{5,8},{6,9},... | collective-permute-start | bytes 115208 | tf_op jit(solution)/shard_map/ppermute | solution.py:18
  11.2 11.2 %collective-permute-start.2 = (bf16[150,128]{1,0:T(8,128)(2,1)S(1)}, bf16[150,128]{1,0:T(8,128)(2,1)S(1)}, u32[]{:S(2)}, u32[]{:S(2)}) collective-permute-start(bf16[150,128]{1,0:T(8,128)(2,1)S(1)} %bitcast.69), channel_id=1, source_target_pairs={{126,0},{127,1},{0,2},{1,3},{2,4},{3,5},{4,6},{5,7},{6,8},{7,9},{8... | collective-permute-start | bytes 115208 | tf_op jit(solution)/shard_map/ppermute | solution.py:18
  12.3 13.7 %collective-permute-start.3 = (bf16[150,128]{1,0:T(8,128)(2,1)S(1)}, bf16[150,128]{1,0:T(8,128)(2,1)S(1)}, u32[]{:S(2)}, u32[]{:S(2)}) collective-permute-start(bf16[150,128]{1,0:T(8,128)(2,1)S(1)} %bitcast.67), channel_id=1, source_target_pairs={{127,0},{0,1},{1,2},{2,3},{3,4},{4,5},{5,6},{6,7},{7,8},{8,9},{9,1... | collective-permute-start | bytes 115208 | tf_op jit(solution)/shard_map/ppermute | solution.py:18
  14.6 11.5 %collective-permute-start.4 = (bf16[150,128]{1,0:T(8,128)(2,1)S(1)}, bf16[150,128]{1,0:T(8,128)(2,1)S(1)}, u32[]{:S(2)}, u32[]{:S(2)}) collective-permute-start(bf16[150,128]{1,0:T(8,128)(2,1)S(1)} %bitcast.66), channel_id=1, source_target_pairs={{1,0},{2,1},{3,2},{4,3},{5,4},{6,5},{7,6},{8,7},{9,8},{10,9},{11,1... | collective-permute-start | bytes 115208 | tf_op jit(solution)/shard_map/ppermute | solution.py:18
  20.3 5.7 %collective-permute-start.5 = (bf16[150,128]{1,0:T(8,128)(2,1)S(1)}, bf16[150,128]{1,0:T(8,128)(2,1)S(1)}, u32[]{:S(2)}, u32[]{:S(2)}) collective-permute-start(bf16[150,128]{1,0:T(8,128)(2,1)S(1)} %bitcast.68), channel_id=1, source_target_pairs={{2,0},{3,1},{4,2},{5,3},{6,4},{7,5},{8,6},{9,7},{10,8},{11,9},{12,... | collective-permute-start | bytes 115208 | tf_op jit(solution)/shard_map/ppermute | solution.py:18
  22.3 3.8 %collective-permute-start.6 = (bf16[150,128]{1,0:T(8,128)(2,1)S(1)}, bf16[150,128]{1,0:T(8,128)(2,1)S(1)}, u32[]{:S(2)}, u32[]{:S(2)}) collective-permute-start(bf16[150,128]{1,0:T(8,128)(2,1)S(1)} %bitcast.65), channel_id=1, source_target_pairs={{3,0},{4,1},{5,2},{6,3},{7,4},{8,5},{9,6},{10,7},{11,8},{12,9},{13... | collective-permute-start | bytes 115208 | tf_op jit(solution)/shard_map/ppermute | solution.py:18
  22.5 6.0 %collective-permute-start.7 = (bf16[150,128]{1,0:T(8,128)(2,1)S(1)}, bf16[150,128]{1,0:T(8,128)(2,1)S(1)}, u32[]{:S(2)}, u32[]{:S(2)}) collective-permute-start(bf16[150,128]{1,0:T(8,128)(2,1)S(1)} %bitcast.64), channel_id=1, source_target_pairs={{4,0},{5,1},{6,2},{7,3},{8,4},{9,5},{10,6},{11,7},{12,8},{13,9},{1... | collective-permute-start | bytes 115208 | tf_op jit(solution)/shard_map/ppermute | solution.py:18
  28.6 7.1 %copy-start = (bf16[150,8192]{1,0:T(8,128)(2,1)S(1)}, bf16[150,8192]{1,0:T(8,128)(2,1)}, u32[]{:S(2)}) copy-start(bf16[150,8192]{1,0:T(8,128)(2,1)} %param.13) | copy-start | bytes 7372804
  35.8 12.4 %copy-start.5 = (s32[64,3]{0,1:T(4,128)S(1)}, s32[64,3]{0,1:T(4,128)}, u32[]{:S(2)}) copy-start(s32[64,3]{0,1:T(4,128)} %param.18) | copy-start | bytes 2308
  35.8 13.1 %copy-start.6 = (f32[256]{0:T(256)S(1)}, f32[256]{0:T(256)}, u32[]{:S(2)}) copy-start(f32[256]{0:T(256)} %param.23) | copy-start | bytes 3076
  35.8 13.1 %copy-start.7 = (f32[256]{0:T(256)S(1)}, f32[256]{0:T(256)}, u32[]{:S(2)}) copy-start(f32[256]{0:T(256)} %param.22) | copy-start | bytes 3076
  35.8 13.9 %copy-start.3 = (f32[256,150]{0,1:T(8,128)S(1)}, f32[256,150]{0,1:T(8,128)}, u32[]{:S(2)}) copy-start(f32[256,150]{0,1:T(8,128)} %param.21) | copy-start | bytes 460804
  41.0 15.4 %collective-permute-start.8 = (bf16[150,2048]{1,0:T(8,128)(2,1)}, bf16[150,2048]{1,0:T(8,128)(2,1)S(1)}, u32[]{:S(2)}, u32[]{:S(2)}) collective-permute-start(bf16[150,2048]{1,0:T(8,128)(2,1)} %get-tuple-element.7), channel_id=1, source_target_pairs={{127,0},{0,1},{1,2},{2,3},{3,4},{4,5},{5,6},{6,7},{7,8},{8,9},{9,1... | collective-permute-start | bytes 1843208 | tf_op jit(solution)/shard_map/ppermute | solution.py:18
  41.1 15.2 %collective-permute-start.9 = (bf16[150,2048]{1,0:T(8,128)(2,1)}, bf16[150,2048]{1,0:T(8,128)(2,1)S(1)}, u32[]{:S(2)}, u32[]{:S(2)}) collective-permute-start(bf16[150,2048]{1,0:T(8,128)(2,1)} %get-tuple-element.8), channel_id=1, source_target_pairs={{1,0},{2,1},{3,2},{4,3},{5,4},{6,5},{7,6},{8,7},{9,8},{10,9},{11,1... | collective-permute-start | bytes 1843208 | tf_op jit(solution)/shard_map/ppermute | solution.py:18
  56.3 0.8 %copy-start.1 = (bf16[150,2048]{1,0:T(8,128)(2,1)}, bf16[150,2048]{1,0:T(8,128)(2,1)S(1)}, u32[]{:S(2)}) copy-start(bf16[150,2048]{1,0:T(8,128)(2,1)S(1)} %collective-permute-done.8.lower_hbm) | copy-start | bytes 1843204
  56.3 1.0 %copy-start.2 = (bf16[150,2048]{1,0:T(8,128)(2,1)}, bf16[150,2048]{1,0:T(8,128)(2,1)S(1)}, u32[]{:S(2)}) copy-start(bf16[150,2048]{1,0:T(8,128)(2,1)S(1)} %collective-permute-done.9.upper_hbm) | copy-start | bytes 1843204

commit v5 on v4

--- a/solution.py
+++ b/solution.py
@@ -22,21 +22,70 @@
     return [column - HOP if column < HOP else column - HOP + 1 for column in range(2 * HOP)]
 
 
-def one_hot(rows, size, axis):
-    positions = lax.broadcasted_iota(jnp.int32, (size, rows.shape[0]), 0)
-    if axis == 0:
-        return (positions == rows[None, :]).astype(jnp.bfloat16)
-    return (positions.T == rows[:, None]).astype(jnp.bfloat16)
-
-
-def migrate(mixing_ratio, send_rows, migrant_count, arrival_slot):
+def pick_kernel(chunk, mixing_ref, rows_ref, out_ref):
+    species, parcels = mixing_ref.shape
+    wanted = rows_ref[...]
+    total = jnp.zeros(out_ref.shape, jnp.float32)
+    for part in range(parcels // chunk):
+        position = lax.broadcasted_iota(jnp.int32, (chunk, wanted.shape[1]), 0) + part * chunk
+        pick = (position == wanted).astype(jnp.bfloat16)
+        total = total + jnp.dot(
+            mixing_ref[:, part * chunk:(part + 1) * chunk], pick, preferred_element_type=jnp.float32
+        )
+    out_ref[...] = total.astype(out_ref.dtype)
+
+
+def place_kernel(chunk, block_size, halo_ref, mixing_ref, received_ref, slots_ref,
+                 migrated_ref, lower_ref, upper_ref, sems):
+    species, parcels = mixing_ref.shape
+    slots = slots_ref[...]
+    received = received_ref[...]
+    marks = jnp.ones((8, slots.shape[1]), jnp.bfloat16)
+    contract = (((1,), (1,)), ((), ()))
+    for part in range(parcels // chunk):
+        lanes = slice(part * chunk, (part + 1) * chunk)
+        position = lax.broadcasted_iota(jnp.int32, (chunk, slots.shape[1]), 0) + part * chunk
+        place = (position == slots).astype(jnp.bfloat16)
+        placed = lax.dot_general(received, place, contract, preferred_element_type=jnp.float32)
+        hit = lax.dot_general(marks, place, contract, preferred_element_type=jnp.float32)[0:1]
+        migrated_ref[:, lanes] = jnp.where(
+            hit > 0.5, placed.astype(migrated_ref.dtype), mixing_ref[:, lanes]
+        )
+    sides, listed = halo_ref.shape
+    outs = (lower_ref, upper_ref)
+    copies = []
+    for side in range(sides):
+        for j in range(listed):
+            start = pl.multiple_of(halo_ref[side, j] * block_size, block_size)
+            copy = pltpu.make_async_copy(
+                migrated_ref.at[:, pl.ds(start, block_size)],
+                outs[side].at[:, pl.ds(j * block_size, block_size)],
+                sems.at[side, j],
+            )
+            copy.start()
+            copies.append(copy)
+    for copy in copies:
+        copy.wait()
+
+
+def vmem_whole(shape):
+    return pl.BlockSpec(shape, lambda *_: (0,) * len(shape))
+
+
+def migrate(mixing_ratio, send_rows, migrant_count, arrival_slot, halo_blocks, block_size):
     species, parcels = mixing_ratio.shape
     capacity = send_rows.shape[-1]
     offsets = peer_offsets()
     peer_count = len(offsets)
-    f32 = jnp.float32
-    pick = one_hot(send_rows[0].reshape(-1), parcels, 0)
-    outgoing = jnp.dot(mixing_ratio, pick, preferred_element_type=f32).astype(jnp.bfloat16)
+    chunk = 1024
+    wanted = send_rows[0].reshape(1, -1)
+    outgoing = pl.pallas_call(
+        functools.partial(pick_kernel, chunk),
+        grid=(1,),
+        in_specs=[vmem_whole(mixing_ratio.shape), vmem_whole(wanted.shape)],
+        out_specs=vmem_whole((species, wanted.shape[1])),
+        out_shape=jax.ShapeDtypeStruct((species, wanted.shape[1]), mixing_ratio.dtype),
+    )(mixing_ratio, wanted)
     outgoing = outgoing.reshape(species, peer_count, capacity)
     arrived = []
     for column in range(peer_count):
@@ -45,52 +94,28 @@
     received = jnp.stack(arrived, axis=1).reshape(species, -1)
     lane_index = jnp.arange(capacity, dtype=jnp.int32)
     live_lane = lane_index[None, :] < migrant_count[0][:, None]
-    target_slot = jnp.where(live_lane, arrival_slot[0], parcels).reshape(-1)
-    place = one_hot(target_slot, parcels, 1)
-    marked = jnp.concatenate([received, jnp.ones((1, received.shape[1]), received.dtype)], axis=0)
-    placed = jnp.dot(marked, place, preferred_element_type=f32)
-    hit = placed[species:] > 0.5
-    return jnp.where(hit, placed[:species].astype(jnp.bfloat16), mixing_ratio)
-
-
-def halo_kernel(block_size, halo_ref, migrated_hbm, lower_ref, upper_ref, sems):
-    sides, listed = halo_ref.shape
-    outs = (lower_ref, upper_ref)
-    copies = []
-    for side in range(sides):
-        for j in range(listed):
-            start = pl.multiple_of(halo_ref[side, j] * block_size, block_size)
-            copy = pltpu.make_async_copy(
-                migrated_hbm.at[:, pl.ds(start, block_size)],
-                outs[side].at[:, pl.ds(j * block_size, block_size)],
-                sems.at[side, j],
-            )
-            copy.start()
-            copies.append(copy)
-    for copy in copies:
-        copy.wait()
-
-
-def halo_exchange(migrated, halo_blocks, block_size):
-    species = migrated.shape[0]
+    slots = jnp.where(live_lane, arrival_slot[0], parcels).reshape(1, -1)
     sides, listed = halo_blocks.shape[1:]
+    halo_shape = (species, listed * block_size)
     grid_spec = pltpu.PrefetchScalarGridSpec(
         num_scalar_prefetch=1,
         grid=(1,),
-        in_specs=[pl.BlockSpec(memory_space=pl.ANY)],
-        out_specs=[
-            pl.BlockSpec((species, listed * block_size), lambda i, halo: (0, 0))
-        ] * sides,
+        in_specs=[vmem_whole(mixing_ratio.shape), vmem_whole(received.shape), vmem_whole(slots.shape)],
+        out_specs=[vmem_whole(mixing_ratio.shape), vmem_whole(halo_shape), vmem_whole(halo_shape)],
         scratch_shapes=[pltpu.SemaphoreType.DMA((sides, listed))],
     )
-    listed_blocks = pl.pallas_call(
-        functools.partial(halo_kernel, block_size),
+    migrated, to_lower, to_upper = pl.pallas_call(
+        functools.partial(place_kernel, chunk, block_size),
         grid_spec=grid_spec,
-        out_shape=[jax.ShapeDtypeStruct((species, listed * block_size), migrated.dtype)] * sides,
-    )(halo_blocks[0], migrated)
-    from_lower = from_behind(listed_blocks[1], "region", 1)
-    from_upper = from_behind(listed_blocks[0], "region", -1)
-    return from_lower, from_upper
+        out_shape=[
+            jax.ShapeDtypeStruct(mixing_ratio.shape, mixing_ratio.dtype),
+            jax.ShapeDtypeStruct(halo_shape, mixing_ratio.dtype),
+            jax.ShapeDtypeStruct(halo_shape, mixing_ratio.dtype),
+        ],
+    )(halo_blocks[0], mixing_ratio, received, slots)
+    from_lower = from_behind(to_upper, "region", 1)
+    from_upper = from_behind(to_lower, "region", -1)
+    return migrated, from_lower, from_upper
 
 
 def split3(x):
@@ -309,8 +334,9 @@
     production,
     loss_coefficient,
 ):
-    migrated = migrate(mixing_ratio, send_rows, migrant_count, arrival_slot)
-    from_lower, from_upper = halo_exchange(migrated, halo_blocks, mix_weight.shape[-1])
+    migrated, from_lower, from_upper = migrate(
+        mixing_ratio, send_rows, migrant_count, arrival_slot, halo_blocks, mix_weight.shape[-1]
+    )
     return mix_react(
         migrated,
         from_lower,

time: 78.2 us -> 81.2 us (1.038)
  Pallas kernels: 23.5 us -> 41.1 us
  matrix products: 14.3 us -> 0 us
  local copies, waits for them, and re-layouts: 4.21 us -> 5.85 us
  other arithmetic: 2.02 us -> 0.68 us
    pallas_call x1 -> x2, Pallas kernels: 3.31 us -> 21 us  [the longest x1 15.6 us: migrate(): pl.pallas_call(functools.partial(place_kernel, chunk, block_size), grid_s...]
    dot_general x2 -> x0, matrix products: 14.3 us -> none  [the longest x1 7.33 us: migrate(): jnp.dot(mixing_ratio, pick, preferred_element_type=f32).astype(jnp.bfloat16)]
    unnamed x38 -> x36, local copies, waits for them, and re-layouts: 2.86 us -> 4.51 us
    select_n x2 -> x1, other arithmetic: 1.9 us -> 0.6 us  [migrate(): slots = jnp.where(live_lane, arrival_slot[0], parcels).reshape(1, -1)]
  transfers between devices with their start and end apart: 10 -> 10, of which waited for: 2 -> 2; matrix products, arithmetic and copies ran while one was open for 3% -> 4% of each run, Pallas kernels for 0% -> 0%
where the time goes in v5:
time: 81.2 us; the launch traced here: 80.7 us
  Pallas kernels  41.1 us (51%)
  starting transfers between devices  24.7 us (30%)
  waiting for transfers between devices  8.05 us (10%)
  local copies, waits for them, and re-layouts  5.85 us (7%)
    ppermute x10, starting transfers between devices, from_behind(): return lax.ppermute(block, axis, route)  24.7 us
    pallas_call x1, Pallas kernels, mix_react(): pl.pallas_call(kernel, grid_spec=grid_spec, out_shape=jax.ShapeDtypeStruc...  20.2 us
    pallas_call x1, Pallas kernels, migrate(): pl.pallas_call(functools.partial(place_kernel, chunk, block_size), grid_s...  15.6 us
    ppermute x10, waiting for transfers between devices, from_behind(): return lax.ppermute(block, axis, route)  8.05 us
    pallas_call x1, Pallas kernels, migrate(): pl.pallas_call(functools.partial(pick_kernel, chunk), grid=(1,), in_specs...  5.39 us
    unnamed x36, local copies, waits for them, and re-layouts  4.51 us
  transfers between devices with their start and end apart: 10, of which 2 were waited for; matrix products, arithmetic and copies ran while one was open for 4% of the time, Pallas kernels for 0%

profile of v5, /device:TPU:0, one launch (start us, length us, event | category | flops | bytes accessed | tf_op | source)
XLA Modules:
  0.0 80.7 jit_solution(4194533719338383203)
XLA Ops:
  0.0 0.0 copy-start.7
  0.0 0.0 copy-start.3
  0.0 0.0 copy-start.4
  0.0 0.0 copy-start.5
  0.0 0.0 copy-start.6
  0.0 0.0 copy-start.2
  0.0 5.4 %shard_map.127 = bf16[150,1024]{1,0:T(8,128)(2,1)} custom-call(bf16[150,8192]{1,0:T(8,128)(2,1)} %mixing_ref.3, s32[1,1024]{1,0:T(1,128)} %bitcast.71), custom_call_target="tpu_custom_call" | custom-call | tf_op jit(solution)/shard_map/pallas_call | solution.py:82
  5.4 1.0 %copy.57 = bf16[19,8,8,128]{3,2,1,0:T(8,128)(2,1)S(1)} copy(bf16[19,8,8,128]{3,1,2,0:T(8,128)(2,1)} %bitcast.61) | data formatting | bytes 622592
  6.4 0.5 fusion.1
  7.0 3.2 %collective-permute-start = (bf16[150,128]{1,0:T(8,128)(2,1)S(1)}, bf16[150,128]{1,0:T(8,128)(2,1)S(1)}, u32[]{:S(2)}, u32[]{:S(2)}) collective-permute-start(bf16[150,128]{1,0:T(8,128)(2,1)S(1)} %bitcast.69), channel_id=1, source_target_pairs={{124,0},{125,1},{126,2},{127,3},{0,4},{1,5},{2,6},{3,7},{4,8},{5,9... | collective-permute-start | bytes 115208 | tf_op jit(solution)/shard_map/ppermute | solution.py:18
  10.2 0.1 collective-permute-start.1
  10.3 1.0 %collective-permute-start.2 = (bf16[150,128]{1,0:T(8,128)(2,1)S(1)}, bf16[150,128]{1,0:T(8,128)(2,1)S(1)}, u32[]{:S(2)}, u32[]{:S(2)}) collective-permute-start(bf16[150,128]{1,0:T(8,128)(2,1)S(1)} %bitcast.66), channel_id=1, source_target_pairs={{126,0},{127,1},{0,2},{1,3},{2,4},{3,5},{4,6},{5,7},{6,8},{7,9},{8... | collective-permute-start | bytes 115208 | tf_op jit(solution)/shard_map/ppermute | solution.py:18
  11.3 2.3 %collective-permute-start.3 = (bf16[150,128]{1,0:T(8,128)(2,1)S(1)}, bf16[150,128]{1,0:T(8,128)(2,1)S(1)}, u32[]{:S(2)}, u32[]{:S(2)}) collective-permute-start(bf16[150,128]{1,0:T(8,128)(2,1)S(1)} %bitcast.65), channel_id=1, source_target_pairs={{127,0},{0,1},{1,2},{2,3},{3,4},{4,5},{5,6},{6,7},{7,8},{8,9},{9,1... | collective-permute-start | bytes 115208 | tf_op jit(solution)/shard_map/ppermute | solution.py:18
  13.6 5.7 %collective-permute-start.4 = (bf16[150,128]{1,0:T(8,128)(2,1)S(1)}, bf16[150,128]{1,0:T(8,128)(2,1)S(1)}, u32[]{:S(2)}, u32[]{:S(2)}) collective-permute-start(bf16[150,128]{1,0:T(8,128)(2,1)S(1)} %bitcast.64), channel_id=1, source_target_pairs={{1,0},{2,1},{3,2},{4,3},{5,4},{6,5},{7,6},{8,7},{9,8},{10,9},{11,1... | collective-permute-start | bytes 115208 | tf_op jit(solution)/shard_map/ppermute | solution.py:18
  19.2 0.0 copy-done.7
  19.3 0.1 fusion
  19.3 0.0 copy-done.3
  19.3 0.6 bitcast_select_fusion.slots_ref
  20.0 0.0 collective-permute-done
  20.0 1.3 %collective-permute-start.5 = (bf16[150,128]{1,0:T(8,128)(2,1)S(1)}, bf16[150,128]{1,0:T(8,128)(2,1)S(1)}, u32[]{:S(2)}, u32[]{:S(2)}) collective-permute-start(bf16[150,128]{1,0:T(8,128)(2,1)S(1)} %bitcast.67), channel_id=1, source_target_pairs={{2,0},{3,1},{4,2},{5,3},{6,4},{7,5},{8,6},{9,7},{10,8},{11,9},{12,... | collective-permute-start | bytes 115208 | tf_op jit(solution)/shard_map/ppermute | solution.py:18
  21.3 0.0 collective-permute-done.1
  21.3 0.2 collective-permute-start.6
  21.5 0.0 collective-permute-done.2
  21.5 3.7 %collective-permute-start.7 = (bf16[150,128]{1,0:T(8,128)(2,1)S(1)}, bf16[150,128]{1,0:T(8,128)(2,1)S(1)}, u32[]{:S(2)}, u32[]{:S(2)}) collective-permute-start(bf16[150,128]{1,0:T(8,128)(2,1)S(1)} %bitcast.62), channel_id=1, source_target_pairs={{4,0},{5,1},{6,2},{7,3},{8,4},{9,5},{10,6},{11,7},{12,8},{13,9},{1... | collective-permute-start | bytes 115208 | tf_op jit(solution)/shard_map/ppermute | solution.py:18
  25.2 0.0 collective-permute-done.3
  25.2 0.0 collective-permute-done.4
  25.3 0.0 collective-permute-done.5
  25.3 0.0 collective-permute-done.6
  25.3 2.2 %collective-permute-done.7 = bf16[150,128]{1,0:T(8,128)(2,1)S(1)} collective-permute-done((bf16[150,128]{1,0:T(8,128)(2,1)S(1)}, bf16[150,128]{1,0:T(8,128)(2,1)S(1)}, u32[]{:S(2)}, u32[]{:S(2)}) %collective-permute-start.7) | collective-permute-done | bytes 38432 | tf_op jit(solution)/shard_map/ppermute | solution.py:18
  27.6 0.8 copy.58
  28.4 15.6 %shard_map.128 = (bf16[150,8192]{1,0:T(8,128)(2,1)}, bf16[150,2048]{1,0:T(8,128)(2,1)}, bf16[150,2048]{1,0:T(8,128)(2,1)}) custom-call(s32[2,16]{1,0:T(2,128)} %bitcast.73, bf16[150,8192]{1,0:T(8,128)(2,1)} %mixing_ref.3, bf16[150,1024]{1,0:T(8,128)(2,1)} %bitcast.59, s32[1,1024]{1,0:T(1,128)} %bitcast_select_fusion.slots_ref), custom_call_target="tpu_custom_call" | custom-call | tf_op jit(solution)/shard_map/pallas_call | solution.py:107
  44.0 0.2 collective-permute-start.8
  44.2 7.1 %collective-permute-start.9 = (bf16[150,2048]{1,0:T(8,128)(2,1)}, bf16[150,2048]{1,0:T(8,128)(2,1)S(1)}, u32[]{:S(2)}, u32[]{:S(2)}) collective-permute-start(bf16[150,2048]{1,0:T(8,128)(2,1)} %get-tuple-element.10), channel_id=1, source_target_pairs={{1,0},{2,1},{3,2},{4,3},{5,4},{6,5},{7,6},{8,7},{9,8},{10,9},{11,1... | collective-permute-start | bytes 1843208 | tf_op jit(solution)/shard_map/ppermute | solution.py:18
  51.2 0.0 copy-done.4
  51.2 0.7 copy.46.nb_ref
  51.9 0.0 copy-done.5
  51.9 0.0 copy-done.6
  51.9 0.8 copy.48.rate_terms_ref
  52.7 0.0 copy-done.2
  52.7 0.8 %copy.47.order_ref = f32[256,150]{1,0:T(8,128)} copy(f32[256,150]{0,1:T(8,128)S(1)} %copy-done.2) | data formatting | bytes 307200 | tf_op args[8]
  53.6 5.8 %collective-permute-done.8.lower_hbm = bf16[150,2048]{1,0:T(8,128)(2,1)S(1)} collective-permute-done((bf16[150,2048]{1,0:T(8,128)(2,1)}, bf16[150,2048]{1,0:T(8,128)(2,1)S(1)}, u32[]{:S(2)}, u32[]{:S(2)}) %collective-permute-start.8) | collective-permute-done | bytes 614432 | tf_op jit(solution)/shard_map/ppermute | solution.py:18
  59.4 0.0 copy-start
  59.4 0.0 collective-permute-done.9.upper_hbm
  59.4 0.0 copy-start.1
  59.4 0.8 %copy-done = bf16[150,2048]{1,0:T(8,128)(2,1)} copy-done((bf16[150,2048]{1,0:T(8,128)(2,1)}, bf16[150,2048]{1,0:T(8,128)(2,1)S(1)}, u32[]{:S(2)}) %copy-start) | copy-done | bytes 614424
  60.2 0.2 copy-done.1
  60.4 20.2 %shard_map.129 = f32[150,8192]{1,0:T(8,128)} custom-call(s32[64,3]{1,0:T(8,128)} %copy.46.nb_ref, bf16[150,8192]{1,0:T(8,128)(2,1)} %get-tuple-element.8.own_ref.migrated_hbm, bf16[64,4,128,128]{3,2,1,0:T(8,128)(2,1)} %weight_ref.1, f32[1,8192]{1,0:T(1,128)} %bitcast.70, f32[256,150]{1,0:T(8,128)} %copy.47.order_ref, f32[256,2]{1,0:T(8,128)} %copy.48.rate_terms_ref, ...), custom_call_target="tpu_custom_call" | custom-call | tf_op jit(solution)/shard_map/pallas_call | solution.py:302
  (19 shorter events, 0.2 us)
Async XLA Ops:
  0.0 19.2 %copy-start.7 = (s32[1,8]{1,0:T(1,128)S(1)}, s32[1,8]{1,0:T(1,128)}, u32[]{:S(2)}) copy-start(s32[1,8]{1,0:T(1,128)} %param.15) | copy-start | bytes 100
  0.0 19.3 %copy-start.3 = (s32[1,8,128]{2,1,0:T(8,128)S(1)}, s32[1,8,128]{2,1,0:T(8,128)}, u32[]{:S(2)}) copy-start(s32[1,8,128]{2,1,0:T(8,128)} %param.16) | copy-start | bytes 12292
  0.0 51.2 %copy-start.4 = (s32[64,3]{0,1:T(4,128)S(1)}, s32[64,3]{0,1:T(4,128)}, u32[]{:S(2)}) copy-start(s32[64,3]{0,1:T(4,128)} %param.18) | copy-start | bytes 2308
  0.0 51.9 %copy-start.5 = (f32[256]{0:T(256)S(1)}, f32[256]{0:T(256)}, u32[]{:S(2)}) copy-start(f32[256]{0:T(256)} %param.23) | copy-start | bytes 3076
  0.0 51.9 %copy-start.6 = (f32[256]{0:T(256)S(1)}, f32[256]{0:T(256)}, u32[]{:S(2)}) copy-start(f32[256]{0:T(256)} %param.22) | copy-start | bytes 3076
  0.0 52.7 %copy-start.2 = (f32[256,150]{0,1:T(8,128)S(1)}, f32[256,150]{0,1:T(8,128)}, u32[]{:S(2)}) copy-start(f32[256,150]{0,1:T(8,128)} %param.21) | copy-start | bytes 460804
  7.0 13.0 %collective-permute-start = (bf16[150,128]{1,0:T(8,128)(2,1)S(1)}, bf16[150,128]{1,0:T(8,128)(2,1)S(1)}, u32[]{:S(2)}, u32[]{:S(2)}) collective-permute-start(bf16[150,128]{1,0:T(8,128)(2,1)S(1)} %bitcast.69), channel_id=1, source_target_pairs={{124,0},{125,1},{126,2},{127,3},{0,4},{1,5},{2,6},{3,7},{4,8},{5,9... | collective-permute-start | bytes 115208 | tf_op jit(solution)/shard_map/ppermute | solution.py:18
  10.2 11.1 %collective-permute-start.1 = (bf16[150,128]{1,0:T(8,128)(2,1)S(1)}, bf16[150,128]{1,0:T(8,128)(2,1)S(1)}, u32[]{:S(2)}, u32[]{:S(2)}) collective-permute-start(bf16[150,128]{1,0:T(8,128)(2,1)S(1)} %bitcast.68), channel_id=1, source_target_pairs={{125,0},{126,1},{127,2},{0,3},{1,4},{2,5},{3,6},{4,7},{5,8},{6,9},... | collective-permute-start | bytes 115208 | tf_op jit(solution)/shard_map/ppermute | solution.py:18
  10.3 11.2 %collective-permute-start.2 = (bf16[150,128]{1,0:T(8,128)(2,1)S(1)}, bf16[150,128]{1,0:T(8,128)(2,1)S(1)}, u32[]{:S(2)}, u32[]{:S(2)}) collective-permute-start(bf16[150,128]{1,0:T(8,128)(2,1)S(1)} %bitcast.66), channel_id=1, source_target_pairs={{126,0},{127,1},{0,2},{1,3},{2,4},{3,5},{4,6},{5,7},{6,8},{7,9},{8... | collective-permute-start | bytes 115208 | tf_op jit(solution)/shard_map/ppermute | solution.py:18
  11.3 13.9 %collective-permute-start.3 = (bf16[150,128]{1,0:T(8,128)(2,1)S(1)}, bf16[150,128]{1,0:T(8,128)(2,1)S(1)}, u32[]{:S(2)}, u32[]{:S(2)}) collective-permute-start(bf16[150,128]{1,0:T(8,128)(2,1)S(1)} %bitcast.65), channel_id=1, source_target_pairs={{127,0},{0,1},{1,2},{2,3},{3,4},{4,5},{5,6},{6,7},{7,8},{8,9},{9,1... | collective-permute-start | bytes 115208 | tf_op jit(solution)/shard_map/ppermute | solution.py:18
  13.6 11.6 %collective-permute-start.4 = (bf16[150,128]{1,0:T(8,128)(2,1)S(1)}, bf16[150,128]{1,0:T(8,128)(2,1)S(1)}, u32[]{:S(2)}, u32[]{:S(2)}) collective-permute-start(bf16[150,128]{1,0:T(8,128)(2,1)S(1)} %bitcast.64), channel_id=1, source_target_pairs={{1,0},{2,1},{3,2},{4,3},{5,4},{6,5},{7,6},{8,7},{9,8},{10,9},{11,1... | collective-permute-start | bytes 115208 | tf_op jit(solution)/shard_map/ppermute | solution.py:18
  20.0 5.3 %collective-permute-start.5 = (bf16[150,128]{1,0:T(8,128)(2,1)S(1)}, bf16[150,128]{1,0:T(8,128)(2,1)S(1)}, u32[]{:S(2)}, u32[]{:S(2)}) collective-permute-start(bf16[150,128]{1,0:T(8,128)(2,1)S(1)} %bitcast.67), channel_id=1, source_target_pairs={{2,0},{3,1},{4,2},{5,3},{6,4},{7,5},{8,6},{9,7},{10,8},{11,9},{12,... | collective-permute-start | bytes 115208 | tf_op jit(solution)/shard_map/ppermute | solution.py:18
  21.3 4.0 %collective-permute-start.6 = (bf16[150,128]{1,0:T(8,128)(2,1)S(1)}, bf16[150,128]{1,0:T(8,128)(2,1)S(1)}, u32[]{:S(2)}, u32[]{:S(2)}) collective-permute-start(bf16[150,128]{1,0:T(8,128)(2,1)S(1)} %bitcast.63), channel_id=1, source_target_pairs={{3,0},{4,1},{5,2},{6,3},{7,4},{8,5},{9,6},{10,7},{11,8},{12,9},{13... | collective-permute-start | bytes 115208 | tf_op jit(solution)/shard_map/ppermute | solution.py:18
  21.5 6.0 %collective-permute-start.7 = (bf16[150,128]{1,0:T(8,128)(2,1)S(1)}, bf16[150,128]{1,0:T(8,128)(2,1)S(1)}, u32[]{:S(2)}, u32[]{:S(2)}) collective-permute-start(bf16[150,128]{1,0:T(8,128)(2,1)S(1)} %bitcast.62), channel_id=1, source_target_pairs={{4,0},{5,1},{6,2},{7,3},{8,4},{9,5},{10,6},{11,7},{12,8},{13,9},{1... | collective-permute-start | bytes 115208 | tf_op jit(solution)/shard_map/ppermute | solution.py:18
  44.0 15.4 %collective-permute-start.8 = (bf16[150,2048]{1,0:T(8,128)(2,1)}, bf16[150,2048]{1,0:T(8,128)(2,1)S(1)}, u32[]{:S(2)}, u32[]{:S(2)}) collective-permute-start(bf16[150,2048]{1,0:T(8,128)(2,1)} %get-tuple-element.9), channel_id=1, source_target_pairs={{127,0},{0,1},{1,2},{2,3},{3,4},{4,5},{5,6},{6,7},{7,8},{8,9},{9,1... | collective-permute-start | bytes 1843208 | tf_op jit(solution)/shard_map/ppermute | solution.py:18
  44.2 15.2 %collective-permute-start.9 = (bf16[150,2048]{1,0:T(8,128)(2,1)}, bf16[150,2048]{1,0:T(8,128)(2,1)S(1)}, u32[]{:S(2)}, u32[]{:S(2)}) collective-permute-start(bf16[150,2048]{1,0:T(8,128)(2,1)} %get-tuple-element.10), channel_id=1, source_target_pairs={{1,0},{2,1},{3,2},{4,3},{5,4},{6,5},{7,6},{8,7},{9,8},{10,9},{11,1... | collective-permute-start | bytes 1843208 | tf_op jit(solution)/shard_map/ppermute | solution.py:18
  59.4 0.8 %copy-start = (bf16[150,2048]{1,0:T(8,128)(2,1)}, bf16[150,2048]{1,0:T(8,128)(2,1)S(1)}, u32[]{:S(2)}) copy-start(bf16[150,2048]{1,0:T(8,128)(2,1)S(1)} %collective-permute-done.8.lower_hbm) | copy-start | bytes 1843204
  59.4 1.0 %copy-start.1 = (bf16[150,2048]{1,0:T(8,128)(2,1)}, bf16[150,2048]{1,0:T(8,128)(2,1)S(1)}, u32[]{:S(2)}) copy-start(bf16[150,2048]{1,0:T(8,128)(2,1)S(1)} %collective-permute-done.9.upper_hbm) | copy-start | bytes 1843204

commit v6 on v5

--- a/solution.py
+++ b/solution.py
@@ -40,14 +40,13 @@
     species, parcels = mixing_ref.shape
     slots = slots_ref[...]
     received = received_ref[...]
-    marks = jnp.ones((8, slots.shape[1]), jnp.bfloat16)
-    contract = (((1,), (1,)), ((), ()))
+    marks = jnp.ones((8, slots.shape[0]), jnp.bfloat16)
     for part in range(parcels // chunk):
         lanes = slice(part * chunk, (part + 1) * chunk)
-        position = lax.broadcasted_iota(jnp.int32, (chunk, slots.shape[1]), 0) + part * chunk
+        position = lax.broadcasted_iota(jnp.int32, (slots.shape[0], chunk), 1) + part * chunk
         place = (position == slots).astype(jnp.bfloat16)
-        placed = lax.dot_general(received, place, contract, preferred_element_type=jnp.float32)
-        hit = lax.dot_general(marks, place, contract, preferred_element_type=jnp.float32)[0:1]
+        placed = jnp.dot(received, place, preferred_element_type=jnp.float32)
+        hit = jnp.dot(marks, place, preferred_element_type=jnp.float32)[0:1]
         migrated_ref[:, lanes] = jnp.where(
             hit > 0.5, placed.astype(migrated_ref.dtype), mixing_ref[:, lanes]
         )
@@ -94,7 +93,7 @@
     received = jnp.stack(arrived, axis=1).reshape(species, -1)
     lane_index = jnp.arange(capacity, dtype=jnp.int32)
     live_lane = lane_index[None, :] < migrant_count[0][:, None]
-    slots = jnp.where(live_lane, arrival_slot[0], parcels).reshape(1, -1)
+    slots = jnp.where(live_lane, arrival_slot[0], parcels).reshape(-1, 1)
     sides, listed = halo_blocks.shape[1:]
     halo_shape = (species, listed * block_size)
     grid_spec = pltpu.PrefetchScalarGridSpec(

time: 81.2 us -> 77.4 us (0.953)
  Pallas kernels: 41.1 us -> 37 us
    pallas_call x1, Pallas kernels: 15.6 us -> 11.5 us  [migrate(): pl.pallas_call(functools.partial(place_kernel, chunk, block_size), grid_s...]
    unnamed x36 -> x38, local copies, waits for them, and re-layouts: 4.51 us -> 4.81 us
  transfers between devices with their start and end apart: 10 -> 10, of which waited for: 2 -> 2; matrix products, arithmetic and copies ran while one was open for 4% -> 5% of each run, Pallas kernels for 0% -> 0%
where the time goes in v6:
time: 77.4 us; the launch traced here: 77 us
  Pallas kernels  37 us (48%)
  starting transfers between devices  24.7 us (32%)
  waiting for transfers between devices  7.63 us (10%)
  local copies, waits for them, and re-layouts  6.38 us (8%)
  other arithmetic  0.93 us (1%)
    ppermute x10, starting transfers between devices, from_behind(): return lax.ppermute(block, axis, route)  24.7 us
    pallas_call x1, Pallas kernels, mix_react(): pl.pallas_call(kernel, grid_spec=grid_spec, out_shape=jax.ShapeDtypeStruc...  20.2 us
    pallas_call x1, Pallas kernels, migrate(): pl.pallas_call(functools.partial(place_kernel, chunk, block_size), grid_s...  11.5 us
    ppermute x10, waiting for transfers between devices, from_behind(): return lax.ppermute(block, axis, route)  7.63 us
    pallas_call x1, Pallas kernels, migrate(): pl.pallas_call(functools.partial(pick_kernel, chunk), grid=(1,), in_specs...  5.34 us
    unnamed x38, local copies, waits for them, and re-layouts  4.81 us
  transfers between devices with their start and end apart: 10, of which 2 were waited for; matrix products, arithmetic and copies ran while one was open for 5% of the time, Pallas kernels for 0%

profile of v6, /device:TPU:0, one launch (start us, length us, event | category | flops | bytes accessed | tf_op | source)
XLA Modules:
  0.0 77.0 jit_solution(12909515402896049212)
XLA Ops:
  0.0 0.0 copy-start.7
  0.0 0.0 copy-start.3
  0.0 5.3 %shard_map.127 = bf16[150,1024]{1,0:T(8,128)(2,1)} custom-call(bf16[150,8192]{1,0:T(8,128)(2,1)} %mixing_ref.3, s32[1,1024]{1,0:T(1,128)} %bitcast.75), custom_call_target="tpu_custom_call" | custom-call | tf_op jit(solution)/shard_map/pallas_call | solution.py:81
  5.3 1.0 %copy.61 = bf16[19,8,8,128]{3,2,1,0:T(8,128)(2,1)S(1)} copy(bf16[19,8,8,128]{3,1,2,0:T(8,128)(2,1)} %bitcast.64) | data formatting | bytes 622592
  6.4 0.0 copy-start.4
  6.4 0.0 copy-start.5
  6.4 0.0 copy-start.6
  6.4 0.0 copy-start.2
  6.4 0.5 fusion.1
  6.9 3.2 %collective-permute-start = (bf16[150,128]{1,0:T(8,128)(2,1)S(1)}, bf16[150,128]{1,0:T(8,128)(2,1)S(1)}, u32[]{:S(2)}, u32[]{:S(2)}) collective-permute-start(bf16[150,128]{1,0:T(8,128)(2,1)S(1)} %bitcast.72), channel_id=1, source_target_pairs={{124,0},{125,1},{126,2},{127,3},{0,4},{1,5},{2,6},{3,7},{4,8},{5,9... | collective-permute-start | bytes 115208 | tf_op jit(solution)/shard_map/ppermute | solution.py:18
  10.1 0.1 collective-permute-start.1
  10.2 1.0 %collective-permute-start.2 = (bf16[150,128]{1,0:T(8,128)(2,1)S(1)}, bf16[150,128]{1,0:T(8,128)(2,1)S(1)}, u32[]{:S(2)}, u32[]{:S(2)}) collective-permute-start(bf16[150,128]{1,0:T(8,128)(2,1)S(1)} %bitcast.69), channel_id=1, source_target_pairs={{126,0},{127,1},{0,2},{1,3},{2,4},{3,5},{4,6},{5,7},{6,8},{7,9},{8... | collective-permute-start | bytes 115208 | tf_op jit(solution)/shard_map/ppermute | solution.py:18
  11.3 2.3 %collective-permute-start.3 = (bf16[150,128]{1,0:T(8,128)(2,1)S(1)}, bf16[150,128]{1,0:T(8,128)(2,1)S(1)}, u32[]{:S(2)}, u32[]{:S(2)}) collective-permute-start(bf16[150,128]{1,0:T(8,128)(2,1)S(1)} %bitcast.67), channel_id=1, source_target_pairs={{127,0},{0,1},{1,2},{2,3},{3,4},{4,5},{5,6},{6,7},{7,8},{8,9},{9,1... | collective-permute-start | bytes 115208 | tf_op jit(solution)/shard_map/ppermute | solution.py:18
  13.6 5.7 %collective-permute-start.4 = (bf16[150,128]{1,0:T(8,128)(2,1)S(1)}, bf16[150,128]{1,0:T(8,128)(2,1)S(1)}, u32[]{:S(2)}, u32[]{:S(2)}) collective-permute-start(bf16[150,128]{1,0:T(8,128)(2,1)S(1)} %bitcast.66), channel_id=1, source_target_pairs={{1,0},{2,1},{3,2},{4,3},{5,4},{6,5},{7,6},{8,7},{9,8},{10,9},{11,1... | collective-permute-start | bytes 115208 | tf_op jit(solution)/shard_map/ppermute | solution.py:18
  19.2 0.0 copy-done.7
  19.2 0.1 fusion
  19.3 0.3 copy.64
  19.6 0.0 copy-done.3
  19.6 0.2 copy.49
  19.8 0.9 %bitcast_select_fusion.slots_ref = s32[1024,1]{1,0:T(8,128)} fusion(s32[1024,1]{1,0:T(8,128)S(1)} %copy.49, pred[1,1024]{0,1:T(8,128)(4,1)S(1)} %copy.64), kind=kLoop, calls=%fused_computation | loop fusion | flops 1024 | bytes 9216 | tf_op jit(solution)/shard_map/jit(_where)/select_n | solution.py:96
  20.7 0.0 collective-permute-done
  20.7 0.5 collective-permute-start.5
  21.3 0.0 collective-permute-done.1
  21.3 0.3 collective-permute-start.6
  21.6 0.0 collective-permute-done.2
  21.6 4.3 %collective-permute-start.7 = (bf16[150,128]{1,0:T(8,128)(2,1)S(1)}, bf16[150,128]{1,0:T(8,128)(2,1)S(1)}, u32[]{:S(2)}, u32[]{:S(2)}) collective-permute-start(bf16[150,128]{1,0:T(8,128)(2,1)S(1)} %bitcast.65), channel_id=1, source_target_pairs={{4,0},{5,1},{6,2},{7,3},{8,4},{9,5},{10,6},{11,7},{12,8},{13,9},{1... | collective-permute-start | bytes 115208 | tf_op jit(solution)/shard_map/ppermute | solution.py:18
  26.0 0.0 collective-permute-done.3
  26.0 0.0 collective-permute-done.4
  26.0 0.0 collective-permute-done.5
  26.1 0.0 collective-permute-done.6
  26.1 1.8 %collective-permute-done.7 = bf16[150,128]{1,0:T(8,128)(2,1)S(1)} collective-permute-done((bf16[150,128]{1,0:T(8,128)(2,1)S(1)}, bf16[150,128]{1,0:T(8,128)(2,1)S(1)}, u32[]{:S(2)}, u32[]{:S(2)}) %collective-permute-start.7) | collective-permute-done | bytes 38432 | tf_op jit(solution)/shard_map/ppermute | solution.py:18
  28.0 0.8 copy.62
  28.7 11.5 %shard_map.128 = (bf16[150,8192]{1,0:T(8,128)(2,1)}, bf16[150,2048]{1,0:T(8,128)(2,1)}, bf16[150,2048]{1,0:T(8,128)(2,1)}) custom-call(s32[2,16]{1,0:T(2,128)} %bitcast.77, bf16[150,8192]{1,0:T(8,128)(2,1)} %mixing_ref.3, bf16[150,1024]{1,0:T(8,128)(2,1)} %bitcast.62, s32[1024,1]{1,0:T(8,128)} %bitcast_select_fusion.slots_ref), custom_call_target="tpu_custom_call" | custom-call | tf_op jit(solution)/shard_map/pallas_call | solution.py:106
  40.3 0.1 collective-permute-start.8
  40.4 7.1 %collective-permute-start.9 = (bf16[150,2048]{1,0:T(8,128)(2,1)}, bf16[150,2048]{1,0:T(8,128)(2,1)S(1)}, u32[]{:S(2)}, u32[]{:S(2)}) collective-permute-start(bf16[150,2048]{1,0:T(8,128)(2,1)} %get-tuple-element.10), channel_id=1, source_target_pairs={{1,0},{2,1},{3,2},{4,3},{5,4},{6,5},{7,6},{8,7},{9,8},{10,9},{11,1... | collective-permute-start | bytes 1843208 | tf_op jit(solution)/shard_map/ppermute | solution.py:18
  47.5 0.0 copy-done.4
  47.5 0.7 copy.50.nb_ref
  48.2 0.0 copy-done.5
  48.2 0.0 copy-done.6
  48.3 0.8 %copy.52.rate_terms_ref = f32[256,2]{1,0:T(8,128)} copy(f32[256,2]{0,1:T(2,128)S(1)} %pad_maximum_fusion) | data formatting | bytes 4096 | tf_op jit(solution)/shard_map/stack | solution.py:312
  49.0 0.0 copy-done.2
  49.0 0.8 %copy.51.order_ref = f32[256,150]{1,0:T(8,128)} copy(f32[256,150]{0,1:T(8,128)S(1)} %copy-done.2) | data formatting | bytes 307200 | tf_op args[8]
  49.9 5.8 %collective-permute-done.8.lower_hbm = bf16[150,2048]{1,0:T(8,128)(2,1)S(1)} collective-permute-done((bf16[150,2048]{1,0:T(8,128)(2,1)}, bf16[150,2048]{1,0:T(8,128)(2,1)S(1)}, u32[]{:S(2)}, u32[]{:S(2)}) %collective-permute-start.8) | collective-permute-done | bytes 614432 | tf_op jit(solution)/shard_map/ppermute | solution.py:18
  55.7 0.0 copy-start
  55.7 0.0 collective-permute-done.9.upper_hbm
  55.7 0.0 copy-start.1
  55.7 0.8 %copy-done = bf16[150,2048]{1,0:T(8,128)(2,1)} copy-done((bf16[150,2048]{1,0:T(8,128)(2,1)}, bf16[150,2048]{1,0:T(8,128)(2,1)S(1)}, u32[]{:S(2)}) %copy-start) | copy-done | bytes 614424
  56.5 0.2 copy-done.1
  56.7 20.2 %shard_map.129 = f32[150,8192]{1,0:T(8,128)} custom-call(s32[64,3]{1,0:T(8,128)} %copy.50.nb_ref, bf16[150,8192]{1,0:T(8,128)(2,1)} %get-tuple-element.8.own_ref.migrated_hbm, bf16[64,4,128,128]{3,2,1,0:T(8,128)(2,1)} %weight_ref.1, f32[1,8192]{1,0:T(1,128)} %bitcast.73, f32[256,150]{1,0:T(8,128)} %copy.51.order_ref, f32[256,2]{1,0:T(8,128)} %copy.52.rate_terms_ref, ...), custom_call_target="tpu_custom_call" | custom-call | tf_op jit(solution)/shard_map/pallas_call | solution.py:301
  (20 shorter events, 0.2 us)
Async XLA Ops:
  0.0 19.2 %copy-start.7 = (s32[1,8]{1,0:T(1,128)S(1)}, s32[1,8]{1,0:T(1,128)}, u32[]{:S(2)}) copy-start(s32[1,8]{1,0:T(1,128)} %param.15) | copy-start | bytes 100
  0.0 19.6 %copy-start.3 = (s32[1,8,128]{2,1,0:T(8,128)S(1)}, s32[1,8,128]{2,1,0:T(8,128)}, u32[]{:S(2)}) copy-start(s32[1,8,128]{2,1,0:T(8,128)} %param.16) | copy-start | bytes 12292
  6.4 41.2 %copy-start.4 = (s32[64,3]{0,1:T(4,128)S(1)}, s32[64,3]{0,1:T(4,128)}, u32[]{:S(2)}) copy-start(s32[64,3]{0,1:T(4,128)} %param.18) | copy-start | bytes 2308
  6.4 41.9 %copy-start.5 = (f32[256]{0:T(256)S(1)}, f32[256]{0:T(256)}, u32[]{:S(2)}) copy-start(f32[256]{0:T(256)} %param.23) | copy-start | bytes 3076
  6.4 41.9 %copy-start.6 = (f32[256]{0:T(256)S(1)}, f32[256]{0:T(256)}, u32[]{:S(2)}) copy-start(f32[256]{0:T(256)} %param.22) | copy-start | bytes 3076
  6.4 42.6 %copy-start.2 = (f32[256,150]{0,1:T(8,128)S(1)}, f32[256,150]{0,1:T(8,128)}, u32[]{:S(2)}) copy-start(f32[256,150]{0,1:T(8,128)} %param.21) | copy-start | bytes 460804
  6.9 13.8 %collective-permute-start = (bf16[150,128]{1,0:T(8,128)(2,1)S(1)}, bf16[150,128]{1,0:T(8,128)(2,1)S(1)}, u32[]{:S(2)}, u32[]{:S(2)}) collective-permute-start(bf16[150,128]{1,0:T(8,128)(2,1)S(1)} %bitcast.72), channel_id=1, source_target_pairs={{124,0},{125,1},{126,2},{127,3},{0,4},{1,5},{2,6},{3,7},{4,8},{5,9... | collective-permute-start | bytes 115208 | tf_op jit(solution)/shard_map/ppermute | solution.py:18
  10.1 11.1 %collective-permute-start.1 = (bf16[150,128]{1,0:T(8,128)(2,1)S(1)}, bf16[150,128]{1,0:T(8,128)(2,1)S(1)}, u32[]{:S(2)}, u32[]{:S(2)}) collective-permute-start(bf16[150,128]{1,0:T(8,128)(2,1)S(1)} %bitcast.70), channel_id=1, source_target_pairs={{125,0},{126,1},{127,2},{0,3},{1,4},{2,5},{3,6},{4,7},{5,8},{6,9},... | collective-permute-start | bytes 115208 | tf_op jit(solution)/shard_map/ppermute | solution.py:18
  10.2 11.4 %collective-permute-start.2 = (bf16[150,128]{1,0:T(8,128)(2,1)S(1)}, bf16[150,128]{1,0:T(8,128)(2,1)S(1)}, u32[]{:S(2)}, u32[]{:S(2)}) collective-permute-start(bf16[150,128]{1,0:T(8,128)(2,1)S(1)} %bitcast.69), channel_id=1, source_target_pairs={{126,0},{127,1},{0,2},{1,3},{2,4},{3,5},{4,6},{5,7},{6,8},{7,9},{8... | collective-permute-start | bytes 115208 | tf_op jit(solution)/shard_map/ppermute | solution.py:18
  11.3 14.7 %collective-permute-start.3 = (bf16[150,128]{1,0:T(8,128)(2,1)S(1)}, bf16[150,128]{1,0:T(8,128)(2,1)S(1)}, u32[]{:S(2)}, u32[]{:S(2)}) collective-permute-start(bf16[150,128]{1,0:T(8,128)(2,1)S(1)} %bitcast.67), channel_id=1, source_target_pairs={{127,0},{0,1},{1,2},{2,3},{3,4},{4,5},{5,6},{6,7},{7,8},{8,9},{9,1... | collective-permute-start | bytes 115208 | tf_op jit(solution)/shard_map/ppermute | solution.py:18
  13.6 12.4 %collective-permute-start.4 = (bf16[150,128]{1,0:T(8,128)(2,1)S(1)}, bf16[150,128]{1,0:T(8,128)(2,1)S(1)}, u32[]{:S(2)}, u32[]{:S(2)}) collective-permute-start(bf16[150,128]{1,0:T(8,128)(2,1)S(1)} %bitcast.66), channel_id=1, source_target_pairs={{1,0},{2,1},{3,2},{4,3},{5,4},{6,5},{7,6},{8,7},{9,8},{10,9},{11,1... | collective-permute-start | bytes 115208 | tf_op jit(solution)/shard_map/ppermute | solution.py:18
  20.7 5.3 %collective-permute-start.5 = (bf16[150,128]{1,0:T(8,128)(2,1)S(1)}, bf16[150,128]{1,0:T(8,128)(2,1)S(1)}, u32[]{:S(2)}, u32[]{:S(2)}) collective-permute-start(bf16[150,128]{1,0:T(8,128)(2,1)S(1)} %bitcast.71), channel_id=1, source_target_pairs={{2,0},{3,1},{4,2},{5,3},{6,4},{7,5},{8,6},{9,7},{10,8},{11,9},{12,... | collective-permute-start | bytes 115208 | tf_op jit(solution)/shard_map/ppermute | solution.py:18
  21.3 4.8 %collective-permute-start.6 = (bf16[150,128]{1,0:T(8,128)(2,1)S(1)}, bf16[150,128]{1,0:T(8,128)(2,1)S(1)}, u32[]{:S(2)}, u32[]{:S(2)}) collective-permute-start(bf16[150,128]{1,0:T(8,128)(2,1)S(1)} %bitcast.68), channel_id=1, source_target_pairs={{3,0},{4,1},{5,2},{6,3},{7,4},{8,5},{9,6},{10,7},{11,8},{12,9},{13... | collective-permute-start | bytes 115208 | tf_op jit(solution)/shard_map/ppermute | solution.py:18
  21.6 6.3 %collective-permute-start.7 = (bf16[150,128]{1,0:T(8,128)(2,1)S(1)}, bf16[150,128]{1,0:T(8,128)(2,1)S(1)}, u32[]{:S(2)}, u32[]{:S(2)}) collective-permute-start(bf16[150,128]{1,0:T(8,128)(2,1)S(1)} %bitcast.65), channel_id=1, source_target_pairs={{4,0},{5,1},{6,2},{7,3},{8,4},{9,5},{10,6},{11,7},{12,8},{13,9},{1... | collective-permute-start | bytes 115208 | tf_op jit(solution)/shard_map/ppermute | solution.py:18
  40.3 15.4 %collective-permute-start.8 = (bf16[150,2048]{1,0:T(8,128)(2,1)}, bf16[150,2048]{1,0:T(8,128)(2,1)S(1)}, u32[]{:S(2)}, u32[]{:S(2)}) collective-permute-start(bf16[150,2048]{1,0:T(8,128)(2,1)} %get-tuple-element.9), channel_id=1, source_target_pairs={{127,0},{0,1},{1,2},{2,3},{3,4},{4,5},{5,6},{6,7},{7,8},{8,9},{9,1... | collective-permute-start | bytes 1843208 | tf_op jit(solution)/shard_map/ppermute | solution.py:18
  40.4 15.3 %collective-permute-start.9 = (bf16[150,2048]{1,0:T(8,128)(2,1)}, bf16[150,2048]{1,0:T(8,128)(2,1)S(1)}, u32[]{:S(2)}, u32[]{:S(2)}) collective-permute-start(bf16[150,2048]{1,0:T(8,128)(2,1)} %get-tuple-element.10), channel_id=1, source_target_pairs={{1,0},{2,1},{3,2},{4,3},{5,4},{6,5},{7,6},{8,7},{9,8},{10,9},{11,1... | collective-permute-start | bytes 1843208 | tf_op jit(solution)/shard_map/ppermute | solution.py:18
  55.7 0.8 %copy-start = (bf16[150,2048]{1,0:T(8,128)(2,1)}, bf16[150,2048]{1,0:T(8,128)(2,1)S(1)}, u32[]{:S(2)}) copy-start(bf16[150,2048]{1,0:T(8,128)(2,1)S(1)} %collective-permute-done.8.lower_hbm) | copy-start | bytes 1843204
  55.7 1.0 %copy-start.1 = (bf16[150,2048]{1,0:T(8,128)(2,1)}, bf16[150,2048]{1,0:T(8,128)(2,1)S(1)}, u32[]{:S(2)}) copy-start(bf16[150,2048]{1,0:T(8,128)(2,1)S(1)} %collective-permute-done.9.upper_hbm) | copy-start | bytes 1843204

commit v7 on v6

--- a/solution.py
+++ b/solution.py
@@ -22,33 +22,37 @@
     return [column - HOP if column < HOP else column - HOP + 1 for column in range(2 * HOP)]
 
 
-def pick_kernel(chunk, mixing_ref, rows_ref, out_ref):
+def pick_kernel(chunk, mixing_ref, rows_ref, *out_refs):
     species, parcels = mixing_ref.shape
     wanted = rows_ref[...]
-    total = jnp.zeros(out_ref.shape, jnp.float32)
+    total = jnp.zeros((species, wanted.shape[1]), jnp.float32)
     for part in range(parcels // chunk):
         position = lax.broadcasted_iota(jnp.int32, (chunk, wanted.shape[1]), 0) + part * chunk
         pick = (position == wanted).astype(jnp.bfloat16)
         total = total + jnp.dot(
             mixing_ref[:, part * chunk:(part + 1) * chunk], pick, preferred_element_type=jnp.float32
         )
-    out_ref[...] = total.astype(out_ref.dtype)
-
-
-def place_kernel(chunk, block_size, halo_ref, mixing_ref, received_ref, slots_ref,
-                 migrated_ref, lower_ref, upper_ref, sems):
+    width = out_refs[0].shape[1]
+    for column, out_ref in enumerate(out_refs):
+        out_ref[...] = total[:, column * width:(column + 1) * width].astype(out_ref.dtype)
+
+
+def place_kernel(chunk, block_size, peer_count, halo_ref, mixing_ref, *refs):
+    received_refs = refs[:peer_count]
+    slots_ref, migrated_ref, lower_ref, upper_ref, sems = refs[peer_count:]
     species, parcels = mixing_ref.shape
     slots = slots_ref[...]
-    received = received_ref[...]
-    marks = jnp.ones((8, slots.shape[0]), jnp.bfloat16)
+    received = jnp.concatenate([ref[...] for ref in received_refs], axis=1)
+    pad = (-species) % 16 or 16
+    marked = jnp.concatenate([received, jnp.ones((pad, slots.shape[0]), received.dtype)], axis=0)
     for part in range(parcels // chunk):
         lanes = slice(part * chunk, (part + 1) * chunk)
         position = lax.broadcasted_iota(jnp.int32, (slots.shape[0], chunk), 1) + part * chunk
         place = (position == slots).astype(jnp.bfloat16)
-        placed = jnp.dot(received, place, preferred_element_type=jnp.float32)
-        hit = jnp.dot(marks, place, preferred_element_type=jnp.float32)[0:1]
+        placed = jnp.dot(marked, place, preferred_element_type=jnp.float32)
+        hit = placed[species:species + 1]
         migrated_ref[:, lanes] = jnp.where(
-            hit > 0.5, placed.astype(migrated_ref.dtype), mixing_ref[:, lanes]
+            hit > 0.5, placed[:species].astype(migrated_ref.dtype), mixing_ref[:, lanes]
         )
     sides, listed = halo_ref.shape
     outs = (lower_ref, upper_ref)
@@ -82,15 +86,13 @@
         functools.partial(pick_kernel, chunk),
         grid=(1,),
         in_specs=[vmem_whole(mixing_ratio.shape), vmem_whole(wanted.shape)],
-        out_specs=vmem_whole((species, wanted.shape[1])),
-        out_shape=jax.ShapeDtypeStruct((species, wanted.shape[1]), mixing_ratio.dtype),
+        out_specs=[vmem_whole((species, capacity))] * peer_count,
+        out_shape=[jax.ShapeDtypeStruct((species, capacity), mixing_ratio.dtype)] * peer_count,
     )(mixing_ratio, wanted)
-    outgoing = outgoing.reshape(species, peer_count, capacity)
     arrived = []
     for column in range(peer_count):
         opposite = peer_count - 1 - column
-        arrived.append(from_behind(outgoing[:, opposite, :], "region", -offsets[column]))
-    received = jnp.stack(arrived, axis=1).reshape(species, -1)
+        arrived.append(from_behind(outgoing[opposite], "region", -offsets[column]))
     lane_index = jnp.arange(capacity, dtype=jnp.int32)
     live_lane = lane_index[None, :] < migrant_count[0][:, None]
     slots = jnp.where(live_lane, arrival_slot[0], parcels).reshape(-1, 1)
@@ -99,19 +101,21 @@
     grid_spec = pltpu.PrefetchScalarGridSpec(
         num_scalar_prefetch=1,
         grid=(1,),
-        in_specs=[vmem_whole(mixing_ratio.shape), vmem_whole(received.shape), vmem_whole(slots.shape)],
+        in_specs=[vmem_whole(mixing_ratio.shape)]
+        + [vmem_whole((species, capacity))] * peer_count
+        + [vmem_whole(slots.shape)],
         out_specs=[vmem_whole(mixing_ratio.shape), vmem_whole(halo_shape), vmem_whole(halo_shape)],
         scratch_shapes=[pltpu.SemaphoreType.DMA((sides, listed))],
     )
     migrated, to_lower, to_upper = pl.pallas_call(
-        functools.partial(place_kernel, chunk, block_size),
+        functools.partial(place_kernel, chunk, block_size, peer_count),
         grid_spec=grid_spec,
         out_shape=[
             jax.ShapeDtypeStruct(mixing_ratio.shape, mixing_ratio.dtype),
             jax.ShapeDtypeStruct(halo_shape, mixing_ratio.dtype),
             jax.ShapeDtypeStruct(halo_shape, mixing_ratio.dtype),
         ],
-    )(halo_blocks[0], mixing_ratio, received, slots)
+    )(halo_blocks[0], mixing_ratio, *arrived, slots)
     from_lower = from_behind(to_upper, "region", 1)
     from_upper = from_behind(to_lower, "region", -1)
     return migrated, from_lower, from_upper

time: 77.4 us -> 72.7 us (0.939)
  Pallas kernels: 37 us -> 34.2 us
  local copies, waits for them, and re-layouts: 6.38 us -> 5.15 us
    pallas_call x1, Pallas kernels: 11.5 us -> 8.76 us  [migrate(): pl.pallas_call(functools.partial(place_kernel, chunk, block_size, peer_co...]
    unnamed x38 -> x32, local copies, waits for them, and re-layouts: 4.81 us -> 3.46 us
  transfers between devices with their start and end apart: 10 -> 10, of which waited for: 2 -> 2; matrix products, arithmetic and copies ran while one was open for 5% -> 7% of each run, Pallas kernels for 0% -> 0%
where the time goes in v7:
time: 72.7 us; the launch traced here: 72.3 us
  Pallas kernels  34.2 us (47%)
  starting transfers between devices  24.1 us (33%)
  waiting for transfers between devices  7.14 us (10%)
  local copies, waits for them, and re-layouts  5.15 us (7%)
  other arithmetic  1.57 us (2%)
    ppermute x10, starting transfers between devices, from_behind(): return lax.ppermute(block, axis, route)  24.1 us
    pallas_call x1, Pallas kernels, mix_react(): pl.pallas_call(kernel, grid_spec=grid_spec, out_shape=jax.ShapeDtypeStruc...  20.2 us
    pallas_call x1, Pallas kernels, migrate(): pl.pallas_call(functools.partial(place_kernel, chunk, block_size, peer_co...  8.76 us
    ppermute x10, waiting for transfers between devices, from_behind(): return lax.ppermute(block, axis, route)  7.14 us
    pallas_call x1, Pallas kernels, migrate(): pl.pallas_call(functools.partial(pick_kernel, chunk), grid=(1,), in_specs...  5.28 us
    unnamed x32, local copies, waits for them, and re-layouts  3.46 us
  transfers between devices with their start and end apart: 10, of which 2 were waited for; matrix products, arithmetic and copies ran while one was open for 7% of the time, Pallas kernels for 0%

profile of v7, /device:TPU:0, one launch (start us, length us, event | category | flops | bytes accessed | tf_op | source)
XLA Modules:
  0.0 72.3 jit_solution(2579250729935580545)
XLA Ops:
  0.0 0.0 copy-start.11
  0.0 0.0 copy-start.12
  0.0 0.0 copy-start.13
  0.0 0.0 copy-start.2
  0.0 5.3 %shard_map.127 = (bf16[150,128]{1,0:T(8,128)(2,1)}, bf16[150,128]{1,0:T(8,128)(2,1)}, bf16[150,128]{1,0:T(8,128)(2,1)}, bf16[150,128]{1,0:T(8,128)(2,1)}, bf16[1...) custom-call(bf16[150,8192]{1,0:T(8,128)(2,1)} %mixing_ref.3, ...), custom_call_target="tpu_custom_call" | custom-call | tf_op jit(solution)/shard_map/pallas_call | solution.py:85
  5.3 3.1 %collective-permute-start = (bf16[150,128]{1,0:T(8,128)(2,1)}, bf16[150,128]{1,0:T(8,128)(2,1)S(1)}, u32[]{:S(2)}, u32[]{:S(2)}) collective-permute-start(bf16[150,128]{1,0:T(8,128)(2,1)} %get-tuple-element.16), channel_id=1, source_target_pairs={{124,0},{125,1},{126,2},{127,3},{0,4},{1,5},{2,6},{3,7},{4,8},{5,9... | collective-permute-start | bytes 115208 | tf_op jit(solution)/shard_map/ppermute | solution.py:18
  8.4 0.0 collective-permute-start.1
  8.4 1.0 %collective-permute-start.2 = (bf16[150,128]{1,0:T(8,128)(2,1)}, bf16[150,128]{1,0:T(8,128)(2,1)S(1)}, u32[]{:S(2)}, u32[]{:S(2)}) collective-permute-start(bf16[150,128]{1,0:T(8,128)(2,1)} %get-tuple-element.18), channel_id=1, source_target_pairs={{126,0},{127,1},{0,2},{1,3},{2,4},{3,5},{4,6},{5,7},{6,8},{7,9},{8... | collective-permute-start | bytes 115208 | tf_op jit(solution)/shard_map/ppermute | solution.py:18
  9.4 2.2 %collective-permute-start.3 = (bf16[150,128]{1,0:T(8,128)(2,1)}, bf16[150,128]{1,0:T(8,128)(2,1)S(1)}, u32[]{:S(2)}, u32[]{:S(2)}) collective-permute-start(bf16[150,128]{1,0:T(8,128)(2,1)} %get-tuple-element.19), channel_id=1, source_target_pairs={{127,0},{0,1},{1,2},{2,3},{3,4},{4,5},{5,6},{6,7},{7,8},{8,9},{9,1... | collective-permute-start | bytes 115208 | tf_op jit(solution)/shard_map/ppermute | solution.py:18
  11.6 5.6 %collective-permute-start.4 = (bf16[150,128]{1,0:T(8,128)(2,1)}, bf16[150,128]{1,0:T(8,128)(2,1)S(1)}, u32[]{:S(2)}, u32[]{:S(2)}) collective-permute-start(bf16[150,128]{1,0:T(8,128)(2,1)} %get-tuple-element.20), channel_id=1, source_target_pairs={{1,0},{2,1},{3,2},{4,3},{5,4},{6,5},{7,6},{8,7},{9,8},{10,9},{11,1... | collective-permute-start | bytes 115208 | tf_op jit(solution)/shard_map/ppermute | solution.py:18
  17.2 0.7 %fusion = pred[1,1,8,128]{3,2,1,0:T(8,128)(4,1)S(1)} fusion(s32[8]{0:T(128)} %bitcast.22), kind=kLoop, calls=%fused_computation.3 | loop fusion | flops 1024 | bytes 1056
  17.9 0.3 copy.28
  18.2 0.9 %copy.23 = s32[1024,1]{1,0:T(8,128)S(1)} copy(s32[1024,1]{0,1:T(1,128)} %bitcast.18) | data formatting | bytes 8192 | tf_op jit(solution)/shard_map/squeeze | solution.py:98
  19.1 0.0 collective-permute-done.refs_0_
  19.1 0.0 copy-start.3
  19.2 0.6 collective-permute-start.5
  19.8 0.0 collective-permute-done.1.refs_1_
  19.8 0.0 copy-start.4
  19.8 0.3 collective-permute-start.6
  20.1 0.0 collective-permute-done.2.refs_2_
  20.1 0.0 copy-start.5
  20.1 4.0 %collective-permute-start.7 = (bf16[150,128]{1,0:T(8,128)(2,1)}, bf16[150,128]{1,0:T(8,128)(2,1)S(1)}, u32[]{:S(2)}, u32[]{:S(2)}) collective-permute-start(bf16[150,128]{1,0:T(8,128)(2,1)} %get-tuple-element.23), channel_id=1, source_target_pairs={{4,0},{5,1},{6,2},{7,3},{8,4},{9,5},{10,6},{11,7},{12,8},{13,9},{1... | collective-permute-start | bytes 115208 | tf_op jit(solution)/shard_map/ppermute | solution.py:18
  24.1 0.8 %bitcast_select_fusion.refs_8_ = s32[1024,1]{1,0:T(8,128)} fusion(s32[1024,1]{1,0:T(8,128)S(1)} %copy.23, pred[1,1024]{0,1:T(8,128)(4,1)S(1)} %copy.28), kind=kLoop, calls=%fused_computation | loop fusion | flops 1024 | bytes 9216 | tf_op jit(solution)/shard_map/jit(_where)/select_n | solution.py:98
  24.9 0.0 collective-permute-done.3.refs_3_
  24.9 0.0 copy-start.6
  24.9 0.0 collective-permute-done.4.refs_4_
  24.9 0.0 copy-start.7
  25.0 0.0 collective-permute-done.5.refs_5_
  25.0 0.0 copy-start.8
  25.0 0.0 collective-permute-done.6.refs_6_
  25.0 0.0 copy-start.9
  25.0 1.3 %collective-permute-done.7.refs_7_ = bf16[150,128]{1,0:T(8,128)(2,1)S(1)} collective-permute-done((bf16[150,128]{1,0:T(8,128)(2,1)}, bf16[150,128]{1,0:T(8,128)(2,1)S(1)}, u32[]{:S(2)}, u32[]{:S(2)}) %collective-permute-start.7) | collective-permute-done | bytes 38432 | tf_op jit(solution)/shard_map/ppermute | solution.py:18
  26.3 0.0 copy-start.10
  26.3 0.0 copy-done.3
  26.3 0.0 copy-done.4
  26.3 0.0 copy-done.5
  26.3 0.0 copy-done.6
  26.3 0.0 copy-done.7
  26.4 0.0 copy-done.8
  26.4 0.0 copy-done.9
  26.4 0.6 copy-done.10
  26.9 8.8 %shard_map.128 = (bf16[150,8192]{1,0:T(8,128)(2,1)}, bf16[150,2048]{1,0:T(8,128)(2,1)}, bf16[150,2048]{1,0:T(8,128)(2,1)}) custom-call(s32[2,16]{1,0:T(2,128)} %bitcast.19, bf16[150,8192]{1,0:T(8,128)(2,1)} %mixing_ref.3, bf16[150,128]{1,0:T(8,128)(2,1)} %copy-done.3, bf16[150,128]{1,0:T(8,128)(2,1)} %copy-done.4, bf16[150,128]{1,0:T(8,128)(2,1)} %copy-done.5, ...), custom_call_target="tpu_custom_call" | custom-call | tf_op jit(solution)/shard_map/pallas_call | solution.py:110
  35.7 0.2 collective-permute-start.8
  35.9 7.1 %collective-permute-start.9 = (bf16[150,2048]{1,0:T(8,128)(2,1)}, bf16[150,2048]{1,0:T(8,128)(2,1)S(1)}, u32[]{:S(2)}, u32[]{:S(2)}) collective-permute-start(bf16[150,2048]{1,0:T(8,128)(2,1)} %get-tuple-element.26), channel_id=1, source_target_pairs={{1,0},{2,1},{3,2},{4,3},{5,4},{6,5},{7,6},{8,7},{9,8},{10,9},{11,1... | collective-permute-start | bytes 1843208 | tf_op jit(solution)/shard_map/ppermute | solution.py:18
  43.0 0.0 copy-done.11
  43.0 0.7 copy.24.nb_ref
  43.7 0.0 copy-done.12
  43.7 0.0 copy-done.13
  43.7 0.8 %copy.26.rate_terms_ref = f32[256,2]{1,0:T(8,128)} copy(f32[256,2]{0,1:T(2,128)S(1)} %pad_maximum_fusion) | data formatting | bytes 4096 | tf_op jit(solution)/shard_map/stack | solution.py:316
  44.5 0.0 copy-done.2
  44.5 0.8 %copy.25.order_ref = f32[256,150]{1,0:T(8,128)} copy(f32[256,150]{0,1:T(8,128)S(1)} %copy-done.2) | data formatting | bytes 307200 | tf_op args[8]
  45.3 5.8 %collective-permute-done.8.lower_hbm = bf16[150,2048]{1,0:T(8,128)(2,1)S(1)} collective-permute-done((bf16[150,2048]{1,0:T(8,128)(2,1)}, bf16[150,2048]{1,0:T(8,128)(2,1)S(1)}, u32[]{:S(2)}, u32[]{:S(2)}) %collective-permute-start.8) | collective-permute-done | bytes 614432 | tf_op jit(solution)/shard_map/ppermute | solution.py:18
  51.1 0.0 copy-start
  51.1 0.0 collective-permute-done.9.upper_hbm
  51.1 0.0 copy-start.1
  51.1 0.8 %copy-done = bf16[150,2048]{1,0:T(8,128)(2,1)} copy-done((bf16[150,2048]{1,0:T(8,128)(2,1)}, bf16[150,2048]{1,0:T(8,128)(2,1)S(1)}, u32[]{:S(2)}) %copy-start) | copy-done | bytes 614424
  51.9 0.2 copy-done.1
  52.1 20.2 %shard_map.129 = f32[150,8192]{1,0:T(8,128)} custom-call(s32[64,3]{1,0:T(8,128)} %copy.24.nb_ref, bf16[150,8192]{1,0:T(8,128)(2,1)} %get-tuple-element.24.own_ref.migrated_hbm, bf16[64,4,128,128]{3,2,1,0:T(8,128)(2,1)} %weight_ref.1, f32[1,8192]{1,0:T(1,128)} %bitcast.15, f32[256,150]{1,0:T(8,128)} %copy.25.order_ref, f32[256,2]{1,0:T(8,128)} %copy.26.rate_terms_ref, ...), custom_call_target="tpu_custom_call" | custom-call | tf_op jit(solution)/shard_map/pallas_call | solution.py:305
  (2 shorter events, 0.0 us)
Async XLA Ops:
  0.0 43.0 %copy-start.11 = (s32[64,3]{0,1:T(4,128)S(1)}, s32[64,3]{0,1:T(4,128)}, u32[]{:S(2)}) copy-start(s32[64,3]{0,1:T(4,128)} %param.18) | copy-start | bytes 2308
  0.0 43.7 %copy-start.12 = (f32[256]{0:T(256)S(1)}, f32[256]{0:T(256)}, u32[]{:S(2)}) copy-start(f32[256]{0:T(256)} %param.23) | copy-start | bytes 3076
  0.0 43.7 %copy-start.13 = (f32[256]{0:T(256)S(1)}, f32[256]{0:T(256)}, u32[]{:S(2)}) copy-start(f32[256]{0:T(256)} %param.22) | copy-start | bytes 3076
  0.0 44.5 %copy-start.2 = (f32[256,150]{0,1:T(8,128)S(1)}, f32[256,150]{0,1:T(8,128)}, u32[]{:S(2)}) copy-start(f32[256,150]{0,1:T(8,128)} %param.21) | copy-start | bytes 460804
  5.3 13.8 %collective-permute-start = (bf16[150,128]{1,0:T(8,128)(2,1)}, bf16[150,128]{1,0:T(8,128)(2,1)S(1)}, u32[]{:S(2)}, u32[]{:S(2)}) collective-permute-start(bf16[150,128]{1,0:T(8,128)(2,1)} %get-tuple-element.16), channel_id=1, source_target_pairs={{124,0},{125,1},{126,2},{127,3},{0,4},{1,5},{2,6},{3,7},{4,8},{5,9... | collective-permute-start | bytes 115208 | tf_op jit(solution)/shard_map/ppermute | solution.py:18
  8.4 11.4 %collective-permute-start.1 = (bf16[150,128]{1,0:T(8,128)(2,1)}, bf16[150,128]{1,0:T(8,128)(2,1)S(1)}, u32[]{:S(2)}, u32[]{:S(2)}) collective-permute-start(bf16[150,128]{1,0:T(8,128)(2,1)} %get-tuple-element.17), channel_id=1, source_target_pairs={{125,0},{126,1},{127,2},{0,3},{1,4},{2,5},{3,6},{4,7},{5,8},{6,9},... | collective-permute-start | bytes 115208 | tf_op jit(solution)/shard_map/ppermute | solution.py:18
  8.4 11.7 %collective-permute-start.2 = (bf16[150,128]{1,0:T(8,128)(2,1)}, bf16[150,128]{1,0:T(8,128)(2,1)S(1)}, u32[]{:S(2)}, u32[]{:S(2)}) collective-permute-start(bf16[150,128]{1,0:T(8,128)(2,1)} %get-tuple-element.18), channel_id=1, source_target_pairs={{126,0},{127,1},{0,2},{1,3},{2,4},{3,5},{4,6},{5,7},{6,8},{7,9},{8... | collective-permute-start | bytes 115208 | tf_op jit(solution)/shard_map/ppermute | solution.py:18
  9.4 15.5 %collective-permute-start.3 = (bf16[150,128]{1,0:T(8,128)(2,1)}, bf16[150,128]{1,0:T(8,128)(2,1)S(1)}, u32[]{:S(2)}, u32[]{:S(2)}) collective-permute-start(bf16[150,128]{1,0:T(8,128)(2,1)} %get-tuple-element.19), channel_id=1, source_target_pairs={{127,0},{0,1},{1,2},{2,3},{3,4},{4,5},{5,6},{6,7},{7,8},{8,9},{9,1... | collective-permute-start | bytes 115208 | tf_op jit(solution)/shard_map/ppermute | solution.py:18
  11.6 13.3 %collective-permute-start.4 = (bf16[150,128]{1,0:T(8,128)(2,1)}, bf16[150,128]{1,0:T(8,128)(2,1)S(1)}, u32[]{:S(2)}, u32[]{:S(2)}) collective-permute-start(bf16[150,128]{1,0:T(8,128)(2,1)} %get-tuple-element.20), channel_id=1, source_target_pairs={{1,0},{2,1},{3,2},{4,3},{5,4},{6,5},{7,6},{8,7},{9,8},{10,9},{11,1... | collective-permute-start | bytes 115208 | tf_op jit(solution)/shard_map/ppermute | solution.py:18
  19.1 7.2 %copy-start.3 = (bf16[150,128]{1,0:T(8,128)(2,1)}, bf16[150,128]{1,0:T(8,128)(2,1)S(1)}, u32[]{:S(2)}) copy-start(bf16[150,128]{1,0:T(8,128)(2,1)S(1)} %collective-permute-done.refs_0_) | copy-start | bytes 115204
  19.2 5.8 %collective-permute-start.5 = (bf16[150,128]{1,0:T(8,128)(2,1)}, bf16[150,128]{1,0:T(8,128)(2,1)S(1)}, u32[]{:S(2)}, u32[]{:S(2)}) collective-permute-start(bf16[150,128]{1,0:T(8,128)(2,1)} %get-tuple-element.21), channel_id=1, source_target_pairs={{2,0},{3,1},{4,2},{5,3},{6,4},{7,5},{8,6},{9,7},{10,8},{11,9},{12,... | collective-permute-start | bytes 115208 | tf_op jit(solution)/shard_map/ppermute | solution.py:18
  19.8 6.5 %copy-start.4 = (bf16[150,128]{1,0:T(8,128)(2,1)}, bf16[150,128]{1,0:T(8,128)(2,1)S(1)}, u32[]{:S(2)}) copy-start(bf16[150,128]{1,0:T(8,128)(2,1)S(1)} %collective-permute-done.1.refs_1_) | copy-start | bytes 115204
  19.8 5.2 %collective-permute-start.6 = (bf16[150,128]{1,0:T(8,128)(2,1)}, bf16[150,128]{1,0:T(8,128)(2,1)S(1)}, u32[]{:S(2)}, u32[]{:S(2)}) collective-permute-start(bf16[150,128]{1,0:T(8,128)(2,1)} %get-tuple-element.22), channel_id=1, source_target_pairs={{3,0},{4,1},{5,2},{6,3},{7,4},{8,5},{9,6},{10,7},{11,8},{12,9},{13... | collective-permute-start | bytes 115208 | tf_op jit(solution)/shard_map/ppermute | solution.py:18
  20.1 6.2 %copy-start.5 = (bf16[150,128]{1,0:T(8,128)(2,1)}, bf16[150,128]{1,0:T(8,128)(2,1)S(1)}, u32[]{:S(2)}) copy-start(bf16[150,128]{1,0:T(8,128)(2,1)S(1)} %collective-permute-done.2.refs_2_) | copy-start | bytes 115204
  20.1 6.2 %collective-permute-start.7 = (bf16[150,128]{1,0:T(8,128)(2,1)}, bf16[150,128]{1,0:T(8,128)(2,1)S(1)}, u32[]{:S(2)}, u32[]{:S(2)}) collective-permute-start(bf16[150,128]{1,0:T(8,128)(2,1)} %get-tuple-element.23), channel_id=1, source_target_pairs={{4,0},{5,1},{6,2},{7,3},{8,4},{9,5},{10,6},{11,7},{12,8},{13,9},{1... | collective-permute-start | bytes 115208 | tf_op jit(solution)/shard_map/ppermute | solution.py:18
  24.9 1.4 %copy-start.6 = (bf16[150,128]{1,0:T(8,128)(2,1)}, bf16[150,128]{1,0:T(8,128)(2,1)S(1)}, u32[]{:S(2)}) copy-start(bf16[150,128]{1,0:T(8,128)(2,1)S(1)} %collective-permute-done.3.refs_3_) | copy-start | bytes 115204
  24.9 1.4 %copy-start.7 = (bf16[150,128]{1,0:T(8,128)(2,1)}, bf16[150,128]{1,0:T(8,128)(2,1)S(1)}, u32[]{:S(2)}) copy-start(bf16[150,128]{1,0:T(8,128)(2,1)S(1)} %collective-permute-done.4.refs_4_) | copy-start | bytes 115204
  25.0 1.4 %copy-start.8 = (bf16[150,128]{1,0:T(8,128)(2,1)}, bf16[150,128]{1,0:T(8,128)(2,1)S(1)}, u32[]{:S(2)}) copy-start(bf16[150,128]{1,0:T(8,128)(2,1)S(1)} %collective-permute-done.5.refs_5_) | copy-start | bytes 115204
  25.0 1.4 %copy-start.9 = (bf16[150,128]{1,0:T(8,128)(2,1)}, bf16[150,128]{1,0:T(8,128)(2,1)S(1)}, u32[]{:S(2)}) copy-start(bf16[150,128]{1,0:T(8,128)(2,1)S(1)} %collective-permute-done.6.refs_6_) | copy-start | bytes 115204
  26.3 0.6 copy-start.10
  35.7 15.4 %collective-permute-start.8 = (bf16[150,2048]{1,0:T(8,128)(2,1)}, bf16[150,2048]{1,0:T(8,128)(2,1)S(1)}, u32[]{:S(2)}, u32[]{:S(2)}) collective-permute-start(bf16[150,2048]{1,0:T(8,128)(2,1)} %get-tuple-element.25), channel_id=1, source_target_pairs={{127,0},{0,1},{1,2},{2,3},{3,4},{4,5},{5,6},{6,7},{7,8},{8,9},{9,1... | collective-permute-start | bytes 1843208 | tf_op jit(solution)/shard_map/ppermute | solution.py:18
  35.9 15.2 %collective-permute-start.9 = (bf16[150,2048]{1,0:T(8,128)(2,1)}, bf16[150,2048]{1,0:T(8,128)(2,1)S(1)}, u32[]{:S(2)}, u32[]{:S(2)}) collective-permute-start(bf16[150,2048]{1,0:T(8,128)(2,1)} %get-tuple-element.26), channel_id=1, source_target_pairs={{1,0},{2,1},{3,2},{4,3},{5,4},{6,5},{7,6},{8,7},{9,8},{10,9},{11,1... | collective-permute-start | bytes 1843208 | tf_op jit(solution)/shard_map/ppermute | solution.py:18
  51.1 0.8 %copy-start = (bf16[150,2048]{1,0:T(8,128)(2,1)}, bf16[150,2048]{1,0:T(8,128)(2,1)S(1)}, u32[]{:S(2)}) copy-start(bf16[150,2048]{1,0:T(8,128)(2,1)S(1)} %collective-permute-done.8.lower_hbm) | copy-start | bytes 1843204
  51.1 1.0 %copy-start.1 = (bf16[150,2048]{1,0:T(8,128)(2,1)}, bf16[150,2048]{1,0:T(8,128)(2,1)S(1)}, u32[]{:S(2)}) copy-start(bf16[150,2048]{1,0:T(8,128)(2,1)S(1)} %collective-permute-done.9.upper_hbm) | copy-start | bytes 1843204

commit v8 on v7

--- a/solution.py
+++ b/solution.py
@@ -26,9 +26,9 @@
     species, parcels = mixing_ref.shape
     wanted = rows_ref[...]
     total = jnp.zeros((species, wanted.shape[1]), jnp.float32)
+    position = lax.broadcasted_iota(jnp.int32, (chunk, wanted.shape[1]), 0)
     for part in range(parcels // chunk):
-        position = lax.broadcasted_iota(jnp.int32, (chunk, wanted.shape[1]), 0) + part * chunk
-        pick = (position == wanted).astype(jnp.bfloat16)
+        pick = (position == wanted - part * chunk).astype(jnp.bfloat16)
         total = total + jnp.dot(
             mixing_ref[:, part * chunk:(part + 1) * chunk], pick, preferred_element_type=jnp.float32
         )
@@ -45,10 +45,10 @@
     received = jnp.concatenate([ref[...] for ref in received_refs], axis=1)
     pad = (-species) % 16 or 16
     marked = jnp.concatenate([received, jnp.ones((pad, slots.shape[0]), received.dtype)], axis=0)
+    position = lax.broadcasted_iota(jnp.int32, (slots.shape[0], chunk), 1)
     for part in range(parcels // chunk):
         lanes = slice(part * chunk, (part + 1) * chunk)
-        position = lax.broadcasted_iota(jnp.int32, (slots.shape[0], chunk), 1) + part * chunk
-        place = (position == slots).astype(jnp.bfloat16)
+        place = (position == slots - part * chunk).astype(jnp.bfloat16)
         placed = jnp.dot(marked, place, preferred_element_type=jnp.float32)
         hit = placed[species:species + 1]
         migrated_ref[:, lanes] = jnp.where(

time: 72.7 us -> 73.3 us (level)
  no operation moved by 1% of the time
where the time goes in v8:
time: 73.3 us; the launch traced here: 72.9 us
  Pallas kernels  34.9 us (48%)
  starting transfers between devices  24.1 us (33%)
  waiting for transfers between devices  7.14 us (10%)
  local copies, waits for them, and re-layouts  5.15 us (7%)
  other arithmetic  1.57 us (2%)
    ppermute x10, starting transfers between devices, from_behind(): return lax.ppermute(block, axis, route)  24.1 us
    pallas_call x1, Pallas kernels, mix_react(): pl.pallas_call(kernel, grid_spec=grid_spec, out_shape=jax.ShapeDtypeStruc...  20.2 us
    pallas_call x1, Pallas kernels, migrate(): pl.pallas_call(functools.partial(place_kernel, chunk, block_size, peer_co...  9.34 us
    ppermute x10, waiting for transfers between devices, from_behind(): return lax.ppermute(block, axis, route)  7.14 us
    pallas_call x1, Pallas kernels, migrate(): pl.pallas_call(functools.partial(pick_kernel, chunk), grid=(1,), in_specs...  5.37 us
    unnamed x32, local copies, waits for them, and re-layouts  3.46 us
  transfers between devices with their start and end apart: 10, of which 2 were waited for; matrix products, arithmetic and copies ran while one was open for 7% of the time, Pallas kernels for 0%

profile of v8, /device:TPU:0, one launch (start us, length us, event | category | flops | bytes accessed | tf_op | source)
XLA Modules:
  0.0 72.9 jit_solution(13887264156734397982)
XLA Ops:
  0.0 0.0 copy-start.11
  0.0 0.0 copy-start.12
  0.0 0.0 copy-start.13
  0.0 0.0 copy-start.2
  0.0 5.4 %shard_map.127 = (bf16[150,128]{1,0:T(8,128)(2,1)}, bf16[150,128]{1,0:T(8,128)(2,1)}, bf16[150,128]{1,0:T(8,128)(2,1)}, bf16[150,128]{1,0:T(8,128)(2,1)}, bf16[1...) custom-call(bf16[150,8192]{1,0:T(8,128)(2,1)} %mixing_ref.3, ...), custom_call_target="tpu_custom_call" | custom-call | tf_op jit(solution)/shard_map/pallas_call | solution.py:85
  5.4 3.1 %collective-permute-start = (bf16[150,128]{1,0:T(8,128)(2,1)}, bf16[150,128]{1,0:T(8,128)(2,1)S(1)}, u32[]{:S(2)}, u32[]{:S(2)}) collective-permute-start(bf16[150,128]{1,0:T(8,128)(2,1)} %get-tuple-element.16), channel_id=1, source_target_pairs={{124,0},{125,1},{126,2},{127,3},{0,4},{1,5},{2,6},{3,7},{4,8},{5,9... | collective-permute-start | bytes 115208 | tf_op jit(solution)/shard_map/ppermute | solution.py:18
  8.5 0.0 collective-permute-start.1
  8.5 1.0 %collective-permute-start.2 = (bf16[150,128]{1,0:T(8,128)(2,1)}, bf16[150,128]{1,0:T(8,128)(2,1)S(1)}, u32[]{:S(2)}, u32[]{:S(2)}) collective-permute-start(bf16[150,128]{1,0:T(8,128)(2,1)} %get-tuple-element.18), channel_id=1, source_target_pairs={{126,0},{127,1},{0,2},{1,3},{2,4},{3,5},{4,6},{5,7},{6,8},{7,9},{8... | collective-permute-start | bytes 115208 | tf_op jit(solution)/shard_map/ppermute | solution.py:18
  9.5 2.2 %collective-permute-start.3 = (bf16[150,128]{1,0:T(8,128)(2,1)}, bf16[150,128]{1,0:T(8,128)(2,1)S(1)}, u32[]{:S(2)}, u32[]{:S(2)}) collective-permute-start(bf16[150,128]{1,0:T(8,128)(2,1)} %get-tuple-element.19), channel_id=1, source_target_pairs={{127,0},{0,1},{1,2},{2,3},{3,4},{4,5},{5,6},{6,7},{7,8},{8,9},{9,1... | collective-permute-start | bytes 115208 | tf_op jit(solution)/shard_map/ppermute | solution.py:18
  11.7 5.6 %collective-permute-start.4 = (bf16[150,128]{1,0:T(8,128)(2,1)}, bf16[150,128]{1,0:T(8,128)(2,1)S(1)}, u32[]{:S(2)}, u32[]{:S(2)}) collective-permute-start(bf16[150,128]{1,0:T(8,128)(2,1)} %get-tuple-element.20), channel_id=1, source_target_pairs={{1,0},{2,1},{3,2},{4,3},{5,4},{6,5},{7,6},{8,7},{9,8},{10,9},{11,1... | collective-permute-start | bytes 115208 | tf_op jit(solution)/shard_map/ppermute | solution.py:18
  17.3 0.7 fusion
  18.0 0.3 copy.28
  18.3 0.9 %copy.23 = s32[1024,1]{1,0:T(8,128)S(1)} copy(s32[1024,1]{0,1:T(1,128)} %bitcast.18) | data formatting | bytes 8192 | tf_op jit(solution)/shard_map/squeeze | solution.py:98
  19.2 0.0 collective-permute-done.refs_0_
  19.2 0.0 copy-start.3
  19.2 0.6 collective-permute-start.5
  19.9 0.0 collective-permute-done.1.refs_1_
  19.9 0.0 copy-start.4
  19.9 0.3 collective-permute-start.6
  20.2 0.0 collective-permute-done.2.refs_2_
  20.2 0.0 copy-start.5
  20.2 4.0 %collective-permute-start.7 = (bf16[150,128]{1,0:T(8,128)(2,1)}, bf16[150,128]{1,0:T(8,128)(2,1)S(1)}, u32[]{:S(2)}, u32[]{:S(2)}) collective-permute-start(bf16[150,128]{1,0:T(8,128)(2,1)} %get-tuple-element.23), channel_id=1, source_target_pairs={{4,0},{5,1},{6,2},{7,3},{8,4},{9,5},{10,6},{11,7},{12,8},{13,9},{1... | collective-permute-start | bytes 115208 | tf_op jit(solution)/shard_map/ppermute | solution.py:18
  24.2 0.8 %bitcast_select_fusion.refs_8_ = s32[1024,1]{1,0:T(8,128)} fusion(s32[1024,1]{1,0:T(8,128)S(1)} %copy.23, pred[1,1024]{0,1:T(8,128)(4,1)S(1)} %copy.28), kind=kLoop, calls=%fused_computation | loop fusion | flops 1024 | bytes 9216 | tf_op jit(solution)/shard_map/jit(_where)/select_n | solution.py:98
  25.0 0.0 collective-permute-done.3.refs_3_
  25.0 0.0 copy-start.6
  25.0 0.0 collective-permute-done.4.refs_4_
  25.0 0.0 copy-start.7
  25.0 0.0 collective-permute-done.5.refs_5_
  25.0 0.0 copy-start.8
  25.1 0.0 collective-permute-done.6.refs_6_
  25.1 0.0 copy-start.9
  25.1 1.3 %collective-permute-done.7.refs_7_ = bf16[150,128]{1,0:T(8,128)(2,1)S(1)} collective-permute-done((bf16[150,128]{1,0:T(8,128)(2,1)}, bf16[150,128]{1,0:T(8,128)(2,1)S(1)}, u32[]{:S(2)}, u32[]{:S(2)}) %collective-permute-start.7) | collective-permute-done | bytes 38432 | tf_op jit(solution)/shard_map/ppermute | solution.py:18
  26.4 0.0 copy-start.10
  26.4 0.0 copy-done.3
  26.4 0.0 copy-done.4
  26.4 0.0 copy-done.5
  26.4 0.0 copy-done.6
  26.4 0.0 copy-done.7
  26.4 0.0 copy-done.8
  26.4 0.0 copy-done.9
  26.5 0.6 copy-done.10
  27.0 9.3 %shard_map.128 = (bf16[150,8192]{1,0:T(8,128)(2,1)}, bf16[150,2048]{1,0:T(8,128)(2,1)}, bf16[150,2048]{1,0:T(8,128)(2,1)}) custom-call(s32[2,16]{1,0:T(2,128)} %bitcast.19, bf16[150,8192]{1,0:T(8,128)(2,1)} %mixing_ref.3, bf16[150,128]{1,0:T(8,128)(2,1)} %copy-done.3, bf16[150,128]{1,0:T(8,128)(2,1)} %copy-done.4, bf16[150,128]{1,0:T(8,128)(2,1)} %copy-done.5, ...), custom_call_target="tpu_custom_call" | custom-call | tf_op jit(solution)/shard_map/pallas_call | solution.py:110
  36.4 0.2 collective-permute-start.8
  36.5 7.1 %collective-permute-start.9 = (bf16[150,2048]{1,0:T(8,128)(2,1)}, bf16[150,2048]{1,0:T(8,128)(2,1)S(1)}, u32[]{:S(2)}, u32[]{:S(2)}) collective-permute-start(bf16[150,2048]{1,0:T(8,128)(2,1)} %get-tuple-element.26), channel_id=1, source_target_pairs={{1,0},{2,1},{3,2},{4,3},{5,4},{6,5},{7,6},{8,7},{9,8},{10,9},{11,1... | collective-permute-start | bytes 1843208 | tf_op jit(solution)/shard_map/ppermute | solution.py:18
  43.6 0.0 copy-done.11
  43.6 0.7 copy.24.nb_ref
  44.3 0.0 copy-done.12
  44.3 0.0 copy-done.13
  44.3 0.8 %copy.26.rate_terms_ref = f32[256,2]{1,0:T(8,128)} copy(f32[256,2]{0,1:T(2,128)S(1)} %pad_maximum_fusion) | data formatting | bytes 4096 | tf_op jit(solution)/shard_map/stack | solution.py:316
  45.1 0.0 copy-done.2
  45.1 0.8 %copy.25.order_ref = f32[256,150]{1,0:T(8,128)} copy(f32[256,150]{0,1:T(8,128)S(1)} %copy-done.2) | data formatting | bytes 307200 | tf_op args[8]
  45.9 5.8 %collective-permute-done.8.lower_hbm = bf16[150,2048]{1,0:T(8,128)(2,1)S(1)} collective-permute-done((bf16[150,2048]{1,0:T(8,128)(2,1)}, bf16[150,2048]{1,0:T(8,128)(2,1)S(1)}, u32[]{:S(2)}, u32[]{:S(2)}) %collective-permute-start.8) | collective-permute-done | bytes 614432 | tf_op jit(solution)/shard_map/ppermute | solution.py:18
  51.7 0.0 copy-start
  51.7 0.0 collective-permute-done.9.upper_hbm
  51.7 0.0 copy-start.1
  51.7 0.8 %copy-done = bf16[150,2048]{1,0:T(8,128)(2,1)} copy-done((bf16[150,2048]{1,0:T(8,128)(2,1)}, bf16[150,2048]{1,0:T(8,128)(2,1)S(1)}, u32[]{:S(2)}) %copy-start) | copy-done | bytes 614424
  52.6 0.2 copy-done.1
  52.8 20.2 %shard_map.129 = f32[150,8192]{1,0:T(8,128)} custom-call(s32[64,3]{1,0:T(8,128)} %copy.24.nb_ref, bf16[150,8192]{1,0:T(8,128)(2,1)} %get-tuple-element.24.own_ref.migrated_hbm, bf16[64,4,128,128]{3,2,1,0:T(8,128)(2,1)} %weight_ref.1, f32[1,8192]{1,0:T(1,128)} %bitcast.15, f32[256,150]{1,0:T(8,128)} %copy.25.order_ref, f32[256,2]{1,0:T(8,128)} %copy.26.rate_terms_ref, ...), custom_call_target="tpu_custom_call" | custom-call | tf_op jit(solution)/shard_map/pallas_call | solution.py:305
  (2 shorter events, 0.0 us)
Async XLA Ops:
  0.0 43.6 %copy-start.11 = (s32[64,3]{0,1:T(4,128)S(1)}, s32[64,3]{0,1:T(4,128)}, u32[]{:S(2)}) copy-start(s32[64,3]{0,1:T(4,128)} %param.18) | copy-start | bytes 2308
  0.0 44.3 %copy-start.12 = (f32[256]{0:T(256)S(1)}, f32[256]{0:T(256)}, u32[]{:S(2)}) copy-start(f32[256]{0:T(256)} %param.23) | copy-start | bytes 3076
  0.0 44.3 %copy-start.13 = (f32[256]{0:T(256)S(1)}, f32[256]{0:T(256)}, u32[]{:S(2)}) copy-start(f32[256]{0:T(256)} %param.22) | copy-start | bytes 3076
  0.0 45.1 %copy-start.2 = (f32[256,150]{0,1:T(8,128)S(1)}, f32[256,150]{0,1:T(8,128)}, u32[]{:S(2)}) copy-start(f32[256,150]{0,1:T(8,128)} %param.21) | copy-start | bytes 460804
  5.4 13.8 %collective-permute-start = (bf16[150,128]{1,0:T(8,128)(2,1)}, bf16[150,128]{1,0:T(8,128)(2,1)S(1)}, u32[]{:S(2)}, u32[]{:S(2)}) collective-permute-start(bf16[150,128]{1,0:T(8,128)(2,1)} %get-tuple-element.16), channel_id=1, source_target_pairs={{124,0},{125,1},{126,2},{127,3},{0,4},{1,5},{2,6},{3,7},{4,8},{5,9... | collective-permute-start | bytes 115208 | tf_op jit(solution)/shard_map/ppermute | solution.py:18
  8.5 11.4 %collective-permute-start.1 = (bf16[150,128]{1,0:T(8,128)(2,1)}, bf16[150,128]{1,0:T(8,128)(2,1)S(1)}, u32[]{:S(2)}, u32[]{:S(2)}) collective-permute-start(bf16[150,128]{1,0:T(8,128)(2,1)} %get-tuple-element.17), channel_id=1, source_target_pairs={{125,0},{126,1},{127,2},{0,3},{1,4},{2,5},{3,6},{4,7},{5,8},{6,9},... | collective-permute-start | bytes 115208 | tf_op jit(solution)/shard_map/ppermute | solution.py:18
  8.5 11.7 %collective-permute-start.2 = (bf16[150,128]{1,0:T(8,128)(2,1)}, bf16[150,128]{1,0:T(8,128)(2,1)S(1)}, u32[]{:S(2)}, u32[]{:S(2)}) collective-permute-start(bf16[150,128]{1,0:T(8,128)(2,1)} %get-tuple-element.18), channel_id=1, source_target_pairs={{126,0},{127,1},{0,2},{1,3},{2,4},{3,5},{4,6},{5,7},{6,8},{7,9},{8... | collective-permute-start | bytes 115208 | tf_op jit(solution)/shard_map/ppermute | solution.py:18
  9.5 15.5 %collective-permute-start.3 = (bf16[150,128]{1,0:T(8,128)(2,1)}, bf16[150,128]{1,0:T(8,128)(2,1)S(1)}, u32[]{:S(2)}, u32[]{:S(2)}) collective-permute-start(bf16[150,128]{1,0:T(8,128)(2,1)} %get-tuple-element.19), channel_id=1, source_target_pairs={{127,0},{0,1},{1,2},{2,3},{3,4},{4,5},{5,6},{6,7},{7,8},{8,9},{9,1... | collective-permute-start | bytes 115208 | tf_op jit(solution)/shard_map/ppermute | solution.py:18
  11.7 13.3 %collective-permute-start.4 = (bf16[150,128]{1,0:T(8,128)(2,1)}, bf16[150,128]{1,0:T(8,128)(2,1)S(1)}, u32[]{:S(2)}, u32[]{:S(2)}) collective-permute-start(bf16[150,128]{1,0:T(8,128)(2,1)} %get-tuple-element.20), channel_id=1, source_target_pairs={{1,0},{2,1},{3,2},{4,3},{5,4},{6,5},{7,6},{8,7},{9,8},{10,9},{11,1... | collective-permute-start | bytes 115208 | tf_op jit(solution)/shard_map/ppermute | solution.py:18
  19.2 7.2 %copy-start.3 = (bf16[150,128]{1,0:T(8,128)(2,1)}, bf16[150,128]{1,0:T(8,128)(2,1)S(1)}, u32[]{:S(2)}) copy-start(bf16[150,128]{1,0:T(8,128)(2,1)S(1)} %collective-permute-done.refs_0_) | copy-start | bytes 115204
  19.2 5.8 %collective-permute-start.5 = (bf16[150,128]{1,0:T(8,128)(2,1)}, bf16[150,128]{1,0:T(8,128)(2,1)S(1)}, u32[]{:S(2)}, u32[]{:S(2)}) collective-permute-start(bf16[150,128]{1,0:T(8,128)(2,1)} %get-tuple-element.21), channel_id=1, source_target_pairs={{2,0},{3,1},{4,2},{5,3},{6,4},{7,5},{8,6},{9,7},{10,8},{11,9},{12,... | collective-permute-start | bytes 115208 | tf_op jit(solution)/shard_map/ppermute | solution.py:18
  19.9 6.5 %copy-start.4 = (bf16[150,128]{1,0:T(8,128)(2,1)}, bf16[150,128]{1,0:T(8,128)(2,1)S(1)}, u32[]{:S(2)}) copy-start(bf16[150,128]{1,0:T(8,128)(2,1)S(1)} %collective-permute-done.1.refs_1_) | copy-start | bytes 115204
  19.9 5.2 %collective-permute-start.6 = (bf16[150,128]{1,0:T(8,128)(2,1)}, bf16[150,128]{1,0:T(8,128)(2,1)S(1)}, u32[]{:S(2)}, u32[]{:S(2)}) collective-permute-start(bf16[150,128]{1,0:T(8,128)(2,1)} %get-tuple-element.22), channel_id=1, source_target_pairs={{3,0},{4,1},{5,2},{6,3},{7,4},{8,5},{9,6},{10,7},{11,8},{12,9},{13... | collective-permute-start | bytes 115208 | tf_op jit(solution)/shard_map/ppermute | solution.py:18
  20.2 6.2 %copy-start.5 = (bf16[150,128]{1,0:T(8,128)(2,1)}, bf16[150,128]{1,0:T(8,128)(2,1)S(1)}, u32[]{:S(2)}) copy-start(bf16[150,128]{1,0:T(8,128)(2,1)S(1)} %collective-permute-done.2.refs_2_) | copy-start | bytes 115204
  20.2 6.2 %collective-permute-start.7 = (bf16[150,128]{1,0:T(8,128)(2,1)}, bf16[150,128]{1,0:T(8,128)(2,1)S(1)}, u32[]{:S(2)}, u32[]{:S(2)}) collective-permute-start(bf16[150,128]{1,0:T(8,128)(2,1)} %get-tuple-element.23), channel_id=1, source_target_pairs={{4,0},{5,1},{6,2},{7,3},{8,4},{9,5},{10,6},{11,7},{12,8},{13,9},{1... | collective-permute-start | bytes 115208 | tf_op jit(solution)/shard_map/ppermute | solution.py:18
  25.0 1.4 %copy-start.6 = (bf16[150,128]{1,0:T(8,128)(2,1)}, bf16[150,128]{1,0:T(8,128)(2,1)S(1)}, u32[]{:S(2)}) copy-start(bf16[150,128]{1,0:T(8,128)(2,1)S(1)} %collective-permute-done.3.refs_3_) | copy-start | bytes 115204
  25.0 1.4 %copy-start.7 = (bf16[150,128]{1,0:T(8,128)(2,1)}, bf16[150,128]{1,0:T(8,128)(2,1)S(1)}, u32[]{:S(2)}) copy-start(bf16[150,128]{1,0:T(8,128)(2,1)S(1)} %collective-permute-done.4.refs_4_) | copy-start | bytes 115204
  25.0 1.4 %copy-start.8 = (bf16[150,128]{1,0:T(8,128)(2,1)}, bf16[150,128]{1,0:T(8,128)(2,1)S(1)}, u32[]{:S(2)}) copy-start(bf16[150,128]{1,0:T(8,128)(2,1)S(1)} %collective-permute-done.5.refs_5_) | copy-start | bytes 115204
  25.1 1.4 %copy-start.9 = (bf16[150,128]{1,0:T(8,128)(2,1)}, bf16[150,128]{1,0:T(8,128)(2,1)S(1)}, u32[]{:S(2)}) copy-start(bf16[150,128]{1,0:T(8,128)(2,1)S(1)} %collective-permute-done.6.refs_6_) | copy-start | bytes 115204
  26.4 0.6 copy-start.10
  36.4 15.4 %collective-permute-start.8 = (bf16[150,2048]{1,0:T(8,128)(2,1)}, bf16[150,2048]{1,0:T(8,128)(2,1)S(1)}, u32[]{:S(2)}, u32[]{:S(2)}) collective-permute-start(bf16[150,2048]{1,0:T(8,128)(2,1)} %get-tuple-element.25), channel_id=1, source_target_pairs={{127,0},{0,1},{1,2},{2,3},{3,4},{4,5},{5,6},{6,7},{7,8},{8,9},{9,1... | collective-permute-start | bytes 1843208 | tf_op jit(solution)/shard_map/ppermute | solution.py:18
  36.5 15.2 %collective-permute-start.9 = (bf16[150,2048]{1,0:T(8,128)(2,1)}, bf16[150,2048]{1,0:T(8,128)(2,1)S(1)}, u32[]{:S(2)}, u32[]{:S(2)}) collective-permute-start(bf16[150,2048]{1,0:T(8,128)(2,1)} %get-tuple-element.26), channel_id=1, source_target_pairs={{1,0},{2,1},{3,2},{4,3},{5,4},{6,5},{7,6},{8,7},{9,8},{10,9},{11,1... | collective-permute-start | bytes 1843208 | tf_op jit(solution)/shard_map/ppermute | solution.py:18
  51.7 0.8 %copy-start = (bf16[150,2048]{1,0:T(8,128)(2,1)}, bf16[150,2048]{1,0:T(8,128)(2,1)S(1)}, u32[]{:S(2)}) copy-start(bf16[150,2048]{1,0:T(8,128)(2,1)S(1)} %collective-permute-done.8.lower_hbm) | copy-start | bytes 1843204
  51.7 1.0 %copy-start.1 = (bf16[150,2048]{1,0:T(8,128)(2,1)}, bf16[150,2048]{1,0:T(8,128)(2,1)S(1)}, u32[]{:S(2)}) copy-start(bf16[150,2048]{1,0:T(8,128)(2,1)S(1)} %collective-permute-done.9.upper_hbm) | copy-start | bytes 1843204

commit v9 on v7

--- a/solution.py
+++ b/solution.py
@@ -37,14 +37,19 @@
         out_ref[...] = total[:, column * width:(column + 1) * width].astype(out_ref.dtype)
 
 
-def place_kernel(chunk, block_size, peer_count, halo_ref, mixing_ref, *refs):
+def marked_arrivals(received_refs, rows):
+    received = jnp.concatenate([ref[...] for ref in received_refs], axis=1)
+    species = received.shape[0]
+    pad = (-species) % 16 or 16
+    return jnp.concatenate([received, jnp.ones((pad, rows), received.dtype)], axis=0)
+
+
+def place_kernel(chunk, peer_count, mixing_ref, *refs):
     received_refs = refs[:peer_count]
-    slots_ref, migrated_ref, lower_ref, upper_ref, sems = refs[peer_count:]
+    slots_ref, migrated_ref = refs[peer_count:]
     species, parcels = mixing_ref.shape
     slots = slots_ref[...]
-    received = jnp.concatenate([ref[...] for ref in received_refs], axis=1)
-    pad = (-species) % 16 or 16
-    marked = jnp.concatenate([received, jnp.ones((pad, slots.shape[0]), received.dtype)], axis=0)
+    marked = marked_arrivals(received_refs, slots.shape[0])
     for part in range(parcels // chunk):
         lanes = slice(part * chunk, (part + 1) * chunk)
         position = lax.broadcasted_iota(jnp.int32, (slots.shape[0], chunk), 1) + part * chunk
@@ -54,6 +59,12 @@
         migrated_ref[:, lanes] = jnp.where(
             hit > 0.5, placed[:species].astype(migrated_ref.dtype), mixing_ref[:, lanes]
         )
+
+
+def halo_kernel(chunk, block_size, peer_count, halo_ref, mixing_ref, *refs):
+    received_refs = refs[:peer_count]
+    slots_ref, lower_ref, upper_ref, sems = refs[peer_count:]
+    species = mixing_ref.shape[0]
     sides, listed = halo_ref.shape
     outs = (lower_ref, upper_ref)
     copies = []
@@ -61,14 +72,32 @@
         for j in range(listed):
             start = pl.multiple_of(halo_ref[side, j] * block_size, block_size)
             copy = pltpu.make_async_copy(
-                migrated_ref.at[:, pl.ds(start, block_size)],
+                mixing_ref.at[:, pl.ds(start, block_size)],
                 outs[side].at[:, pl.ds(j * block_size, block_size)],
                 sems.at[side, j],
             )
             copy.start()
             copies.append(copy)
+    slots = slots_ref[...]
+    marked = marked_arrivals(received_refs, slots.shape[0])
+    lane = lax.broadcasted_iota(jnp.int32, (1, block_size), 1)
+    per_chunk = chunk // block_size
     for copy in copies:
         copy.wait()
+    for side in range(sides):
+        for part in range(listed // per_chunk):
+            first = part * per_chunk
+            where_to = jnp.concatenate(
+                [lane + halo_ref[side, j] * block_size for j in range(first, first + per_chunk)],
+                axis=1,
+            )
+            place = (where_to == slots).astype(jnp.bfloat16)
+            placed = jnp.dot(marked, place, preferred_element_type=jnp.float32)
+            hit = placed[species:species + 1]
+            lanes = slice(first * block_size, (first + per_chunk) * block_size)
+            outs[side][:, lanes] = jnp.where(
+                hit > 0.5, placed[:species].astype(outs[side].dtype), outs[side][:, lanes]
+            )
 
 
 def vmem_whole(shape):
@@ -104,18 +133,23 @@
         in_specs=[vmem_whole(mixing_ratio.shape)]
         + [vmem_whole((species, capacity))] * peer_count
         + [vmem_whole(slots.shape)],
-        out_specs=[vmem_whole(mixing_ratio.shape), vmem_whole(halo_shape), vmem_whole(halo_shape)],
+        out_specs=[vmem_whole(halo_shape), vmem_whole(halo_shape)],
         scratch_shapes=[pltpu.SemaphoreType.DMA((sides, listed))],
     )
-    migrated, to_lower, to_upper = pl.pallas_call(
-        functools.partial(place_kernel, chunk, block_size, peer_count),
+    to_lower, to_upper = pl.pallas_call(
+        functools.partial(halo_kernel, chunk, block_size, peer_count),
         grid_spec=grid_spec,
-        out_shape=[
-            jax.ShapeDtypeStruct(mixing_ratio.shape, mixing_ratio.dtype),
-            jax.ShapeDtypeStruct(halo_shape, mixing_ratio.dtype),
-            jax.ShapeDtypeStruct(halo_shape, mixing_ratio.dtype),
-        ],
+        out_shape=[jax.ShapeDtypeStruct(halo_shape, mixing_ratio.dtype)] * sides,
     )(halo_blocks[0], mixing_ratio, *arrived, slots)
+    migrated = pl.pallas_call(
+        functools.partial(place_kernel, chunk, peer_count),
+        grid=(1,),
+        in_specs=[vmem_whole(mixing_ratio.shape)]
+        + [vmem_whole((species, capacity))] * peer_count
+        + [vmem_whole(slots.shape)],
+        out_specs=vmem_whole(mixing_ratio.shape),
+        out_shape=jax.ShapeDtypeStruct(mixing_ratio.shape, mixing_ratio.dtype),
+    )(mixing_ratio, *arrived, slots)
     from_lower = from_behind(to_upper, "region", 1)
     from_upper = from_behind(to_lower, "region", -1)
     return migrated, from_lower, from_upper

time: 72.7 us -> 71.3 us (0.981)
  waiting for transfers between devices: 7.14 us -> 1.31 us
  Pallas kernels: 34.2 us -> 38.4 us
    ppermute x10, waiting for transfers between devices: 7.14 us -> 1.31 us  [from_behind(): return lax.ppermute(block, axis, route)]
    pallas_call x1 -> x2, Pallas kernels: 8.76 us -> 13 us  [the longest x1 6.82 us: migrate(): pl.pallas_call(functools.partial(place_kernel, chunk, peer_count), grid=(...]
  transfers between devices with their start and end apart: 10 -> 10, of which waited for: 2 -> 1; matrix products, arithmetic and copies ran while one was open for 7% -> 7% of each run, Pallas kernels for 0% -> 10%
where the time goes in v9:
time: 71.3 us; the launch traced here: 70.9 us
  Pallas kernels  38.4 us (54%)
  starting transfers between devices  24.1 us (34%)
  local copies, waits for them, and re-layouts  5.17 us (7%)
  other arithmetic  1.6 us (2%)
  waiting for transfers between devices  1.31 us (2%)
    ppermute x10, starting transfers between devices, from_behind(): return lax.ppermute(block, axis, route)  24.1 us
    pallas_call x1, Pallas kernels, mix_react(): pl.pallas_call(kernel, grid_spec=grid_spec, out_shape=jax.ShapeDtypeStruc...  20.2 us
    pallas_call x1, Pallas kernels, migrate(): pl.pallas_call(functools.partial(place_kernel, chunk, peer_count), grid=(...  6.82 us
    pallas_call x1, Pallas kernels, migrate(): pl.pallas_call(functools.partial(halo_kernel, chunk, block_size, peer_cou...  6.18 us
    pallas_call x1, Pallas kernels, migrate(): pl.pallas_call(functools.partial(pick_kernel, chunk), grid=(1,), in_specs...  5.3 us
    unnamed x32, local copies, waits for them, and re-layouts  3.47 us
  transfers between devices with their start and end apart: 10, of which 1 were waited for; matrix products, arithmetic and copies ran while one was open for 7% of the time, Pallas kernels for 10%

profile of v9, /device:TPU:0, one launch (start us, length us, event | category | flops | bytes accessed | tf_op | source)
XLA Modules:
  0.0 70.9 jit_solution(376099031765125162)
XLA Ops:
  0.0 0.0 copy-start.11
  0.0 0.0 copy-start.12
  0.0 0.0 copy-start.13
  0.0 0.0 copy-start.10
  0.0 5.3 %shard_map.127 = (bf16[150,128]{1,0:T(8,128)(2,1)}, bf16[150,128]{1,0:T(8,128)(2,1)}, bf16[150,128]{1,0:T(8,128)(2,1)}, bf16[150,128]{1,0:T(8,128)(2,1)}, bf16[1...) custom-call(bf16[150,8192]{1,0:T(8,128)(2,1)} %mixing_ref.5, ...), custom_call_target="tpu_custom_call" | custom-call | tf_op jit(solution)/shard_map/pallas_call | solution.py:114
  5.3 3.1 %collective-permute-start = (bf16[150,128]{1,0:T(8,128)(2,1)}, bf16[150,128]{1,0:T(8,128)(2,1)S(1)}, u32[]{:S(2)}, u32[]{:S(2)}) collective-permute-start(bf16[150,128]{1,0:T(8,128)(2,1)} %get-tuple-element.15), channel_id=1, source_target_pairs={{124,0},{125,1},{126,2},{127,3},{0,4},{1,5},{2,6},{3,7},{4,8},{5,9... | collective-permute-start | bytes 115208 | tf_op jit(solution)/shard_map/ppermute | solution.py:18
  8.4 0.0 collective-permute-start.1
  8.4 1.0 %collective-permute-start.2 = (bf16[150,128]{1,0:T(8,128)(2,1)}, bf16[150,128]{1,0:T(8,128)(2,1)S(1)}, u32[]{:S(2)}, u32[]{:S(2)}) collective-permute-start(bf16[150,128]{1,0:T(8,128)(2,1)} %get-tuple-element.17), channel_id=1, source_target_pairs={{126,0},{127,1},{0,2},{1,3},{2,4},{3,5},{4,6},{5,7},{6,8},{7,9},{8... | collective-permute-start | bytes 115208 | tf_op jit(solution)/shard_map/ppermute | solution.py:18
  9.4 2.2 %collective-permute-start.3 = (bf16[150,128]{1,0:T(8,128)(2,1)}, bf16[150,128]{1,0:T(8,128)(2,1)S(1)}, u32[]{:S(2)}, u32[]{:S(2)}) collective-permute-start(bf16[150,128]{1,0:T(8,128)(2,1)} %get-tuple-element.18), channel_id=1, source_target_pairs={{127,0},{0,1},{1,2},{2,3},{3,4},{4,5},{5,6},{6,7},{7,8},{8,9},{9,1... | collective-permute-start | bytes 115208 | tf_op jit(solution)/shard_map/ppermute | solution.py:18
  11.6 5.6 %collective-permute-start.4 = (bf16[150,128]{1,0:T(8,128)(2,1)}, bf16[150,128]{1,0:T(8,128)(2,1)S(1)}, u32[]{:S(2)}, u32[]{:S(2)}) collective-permute-start(bf16[150,128]{1,0:T(8,128)(2,1)} %get-tuple-element.19), channel_id=1, source_target_pairs={{1,0},{2,1},{3,2},{4,3},{5,4},{6,5},{7,6},{8,7},{9,8},{10,9},{11,1... | collective-permute-start | bytes 115208 | tf_op jit(solution)/shard_map/ppermute | solution.py:18
  17.2 0.7 %fusion = pred[1,1,8,128]{3,2,1,0:T(8,128)(4,1)S(1)} fusion(s32[8]{0:T(128)} %bitcast.22), kind=kLoop, calls=%fused_computation.3 | loop fusion | flops 1024 | bytes 1056
  17.9 0.3 copy.28
  18.2 0.9 %copy.23 = s32[1024,1]{1,0:T(8,128)S(1)} copy(s32[1024,1]{0,1:T(1,128)} %bitcast.18) | data formatting | bytes 8192 | tf_op jit(solution)/shard_map/squeeze | solution.py:127
  19.1 0.0 collective-permute-done.refs_0_
  19.2 0.0 copy-start.2
  19.2 0.6 collective-permute-start.5
  19.8 0.0 collective-permute-done.1.refs_1_
  19.8 0.0 copy-start.3
  19.8 0.3 collective-permute-start.6
  20.1 0.0 collective-permute-done.2.refs_2_
  20.1 0.0 copy-start.4
  20.1 4.0 %collective-permute-start.7 = (bf16[150,128]{1,0:T(8,128)(2,1)}, bf16[150,128]{1,0:T(8,128)(2,1)S(1)}, u32[]{:S(2)}, u32[]{:S(2)}) collective-permute-start(bf16[150,128]{1,0:T(8,128)(2,1)} %get-tuple-element.22), channel_id=1, source_target_pairs={{4,0},{5,1},{6,2},{7,3},{8,4},{9,5},{10,6},{11,7},{12,8},{13,9},{1... | collective-permute-start | bytes 115208 | tf_op jit(solution)/shard_map/ppermute | solution.py:18
  24.1 0.9 %bitcast_select_fusion.refs_8_ = s32[1024,1]{1,0:T(8,128)} fusion(s32[1024,1]{1,0:T(8,128)S(1)} %copy.23, pred[1,1024]{0,1:T(8,128)(4,1)S(1)} %copy.28), kind=kLoop, calls=%fused_computation | loop fusion | flops 1024 | bytes 9216 | tf_op jit(solution)/shard_map/jit(_where)/select_n | solution.py:127
  25.0 0.0 collective-permute-done.3.refs_3_
  25.0 0.0 copy-start.5
  25.0 0.0 collective-permute-done.4.refs_4_
  25.0 0.0 copy-start.6
  25.0 0.0 collective-permute-done.5.refs_5_
  25.0 0.0 copy-start.7
  25.0 0.0 collective-permute-done.6.refs_6_
  25.0 0.0 copy-start.8
  25.0 1.3 %collective-permute-done.7.refs_7_ = bf16[150,128]{1,0:T(8,128)(2,1)S(1)} collective-permute-done((bf16[150,128]{1,0:T(8,128)(2,1)}, bf16[150,128]{1,0:T(8,128)(2,1)S(1)}, u32[]{:S(2)}, u32[]{:S(2)}) %collective-permute-start.7) | collective-permute-done | bytes 38432 | tf_op jit(solution)/shard_map/ppermute | solution.py:18
  26.3 0.0 copy-start.9
  26.3 0.0 copy-done.2
  26.3 0.0 copy-done.3
  26.3 0.0 copy-done.4
  26.3 0.0 copy-done.5
  26.4 0.0 copy-done.6
  26.4 0.0 copy-done.7
  26.4 0.0 copy-done.8
  26.4 0.6 copy-done.9
  26.9 6.2 %shard_map.129 = (bf16[150,2048]{1,0:T(8,128)(2,1)}, bf16[150,2048]{1,0:T(8,128)(2,1)}) custom-call(s32[2,16]{1,0:T(2,128)} %bitcast.19, bf16[150,8192]{1,0:T(8,128)(2,1)} %mixing_ref.5, bf16[150,128]{1,0:T(8,128)(2,1)} %copy-done.2, bf16[150,128]{1,0:T(8,128)(2,1)} %copy-done.3, bf16[150,128]{1,0:T(8,128)(2,1)} %copy-done.4, bf16[150,128]{1,0:T(8,128)(2,1)} %copy-done.5, ...), custom_call_target="tpu_custom_call" | custom-call | tf_op jit(solution)/shard_map/pallas_call | solution.py:139
  33.1 0.2 collective-permute-start.8
  33.3 7.1 %collective-permute-start.9 = (bf16[150,2048]{1,0:T(8,128)(2,1)}, bf16[150,2048]{1,0:T(8,128)(2,1)S(1)}, u32[]{:S(2)}, u32[]{:S(2)}) collective-permute-start(bf16[150,2048]{1,0:T(8,128)(2,1)} %get-tuple-element.24), channel_id=1, source_target_pairs={{1,0},{2,1},{3,2},{4,3},{5,4},{6,5},{7,6},{8,7},{9,8},{10,9},{11,1... | collective-permute-start | bytes 1843208 | tf_op jit(solution)/shard_map/ppermute | solution.py:18
  40.4 0.0 copy-done.11
  40.4 0.7 %copy.24.nb_ref = s32[64,3]{1,0:T(8,128)} copy(s32[64,3]{0,1:T(4,128)S(1)} %copy-done.11) | data formatting | bytes 1536 | tf_op args[5]
  41.1 0.0 copy-done.12
  41.1 0.0 copy-done.13
  41.1 0.8 %copy.26.rate_terms_ref = f32[256,2]{1,0:T(8,128)} copy(f32[256,2]{0,1:T(2,128)S(1)} %pad_maximum_fusion) | data formatting | bytes 4096 | tf_op jit(solution)/shard_map/stack | solution.py:350
  41.9 0.0 copy-done.10
  41.9 0.8 %copy.25.order_ref = f32[256,150]{1,0:T(8,128)} copy(f32[256,150]{0,1:T(8,128)S(1)} %copy-done.10) | data formatting | bytes 307200 | tf_op args[8]
  42.7 6.8 %shard_map.128.own_ref.migrated_hbm = bf16[150,8192]{1,0:T(8,128)(2,1)} custom-call(bf16[150,8192]{1,0:T(8,128)(2,1)} %mixing_ref.5, bf16[150,128]{1,0:T(8,128)(2,1)} %copy-done.2, bf16[150,128]{1,0:T(8,128)(2,1)} %copy-done.3, bf16[150,128]{1,0:T(8,128)(2,1)} %copy-done.4, bf16[150,128]{1,0:T(8,128)(2,1)} %copy-done.5, bf16[150,128]{1,0:T(8,128)(2,1)} %copy-done.6, ...), custom_call_target="tpu_custom_call" | custom-call | tf_op jit(solution)/shard_map/pallas_call | solution.py:144
  49.5 0.0 collective-permute-done.8.lower_hbm
  49.6 0.0 copy-start
  49.6 0.0 collective-permute-done.9.upper_hbm
  49.6 0.0 copy-start.1
  49.6 0.8 %copy-done = bf16[150,2048]{1,0:T(8,128)(2,1)} copy-done((bf16[150,2048]{1,0:T(8,128)(2,1)}, bf16[150,2048]{1,0:T(8,128)(2,1)S(1)}, u32[]{:S(2)}) %copy-start) | copy-done | bytes 614424
  50.4 0.2 copy-done.1
  50.6 20.2 %shard_map.130 = f32[150,8192]{1,0:T(8,128)} custom-call(s32[64,3]{1,0:T(8,128)} %copy.24.nb_ref, bf16[150,8192]{1,0:T(8,128)(2,1)} %shard_map.128.own_ref.migrated_hbm, bf16[64,4,128,128]{3,2,1,0:T(8,128)(2,1)} %weight_ref.1, f32[1,8192]{1,0:T(1,128)} %bitcast.15, f32[256,150]{1,0:T(8,128)} %copy.25.order_ref, f32[256,2]{1,0:T(8,128)} %copy.26.rate_terms_ref, ...), custom_call_target="tpu_custom_call" | custom-call | tf_op jit(solution)/shard_map/pallas_call | solution.py:339
  (2 shorter events, 0.0 us)
Async XLA Ops:
  0.0 40.4 %copy-start.11 = (s32[64,3]{0,1:T(4,128)S(1)}, s32[64,3]{0,1:T(4,128)}, u32[]{:S(2)}) copy-start(s32[64,3]{0,1:T(4,128)} %param.18) | copy-start | bytes 2308
  0.0 41.1 %copy-start.12 = (f32[256]{0:T(256)S(1)}, f32[256]{0:T(256)}, u32[]{:S(2)}) copy-start(f32[256]{0:T(256)} %param.23) | copy-start | bytes 3076
  0.0 41.1 %copy-start.13 = (f32[256]{0:T(256)S(1)}, f32[256]{0:T(256)}, u32[]{:S(2)}) copy-start(f32[256]{0:T(256)} %param.22) | copy-start | bytes 3076
  0.0 41.9 %copy-start.10 = (f32[256,150]{0,1:T(8,128)S(1)}, f32[256,150]{0,1:T(8,128)}, u32[]{:S(2)}) copy-start(f32[256,150]{0,1:T(8,128)} %param.21) | copy-start | bytes 460804
  5.3 13.8 %collective-permute-start = (bf16[150,128]{1,0:T(8,128)(2,1)}, bf16[150,128]{1,0:T(8,128)(2,1)S(1)}, u32[]{:S(2)}, u32[]{:S(2)}) collective-permute-start(bf16[150,128]{1,0:T(8,128)(2,1)} %get-tuple-element.15), channel_id=1, source_target_pairs={{124,0},{125,1},{126,2},{127,3},{0,4},{1,5},{2,6},{3,7},{4,8},{5,9... | collective-permute-start | bytes 115208 | tf_op jit(solution)/shard_map/ppermute | solution.py:18
  8.4 11.4 %collective-permute-start.1 = (bf16[150,128]{1,0:T(8,128)(2,1)}, bf16[150,128]{1,0:T(8,128)(2,1)S(1)}, u32[]{:S(2)}, u32[]{:S(2)}) collective-permute-start(bf16[150,128]{1,0:T(8,128)(2,1)} %get-tuple-element.16), channel_id=1, source_target_pairs={{125,0},{126,1},{127,2},{0,3},{1,4},{2,5},{3,6},{4,7},{5,8},{6,9},... | collective-permute-start | bytes 115208 | tf_op jit(solution)/shard_map/ppermute | solution.py:18
  8.4 11.7 %collective-permute-start.2 = (bf16[150,128]{1,0:T(8,128)(2,1)}, bf16[150,128]{1,0:T(8,128)(2,1)S(1)}, u32[]{:S(2)}, u32[]{:S(2)}) collective-permute-start(bf16[150,128]{1,0:T(8,128)(2,1)} %get-tuple-element.17), channel_id=1, source_target_pairs={{126,0},{127,1},{0,2},{1,3},{2,4},{3,5},{4,6},{5,7},{6,8},{7,9},{8... | collective-permute-start | bytes 115208 | tf_op jit(solution)/shard_map/ppermute | solution.py:18
  9.4 15.6 %collective-permute-start.3 = (bf16[150,128]{1,0:T(8,128)(2,1)}, bf16[150,128]{1,0:T(8,128)(2,1)S(1)}, u32[]{:S(2)}, u32[]{:S(2)}) collective-permute-start(bf16[150,128]{1,0:T(8,128)(2,1)} %get-tuple-element.18), channel_id=1, source_target_pairs={{127,0},{0,1},{1,2},{2,3},{3,4},{4,5},{5,6},{6,7},{7,8},{8,9},{9,1... | collective-permute-start | bytes 115208 | tf_op jit(solution)/shard_map/ppermute | solution.py:18
  11.6 13.4 %collective-permute-start.4 = (bf16[150,128]{1,0:T(8,128)(2,1)}, bf16[150,128]{1,0:T(8,128)(2,1)S(1)}, u32[]{:S(2)}, u32[]{:S(2)}) collective-permute-start(bf16[150,128]{1,0:T(8,128)(2,1)} %get-tuple-element.19), channel_id=1, source_target_pairs={{1,0},{2,1},{3,2},{4,3},{5,4},{6,5},{7,6},{8,7},{9,8},{10,9},{11,1... | collective-permute-start | bytes 115208 | tf_op jit(solution)/shard_map/ppermute | solution.py:18
  19.2 7.2 %copy-start.2 = (bf16[150,128]{1,0:T(8,128)(2,1)}, bf16[150,128]{1,0:T(8,128)(2,1)S(1)}, u32[]{:S(2)}) copy-start(bf16[150,128]{1,0:T(8,128)(2,1)S(1)} %collective-permute-done.refs_0_) | copy-start | bytes 115204
  19.2 5.8 %collective-permute-start.5 = (bf16[150,128]{1,0:T(8,128)(2,1)}, bf16[150,128]{1,0:T(8,128)(2,1)S(1)}, u32[]{:S(2)}, u32[]{:S(2)}) collective-permute-start(bf16[150,128]{1,0:T(8,128)(2,1)} %get-tuple-element.20), channel_id=1, source_target_pairs={{2,0},{3,1},{4,2},{5,3},{6,4},{7,5},{8,6},{9,7},{10,8},{11,9},{12,... | collective-permute-start | bytes 115208 | tf_op jit(solution)/shard_map/ppermute | solution.py:18
  19.8 6.5 %copy-start.3 = (bf16[150,128]{1,0:T(8,128)(2,1)}, bf16[150,128]{1,0:T(8,128)(2,1)S(1)}, u32[]{:S(2)}) copy-start(bf16[150,128]{1,0:T(8,128)(2,1)S(1)} %collective-permute-done.1.refs_1_) | copy-start | bytes 115204
  19.8 5.2 %collective-permute-start.6 = (bf16[150,128]{1,0:T(8,128)(2,1)}, bf16[150,128]{1,0:T(8,128)(2,1)S(1)}, u32[]{:S(2)}, u32[]{:S(2)}) collective-permute-start(bf16[150,128]{1,0:T(8,128)(2,1)} %get-tuple-element.21), channel_id=1, source_target_pairs={{3,0},{4,1},{5,2},{6,3},{7,4},{8,5},{9,6},{10,7},{11,8},{12,9},{13... | collective-permute-start | bytes 115208 | tf_op jit(solution)/shard_map/ppermute | solution.py:18
  20.1 6.2 %copy-start.4 = (bf16[150,128]{1,0:T(8,128)(2,1)}, bf16[150,128]{1,0:T(8,128)(2,1)S(1)}, u32[]{:S(2)}) copy-start(bf16[150,128]{1,0:T(8,128)(2,1)S(1)} %collective-permute-done.2.refs_2_) | copy-start | bytes 115204
  20.1 6.2 %collective-permute-start.7 = (bf16[150,128]{1,0:T(8,128)(2,1)}, bf16[150,128]{1,0:T(8,128)(2,1)S(1)}, u32[]{:S(2)}, u32[]{:S(2)}) collective-permute-start(bf16[150,128]{1,0:T(8,128)(2,1)} %get-tuple-element.22), channel_id=1, source_target_pairs={{4,0},{5,1},{6,2},{7,3},{8,4},{9,5},{10,6},{11,7},{12,8},{13,9},{1... | collective-permute-start | bytes 115208 | tf_op jit(solution)/shard_map/ppermute | solution.py:18
  25.0 1.4 %copy-start.5 = (bf16[150,128]{1,0:T(8,128)(2,1)}, bf16[150,128]{1,0:T(8,128)(2,1)S(1)}, u32[]{:S(2)}) copy-start(bf16[150,128]{1,0:T(8,128)(2,1)S(1)} %collective-permute-done.3.refs_3_) | copy-start | bytes 115204
  25.0 1.4 %copy-start.6 = (bf16[150,128]{1,0:T(8,128)(2,1)}, bf16[150,128]{1,0:T(8,128)(2,1)S(1)}, u32[]{:S(2)}) copy-start(bf16[150,128]{1,0:T(8,128)(2,1)S(1)} %collective-permute-done.4.refs_4_) | copy-start | bytes 115204
  25.0 1.4 %copy-start.7 = (bf16[150,128]{1,0:T(8,128)(2,1)}, bf16[150,128]{1,0:T(8,128)(2,1)S(1)}, u32[]{:S(2)}) copy-start(bf16[150,128]{1,0:T(8,128)(2,1)S(1)} %collective-permute-done.5.refs_5_) | copy-start | bytes 115204
  25.0 1.3 %copy-start.8 = (bf16[150,128]{1,0:T(8,128)(2,1)}, bf16[150,128]{1,0:T(8,128)(2,1)S(1)}, u32[]{:S(2)}) copy-start(bf16[150,128]{1,0:T(8,128)(2,1)S(1)} %collective-permute-done.6.refs_6_) | copy-start | bytes 115204
  26.3 0.6 copy-start.9
  33.1 16.4 %collective-permute-start.8 = (bf16[150,2048]{1,0:T(8,128)(2,1)}, bf16[150,2048]{1,0:T(8,128)(2,1)S(1)}, u32[]{:S(2)}, u32[]{:S(2)}) collective-permute-start(bf16[150,2048]{1,0:T(8,128)(2,1)} %get-tuple-element.23), channel_id=1, source_target_pairs={{127,0},{0,1},{1,2},{2,3},{3,4},{4,5},{5,6},{6,7},{7,8},{8,9},{9,1... | collective-permute-start | bytes 1843208 | tf_op jit(solution)/shard_map/ppermute | solution.py:18
  33.3 16.3 %collective-permute-start.9 = (bf16[150,2048]{1,0:T(8,128)(2,1)}, bf16[150,2048]{1,0:T(8,128)(2,1)S(1)}, u32[]{:S(2)}, u32[]{:S(2)}) collective-permute-start(bf16[150,2048]{1,0:T(8,128)(2,1)} %get-tuple-element.24), channel_id=1, source_target_pairs={{1,0},{2,1},{3,2},{4,3},{5,4},{6,5},{7,6},{8,7},{9,8},{10,9},{11,1... | collective-permute-start | bytes 1843208 | tf_op jit(solution)/shard_map/ppermute | solution.py:18
  49.6 0.9 %copy-start = (bf16[150,2048]{1,0:T(8,128)(2,1)}, bf16[150,2048]{1,0:T(8,128)(2,1)S(1)}, u32[]{:S(2)}) copy-start(bf16[150,2048]{1,0:T(8,128)(2,1)S(1)} %collective-permute-done.8.lower_hbm) | copy-start | bytes 1843204
  49.6 1.0 %copy-start.1 = (bf16[150,2048]{1,0:T(8,128)(2,1)}, bf16[150,2048]{1,0:T(8,128)(2,1)S(1)}, u32[]{:S(2)}) copy-start(bf16[150,2048]{1,0:T(8,128)(2,1)S(1)} %collective-permute-done.9.upper_hbm) | copy-start | bytes 1843204

commit v10 on v9

--- a/solution.py
+++ b/solution.py
@@ -130,7 +130,7 @@
     grid_spec = pltpu.PrefetchScalarGridSpec(
         num_scalar_prefetch=1,
         grid=(1,),
-        in_specs=[vmem_whole(mixing_ratio.shape)]
+        in_specs=[pl.BlockSpec(memory_space=pl.ANY)]
         + [vmem_whole((species, capacity))] * peer_count
         + [vmem_whole(slots.shape)],
         out_specs=[vmem_whole(halo_shape), vmem_whole(halo_shape)],

time: 71.3 us -> 71.5 us (level)
  no operation moved by 1% of the time
where the time goes in v10:
time: 71.5 us; the launch traced here: 71 us
  Pallas kernels  38.5 us (54%)
  starting transfers between devices  24.1 us (34%)
  local copies, waits for them, and re-layouts  5.17 us (7%)
  other arithmetic  1.6 us (2%)
  waiting for transfers between devices  1.31 us (2%)
    ppermute x10, starting transfers between devices, from_behind(): return lax.ppermute(block, axis, route)  24.1 us
    pallas_call x1, Pallas kernels, mix_react(): pl.pallas_call(kernel, grid_spec=grid_spec, out_shape=jax.ShapeDtypeStruc...  20.2 us
    pallas_call x1, Pallas kernels, migrate(): pl.pallas_call(functools.partial(place_kernel, chunk, peer_count), grid=(...  6.82 us
    pallas_call x1, Pallas kernels, migrate(): pl.pallas_call(functools.partial(halo_kernel, chunk, block_size, peer_cou...  6.21 us
    pallas_call x1, Pallas kernels, migrate(): pl.pallas_call(functools.partial(pick_kernel, chunk), grid=(1,), in_specs...  5.3 us
    unnamed x32, local copies, waits for them, and re-layouts  3.47 us
  transfers between devices with their start and end apart: 10, of which 1 were waited for; matrix products, arithmetic and copies ran while one was open for 7% of the time, Pallas kernels for 10%

profile of v10, /device:TPU:0, one launch (start us, length us, event | category | flops | bytes accessed | tf_op | source)
XLA Modules:
  0.0 71.0 jit_solution(13097634105883879899)
XLA Ops:
  0.0 0.0 copy-start.11
  0.0 0.0 copy-start.12
  0.0 0.0 copy-start.13
  0.0 0.0 copy-start.10
  0.0 5.3 %shard_map.127 = (bf16[150,128]{1,0:T(8,128)(2,1)}, bf16[150,128]{1,0:T(8,128)(2,1)}, bf16[150,128]{1,0:T(8,128)(2,1)}, bf16[150,128]{1,0:T(8,128)(2,1)}, bf16[1...) custom-call(bf16[150,8192]{1,0:T(8,128)(2,1)} %mixing_ref.5, ...), custom_call_target="tpu_custom_call" | custom-call | tf_op jit(solution)/shard_map/pallas_call | solution.py:114
  5.3 3.1 %collective-permute-start = (bf16[150,128]{1,0:T(8,128)(2,1)}, bf16[150,128]{1,0:T(8,128)(2,1)S(1)}, u32[]{:S(2)}, u32[]{:S(2)}) collective-permute-start(bf16[150,128]{1,0:T(8,128)(2,1)} %get-tuple-element.15), channel_id=1, source_target_pairs={{124,0},{125,1},{126,2},{127,3},{0,4},{1,5},{2,6},{3,7},{4,8},{5,9... | collective-permute-start | bytes 115208 | tf_op jit(solution)/shard_map/ppermute | solution.py:18
  8.4 0.0 collective-permute-start.1
  8.4 1.0 %collective-permute-start.2 = (bf16[150,128]{1,0:T(8,128)(2,1)}, bf16[150,128]{1,0:T(8,128)(2,1)S(1)}, u32[]{:S(2)}, u32[]{:S(2)}) collective-permute-start(bf16[150,128]{1,0:T(8,128)(2,1)} %get-tuple-element.17), channel_id=1, source_target_pairs={{126,0},{127,1},{0,2},{1,3},{2,4},{3,5},{4,6},{5,7},{6,8},{7,9},{8... | collective-permute-start | bytes 115208 | tf_op jit(solution)/shard_map/ppermute | solution.py:18
  9.4 2.2 %collective-permute-start.3 = (bf16[150,128]{1,0:T(8,128)(2,1)}, bf16[150,128]{1,0:T(8,128)(2,1)S(1)}, u32[]{:S(2)}, u32[]{:S(2)}) collective-permute-start(bf16[150,128]{1,0:T(8,128)(2,1)} %get-tuple-element.18), channel_id=1, source_target_pairs={{127,0},{0,1},{1,2},{2,3},{3,4},{4,5},{5,6},{6,7},{7,8},{8,9},{9,1... | collective-permute-start | bytes 115208 | tf_op jit(solution)/shard_map/ppermute | solution.py:18
  11.6 5.6 %collective-permute-start.4 = (bf16[150,128]{1,0:T(8,128)(2,1)}, bf16[150,128]{1,0:T(8,128)(2,1)S(1)}, u32[]{:S(2)}, u32[]{:S(2)}) collective-permute-start(bf16[150,128]{1,0:T(8,128)(2,1)} %get-tuple-element.19), channel_id=1, source_target_pairs={{1,0},{2,1},{3,2},{4,3},{5,4},{6,5},{7,6},{8,7},{9,8},{10,9},{11,1... | collective-permute-start | bytes 115208 | tf_op jit(solution)/shard_map/ppermute | solution.py:18
  17.2 0.7 %fusion = pred[1,1,8,128]{3,2,1,0:T(8,128)(4,1)S(1)} fusion(s32[8]{0:T(128)} %bitcast.22), kind=kLoop, calls=%fused_computation.3 | loop fusion | flops 1024 | bytes 1056
  17.9 0.3 copy.28
  18.2 0.9 %copy.23 = s32[1024,1]{1,0:T(8,128)S(1)} copy(s32[1024,1]{0,1:T(1,128)} %bitcast.18) | data formatting | bytes 8192 | tf_op jit(solution)/shard_map/squeeze | solution.py:127
  19.1 0.0 collective-permute-done.refs_0_
  19.2 0.0 copy-start.2
  19.2 0.6 collective-permute-start.5
  19.8 0.0 collective-permute-done.1.refs_1_
  19.8 0.0 copy-start.3
  19.8 0.3 collective-permute-start.6
  20.1 0.0 collective-permute-done.2.refs_2_
  20.1 0.0 copy-start.4
  20.1 4.0 %collective-permute-start.7 = (bf16[150,128]{1,0:T(8,128)(2,1)}, bf16[150,128]{1,0:T(8,128)(2,1)S(1)}, u32[]{:S(2)}, u32[]{:S(2)}) collective-permute-start(bf16[150,128]{1,0:T(8,128)(2,1)} %get-tuple-element.22), channel_id=1, source_target_pairs={{4,0},{5,1},{6,2},{7,3},{8,4},{9,5},{10,6},{11,7},{12,8},{13,9},{1... | collective-permute-start | bytes 115208 | tf_op jit(solution)/shard_map/ppermute | solution.py:18
  24.1 0.9 %bitcast_select_fusion.refs_8_ = s32[1024,1]{1,0:T(8,128)} fusion(s32[1024,1]{1,0:T(8,128)S(1)} %copy.23, pred[1,1024]{0,1:T(8,128)(4,1)S(1)} %copy.28), kind=kLoop, calls=%fused_computation | loop fusion | flops 1024 | bytes 9216 | tf_op jit(solution)/shard_map/jit(_where)/select_n | solution.py:127
  25.0 0.0 collective-permute-done.3.refs_3_
  25.0 0.0 copy-start.5
  25.0 0.0 collective-permute-done.4.refs_4_
  25.0 0.0 copy-start.6
  25.0 0.0 collective-permute-done.5.refs_5_
  25.0 0.0 copy-start.7
  25.0 0.0 collective-permute-done.6.refs_6_
  25.0 0.0 copy-start.8
  25.0 1.3 %collective-permute-done.7.refs_7_ = bf16[150,128]{1,0:T(8,128)(2,1)S(1)} collective-permute-done((bf16[150,128]{1,0:T(8,128)(2,1)}, bf16[150,128]{1,0:T(8,128)(2,1)S(1)}, u32[]{:S(2)}, u32[]{:S(2)}) %collective-permute-start.7) | collective-permute-done | bytes 38432 | tf_op jit(solution)/shard_map/ppermute | solution.py:18
  26.3 0.0 copy-start.9
  26.3 0.0 copy-done.2
  26.3 0.0 copy-done.3
  26.3 0.0 copy-done.4
  26.3 0.0 copy-done.5
  26.4 0.0 copy-done.6
  26.4 0.0 copy-done.7
  26.4 0.0 copy-done.8
  26.4 0.6 copy-done.9
  26.9 6.2 %shard_map.129 = (bf16[150,2048]{1,0:T(8,128)(2,1)}, bf16[150,2048]{1,0:T(8,128)(2,1)}) custom-call(s32[2,16]{1,0:T(2,128)} %bitcast.19, bf16[150,8192]{1,0:T(8,128)(2,1)} %mixing_ref.5, bf16[150,128]{1,0:T(8,128)(2,1)} %copy-done.2, bf16[150,128]{1,0:T(8,128)(2,1)} %copy-done.3, bf16[150,128]{1,0:T(8,128)(2,1)} %copy-done.4, bf16[150,128]{1,0:T(8,128)(2,1)} %copy-done.5, ...), custom_call_target="tpu_custom_call" | custom-call | tf_op jit(solution)/shard_map/pallas_call | solution.py:139
  33.2 0.3 collective-permute-start.8
  33.4 7.0 %collective-permute-start.9 = (bf16[150,2048]{1,0:T(8,128)(2,1)}, bf16[150,2048]{1,0:T(8,128)(2,1)S(1)}, u32[]{:S(2)}, u32[]{:S(2)}) collective-permute-start(bf16[150,2048]{1,0:T(8,128)(2,1)} %get-tuple-element.24), channel_id=1, source_target_pairs={{1,0},{2,1},{3,2},{4,3},{5,4},{6,5},{7,6},{8,7},{9,8},{10,9},{11,1... | collective-permute-start | bytes 1843208 | tf_op jit(solution)/shard_map/ppermute | solution.py:18
  40.4 0.0 copy-done.11
  40.4 0.7 %copy.24.nb_ref = s32[64,3]{1,0:T(8,128)} copy(s32[64,3]{0,1:T(4,128)S(1)} %copy-done.11) | data formatting | bytes 1536 | tf_op args[5]
  41.1 0.0 copy-done.12
  41.1 0.0 copy-done.13
  41.1 0.8 %copy.26.rate_terms_ref = f32[256,2]{1,0:T(8,128)} copy(f32[256,2]{0,1:T(2,128)S(1)} %pad_maximum_fusion) | data formatting | bytes 4096 | tf_op jit(solution)/shard_map/stack | solution.py:350
  41.9 0.0 copy-done.10
  41.9 0.8 %copy.25.order_ref = f32[256,150]{1,0:T(8,128)} copy(f32[256,150]{0,1:T(8,128)S(1)} %copy-done.10) | data formatting | bytes 307200 | tf_op args[8]
  42.8 6.8 %shard_map.128.own_ref.migrated_hbm = bf16[150,8192]{1,0:T(8,128)(2,1)} custom-call(bf16[150,8192]{1,0:T(8,128)(2,1)} %mixing_ref.5, bf16[150,128]{1,0:T(8,128)(2,1)} %copy-done.2, bf16[150,128]{1,0:T(8,128)(2,1)} %copy-done.3, bf16[150,128]{1,0:T(8,128)(2,1)} %copy-done.4, bf16[150,128]{1,0:T(8,128)(2,1)} %copy-done.5, bf16[150,128]{1,0:T(8,128)(2,1)} %copy-done.6, ...), custom_call_target="tpu_custom_call" | custom-call | tf_op jit(solution)/shard_map/pallas_call | solution.py:144
  49.6 0.0 collective-permute-done.8.lower_hbm
  49.6 0.0 copy-start
  49.6 0.0 collective-permute-done.9.upper_hbm
  49.6 0.0 copy-start.1
  49.6 0.8 %copy-done = bf16[150,2048]{1,0:T(8,128)(2,1)} copy-done((bf16[150,2048]{1,0:T(8,128)(2,1)}, bf16[150,2048]{1,0:T(8,128)(2,1)S(1)}, u32[]{:S(2)}) %copy-start) | copy-done | bytes 614424
  50.4 0.2 copy-done.1
  50.6 20.2 %shard_map.130 = f32[150,8192]{1,0:T(8,128)} custom-call(s32[64,3]{1,0:T(8,128)} %copy.24.nb_ref, bf16[150,8192]{1,0:T(8,128)(2,1)} %shard_map.128.own_ref.migrated_hbm, bf16[64,4,128,128]{3,2,1,0:T(8,128)(2,1)} %weight_ref.1, f32[1,8192]{1,0:T(1,128)} %bitcast.15, f32[256,150]{1,0:T(8,128)} %copy.25.order_ref, f32[256,2]{1,0:T(8,128)} %copy.26.rate_terms_ref, ...), custom_call_target="tpu_custom_call" | custom-call | tf_op jit(solution)/shard_map/pallas_call | solution.py:339
  (2 shorter events, 0.0 us)
Async XLA Ops:
  0.0 40.4 %copy-start.11 = (s32[64,3]{0,1:T(4,128)S(1)}, s32[64,3]{0,1:T(4,128)}, u32[]{:S(2)}) copy-start(s32[64,3]{0,1:T(4,128)} %param.18) | copy-start | bytes 2308
  0.0 41.1 %copy-start.12 = (f32[256]{0:T(256)S(1)}, f32[256]{0:T(256)}, u32[]{:S(2)}) copy-start(f32[256]{0:T(256)} %param.23) | copy-start | bytes 3076
  0.0 41.1 %copy-start.13 = (f32[256]{0:T(256)S(1)}, f32[256]{0:T(256)}, u32[]{:S(2)}) copy-start(f32[256]{0:T(256)} %param.22) | copy-start | bytes 3076
  0.0 41.9 %copy-start.10 = (f32[256,150]{0,1:T(8,128)S(1)}, f32[256,150]{0,1:T(8,128)}, u32[]{:S(2)}) copy-start(f32[256,150]{0,1:T(8,128)} %param.21) | copy-start | bytes 460804
  5.3 13.8 %collective-permute-start = (bf16[150,128]{1,0:T(8,128)(2,1)}, bf16[150,128]{1,0:T(8,128)(2,1)S(1)}, u32[]{:S(2)}, u32[]{:S(2)}) collective-permute-start(bf16[150,128]{1,0:T(8,128)(2,1)} %get-tuple-element.15), channel_id=1, source_target_pairs={{124,0},{125,1},{126,2},{127,3},{0,4},{1,5},{2,6},{3,7},{4,8},{5,9... | collective-permute-start | bytes 115208 | tf_op jit(solution)/shard_map/ppermute | solution.py:18
  8.4 11.4 %collective-permute-start.1 = (bf16[150,128]{1,0:T(8,128)(2,1)}, bf16[150,128]{1,0:T(8,128)(2,1)S(1)}, u32[]{:S(2)}, u32[]{:S(2)}) collective-permute-start(bf16[150,128]{1,0:T(8,128)(2,1)} %get-tuple-element.16), channel_id=1, source_target_pairs={{125,0},{126,1},{127,2},{0,3},{1,4},{2,5},{3,6},{4,7},{5,8},{6,9},... | collective-permute-start | bytes 115208 | tf_op jit(solution)/shard_map/ppermute | solution.py:18
  8.4 11.7 %collective-permute-start.2 = (bf16[150,128]{1,0:T(8,128)(2,1)}, bf16[150,128]{1,0:T(8,128)(2,1)S(1)}, u32[]{:S(2)}, u32[]{:S(2)}) collective-permute-start(bf16[150,128]{1,0:T(8,128)(2,1)} %get-tuple-element.17), channel_id=1, source_target_pairs={{126,0},{127,1},{0,2},{1,3},{2,4},{3,5},{4,6},{5,7},{6,8},{7,9},{8... | collective-permute-start | bytes 115208 | tf_op jit(solution)/shard_map/ppermute | solution.py:18
  9.4 15.6 %collective-permute-start.3 = (bf16[150,128]{1,0:T(8,128)(2,1)}, bf16[150,128]{1,0:T(8,128)(2,1)S(1)}, u32[]{:S(2)}, u32[]{:S(2)}) collective-permute-start(bf16[150,128]{1,0:T(8,128)(2,1)} %get-tuple-element.18), channel_id=1, source_target_pairs={{127,0},{0,1},{1,2},{2,3},{3,4},{4,5},{5,6},{6,7},{7,8},{8,9},{9,1... | collective-permute-start | bytes 115208 | tf_op jit(solution)/shard_map/ppermute | solution.py:18
  11.6 13.4 %collective-permute-start.4 = (bf16[150,128]{1,0:T(8,128)(2,1)}, bf16[150,128]{1,0:T(8,128)(2,1)S(1)}, u32[]{:S(2)}, u32[]{:S(2)}) collective-permute-start(bf16[150,128]{1,0:T(8,128)(2,1)} %get-tuple-element.19), channel_id=1, source_target_pairs={{1,0},{2,1},{3,2},{4,3},{5,4},{6,5},{7,6},{8,7},{9,8},{10,9},{11,1... | collective-permute-start | bytes 115208 | tf_op jit(solution)/shard_map/ppermute | solution.py:18
  19.2 7.2 %copy-start.2 = (bf16[150,128]{1,0:T(8,128)(2,1)}, bf16[150,128]{1,0:T(8,128)(2,1)S(1)}, u32[]{:S(2)}) copy-start(bf16[150,128]{1,0:T(8,128)(2,1)S(1)} %collective-permute-done.refs_0_) | copy-start | bytes 115204
  19.2 5.8 %collective-permute-start.5 = (bf16[150,128]{1,0:T(8,128)(2,1)}, bf16[150,128]{1,0:T(8,128)(2,1)S(1)}, u32[]{:S(2)}, u32[]{:S(2)}) collective-permute-start(bf16[150,128]{1,0:T(8,128)(2,1)} %get-tuple-element.20), channel_id=1, source_target_pairs={{2,0},{3,1},{4,2},{5,3},{6,4},{7,5},{8,6},{9,7},{10,8},{11,9},{12,... | collective-permute-start | bytes 115208 | tf_op jit(solution)/shard_map/ppermute | solution.py:18
  19.8 6.5 %copy-start.3 = (bf16[150,128]{1,0:T(8,128)(2,1)}, bf16[150,128]{1,0:T(8,128)(2,1)S(1)}, u32[]{:S(2)}) copy-start(bf16[150,128]{1,0:T(8,128)(2,1)S(1)} %collective-permute-done.1.refs_1_) | copy-start | bytes 115204
  19.8 5.2 %collective-permute-start.6 = (bf16[150,128]{1,0:T(8,128)(2,1)}, bf16[150,128]{1,0:T(8,128)(2,1)S(1)}, u32[]{:S(2)}, u32[]{:S(2)}) collective-permute-start(bf16[150,128]{1,0:T(8,128)(2,1)} %get-tuple-element.21), channel_id=1, source_target_pairs={{3,0},{4,1},{5,2},{6,3},{7,4},{8,5},{9,6},{10,7},{11,8},{12,9},{13... | collective-permute-start | bytes 115208 | tf_op jit(solution)/shard_map/ppermute | solution.py:18
  20.1 6.2 %copy-start.4 = (bf16[150,128]{1,0:T(8,128)(2,1)}, bf16[150,128]{1,0:T(8,128)(2,1)S(1)}, u32[]{:S(2)}) copy-start(bf16[150,128]{1,0:T(8,128)(2,1)S(1)} %collective-permute-done.2.refs_2_) | copy-start | bytes 115204
  20.1 6.2 %collective-permute-start.7 = (bf16[150,128]{1,0:T(8,128)(2,1)}, bf16[150,128]{1,0:T(8,128)(2,1)S(1)}, u32[]{:S(2)}, u32[]{:S(2)}) collective-permute-start(bf16[150,128]{1,0:T(8,128)(2,1)} %get-tuple-element.22), channel_id=1, source_target_pairs={{4,0},{5,1},{6,2},{7,3},{8,4},{9,5},{10,6},{11,7},{12,8},{13,9},{1... | collective-permute-start | bytes 115208 | tf_op jit(solution)/shard_map/ppermute | solution.py:18
  25.0 1.4 %copy-start.5 = (bf16[150,128]{1,0:T(8,128)(2,1)}, bf16[150,128]{1,0:T(8,128)(2,1)S(1)}, u32[]{:S(2)}) copy-start(bf16[150,128]{1,0:T(8,128)(2,1)S(1)} %collective-permute-done.3.refs_3_) | copy-start | bytes 115204
  25.0 1.4 %copy-start.6 = (bf16[150,128]{1,0:T(8,128)(2,1)}, bf16[150,128]{1,0:T(8,128)(2,1)S(1)}, u32[]{:S(2)}) copy-start(bf16[150,128]{1,0:T(8,128)(2,1)S(1)} %collective-permute-done.4.refs_4_) | copy-start | bytes 115204
  25.0 1.4 %copy-start.7 = (bf16[150,128]{1,0:T(8,128)(2,1)}, bf16[150,128]{1,0:T(8,128)(2,1)S(1)}, u32[]{:S(2)}) copy-start(bf16[150,128]{1,0:T(8,128)(2,1)S(1)} %collective-permute-done.5.refs_5_) | copy-start | bytes 115204
  25.0 1.3 %copy-start.8 = (bf16[150,128]{1,0:T(8,128)(2,1)}, bf16[150,128]{1,0:T(8,128)(2,1)S(1)}, u32[]{:S(2)}) copy-start(bf16[150,128]{1,0:T(8,128)(2,1)S(1)} %collective-permute-done.6.refs_6_) | copy-start | bytes 115204
  26.3 0.6 copy-start.9
  33.2 16.4 %collective-permute-start.8 = (bf16[150,2048]{1,0:T(8,128)(2,1)}, bf16[150,2048]{1,0:T(8,128)(2,1)S(1)}, u32[]{:S(2)}, u32[]{:S(2)}) collective-permute-start(bf16[150,2048]{1,0:T(8,128)(2,1)} %get-tuple-element.23), channel_id=1, source_target_pairs={{127,0},{0,1},{1,2},{2,3},{3,4},{4,5},{5,6},{6,7},{7,8},{8,9},{9,1... | collective-permute-start | bytes 1843208 | tf_op jit(solution)/shard_map/ppermute | solution.py:18
  33.4 16.2 %collective-permute-start.9 = (bf16[150,2048]{1,0:T(8,128)(2,1)}, bf16[150,2048]{1,0:T(8,128)(2,1)S(1)}, u32[]{:S(2)}, u32[]{:S(2)}) collective-permute-start(bf16[150,2048]{1,0:T(8,128)(2,1)} %get-tuple-element.24), channel_id=1, source_target_pairs={{1,0},{2,1},{3,2},{4,3},{5,4},{6,5},{7,6},{8,7},{9,8},{10,9},{11,1... | collective-permute-start | bytes 1843208 | tf_op jit(solution)/shard_map/ppermute | solution.py:18
  49.6 0.9 %copy-start = (bf16[150,2048]{1,0:T(8,128)(2,1)}, bf16[150,2048]{1,0:T(8,128)(2,1)S(1)}, u32[]{:S(2)}) copy-start(bf16[150,2048]{1,0:T(8,128)(2,1)S(1)} %collective-permute-done.8.lower_hbm) | copy-start | bytes 1843204
  49.6 1.0 %copy-start.1 = (bf16[150,2048]{1,0:T(8,128)(2,1)}, bf16[150,2048]{1,0:T(8,128)(2,1)S(1)}, u32[]{:S(2)}) copy-start(bf16[150,2048]{1,0:T(8,128)(2,1)S(1)} %collective-permute-done.9.upper_hbm) | copy-start | bytes 1843204

commit v11 on v10

--- a/solution.py
+++ b/solution.py
@@ -177,7 +177,6 @@
     weight_ref,
     temp_ref,
     order_ref,
-    rate_terms_ref,
     prod_ref,
     loss_ref,
     migrated_hbm,
@@ -187,6 +186,7 @@
     picked,
     sems,
     mixed_ref,
+    terms_ref,
     order_split,
     gain_split,
     gain_high,
@@ -229,7 +229,7 @@
     @pl.when(step == 0)
     def _():
         fetch(0, 0, True)
-        order_high, order_low = split3(order_ref[...])
+        order_high, order_low = split3(order_ref[...].T)
         reactions = order_high.shape[0]
         order_split[0:reactions] = order_high
         order_split[reactions:] = order_low
@@ -264,14 +264,15 @@
         mixed_ref[:, lanes] = jnp.dot(stacked, weight, preferred_element_type=f32)
     mixed = mixed_ref[...]
     species = mixed.shape[0]
-    log_high, log_low = split3(jnp.log(mixed))
+    terms_ref[0:species] = jnp.log(mixed)
+    terms_ref[species:species + 1] = jnp.ones((1, mixed.shape[1]), f32)
+    terms_ref[species + 1:species + 2] = temp_ref[...]
+    log_high, log_low = split3(terms_ref[...])
     reactions = order_split.shape[0] // 2
     both = jnp.dot(order_split[...], log_high, preferred_element_type=f32)
     exponent = both[:reactions] + both[reactions:]
     exponent = exponent + jnp.dot(order_split[0:reactions], log_low, preferred_element_type=f32)
-    prefactor = rate_terms_ref[:, 0:1]
-    energy = rate_terms_ref[:, 1:2]
-    rate = jnp.exp(prefactor - energy * temp_ref[...] + exponent)
+    rate = jnp.exp(exponent)
     rate_high, rate_low = split3(rate)
     by_high = jnp.dot(gain_split[...], rate_high, preferred_element_type=f32)
     by_low = jnp.dot(gain_high[...], rate_low, preferred_element_type=f32)
@@ -312,8 +313,7 @@
         pl.BlockSpec((species, width), lambda i, nb: (0, i)),
         pl.BlockSpec((tile_blocks,) + mix_weight.shape[1:], lambda i, nb: (i, 0, 0, 0)),
         pl.BlockSpec((1, width), lambda i, nb: (0, i)),
-        whole(reactant_order.shape),
-        whole((reactions, 2)),
+        whole((species + 2, reactions)),
         whole(production.shape),
         whole(loss_coefficient.shape),
         pl.BlockSpec(memory_space=pl.ANY),
@@ -330,7 +330,8 @@
             pltpu.VMEM((2, tile_blocks * neighbours, species, block_size), bf16),
             pltpu.SemaphoreType.DMA((2, tile_blocks * neighbours)),
             pltpu.VMEM((species, width), jnp.float32),
-            pltpu.VMEM((2 * reactions, species), bf16),
+            pltpu.VMEM((species + 2, width), jnp.float32),
+            pltpu.VMEM((2 * reactions, species + 2), bf16),
             pltpu.VMEM((4 * PAD_ROWS, reactions), bf16),
             pltpu.VMEM((2 * PAD_ROWS, reactions), bf16),
         ],
@@ -346,8 +347,9 @@
         migrated,
         mix_weight,
         inverse_temp.reshape(1, -1),
-        reactant_order,
-        jnp.stack([log_prefactor, activation_energy], axis=1),
+        jnp.concatenate(
+            [reactant_order.T, log_prefactor[None, :], -activation_energy[None, :]], axis=0
+        ),
         production,
         loss_coefficient,
         migrated,

time: 71.5 us -> 70.3 us (0.983)
  local copies, waits for them, and re-layouts: 5.17 us -> 3.51 us
    unnamed x32 -> x31, local copies, waits for them, and re-layouts: 3.47 us -> 2.6 us
    another operation x1 -> x0, local copies, waits for them, and re-layouts: 0.79 us -> none  [mix_react(): jnp.stack([log_prefactor, activation_energy], axis=1)]
  transfers between devices with their start and end apart: 10 -> 10, of which waited for: 1 -> 1; matrix products, arithmetic and copies ran while one was open for 7% -> 6% of each run, Pallas kernels for 10% -> 10%
where the time goes in v11:
time: 70.3 us; the launch traced here: 69.8 us
  Pallas kernels  38.3 us (54%)
  starting transfers between devices  24.1 us (34%)
  local copies, waits for them, and re-layouts  3.51 us (5%)
  other arithmetic  2.25 us (3%)
  waiting for transfers between devices  1.31 us (2%)
    ppermute x10, starting transfers between devices, from_behind(): return lax.ppermute(block, axis, route)  24.1 us
    pallas_call x1, Pallas kernels, mix_react(): pl.pallas_call(kernel, grid_spec=grid_spec, out_shape=jax.ShapeDtypeStruc...  20 us
    pallas_call x1, Pallas kernels, migrate(): pl.pallas_call(functools.partial(place_kernel, chunk, peer_count), grid=(...  6.82 us
    pallas_call x1, Pallas kernels, migrate(): pl.pallas_call(functools.partial(halo_kernel, chunk, block_size, peer_cou...  6.15 us
    pallas_call x1, Pallas kernels, migrate(): pl.pallas_call(functools.partial(pick_kernel, chunk), grid=(1,), in_specs...  5.3 us
    unnamed x31, local copies, waits for them, and re-layouts  2.6 us
  transfers between devices with their start and end apart: 10, of which 1 were waited for; matrix products, arithmetic and copies ran while one was open for 6% of the time, Pallas kernels for 10%

profile of v11, /device:TPU:0, one launch (start us, length us, event | category | flops | bytes accessed | tf_op | source)
XLA Modules:
  0.0 69.8 jit_solution(9572617023959206188)
XLA Ops:
  0.0 0.0 copy-start.13
  0.0 0.0 copy-start.11
  0.0 0.0 copy-start.12
  0.0 0.0 copy-start.10
  0.0 5.3 %shard_map.127 = (bf16[150,128]{1,0:T(8,128)(2,1)}, bf16[150,128]{1,0:T(8,128)(2,1)}, bf16[150,128]{1,0:T(8,128)(2,1)}, bf16[150,128]{1,0:T(8,128)(2,1)}, bf16[1...) custom-call(bf16[150,8192]{1,0:T(8,128)(2,1)} %mixing_ref.5, ...), custom_call_target="tpu_custom_call" | custom-call | tf_op jit(solution)/shard_map/pallas_call | solution.py:114
  5.3 3.1 %collective-permute-start = (bf16[150,128]{1,0:T(8,128)(2,1)}, bf16[150,128]{1,0:T(8,128)(2,1)S(1)}, u32[]{:S(2)}, u32[]{:S(2)}) collective-permute-start(bf16[150,128]{1,0:T(8,128)(2,1)} %get-tuple-element.15), channel_id=1, source_target_pairs={{124,0},{125,1},{126,2},{127,3},{0,4},{1,5},{2,6},{3,7},{4,8},{5,9... | collective-permute-start | bytes 115208 | tf_op jit(solution)/shard_map/ppermute | solution.py:18
  8.4 0.0 collective-permute-start.1
  8.4 1.0 %collective-permute-start.2 = (bf16[150,128]{1,0:T(8,128)(2,1)}, bf16[150,128]{1,0:T(8,128)(2,1)S(1)}, u32[]{:S(2)}, u32[]{:S(2)}) collective-permute-start(bf16[150,128]{1,0:T(8,128)(2,1)} %get-tuple-element.17), channel_id=1, source_target_pairs={{126,0},{127,1},{0,2},{1,3},{2,4},{3,5},{4,6},{5,7},{6,8},{7,9},{8... | collective-permute-start | bytes 115208 | tf_op jit(solution)/shard_map/ppermute | solution.py:18
  9.4 2.2 %collective-permute-start.3 = (bf16[150,128]{1,0:T(8,128)(2,1)}, bf16[150,128]{1,0:T(8,128)(2,1)S(1)}, u32[]{:S(2)}, u32[]{:S(2)}) collective-permute-start(bf16[150,128]{1,0:T(8,128)(2,1)} %get-tuple-element.18), channel_id=1, source_target_pairs={{127,0},{0,1},{1,2},{2,3},{3,4},{4,5},{5,6},{6,7},{7,8},{8,9},{9,1... | collective-permute-start | bytes 115208 | tf_op jit(solution)/shard_map/ppermute | solution.py:18
  11.6 5.6 %collective-permute-start.4 = (bf16[150,128]{1,0:T(8,128)(2,1)}, bf16[150,128]{1,0:T(8,128)(2,1)S(1)}, u32[]{:S(2)}, u32[]{:S(2)}) collective-permute-start(bf16[150,128]{1,0:T(8,128)(2,1)} %get-tuple-element.19), channel_id=1, source_target_pairs={{1,0},{2,1},{3,2},{4,3},{5,4},{6,5},{7,6},{8,7},{9,8},{10,9},{11,1... | collective-permute-start | bytes 115208 | tf_op jit(solution)/shard_map/ppermute | solution.py:18
  17.2 0.7 %fusion = pred[1,1,8,128]{3,2,1,0:T(8,128)(4,1)S(1)} fusion(s32[8]{0:T(128)} %bitcast.24), kind=kLoop, calls=%fused_computation.4 | loop fusion | flops 1024 | bytes 1056
  17.9 0.3 copy.19
  18.2 0.9 %copy.16 = s32[1024,1]{1,0:T(8,128)S(1)} copy(s32[1024,1]{0,1:T(1,128)} %bitcast.20) | data formatting | bytes 8192 | tf_op jit(solution)/shard_map/squeeze | solution.py:127
  19.1 0.0 collective-permute-done.refs_0_
  19.2 0.0 copy-start.2
  19.2 0.6 collective-permute-start.5
  19.8 0.0 collective-permute-done.1.refs_1_
  19.8 0.0 copy-start.3
  19.8 0.3 collective-permute-start.6
  20.1 0.0 collective-permute-done.2.refs_2_
  20.1 0.0 copy-start.4
  20.1 4.0 %collective-permute-start.7 = (bf16[150,128]{1,0:T(8,128)(2,1)}, bf16[150,128]{1,0:T(8,128)(2,1)S(1)}, u32[]{:S(2)}, u32[]{:S(2)}) collective-permute-start(bf16[150,128]{1,0:T(8,128)(2,1)} %get-tuple-element.22), channel_id=1, source_target_pairs={{4,0},{5,1},{6,2},{7,3},{8,4},{9,5},{10,6},{11,7},{12,8},{13,9},{1... | collective-permute-start | bytes 115208 | tf_op jit(solution)/shard_map/ppermute | solution.py:18
  24.1 0.9 %bitcast_select_fusion.refs_8_ = s32[1024,1]{1,0:T(8,128)} fusion(s32[1024,1]{1,0:T(8,128)S(1)} %copy.16, pred[1,1024]{0,1:T(8,128)(4,1)S(1)} %copy.19), kind=kLoop, calls=%fused_computation | loop fusion | flops 1024 | bytes 9216 | tf_op jit(solution)/shard_map/jit(_where)/select_n | solution.py:127
  25.0 0.0 collective-permute-done.3.refs_3_
  25.0 0.0 copy-start.5
  25.0 0.0 collective-permute-done.4.refs_4_
  25.0 0.0 copy-start.6
  25.0 0.0 collective-permute-done.5.refs_5_
  25.0 0.0 copy-start.7
  25.0 0.0 collective-permute-done.6.refs_6_
  25.0 0.0 copy-start.8
  25.0 1.3 %collective-permute-done.7.refs_7_ = bf16[150,128]{1,0:T(8,128)(2,1)S(1)} collective-permute-done((bf16[150,128]{1,0:T(8,128)(2,1)}, bf16[150,128]{1,0:T(8,128)(2,1)S(1)}, u32[]{:S(2)}, u32[]{:S(2)}) %collective-permute-start.7) | collective-permute-done | bytes 38432 | tf_op jit(solution)/shard_map/ppermute | solution.py:18
  26.3 0.0 copy-start.9
  26.3 0.0 copy-done.2
  26.3 0.0 copy-done.3
  26.3 0.0 copy-done.4
  26.3 0.0 copy-done.5
  26.4 0.0 copy-done.6
  26.4 0.0 copy-done.7
  26.4 0.0 copy-done.8
  26.4 0.6 copy-done.9
  26.9 6.2 %shard_map.129 = (bf16[150,2048]{1,0:T(8,128)(2,1)}, bf16[150,2048]{1,0:T(8,128)(2,1)}) custom-call(s32[2,16]{1,0:T(2,128)} %bitcast.22, bf16[150,8192]{1,0:T(8,128)(2,1)} %mixing_ref.5, bf16[150,128]{1,0:T(8,128)(2,1)} %copy-done.2, bf16[150,128]{1,0:T(8,128)(2,1)} %copy-done.3, bf16[150,128]{1,0:T(8,128)(2,1)} %copy-done.4, bf16[150,128]{1,0:T(8,128)(2,1)} %copy-done.5, ...), custom_call_target="tpu_custom_call" | custom-call | tf_op jit(solution)/shard_map/pallas_call | solution.py:139
  33.1 0.2 collective-permute-start.8
  33.3 7.1 %collective-permute-start.9 = (bf16[150,2048]{1,0:T(8,128)(2,1)}, bf16[150,2048]{1,0:T(8,128)(2,1)S(1)}, u32[]{:S(2)}, u32[]{:S(2)}) collective-permute-start(bf16[150,2048]{1,0:T(8,128)(2,1)} %get-tuple-element.24), channel_id=1, source_target_pairs={{1,0},{2,1},{3,2},{4,3},{5,4},{6,5},{7,6},{8,7},{9,8},{10,9},{11,1... | collective-permute-start | bytes 1843208 | tf_op jit(solution)/shard_map/ppermute | solution.py:18
  40.3 0.0 copy-done.13
  40.4 0.0 copy-done.11
  40.4 0.7 %copy.17.nb_ref = s32[64,3]{1,0:T(8,128)} copy(s32[64,3]{0,1:T(4,128)S(1)} %copy-done.11) | data formatting | bytes 1536 | tf_op args[5]
  41.1 0.0 copy-done.12
  41.1 0.0 copy-done.10
  41.1 0.7 pad_maximum_fusion.order_ref
  41.7 6.8 %shard_map.128.own_ref.migrated_hbm = bf16[150,8192]{1,0:T(8,128)(2,1)} custom-call(bf16[150,8192]{1,0:T(8,128)(2,1)} %mixing_ref.5, bf16[150,128]{1,0:T(8,128)(2,1)} %copy-done.2, bf16[150,128]{1,0:T(8,128)(2,1)} %copy-done.3, bf16[150,128]{1,0:T(8,128)(2,1)} %copy-done.4, bf16[150,128]{1,0:T(8,128)(2,1)} %copy-done.5, bf16[150,128]{1,0:T(8,128)(2,1)} %copy-done.6, ...), custom_call_target="tpu_custom_call" | custom-call | tf_op jit(solution)/shard_map/pallas_call | solution.py:144
  48.5 0.0 collective-permute-done.8.lower_hbm
  48.5 0.0 copy-start
  48.5 0.0 collective-permute-done.9.upper_hbm
  48.6 0.0 copy-start.1
  48.6 0.8 %copy-done = bf16[150,2048]{1,0:T(8,128)(2,1)} copy-done((bf16[150,2048]{1,0:T(8,128)(2,1)}, bf16[150,2048]{1,0:T(8,128)(2,1)S(1)}, u32[]{:S(2)}) %copy-start) | copy-done | bytes 614424
  49.4 0.2 copy-done.1
  49.6 20.0 %shard_map.130 = f32[150,8192]{1,0:T(8,128)} custom-call(s32[64,3]{1,0:T(8,128)} %copy.17.nb_ref, bf16[150,8192]{1,0:T(8,128)(2,1)} %shard_map.128.own_ref.migrated_hbm, bf16[64,4,128,128]{3,2,1,0:T(8,128)(2,1)} %weight_ref.1, f32[1,8192]{1,0:T(1,128)} %bitcast.17, f32[152,256]{1,0:T(8,128)} %pad_maximum_fusion.order_ref, f32[150,256]{1,0:T(8,128)} %prod_ref.1, ...), custom_call_target="tpu_custom_call" | custom-call | tf_op jit(solution)/shard_map/pallas_call | solution.py:340
  (2 shorter events, 0.0 us)
Async XLA Ops:
  0.0 40.4 %copy-start.13 = (f32[256]{0:T(256)S(1)}, f32[256]{0:T(256)}, u32[]{:S(2)}) copy-start(f32[256]{0:T(256)} %param.23) | copy-start | bytes 3076
  0.0 40.4 %copy-start.11 = (s32[64,3]{0,1:T(4,128)S(1)}, s32[64,3]{0,1:T(4,128)}, u32[]{:S(2)}) copy-start(s32[64,3]{0,1:T(4,128)} %param.18) | copy-start | bytes 2308
  0.0 41.1 %copy-start.12 = (f32[256]{0:T(256)S(1)}, f32[256]{0:T(256)}, u32[]{:S(2)}) copy-start(f32[256]{0:T(256)} %param.22) | copy-start | bytes 3076
  0.0 41.1 %copy-start.10 = (f32[256,150]{0,1:T(8,128)S(1)}, f32[256,150]{0,1:T(8,128)}, u32[]{:S(2)}) copy-start(f32[256,150]{0,1:T(8,128)} %param.21) | copy-start | bytes 460804
  5.3 13.8 %collective-permute-start = (bf16[150,128]{1,0:T(8,128)(2,1)}, bf16[150,128]{1,0:T(8,128)(2,1)S(1)}, u32[]{:S(2)}, u32[]{:S(2)}) collective-permute-start(bf16[150,128]{1,0:T(8,128)(2,1)} %get-tuple-element.15), channel_id=1, source_target_pairs={{124,0},{125,1},{126,2},{127,3},{0,4},{1,5},{2,6},{3,7},{4,8},{5,9... | collective-permute-start | bytes 115208 | tf_op jit(solution)/shard_map/ppermute | solution.py:18
  8.4 11.4 %collective-permute-start.1 = (bf16[150,128]{1,0:T(8,128)(2,1)}, bf16[150,128]{1,0:T(8,128)(2,1)S(1)}, u32[]{:S(2)}, u32[]{:S(2)}) collective-permute-start(bf16[150,128]{1,0:T(8,128)(2,1)} %get-tuple-element.16), channel_id=1, source_target_pairs={{125,0},{126,1},{127,2},{0,3},{1,4},{2,5},{3,6},{4,7},{5,8},{6,9},... | collective-permute-start | bytes 115208 | tf_op jit(solution)/shard_map/ppermute | solution.py:18
  8.4 11.7 %collective-permute-start.2 = (bf16[150,128]{1,0:T(8,128)(2,1)}, bf16[150,128]{1,0:T(8,128)(2,1)S(1)}, u32[]{:S(2)}, u32[]{:S(2)}) collective-permute-start(bf16[150,128]{1,0:T(8,128)(2,1)} %get-tuple-element.17), channel_id=1, source_target_pairs={{126,0},{127,1},{0,2},{1,3},{2,4},{3,5},{4,6},{5,7},{6,8},{7,9},{8... | collective-permute-start | bytes 115208 | tf_op jit(solution)/shard_map/ppermute | solution.py:18
  9.4 15.6 %collective-permute-start.3 = (bf16[150,128]{1,0:T(8,128)(2,1)}, bf16[150,128]{1,0:T(8,128)(2,1)S(1)}, u32[]{:S(2)}, u32[]{:S(2)}) collective-permute-start(bf16[150,128]{1,0:T(8,128)(2,1)} %get-tuple-element.18), channel_id=1, source_target_pairs={{127,0},{0,1},{1,2},{2,3},{3,4},{4,5},{5,6},{6,7},{7,8},{8,9},{9,1... | collective-permute-start | bytes 115208 | tf_op jit(solution)/shard_map/ppermute | solution.py:18
  11.6 13.4 %collective-permute-start.4 = (bf16[150,128]{1,0:T(8,128)(2,1)}, bf16[150,128]{1,0:T(8,128)(2,1)S(1)}, u32[]{:S(2)}, u32[]{:S(2)}) collective-permute-start(bf16[150,128]{1,0:T(8,128)(2,1)} %get-tuple-element.19), channel_id=1, source_target_pairs={{1,0},{2,1},{3,2},{4,3},{5,4},{6,5},{7,6},{8,7},{9,8},{10,9},{11,1... | collective-permute-start | bytes 115208 | tf_op jit(solution)/shard_map/ppermute | solution.py:18
  19.2 7.2 %copy-start.2 = (bf16[150,128]{1,0:T(8,128)(2,1)}, bf16[150,128]{1,0:T(8,128)(2,1)S(1)}, u32[]{:S(2)}) copy-start(bf16[150,128]{1,0:T(8,128)(2,1)S(1)} %collective-permute-done.refs_0_) | copy-start | bytes 115204
  19.2 5.8 %collective-permute-start.5 = (bf16[150,128]{1,0:T(8,128)(2,1)}, bf16[150,128]{1,0:T(8,128)(2,1)S(1)}, u32[]{:S(2)}, u32[]{:S(2)}) collective-permute-start(bf16[150,128]{1,0:T(8,128)(2,1)} %get-tuple-element.20), channel_id=1, source_target_pairs={{2,0},{3,1},{4,2},{5,3},{6,4},{7,5},{8,6},{9,7},{10,8},{11,9},{12,... | collective-permute-start | bytes 115208 | tf_op jit(solution)/shard_map/ppermute | solution.py:18
  19.8 6.5 %copy-start.3 = (bf16[150,128]{1,0:T(8,128)(2,1)}, bf16[150,128]{1,0:T(8,128)(2,1)S(1)}, u32[]{:S(2)}) copy-start(bf16[150,128]{1,0:T(8,128)(2,1)S(1)} %collective-permute-done.1.refs_1_) | copy-start | bytes 115204
  19.8 5.2 %collective-permute-start.6 = (bf16[150,128]{1,0:T(8,128)(2,1)}, bf16[150,128]{1,0:T(8,128)(2,1)S(1)}, u32[]{:S(2)}, u32[]{:S(2)}) collective-permute-start(bf16[150,128]{1,0:T(8,128)(2,1)} %get-tuple-element.21), channel_id=1, source_target_pairs={{3,0},{4,1},{5,2},{6,3},{7,4},{8,5},{9,6},{10,7},{11,8},{12,9},{13... | collective-permute-start | bytes 115208 | tf_op jit(solution)/shard_map/ppermute | solution.py:18
  20.1 6.2 %copy-start.4 = (bf16[150,128]{1,0:T(8,128)(2,1)}, bf16[150,128]{1,0:T(8,128)(2,1)S(1)}, u32[]{:S(2)}) copy-start(bf16[150,128]{1,0:T(8,128)(2,1)S(1)} %collective-permute-done.2.refs_2_) | copy-start | bytes 115204
  20.1 6.2 %collective-permute-start.7 = (bf16[150,128]{1,0:T(8,128)(2,1)}, bf16[150,128]{1,0:T(8,128)(2,1)S(1)}, u32[]{:S(2)}, u32[]{:S(2)}) collective-permute-start(bf16[150,128]{1,0:T(8,128)(2,1)} %get-tuple-element.22), channel_id=1, source_target_pairs={{4,0},{5,1},{6,2},{7,3},{8,4},{9,5},{10,6},{11,7},{12,8},{13,9},{1... | collective-permute-start | bytes 115208 | tf_op jit(solution)/shard_map/ppermute | solution.py:18
  25.0 1.4 %copy-start.5 = (bf16[150,128]{1,0:T(8,128)(2,1)}, bf16[150,128]{1,0:T(8,128)(2,1)S(1)}, u32[]{:S(2)}) copy-start(bf16[150,128]{1,0:T(8,128)(2,1)S(1)} %collective-permute-done.3.refs_3_) | copy-start | bytes 115204
  25.0 1.4 %copy-start.6 = (bf16[150,128]{1,0:T(8,128)(2,1)}, bf16[150,128]{1,0:T(8,128)(2,1)S(1)}, u32[]{:S(2)}) copy-start(bf16[150,128]{1,0:T(8,128)(2,1)S(1)} %collective-permute-done.4.refs_4_) | copy-start | bytes 115204
  25.0 1.4 %copy-start.7 = (bf16[150,128]{1,0:T(8,128)(2,1)}, bf16[150,128]{1,0:T(8,128)(2,1)S(1)}, u32[]{:S(2)}) copy-start(bf16[150,128]{1,0:T(8,128)(2,1)S(1)} %collective-permute-done.5.refs_5_) | copy-start | bytes 115204
  25.0 1.3 %copy-start.8 = (bf16[150,128]{1,0:T(8,128)(2,1)}, bf16[150,128]{1,0:T(8,128)(2,1)S(1)}, u32[]{:S(2)}) copy-start(bf16[150,128]{1,0:T(8,128)(2,1)S(1)} %collective-permute-done.6.refs_6_) | copy-start | bytes 115204
  26.3 0.6 copy-start.9
  33.1 15.4 %collective-permute-start.8 = (bf16[150,2048]{1,0:T(8,128)(2,1)}, bf16[150,2048]{1,0:T(8,128)(2,1)S(1)}, u32[]{:S(2)}, u32[]{:S(2)}) collective-permute-start(bf16[150,2048]{1,0:T(8,128)(2,1)} %get-tuple-element.23), channel_id=1, source_target_pairs={{127,0},{0,1},{1,2},{2,3},{3,4},{4,5},{5,6},{6,7},{7,8},{8,9},{9,1... | collective-permute-start | bytes 1843208 | tf_op jit(solution)/shard_map/ppermute | solution.py:18
  33.3 15.3 %collective-permute-start.9 = (bf16[150,2048]{1,0:T(8,128)(2,1)}, bf16[150,2048]{1,0:T(8,128)(2,1)S(1)}, u32[]{:S(2)}, u32[]{:S(2)}) collective-permute-start(bf16[150,2048]{1,0:T(8,128)(2,1)} %get-tuple-element.24), channel_id=1, source_target_pairs={{1,0},{2,1},{3,2},{4,3},{5,4},{6,5},{7,6},{8,7},{9,8},{10,9},{11,1... | collective-permute-start | bytes 1843208 | tf_op jit(solution)/shard_map/ppermute | solution.py:18
  48.5 0.9 %copy-start = (bf16[150,2048]{1,0:T(8,128)(2,1)}, bf16[150,2048]{1,0:T(8,128)(2,1)S(1)}, u32[]{:S(2)}) copy-start(bf16[150,2048]{1,0:T(8,128)(2,1)S(1)} %collective-permute-done.8.lower_hbm) | copy-start | bytes 1843204
  48.6 1.0 %copy-start.1 = (bf16[150,2048]{1,0:T(8,128)(2,1)}, bf16[150,2048]{1,0:T(8,128)(2,1)S(1)}, u32[]{:S(2)}) copy-start(bf16[150,2048]{1,0:T(8,128)(2,1)S(1)} %collective-permute-done.9.upper_hbm) | copy-start | bytes 1843204

commit v12 on v11

--- a/solution.py
+++ b/solution.py
@@ -200,7 +200,7 @@
     def fetch(at, slot, start):
         for t in range(tile_blocks):
             for k in range(neighbours):
-                index = nb_ref[at * tile_blocks + t, k]
+                index = nb_ref[k, at * tile_blocks + t]
                 target = picked.at[slot, t * neighbours + k]
                 sem = sems.at[slot, t * neighbours + k]
                 if not start:
@@ -343,7 +343,7 @@
         out_shape=jax.ShapeDtypeStruct((species, count_blocks * block_size), jnp.float32),
         compiler_params=pltpu.CompilerParams(dimension_semantics=("arbitrary",)),
     )(
-        neighbour_block,
+        neighbour_block.T,
         migrated,
         mix_weight,
         inverse_temp.reshape(1, -1),

time: 70.3 us -> 69.8 us (level)
    unnamed x31 -> x28, local copies, waits for them, and re-layouts: 2.6 us -> 1.92 us
  transfers between devices with their start and end apart: 10 -> 10, of which waited for: 1 -> 2; matrix products, arithmetic and copies ran while one was open for 6% -> 5% of each run, Pallas kernels for 10% -> 10%
where the time goes in v12:
time: 69.8 us; the launch traced here: 69.3 us
  Pallas kernels  38 us (54%)
  starting transfers between devices  24.1 us (35%)
  local copies, waits for them, and re-layouts  2.83 us (4%)
  other arithmetic  2.25 us (3%)
  waiting for transfers between devices  1.93 us (3%)
    ppermute x10, starting transfers between devices, from_behind(): return lax.ppermute(block, axis, route)  24.1 us
    pallas_call x1, Pallas kernels, mix_react(): pl.pallas_call(kernel, grid_spec=grid_spec, out_shape=jax.ShapeDtypeStruc...  19.7 us
    pallas_call x1, Pallas kernels, migrate(): pl.pallas_call(functools.partial(place_kernel, chunk, peer_count), grid=(...  6.84 us
    pallas_call x1, Pallas kernels, migrate(): pl.pallas_call(functools.partial(halo_kernel, chunk, block_size, peer_cou...  6.17 us
    pallas_call x1, Pallas kernels, migrate(): pl.pallas_call(functools.partial(pick_kernel, chunk), grid=(1,), in_specs...  5.28 us
    ppermute x10, waiting for transfers between devices, from_behind(): return lax.ppermute(block, axis, route)  1.93 us
    unnamed x28, local copies, waits for them, and re-layouts  1.92 us
  transfers between devices with their start and end apart: 10, of which 2 were waited for; matrix products, arithmetic and copies ran while one was open for 5% of the time, Pallas kernels for 10%

profile of v12, /device:TPU:0, one launch (start us, length us, event | category | flops | bytes accessed | tf_op | source)
XLA Modules:
  0.0 69.3 jit_solution(16829452870787911407)
XLA Ops:
  0.0 0.0 copy-start.12
  0.0 0.0 copy-start.11
  0.0 0.0 copy-start.10
  0.0 5.3 %shard_map.127 = (bf16[150,128]{1,0:T(8,128)(2,1)}, bf16[150,128]{1,0:T(8,128)(2,1)}, bf16[150,128]{1,0:T(8,128)(2,1)}, bf16[150,128]{1,0:T(8,128)(2,1)}, bf16[1...) custom-call(bf16[150,8192]{1,0:T(8,128)(2,1)} %mixing_ref.5, ...), custom_call_target="tpu_custom_call" | custom-call | tf_op jit(solution)/shard_map/pallas_call | solution.py:114
  5.3 3.1 %collective-permute-start = (bf16[150,128]{1,0:T(8,128)(2,1)}, bf16[150,128]{1,0:T(8,128)(2,1)S(1)}, u32[]{:S(2)}, u32[]{:S(2)}) collective-permute-start(bf16[150,128]{1,0:T(8,128)(2,1)} %get-tuple-element.15), channel_id=1, source_target_pairs={{124,0},{125,1},{126,2},{127,3},{0,4},{1,5},{2,6},{3,7},{4,8},{5,9... | collective-permute-start | bytes 115208 | tf_op jit(solution)/shard_map/ppermute | solution.py:18
  8.4 0.0 collective-permute-start.1
  8.4 1.0 %collective-permute-start.2 = (bf16[150,128]{1,0:T(8,128)(2,1)}, bf16[150,128]{1,0:T(8,128)(2,1)S(1)}, u32[]{:S(2)}, u32[]{:S(2)}) collective-permute-start(bf16[150,128]{1,0:T(8,128)(2,1)} %get-tuple-element.17), channel_id=1, source_target_pairs={{126,0},{127,1},{0,2},{1,3},{2,4},{3,5},{4,6},{5,7},{6,8},{7,9},{8... | collective-permute-start | bytes 115208 | tf_op jit(solution)/shard_map/ppermute | solution.py:18
  9.4 2.2 %collective-permute-start.3 = (bf16[150,128]{1,0:T(8,128)(2,1)}, bf16[150,128]{1,0:T(8,128)(2,1)S(1)}, u32[]{:S(2)}, u32[]{:S(2)}) collective-permute-start(bf16[150,128]{1,0:T(8,128)(2,1)} %get-tuple-element.18), channel_id=1, source_target_pairs={{127,0},{0,1},{1,2},{2,3},{3,4},{4,5},{5,6},{6,7},{7,8},{8,9},{9,1... | collective-permute-start | bytes 115208 | tf_op jit(solution)/shard_map/ppermute | solution.py:18
  11.6 5.6 %collective-permute-start.4 = (bf16[150,128]{1,0:T(8,128)(2,1)}, bf16[150,128]{1,0:T(8,128)(2,1)S(1)}, u32[]{:S(2)}, u32[]{:S(2)}) collective-permute-start(bf16[150,128]{1,0:T(8,128)(2,1)} %get-tuple-element.19), channel_id=1, source_target_pairs={{1,0},{2,1},{3,2},{4,3},{5,4},{6,5},{7,6},{8,7},{9,8},{10,9},{11,1... | collective-permute-start | bytes 115208 | tf_op jit(solution)/shard_map/ppermute | solution.py:18
  17.2 0.7 %fusion = pred[1,1,8,128]{3,2,1,0:T(8,128)(4,1)S(1)} fusion(s32[8]{0:T(128)} %bitcast.26), kind=kLoop, calls=%fused_computation.4 | loop fusion | flops 1024 | bytes 1056
  17.9 0.3 copy.17
  18.2 0.9 %copy.15 = s32[1024,1]{1,0:T(8,128)S(1)} copy(s32[1024,1]{0,1:T(1,128)} %bitcast.21) | data formatting | bytes 8192 | tf_op jit(solution)/shard_map/squeeze | solution.py:127
  19.1 0.0 collective-permute-done.refs_0_
  19.1 0.0 copy-start.2
  19.1 0.6 collective-permute-start.5
  19.8 0.0 collective-permute-done.1.refs_1_
  19.8 0.0 copy-start.3
  19.8 0.3 collective-permute-start.6
  20.1 0.0 collective-permute-done.2.refs_2_
  20.1 0.0 copy-start.4
  20.1 4.0 %collective-permute-start.7 = (bf16[150,128]{1,0:T(8,128)(2,1)}, bf16[150,128]{1,0:T(8,128)(2,1)S(1)}, u32[]{:S(2)}, u32[]{:S(2)}) collective-permute-start(bf16[150,128]{1,0:T(8,128)(2,1)} %get-tuple-element.22), channel_id=1, source_target_pairs={{4,0},{5,1},{6,2},{7,3},{8,4},{9,5},{10,6},{11,7},{12,8},{13,9},{1... | collective-permute-start | bytes 115208 | tf_op jit(solution)/shard_map/ppermute | solution.py:18
  24.1 0.8 %bitcast_select_fusion.refs_8_ = s32[1024,1]{1,0:T(8,128)} fusion(s32[1024,1]{1,0:T(8,128)S(1)} %copy.15, pred[1,1024]{0,1:T(8,128)(4,1)S(1)} %copy.17), kind=kLoop, calls=%fused_computation | loop fusion | flops 1024 | bytes 9216 | tf_op jit(solution)/shard_map/jit(_where)/select_n | solution.py:127
  24.9 0.0 collective-permute-done.3.refs_3_
  24.9 0.0 copy-start.5
  24.9 0.0 collective-permute-done.4.refs_4_
  24.9 0.0 copy-start.6
  24.9 0.0 collective-permute-done.5.refs_5_
  25.0 0.0 copy-start.7
  25.0 0.0 collective-permute-done.6.refs_6_
  25.0 0.0 copy-start.8
  25.0 1.3 %collective-permute-done.7.refs_7_ = bf16[150,128]{1,0:T(8,128)(2,1)S(1)} collective-permute-done((bf16[150,128]{1,0:T(8,128)(2,1)}, bf16[150,128]{1,0:T(8,128)(2,1)S(1)}, u32[]{:S(2)}, u32[]{:S(2)}) %collective-permute-start.7) | collective-permute-done | bytes 38432 | tf_op jit(solution)/shard_map/ppermute | solution.py:18
  26.3 0.0 copy-start.9
  26.3 0.0 copy-done.2
  26.3 0.0 copy-done.3
  26.3 0.0 copy-done.4
  26.3 0.0 copy-done.5
  26.3 0.0 copy-done.6
  26.3 0.0 copy-done.7
  26.3 0.0 copy-done.8
  26.3 0.6 copy-done.9
  26.9 6.2 %shard_map.129 = (bf16[150,2048]{1,0:T(8,128)(2,1)}, bf16[150,2048]{1,0:T(8,128)(2,1)}) custom-call(s32[2,16]{1,0:T(2,128)} %bitcast.24, bf16[150,8192]{1,0:T(8,128)(2,1)} %mixing_ref.5, bf16[150,128]{1,0:T(8,128)(2,1)} %copy-done.2, bf16[150,128]{1,0:T(8,128)(2,1)} %copy-done.3, bf16[150,128]{1,0:T(8,128)(2,1)} %copy-done.4, bf16[150,128]{1,0:T(8,128)(2,1)} %copy-done.5, ...), custom_call_target="tpu_custom_call" | custom-call | tf_op jit(solution)/shard_map/pallas_call | solution.py:139
  33.1 0.2 collective-permute-start.8
  33.2 7.1 %collective-permute-start.9 = (bf16[150,2048]{1,0:T(8,128)(2,1)}, bf16[150,2048]{1,0:T(8,128)(2,1)S(1)}, u32[]{:S(2)}, u32[]{:S(2)}) collective-permute-start(bf16[150,2048]{1,0:T(8,128)(2,1)} %get-tuple-element.24), channel_id=1, source_target_pairs={{1,0},{2,1},{3,2},{4,3},{5,4},{6,5},{7,6},{8,7},{9,8},{10,9},{11,1... | collective-permute-start | bytes 1843208 | tf_op jit(solution)/shard_map/ppermute | solution.py:18
  40.3 0.0 copy-done.12
  40.3 0.0 copy-done.11
  40.3 0.0 copy-done.10
  40.3 0.7 pad_maximum_fusion.order_ref
  41.0 6.8 %shard_map.128.own_ref.migrated_hbm = bf16[150,8192]{1,0:T(8,128)(2,1)} custom-call(bf16[150,8192]{1,0:T(8,128)(2,1)} %mixing_ref.5, bf16[150,128]{1,0:T(8,128)(2,1)} %copy-done.2, bf16[150,128]{1,0:T(8,128)(2,1)} %copy-done.3, bf16[150,128]{1,0:T(8,128)(2,1)} %copy-done.4, bf16[150,128]{1,0:T(8,128)(2,1)} %copy-done.5, bf16[150,128]{1,0:T(8,128)(2,1)} %copy-done.6, ...), custom_call_target="tpu_custom_call" | custom-call | tf_op jit(solution)/shard_map/pallas_call | solution.py:144
  47.9 0.6 collective-permute-done.8.lower_hbm
  48.5 0.0 copy-start
  48.5 0.0 collective-permute-done.9.upper_hbm
  48.5 0.0 copy-start.1
  48.5 0.8 %copy-done = bf16[150,2048]{1,0:T(8,128)(2,1)} copy-done((bf16[150,2048]{1,0:T(8,128)(2,1)}, bf16[150,2048]{1,0:T(8,128)(2,1)S(1)}, u32[]{:S(2)}) %copy-start) | copy-done | bytes 614424
  49.3 0.2 copy-done.1
  49.5 19.7 %shard_map.130 = f32[150,8192]{1,0:T(8,128)} custom-call(s32[3,64]{1,0:T(4,128)} %bitcast.23, bf16[150,8192]{1,0:T(8,128)(2,1)} %shard_map.128.own_ref.migrated_hbm, bf16[64,4,128,128]{3,2,1,0:T(8,128)(2,1)} %weight_ref.1, f32[1,8192]{1,0:T(1,128)} %bitcast.18, f32[152,256]{1,0:T(8,128)} %pad_maximum_fusion.order_ref, f32[150,256]{1,0:T(8,128)} %prod_ref.1, ...), custom_call_target="tpu_custom_call" | custom-call | tf_op jit(solution)/shard_map/pallas_call | solution.py:340
  (2 shorter events, 0.0 us)
Async XLA Ops:
  0.0 40.3 %copy-start.12 = (f32[256]{0:T(256)S(1)}, f32[256]{0:T(256)}, u32[]{:S(2)}) copy-start(f32[256]{0:T(256)} %param.23) | copy-start | bytes 3076
  0.0 40.3 %copy-start.11 = (f32[256]{0:T(256)S(1)}, f32[256]{0:T(256)}, u32[]{:S(2)}) copy-start(f32[256]{0:T(256)} %param.22) | copy-start | bytes 3076
  0.0 40.3 %copy-start.10 = (f32[256,150]{0,1:T(8,128)S(1)}, f32[256,150]{0,1:T(8,128)}, u32[]{:S(2)}) copy-start(f32[256,150]{0,1:T(8,128)} %param.21) | copy-start | bytes 460804
  5.3 13.8 %collective-permute-start = (bf16[150,128]{1,0:T(8,128)(2,1)}, bf16[150,128]{1,0:T(8,128)(2,1)S(1)}, u32[]{:S(2)}, u32[]{:S(2)}) collective-permute-start(bf16[150,128]{1,0:T(8,128)(2,1)} %get-tuple-element.15), channel_id=1, source_target_pairs={{124,0},{125,1},{126,2},{127,3},{0,4},{1,5},{2,6},{3,7},{4,8},{5,9... | collective-permute-start | bytes 115208 | tf_op jit(solution)/shard_map/ppermute | solution.py:18
  8.4 11.4 %collective-permute-start.1 = (bf16[150,128]{1,0:T(8,128)(2,1)}, bf16[150,128]{1,0:T(8,128)(2,1)S(1)}, u32[]{:S(2)}, u32[]{:S(2)}) collective-permute-start(bf16[150,128]{1,0:T(8,128)(2,1)} %get-tuple-element.16), channel_id=1, source_target_pairs={{125,0},{126,1},{127,2},{0,3},{1,4},{2,5},{3,6},{4,7},{5,8},{6,9},... | collective-permute-start | bytes 115208 | tf_op jit(solution)/shard_map/ppermute | solution.py:18
  8.4 11.7 %collective-permute-start.2 = (bf16[150,128]{1,0:T(8,128)(2,1)}, bf16[150,128]{1,0:T(8,128)(2,1)S(1)}, u32[]{:S(2)}, u32[]{:S(2)}) collective-permute-start(bf16[150,128]{1,0:T(8,128)(2,1)} %get-tuple-element.17), channel_id=1, source_target_pairs={{126,0},{127,1},{0,2},{1,3},{2,4},{3,5},{4,6},{5,7},{6,8},{7,9},{8... | collective-permute-start | bytes 115208 | tf_op jit(solution)/shard_map/ppermute | solution.py:18
  9.4 15.5 %collective-permute-start.3 = (bf16[150,128]{1,0:T(8,128)(2,1)}, bf16[150,128]{1,0:T(8,128)(2,1)S(1)}, u32[]{:S(2)}, u32[]{:S(2)}) collective-permute-start(bf16[150,128]{1,0:T(8,128)(2,1)} %get-tuple-element.18), channel_id=1, source_target_pairs={{127,0},{0,1},{1,2},{2,3},{3,4},{4,5},{5,6},{6,7},{7,8},{8,9},{9,1... | collective-permute-start | bytes 115208 | tf_op jit(solution)/shard_map/ppermute | solution.py:18
  11.6 13.3 %collective-permute-start.4 = (bf16[150,128]{1,0:T(8,128)(2,1)}, bf16[150,128]{1,0:T(8,128)(2,1)S(1)}, u32[]{:S(2)}, u32[]{:S(2)}) collective-permute-start(bf16[150,128]{1,0:T(8,128)(2,1)} %get-tuple-element.19), channel_id=1, source_target_pairs={{1,0},{2,1},{3,2},{4,3},{5,4},{6,5},{7,6},{8,7},{9,8},{10,9},{11,1... | collective-permute-start | bytes 115208 | tf_op jit(solution)/shard_map/ppermute | solution.py:18
  19.1 7.2 %copy-start.2 = (bf16[150,128]{1,0:T(8,128)(2,1)}, bf16[150,128]{1,0:T(8,128)(2,1)S(1)}, u32[]{:S(2)}) copy-start(bf16[150,128]{1,0:T(8,128)(2,1)S(1)} %collective-permute-done.refs_0_) | copy-start | bytes 115204
  19.1 5.8 %collective-permute-start.5 = (bf16[150,128]{1,0:T(8,128)(2,1)}, bf16[150,128]{1,0:T(8,128)(2,1)S(1)}, u32[]{:S(2)}, u32[]{:S(2)}) collective-permute-start(bf16[150,128]{1,0:T(8,128)(2,1)} %get-tuple-element.20), channel_id=1, source_target_pairs={{2,0},{3,1},{4,2},{5,3},{6,4},{7,5},{8,6},{9,7},{10,8},{11,9},{12,... | collective-permute-start | bytes 115208 | tf_op jit(solution)/shard_map/ppermute | solution.py:18
  19.8 6.5 %copy-start.3 = (bf16[150,128]{1,0:T(8,128)(2,1)}, bf16[150,128]{1,0:T(8,128)(2,1)S(1)}, u32[]{:S(2)}) copy-start(bf16[150,128]{1,0:T(8,128)(2,1)S(1)} %collective-permute-done.1.refs_1_) | copy-start | bytes 115204
  19.8 5.2 %collective-permute-start.6 = (bf16[150,128]{1,0:T(8,128)(2,1)}, bf16[150,128]{1,0:T(8,128)(2,1)S(1)}, u32[]{:S(2)}, u32[]{:S(2)}) collective-permute-start(bf16[150,128]{1,0:T(8,128)(2,1)} %get-tuple-element.21), channel_id=1, source_target_pairs={{3,0},{4,1},{5,2},{6,3},{7,4},{8,5},{9,6},{10,7},{11,8},{12,9},{13... | collective-permute-start | bytes 115208 | tf_op jit(solution)/shard_map/ppermute | solution.py:18
  20.1 6.2 %copy-start.4 = (bf16[150,128]{1,0:T(8,128)(2,1)}, bf16[150,128]{1,0:T(8,128)(2,1)S(1)}, u32[]{:S(2)}) copy-start(bf16[150,128]{1,0:T(8,128)(2,1)S(1)} %collective-permute-done.2.refs_2_) | copy-start | bytes 115204
  20.1 6.2 %collective-permute-start.7 = (bf16[150,128]{1,0:T(8,128)(2,1)}, bf16[150,128]{1,0:T(8,128)(2,1)S(1)}, u32[]{:S(2)}, u32[]{:S(2)}) collective-permute-start(bf16[150,128]{1,0:T(8,128)(2,1)} %get-tuple-element.22), channel_id=1, source_target_pairs={{4,0},{5,1},{6,2},{7,3},{8,4},{9,5},{10,6},{11,7},{12,8},{13,9},{1... | collective-permute-start | bytes 115208 | tf_op jit(solution)/shard_map/ppermute | solution.py:18
  24.9 1.4 %copy-start.5 = (bf16[150,128]{1,0:T(8,128)(2,1)}, bf16[150,128]{1,0:T(8,128)(2,1)S(1)}, u32[]{:S(2)}) copy-start(bf16[150,128]{1,0:T(8,128)(2,1)S(1)} %collective-permute-done.3.refs_3_) | copy-start | bytes 115204
  24.9 1.4 %copy-start.6 = (bf16[150,128]{1,0:T(8,128)(2,1)}, bf16[150,128]{1,0:T(8,128)(2,1)S(1)}, u32[]{:S(2)}) copy-start(bf16[150,128]{1,0:T(8,128)(2,1)S(1)} %collective-permute-done.4.refs_4_) | copy-start | bytes 115204
  25.0 1.4 %copy-start.7 = (bf16[150,128]{1,0:T(8,128)(2,1)}, bf16[150,128]{1,0:T(8,128)(2,1)S(1)}, u32[]{:S(2)}) copy-start(bf16[150,128]{1,0:T(8,128)(2,1)S(1)} %collective-permute-done.5.refs_5_) | copy-start | bytes 115204
  25.0 1.4 %copy-start.8 = (bf16[150,128]{1,0:T(8,128)(2,1)}, bf16[150,128]{1,0:T(8,128)(2,1)S(1)}, u32[]{:S(2)}) copy-start(bf16[150,128]{1,0:T(8,128)(2,1)S(1)} %collective-permute-done.6.refs_6_) | copy-start | bytes 115204
  26.3 0.6 copy-start.9
  33.1 15.4 %collective-permute-start.8 = (bf16[150,2048]{1,0:T(8,128)(2,1)}, bf16[150,2048]{1,0:T(8,128)(2,1)S(1)}, u32[]{:S(2)}, u32[]{:S(2)}) collective-permute-start(bf16[150,2048]{1,0:T(8,128)(2,1)} %get-tuple-element.23), channel_id=1, source_target_pairs={{127,0},{0,1},{1,2},{2,3},{3,4},{4,5},{5,6},{6,7},{7,8},{8,9},{9,1... | collective-permute-start | bytes 1843208 | tf_op jit(solution)/shard_map/ppermute | solution.py:18
  33.2 15.2 %collective-permute-start.9 = (bf16[150,2048]{1,0:T(8,128)(2,1)}, bf16[150,2048]{1,0:T(8,128)(2,1)S(1)}, u32[]{:S(2)}, u32[]{:S(2)}) collective-permute-start(bf16[150,2048]{1,0:T(8,128)(2,1)} %get-tuple-element.24), channel_id=1, source_target_pairs={{1,0},{2,1},{3,2},{4,3},{5,4},{6,5},{7,6},{8,7},{9,8},{10,9},{11,1... | collective-permute-start | bytes 1843208 | tf_op jit(solution)/shard_map/ppermute | solution.py:18
  48.5 0.8 %copy-start = (bf16[150,2048]{1,0:T(8,128)(2,1)}, bf16[150,2048]{1,0:T(8,128)(2,1)S(1)}, u32[]{:S(2)}) copy-start(bf16[150,2048]{1,0:T(8,128)(2,1)S(1)} %collective-permute-done.8.lower_hbm) | copy-start | bytes 1843204
  48.5 1.0 %copy-start.1 = (bf16[150,2048]{1,0:T(8,128)(2,1)}, bf16[150,2048]{1,0:T(8,128)(2,1)S(1)}, u32[]{:S(2)}) copy-start(bf16[150,2048]{1,0:T(8,128)(2,1)S(1)} %collective-permute-done.9.upper_hbm) | copy-start | bytes 1843204

commit v13 on v12

--- a/solution.py
+++ b/solution.py
@@ -150,6 +150,7 @@
         out_specs=vmem_whole(mixing_ratio.shape),
         out_shape=jax.ShapeDtypeStruct(mixing_ratio.shape, mixing_ratio.dtype),
     )(mixing_ratio, *arrived, slots)
+    to_lower, to_upper, migrated = lax.optimization_barrier((to_lower, to_upper, migrated))
     from_lower = from_behind(to_upper, "region", 1)
     from_upper = from_behind(to_lower, "region", -1)
     return migrated, from_lower, from_upper

time: 69.8 us -> 76.6 us (1.097)
  waiting for transfers between devices: 1.93 us -> 8.77 us
    ppermute x10, waiting for transfers between devices: 1.93 us -> 8.77 us  [from_behind(): return lax.ppermute(block, axis, route)]
  transfers between devices with their start and end apart: 10 -> 10, of which waited for: 2 -> 2; matrix products, arithmetic and copies ran while one was open for 5% -> 5% of each run, Pallas kernels for 10% -> 0%
where the time goes in v13:
time: 76.6 us; the launch traced here: 76.1 us
  Pallas kernels  37.9 us (49%)
  starting transfers between devices  24.1 us (31%)
  waiting for transfers between devices  8.77 us (11%)
  local copies, waits for them, and re-layouts  2.87 us (4%)
  other arithmetic  2.25 us (3%)
    ppermute x10, starting transfers between devices, from_behind(): return lax.ppermute(block, axis, route)  24.1 us
    pallas_call x1, Pallas kernels, mix_react(): pl.pallas_call(kernel, grid_spec=grid_spec, out_shape=jax.ShapeDtypeStruc...  19.7 us
    ppermute x10, waiting for transfers between devices, from_behind(): return lax.ppermute(block, axis, route)  8.77 us
    pallas_call x1, Pallas kernels, migrate(): pl.pallas_call(functools.partial(place_kernel, chunk, peer_count), grid=(...  6.84 us
    pallas_call x1, Pallas kernels, migrate(): pl.pallas_call(functools.partial(halo_kernel, chunk, block_size, peer_cou...  6.17 us
    pallas_call x1, Pallas kernels, migrate(): pl.pallas_call(functools.partial(pick_kernel, chunk), grid=(1,), in_specs...  5.26 us
    unnamed x28, local copies, waits for them, and re-layouts  1.97 us
  transfers between devices with their start and end apart: 10, of which 2 were waited for; matrix products, arithmetic and copies ran while one was open for 5% of the time, Pallas kernels for 0%

profile of v13, /device:TPU:0, one launch (start us, length us, event | category | flops | bytes accessed | tf_op | source)
XLA Modules:
  0.0 76.1 jit_solution(7856948849128294817)
XLA Ops:
  0.0 5.3 %shard_map.127 = (bf16[150,128]{1,0:T(8,128)(2,1)}, bf16[150,128]{1,0:T(8,128)(2,1)}, bf16[150,128]{1,0:T(8,128)(2,1)}, bf16[150,128]{1,0:T(8,128)(2,1)}, bf16[1...) custom-call(bf16[150,8192]{1,0:T(8,128)(2,1)} %mixing_ref.5, ...), custom_call_target="tpu_custom_call" | custom-call | tf_op jit(solution)/shard_map/pallas_call | solution.py:114
  5.3 3.1 %collective-permute-start = (bf16[150,128]{1,0:T(8,128)(2,1)}, bf16[150,128]{1,0:T(8,128)(2,1)S(1)}, u32[]{:S(2)}, u32[]{:S(2)}) collective-permute-start(bf16[150,128]{1,0:T(8,128)(2,1)} %get-tuple-element.18), channel_id=1, source_target_pairs={{124,0},{125,1},{126,2},{127,3},{0,4},{1,5},{2,6},{3,7},{4,8},{5,9... | collective-permute-start | bytes 115208 | tf_op jit(solution)/shard_map/ppermute | solution.py:18
  8.4 0.0 collective-permute-start.1
  8.4 1.0 %collective-permute-start.2 = (bf16[150,128]{1,0:T(8,128)(2,1)}, bf16[150,128]{1,0:T(8,128)(2,1)S(1)}, u32[]{:S(2)}, u32[]{:S(2)}) collective-permute-start(bf16[150,128]{1,0:T(8,128)(2,1)} %get-tuple-element.20), channel_id=1, source_target_pairs={{126,0},{127,1},{0,2},{1,3},{2,4},{3,5},{4,6},{5,7},{6,8},{7,9},{8... | collective-permute-start | bytes 115208 | tf_op jit(solution)/shard_map/ppermute | solution.py:18
  9.3 2.2 %collective-permute-start.3 = (bf16[150,128]{1,0:T(8,128)(2,1)}, bf16[150,128]{1,0:T(8,128)(2,1)S(1)}, u32[]{:S(2)}, u32[]{:S(2)}) collective-permute-start(bf16[150,128]{1,0:T(8,128)(2,1)} %get-tuple-element.21), channel_id=1, source_target_pairs={{127,0},{0,1},{1,2},{2,3},{3,4},{4,5},{5,6},{6,7},{7,8},{8,9},{9,1... | collective-permute-start | bytes 115208 | tf_op jit(solution)/shard_map/ppermute | solution.py:18
  11.6 5.6 %collective-permute-start.4 = (bf16[150,128]{1,0:T(8,128)(2,1)}, bf16[150,128]{1,0:T(8,128)(2,1)S(1)}, u32[]{:S(2)}, u32[]{:S(2)}) collective-permute-start(bf16[150,128]{1,0:T(8,128)(2,1)} %get-tuple-element.22), channel_id=1, source_target_pairs={{1,0},{2,1},{3,2},{4,3},{5,4},{6,5},{7,6},{8,7},{9,8},{10,9},{11,1... | collective-permute-start | bytes 115208 | tf_op jit(solution)/shard_map/ppermute | solution.py:18
  17.1 0.7 fusion
  17.9 0.3 copy.17
  18.2 0.9 %copy.15 = s32[1024,1]{1,0:T(8,128)S(1)} copy(s32[1024,1]{0,1:T(1,128)} %bitcast.21) | data formatting | bytes 8192 | tf_op jit(solution)/shard_map/squeeze | solution.py:127
  19.1 0.0 collective-permute-done.refs_0_
  19.1 0.0 copy-start.2
  19.1 0.6 collective-permute-start.5
  19.7 0.0 collective-permute-done.1.refs_1_
  19.7 0.0 copy-start.3
  19.7 0.3 collective-permute-start.6
  20.0 0.0 collective-permute-done.2.refs_2_
  20.0 0.0 copy-start.4
  20.0 0.0 copy-start.12
  20.1 0.0 copy-start.10
  20.1 0.0 copy-start.11
  20.1 4.1 %collective-permute-start.7 = (bf16[150,128]{1,0:T(8,128)(2,1)}, bf16[150,128]{1,0:T(8,128)(2,1)S(1)}, u32[]{:S(2)}, u32[]{:S(2)}) collective-permute-start(bf16[150,128]{1,0:T(8,128)(2,1)} %get-tuple-element.25), channel_id=1, source_target_pairs={{4,0},{5,1},{6,2},{7,3},{8,4},{9,5},{10,6},{11,7},{12,8},{13,9},{1... | collective-permute-start | bytes 115208 | tf_op jit(solution)/shard_map/ppermute | solution.py:18
  24.1 0.8 %bitcast_select_fusion.refs_8_ = s32[1024,1]{1,0:T(8,128)} fusion(s32[1024,1]{1,0:T(8,128)S(1)} %copy.15, pred[1,1024]{0,1:T(8,128)(4,1)S(1)} %copy.17), kind=kLoop, calls=%fused_computation | loop fusion | flops 1024 | bytes 9216 | tf_op jit(solution)/shard_map/jit(_where)/select_n | solution.py:127
  25.0 0.0 collective-permute-done.3.refs_3_
  25.0 0.0 copy-start.5
  25.0 0.0 collective-permute-done.4.refs_4_
  25.0 0.0 copy-start.6
  25.0 0.0 collective-permute-done.5.refs_5_
  25.0 0.0 copy-start.7
  25.0 0.0 collective-permute-done.6.refs_6_
  25.0 0.0 copy-start.8
  25.0 1.3 %collective-permute-done.7.refs_7_ = bf16[150,128]{1,0:T(8,128)(2,1)S(1)} collective-permute-done((bf16[150,128]{1,0:T(8,128)(2,1)}, bf16[150,128]{1,0:T(8,128)(2,1)S(1)}, u32[]{:S(2)}, u32[]{:S(2)}) %collective-permute-start.7) | collective-permute-done | bytes 38432 | tf_op jit(solution)/shard_map/ppermute | solution.py:18
  26.3 0.0 copy-done.2
  26.3 0.0 copy-done.3
  26.3 0.0 copy-done.4
  26.4 0.0 copy-done.5
  26.4 0.0 copy-done.6
  26.4 0.0 copy-done.7
  26.4 0.0 copy-done.8
  26.4 0.0 copy-start.9
  26.4 0.6 copy-done.9
  27.0 6.8 %shard_map.129.own_ref.migrated_hbm = bf16[150,8192]{1,0:T(8,128)(2,1)} custom-call(bf16[150,8192]{1,0:T(8,128)(2,1)} %mixing_ref.5, bf16[150,128]{1,0:T(8,128)(2,1)} %copy-done.2, bf16[150,128]{1,0:T(8,128)(2,1)} %copy-done.3, bf16[150,128]{1,0:T(8,128)(2,1)} %copy-done.4, bf16[150,128]{1,0:T(8,128)(2,1)} %copy-done.5, bf16[150,128]{1,0:T(8,128)(2,1)} %copy-done.6, ...), custom_call_target="tpu_custom_call" | custom-call | tf_op jit(solution)/shard_map/pallas_call | solution.py:144
  33.8 6.2 %shard_map.128 = (bf16[150,2048]{1,0:T(8,128)(2,1)}, bf16[150,2048]{1,0:T(8,128)(2,1)}) custom-call(s32[2,16]{1,0:T(2,128)} %bitcast.24, bf16[150,8192]{1,0:T(8,128)(2,1)} %mixing_ref.5, bf16[150,128]{1,0:T(8,128)(2,1)} %copy-done.2, bf16[150,128]{1,0:T(8,128)(2,1)} %copy-done.3, bf16[150,128]{1,0:T(8,128)(2,1)} %copy-done.4, bf16[150,128]{1,0:T(8,128)(2,1)} %copy-done.5, ...), custom_call_target="tpu_custom_call" | custom-call | tf_op jit(solution)/shard_map/pallas_call | solution.py:139
  40.0 0.3 collective-permute-start.8
  40.3 7.0 %collective-permute-start.9 = (bf16[150,2048]{1,0:T(8,128)(2,1)}, bf16[150,2048]{1,0:T(8,128)(2,1)S(1)}, u32[]{:S(2)}, u32[]{:S(2)}) collective-permute-start(bf16[150,2048]{1,0:T(8,128)(2,1)} %get-tuple-element.30), channel_id=1, source_target_pairs={{1,0},{2,1},{3,2},{4,3},{5,4},{6,5},{7,6},{8,7},{9,8},{10,9},{11,1... | collective-permute-start | bytes 1843208 | tf_op jit(solution)/shard_map/ppermute | solution.py:18
  47.3 0.0 copy-done.12
  47.3 0.0 copy-done.10
  47.3 0.0 copy-done.11
  47.3 0.7 pad_maximum_fusion.order_ref
  47.9 7.4 %collective-permute-done.8.lower_hbm = bf16[150,2048]{1,0:T(8,128)(2,1)S(1)} collective-permute-done((bf16[150,2048]{1,0:T(8,128)(2,1)}, bf16[150,2048]{1,0:T(8,128)(2,1)S(1)}, u32[]{:S(2)}, u32[]{:S(2)}) %collective-permute-start.8) | collective-permute-done | bytes 614432 | tf_op jit(solution)/shard_map/ppermute | solution.py:18
  55.4 0.0 copy-start
  55.4 0.0 collective-permute-done.9.upper_hbm
  55.4 0.0 copy-start.1
  55.4 0.8 %copy-done = bf16[150,2048]{1,0:T(8,128)(2,1)} copy-done((bf16[150,2048]{1,0:T(8,128)(2,1)}, bf16[150,2048]{1,0:T(8,128)(2,1)S(1)}, u32[]{:S(2)}) %copy-start) | copy-done | bytes 614424
  56.2 0.2 copy-done.1
  56.4 19.7 %shard_map.130 = f32[150,8192]{1,0:T(8,128)} custom-call(s32[3,64]{1,0:T(4,128)} %bitcast.23, bf16[150,8192]{1,0:T(8,128)(2,1)} %shard_map.129.own_ref.migrated_hbm, bf16[64,4,128,128]{3,2,1,0:T(8,128)(2,1)} %weight_ref.1, f32[1,8192]{1,0:T(1,128)} %bitcast.18, f32[152,256]{1,0:T(8,128)} %pad_maximum_fusion.order_ref, f32[150,256]{1,0:T(8,128)} %prod_ref.1, ...), custom_call_target="tpu_custom_call" | custom-call | tf_op jit(solution)/shard_map/pallas_call | solution.py:341
  (2 shorter events, 0.0 us)
Async XLA Ops:
  5.3 13.8 %collective-permute-start = (bf16[150,128]{1,0:T(8,128)(2,1)}, bf16[150,128]{1,0:T(8,128)(2,1)S(1)}, u32[]{:S(2)}, u32[]{:S(2)}) collective-permute-start(bf16[150,128]{1,0:T(8,128)(2,1)} %get-tuple-element.18), channel_id=1, source_target_pairs={{124,0},{125,1},{126,2},{127,3},{0,4},{1,5},{2,6},{3,7},{4,8},{5,9... | collective-permute-start | bytes 115208 | tf_op jit(solution)/shard_map/ppermute | solution.py:18
  8.4 11.4 %collective-permute-start.1 = (bf16[150,128]{1,0:T(8,128)(2,1)}, bf16[150,128]{1,0:T(8,128)(2,1)S(1)}, u32[]{:S(2)}, u32[]{:S(2)}) collective-permute-start(bf16[150,128]{1,0:T(8,128)(2,1)} %get-tuple-element.19), channel_id=1, source_target_pairs={{125,0},{126,1},{127,2},{0,3},{1,4},{2,5},{3,6},{4,7},{5,8},{6,9},... | collective-permute-start | bytes 115208 | tf_op jit(solution)/shard_map/ppermute | solution.py:18
  8.4 11.7 %collective-permute-start.2 = (bf16[150,128]{1,0:T(8,128)(2,1)}, bf16[150,128]{1,0:T(8,128)(2,1)S(1)}, u32[]{:S(2)}, u32[]{:S(2)}) collective-permute-start(bf16[150,128]{1,0:T(8,128)(2,1)} %get-tuple-element.20), channel_id=1, source_target_pairs={{126,0},{127,1},{0,2},{1,3},{2,4},{3,5},{4,6},{5,7},{6,8},{7,9},{8... | collective-permute-start | bytes 115208 | tf_op jit(solution)/shard_map/ppermute | solution.py:18
  9.3 15.6 %collective-permute-start.3 = (bf16[150,128]{1,0:T(8,128)(2,1)}, bf16[150,128]{1,0:T(8,128)(2,1)S(1)}, u32[]{:S(2)}, u32[]{:S(2)}) collective-permute-start(bf16[150,128]{1,0:T(8,128)(2,1)} %get-tuple-element.21), channel_id=1, source_target_pairs={{127,0},{0,1},{1,2},{2,3},{3,4},{4,5},{5,6},{6,7},{7,8},{8,9},{9,1... | collective-permute-start | bytes 115208 | tf_op jit(solution)/shard_map/ppermute | solution.py:18
  11.6 13.4 %collective-permute-start.4 = (bf16[150,128]{1,0:T(8,128)(2,1)}, bf16[150,128]{1,0:T(8,128)(2,1)S(1)}, u32[]{:S(2)}, u32[]{:S(2)}) collective-permute-start(bf16[150,128]{1,0:T(8,128)(2,1)} %get-tuple-element.22), channel_id=1, source_target_pairs={{1,0},{2,1},{3,2},{4,3},{5,4},{6,5},{7,6},{8,7},{9,8},{10,9},{11,1... | collective-permute-start | bytes 115208 | tf_op jit(solution)/shard_map/ppermute | solution.py:18
  19.1 7.3 %copy-start.2 = (bf16[150,128]{1,0:T(8,128)(2,1)}, bf16[150,128]{1,0:T(8,128)(2,1)S(1)}, u32[]{:S(2)}) copy-start(bf16[150,128]{1,0:T(8,128)(2,1)S(1)} %collective-permute-done.refs_0_) | copy-start | bytes 115204
  19.1 5.9 %collective-permute-start.5 = (bf16[150,128]{1,0:T(8,128)(2,1)}, bf16[150,128]{1,0:T(8,128)(2,1)S(1)}, u32[]{:S(2)}, u32[]{:S(2)}) collective-permute-start(bf16[150,128]{1,0:T(8,128)(2,1)} %get-tuple-element.23), channel_id=1, source_target_pairs={{2,0},{3,1},{4,2},{5,3},{6,4},{7,5},{8,6},{9,7},{10,8},{11,9},{12,... | collective-permute-start | bytes 115208 | tf_op jit(solution)/shard_map/ppermute | solution.py:18
  19.7 6.6 %copy-start.3 = (bf16[150,128]{1,0:T(8,128)(2,1)}, bf16[150,128]{1,0:T(8,128)(2,1)S(1)}, u32[]{:S(2)}) copy-start(bf16[150,128]{1,0:T(8,128)(2,1)S(1)} %collective-permute-done.1.refs_1_) | copy-start | bytes 115204
  19.7 5.3 %collective-permute-start.6 = (bf16[150,128]{1,0:T(8,128)(2,1)}, bf16[150,128]{1,0:T(8,128)(2,1)S(1)}, u32[]{:S(2)}, u32[]{:S(2)}) collective-permute-start(bf16[150,128]{1,0:T(8,128)(2,1)} %get-tuple-element.24), channel_id=1, source_target_pairs={{3,0},{4,1},{5,2},{6,3},{7,4},{8,5},{9,6},{10,7},{11,8},{12,9},{13... | collective-permute-start | bytes 115208 | tf_op jit(solution)/shard_map/ppermute | solution.py:18
  20.0 6.3 %copy-start.4 = (bf16[150,128]{1,0:T(8,128)(2,1)}, bf16[150,128]{1,0:T(8,128)(2,1)S(1)}, u32[]{:S(2)}) copy-start(bf16[150,128]{1,0:T(8,128)(2,1)S(1)} %collective-permute-done.2.refs_2_) | copy-start | bytes 115204
  20.0 27.2 %copy-start.12 = (f32[256]{0:T(256)S(1)}, f32[256]{0:T(256)}, u32[]{:S(2)}) copy-start(f32[256]{0:T(256)} %param.23) | copy-start | bytes 3076
  20.1 27.2 %copy-start.10 = (f32[256,150]{0,1:T(8,128)S(1)}, f32[256,150]{0,1:T(8,128)}, u32[]{:S(2)}) copy-start(f32[256,150]{0,1:T(8,128)} %param.21) | copy-start | bytes 460804
  20.1 27.2 %copy-start.11 = (f32[256]{0:T(256)S(1)}, f32[256]{0:T(256)}, u32[]{:S(2)}) copy-start(f32[256]{0:T(256)} %param.22) | copy-start | bytes 3076
  20.1 6.3 %collective-permute-start.7 = (bf16[150,128]{1,0:T(8,128)(2,1)}, bf16[150,128]{1,0:T(8,128)(2,1)S(1)}, u32[]{:S(2)}, u32[]{:S(2)}) collective-permute-start(bf16[150,128]{1,0:T(8,128)(2,1)} %get-tuple-element.25), channel_id=1, source_target_pairs={{4,0},{5,1},{6,2},{7,3},{8,4},{9,5},{10,6},{11,7},{12,8},{13,9},{1... | collective-permute-start | bytes 115208 | tf_op jit(solution)/shard_map/ppermute | solution.py:18
  25.0 1.4 %copy-start.5 = (bf16[150,128]{1,0:T(8,128)(2,1)}, bf16[150,128]{1,0:T(8,128)(2,1)S(1)}, u32[]{:S(2)}) copy-start(bf16[150,128]{1,0:T(8,128)(2,1)S(1)} %collective-permute-done.3.refs_3_) | copy-start | bytes 115204
  25.0 1.4 %copy-start.6 = (bf16[150,128]{1,0:T(8,128)(2,1)}, bf16[150,128]{1,0:T(8,128)(2,1)S(1)}, u32[]{:S(2)}) copy-start(bf16[150,128]{1,0:T(8,128)(2,1)S(1)} %collective-permute-done.4.refs_4_) | copy-start | bytes 115204
  25.0 1.4 %copy-start.7 = (bf16[150,128]{1,0:T(8,128)(2,1)}, bf16[150,128]{1,0:T(8,128)(2,1)S(1)}, u32[]{:S(2)}) copy-start(bf16[150,128]{1,0:T(8,128)(2,1)S(1)} %collective-permute-done.5.refs_5_) | copy-start | bytes 115204
  25.0 1.4 %copy-start.8 = (bf16[150,128]{1,0:T(8,128)(2,1)}, bf16[150,128]{1,0:T(8,128)(2,1)S(1)}, u32[]{:S(2)}) copy-start(bf16[150,128]{1,0:T(8,128)(2,1)S(1)} %collective-permute-done.6.refs_6_) | copy-start | bytes 115204
  26.4 0.6 copy-start.9
  40.0 15.4 %collective-permute-start.8 = (bf16[150,2048]{1,0:T(8,128)(2,1)}, bf16[150,2048]{1,0:T(8,128)(2,1)S(1)}, u32[]{:S(2)}, u32[]{:S(2)}) collective-permute-start(bf16[150,2048]{1,0:T(8,128)(2,1)} %get-tuple-element.29), channel_id=1, source_target_pairs={{127,0},{0,1},{1,2},{2,3},{3,4},{4,5},{5,6},{6,7},{7,8},{8,9},{9,1... | collective-permute-start | bytes 1843208 | tf_op jit(solution)/shard_map/ppermute | solution.py:18
  40.3 15.1 %collective-permute-start.9 = (bf16[150,2048]{1,0:T(8,128)(2,1)}, bf16[150,2048]{1,0:T(8,128)(2,1)S(1)}, u32[]{:S(2)}, u32[]{:S(2)}) collective-permute-start(bf16[150,2048]{1,0:T(8,128)(2,1)} %get-tuple-element.30), channel_id=1, source_target_pairs={{1,0},{2,1},{3,2},{4,3},{5,4},{6,5},{7,6},{8,7},{9,8},{10,9},{11,1... | collective-permute-start | bytes 1843208 | tf_op jit(solution)/shard_map/ppermute | solution.py:18
  55.4 0.8 %copy-start = (bf16[150,2048]{1,0:T(8,128)(2,1)}, bf16[150,2048]{1,0:T(8,128)(2,1)S(1)}, u32[]{:S(2)}) copy-start(bf16[150,2048]{1,0:T(8,128)(2,1)S(1)} %collective-permute-done.8.lower_hbm) | copy-start | bytes 1843204
  55.4 1.0 %copy-start.1 = (bf16[150,2048]{1,0:T(8,128)(2,1)}, bf16[150,2048]{1,0:T(8,128)(2,1)S(1)}, u32[]{:S(2)}) copy-start(bf16[150,2048]{1,0:T(8,128)(2,1)S(1)} %collective-permute-done.9.upper_hbm) | copy-start | bytes 1843204

commit v14 on v12

--- a/solution.py
+++ b/solution.py
@@ -8,7 +8,7 @@
 from jax.sharding import PartitionSpec as P
 
 HOP = 4
-TILE_BLOCKS = 8
+TILE_BLOCKS = 16
 PAD_ROWS = 160
 
 

time: 69.8 us -> 69.4 us (level)
  no operation moved by 1% of the time
where the time goes in v14:
time: 69.4 us; the launch traced here: 68.9 us
  Pallas kernels  37.5 us (54%)
  starting transfers between devices  24.1 us (35%)
  local copies, waits for them, and re-layouts  2.83 us (4%)
  other arithmetic  2.25 us (3%)
  waiting for transfers between devices  1.93 us (3%)
    ppermute x10, starting transfers between devices, from_behind(): return lax.ppermute(block, axis, route)  24.1 us
    pallas_call x1, Pallas kernels, mix_react(): pl.pallas_call(kernel, grid_spec=grid_spec, out_shape=jax.ShapeDtypeStruc...  19.2 us
    pallas_call x1, Pallas kernels, migrate(): pl.pallas_call(functools.partial(place_kernel, chunk, peer_count), grid=(...  6.84 us
    pallas_call x1, Pallas kernels, migrate(): pl.pallas_call(functools.partial(halo_kernel, chunk, block_size, peer_cou...  6.17 us
    pallas_call x1, Pallas kernels, migrate(): pl.pallas_call(functools.partial(pick_kernel, chunk), grid=(1,), in_specs...  5.28 us
    ppermute x10, waiting for transfers between devices, from_behind(): return lax.ppermute(block, axis, route)  1.93 us
    unnamed x28, local copies, waits for them, and re-layouts  1.92 us
  transfers between devices with their start and end apart: 10, of which 2 were waited for; matrix products, arithmetic and copies ran while one was open for 5% of the time, Pallas kernels for 10%

profile of v14, /device:TPU:0, one launch (start us, length us, event | category | flops | bytes accessed | tf_op | source)
XLA Modules:
  0.0 68.9 jit_solution(725916469476104985)
XLA Ops:
  0.0 0.0 copy-start.12
  0.0 0.0 copy-start.11
  0.0 0.0 copy-start.10
  0.0 5.3 %shard_map.127 = (bf16[150,128]{1,0:T(8,128)(2,1)}, bf16[150,128]{1,0:T(8,128)(2,1)}, bf16[150,128]{1,0:T(8,128)(2,1)}, bf16[150,128]{1,0:T(8,128)(2,1)}, bf16[1...) custom-call(bf16[150,8192]{1,0:T(8,128)(2,1)} %mixing_ref.5, ...), custom_call_target="tpu_custom_call" | custom-call | tf_op jit(solution)/shard_map/pallas_call | solution.py:114
  5.3 3.1 %collective-permute-start = (bf16[150,128]{1,0:T(8,128)(2,1)}, bf16[150,128]{1,0:T(8,128)(2,1)S(1)}, u32[]{:S(2)}, u32[]{:S(2)}) collective-permute-start(bf16[150,128]{1,0:T(8,128)(2,1)} %get-tuple-element.15), channel_id=1, source_target_pairs={{124,0},{125,1},{126,2},{127,3},{0,4},{1,5},{2,6},{3,7},{4,8},{5,9... | collective-permute-start | bytes 115208 | tf_op jit(solution)/shard_map/ppermute | solution.py:18
  8.4 0.0 collective-permute-start.1
  8.4 1.0 %collective-permute-start.2 = (bf16[150,128]{1,0:T(8,128)(2,1)}, bf16[150,128]{1,0:T(8,128)(2,1)S(1)}, u32[]{:S(2)}, u32[]{:S(2)}) collective-permute-start(bf16[150,128]{1,0:T(8,128)(2,1)} %get-tuple-element.17), channel_id=1, source_target_pairs={{126,0},{127,1},{0,2},{1,3},{2,4},{3,5},{4,6},{5,7},{6,8},{7,9},{8... | collective-permute-start | bytes 115208 | tf_op jit(solution)/shard_map/ppermute | solution.py:18
  9.4 2.2 %collective-permute-start.3 = (bf16[150,128]{1,0:T(8,128)(2,1)}, bf16[150,128]{1,0:T(8,128)(2,1)S(1)}, u32[]{:S(2)}, u32[]{:S(2)}) collective-permute-start(bf16[150,128]{1,0:T(8,128)(2,1)} %get-tuple-element.18), channel_id=1, source_target_pairs={{127,0},{0,1},{1,2},{2,3},{3,4},{4,5},{5,6},{6,7},{7,8},{8,9},{9,1... | collective-permute-start | bytes 115208 | tf_op jit(solution)/shard_map/ppermute | solution.py:18
  11.6 5.6 %collective-permute-start.4 = (bf16[150,128]{1,0:T(8,128)(2,1)}, bf16[150,128]{1,0:T(8,128)(2,1)S(1)}, u32[]{:S(2)}, u32[]{:S(2)}) collective-permute-start(bf16[150,128]{1,0:T(8,128)(2,1)} %get-tuple-element.19), channel_id=1, source_target_pairs={{1,0},{2,1},{3,2},{4,3},{5,4},{6,5},{7,6},{8,7},{9,8},{10,9},{11,1... | collective-permute-start | bytes 115208 | tf_op jit(solution)/shard_map/ppermute | solution.py:18
  17.2 0.7 %fusion = pred[1,1,8,128]{3,2,1,0:T(8,128)(4,1)S(1)} fusion(s32[8]{0:T(128)} %bitcast.26), kind=kLoop, calls=%fused_computation.4 | loop fusion | flops 1024 | bytes 1056
  17.9 0.3 copy.17
  18.2 0.9 %copy.15 = s32[1024,1]{1,0:T(8,128)S(1)} copy(s32[1024,1]{0,1:T(1,128)} %bitcast.21) | data formatting | bytes 8192 | tf_op jit(solution)/shard_map/squeeze | solution.py:127
  19.1 0.0 collective-permute-done.refs_0_
  19.1 0.0 copy-start.2
  19.1 0.6 collective-permute-start.5
  19.8 0.0 collective-permute-done.1.refs_1_
  19.8 0.0 copy-start.3
  19.8 0.3 collective-permute-start.6
  20.1 0.0 collective-permute-done.2.refs_2_
  20.1 0.0 copy-start.4
  20.1 4.0 %collective-permute-start.7 = (bf16[150,128]{1,0:T(8,128)(2,1)}, bf16[150,128]{1,0:T(8,128)(2,1)S(1)}, u32[]{:S(2)}, u32[]{:S(2)}) collective-permute-start(bf16[150,128]{1,0:T(8,128)(2,1)} %get-tuple-element.22), channel_id=1, source_target_pairs={{4,0},{5,1},{6,2},{7,3},{8,4},{9,5},{10,6},{11,7},{12,8},{13,9},{1... | collective-permute-start | bytes 115208 | tf_op jit(solution)/shard_map/ppermute | solution.py:18
  24.1 0.8 %bitcast_select_fusion.refs_8_ = s32[1024,1]{1,0:T(8,128)} fusion(s32[1024,1]{1,0:T(8,128)S(1)} %copy.15, pred[1,1024]{0,1:T(8,128)(4,1)S(1)} %copy.17), kind=kLoop, calls=%fused_computation | loop fusion | flops 1024 | bytes 9216 | tf_op jit(solution)/shard_map/jit(_where)/select_n | solution.py:127
  24.9 0.0 collective-permute-done.3.refs_3_
  24.9 0.0 copy-start.5
  24.9 0.0 collective-permute-done.4.refs_4_
  24.9 0.0 copy-start.6
  24.9 0.0 collective-permute-done.5.refs_5_
  25.0 0.0 copy-start.7
  25.0 0.0 collective-permute-done.6.refs_6_
  25.0 0.0 copy-start.8
  25.0 1.3 %collective-permute-done.7.refs_7_ = bf16[150,128]{1,0:T(8,128)(2,1)S(1)} collective-permute-done((bf16[150,128]{1,0:T(8,128)(2,1)}, bf16[150,128]{1,0:T(8,128)(2,1)S(1)}, u32[]{:S(2)}, u32[]{:S(2)}) %collective-permute-start.7) | collective-permute-done | bytes 38432 | tf_op jit(solution)/shard_map/ppermute | solution.py:18
  26.3 0.0 copy-start.9
  26.3 0.0 copy-done.2
  26.3 0.0 copy-done.3
  26.3 0.0 copy-done.4
  26.3 0.0 copy-done.5
  26.3 0.0 copy-done.6
  26.3 0.0 copy-done.7
  26.3 0.0 copy-done.8
  26.3 0.6 copy-done.9
  26.9 6.2 %shard_map.129 = (bf16[150,2048]{1,0:T(8,128)(2,1)}, bf16[150,2048]{1,0:T(8,128)(2,1)}) custom-call(s32[2,16]{1,0:T(2,128)} %bitcast.24, bf16[150,8192]{1,0:T(8,128)(2,1)} %mixing_ref.5, bf16[150,128]{1,0:T(8,128)(2,1)} %copy-done.2, bf16[150,128]{1,0:T(8,128)(2,1)} %copy-done.3, bf16[150,128]{1,0:T(8,128)(2,1)} %copy-done.4, bf16[150,128]{1,0:T(8,128)(2,1)} %copy-done.5, ...), custom_call_target="tpu_custom_call" | custom-call | tf_op jit(solution)/shard_map/pallas_call | solution.py:139
  33.1 0.2 collective-permute-start.8
  33.2 7.1 %collective-permute-start.9 = (bf16[150,2048]{1,0:T(8,128)(2,1)}, bf16[150,2048]{1,0:T(8,128)(2,1)S(1)}, u32[]{:S(2)}, u32[]{:S(2)}) collective-permute-start(bf16[150,2048]{1,0:T(8,128)(2,1)} %get-tuple-element.24), channel_id=1, source_target_pairs={{1,0},{2,1},{3,2},{4,3},{5,4},{6,5},{7,6},{8,7},{9,8},{10,9},{11,1... | collective-permute-start | bytes 1843208 | tf_op jit(solution)/shard_map/ppermute | solution.py:18
  40.3 0.0 copy-done.12
  40.3 0.0 copy-done.11
  40.3 0.0 copy-done.10
  40.3 0.7 pad_maximum_fusion.order_ref
  41.0 6.8 %shard_map.128.own_ref.migrated_hbm = bf16[150,8192]{1,0:T(8,128)(2,1)} custom-call(bf16[150,8192]{1,0:T(8,128)(2,1)} %mixing_ref.5, bf16[150,128]{1,0:T(8,128)(2,1)} %copy-done.2, bf16[150,128]{1,0:T(8,128)(2,1)} %copy-done.3, bf16[150,128]{1,0:T(8,128)(2,1)} %copy-done.4, bf16[150,128]{1,0:T(8,128)(2,1)} %copy-done.5, bf16[150,128]{1,0:T(8,128)(2,1)} %copy-done.6, ...), custom_call_target="tpu_custom_call" | custom-call | tf_op jit(solution)/shard_map/pallas_call | solution.py:144
  47.9 0.6 collective-permute-done.8.lower_hbm
  48.5 0.0 copy-start
  48.5 0.0 collective-permute-done.9.upper_hbm
  48.5 0.0 copy-start.1
  48.5 0.8 %copy-done = bf16[150,2048]{1,0:T(8,128)(2,1)} copy-done((bf16[150,2048]{1,0:T(8,128)(2,1)}, bf16[150,2048]{1,0:T(8,128)(2,1)S(1)}, u32[]{:S(2)}) %copy-start) | copy-done | bytes 614424
  49.3 0.2 copy-done.1
  49.5 19.2 %shard_map.130 = f32[150,8192]{1,0:T(8,128)} custom-call(s32[3,64]{1,0:T(4,128)} %bitcast.23, bf16[150,8192]{1,0:T(8,128)(2,1)} %shard_map.128.own_ref.migrated_hbm, bf16[64,4,128,128]{3,2,1,0:T(8,128)(2,1)} %weight_ref.1, f32[1,8192]{1,0:T(1,128)} %bitcast.18, f32[152,256]{1,0:T(8,128)} %pad_maximum_fusion.order_ref, f32[150,256]{1,0:T(8,128)} %prod_ref.1, ...), custom_call_target="tpu_custom_call" | custom-call | tf_op jit(solution)/shard_map/pallas_call | solution.py:340
  (2 shorter events, 0.0 us)
Async XLA Ops:
  0.0 40.3 %copy-start.12 = (f32[256]{0:T(256)S(1)}, f32[256]{0:T(256)}, u32[]{:S(2)}) copy-start(f32[256]{0:T(256)} %param.23) | copy-start | bytes 3076
  0.0 40.3 %copy-start.11 = (f32[256]{0:T(256)S(1)}, f32[256]{0:T(256)}, u32[]{:S(2)}) copy-start(f32[256]{0:T(256)} %param.22) | copy-start | bytes 3076
  0.0 40.3 %copy-start.10 = (f32[256,150]{0,1:T(8,128)S(1)}, f32[256,150]{0,1:T(8,128)}, u32[]{:S(2)}) copy-start(f32[256,150]{0,1:T(8,128)} %param.21) | copy-start | bytes 460804
  5.3 13.8 %collective-permute-start = (bf16[150,128]{1,0:T(8,128)(2,1)}, bf16[150,128]{1,0:T(8,128)(2,1)S(1)}, u32[]{:S(2)}, u32[]{:S(2)}) collective-permute-start(bf16[150,128]{1,0:T(8,128)(2,1)} %get-tuple-element.15), channel_id=1, source_target_pairs={{124,0},{125,1},{126,2},{127,3},{0,4},{1,5},{2,6},{3,7},{4,8},{5,9... | collective-permute-start | bytes 115208 | tf_op jit(solution)/shard_map/ppermute | solution.py:18
  8.4 11.4 %collective-permute-start.1 = (bf16[150,128]{1,0:T(8,128)(2,1)}, bf16[150,128]{1,0:T(8,128)(2,1)S(1)}, u32[]{:S(2)}, u32[]{:S(2)}) collective-permute-start(bf16[150,128]{1,0:T(8,128)(2,1)} %get-tuple-element.16), channel_id=1, source_target_pairs={{125,0},{126,1},{127,2},{0,3},{1,4},{2,5},{3,6},{4,7},{5,8},{6,9},... | collective-permute-start | bytes 115208 | tf_op jit(solution)/shard_map/ppermute | solution.py:18
  8.4 11.7 %collective-permute-start.2 = (bf16[150,128]{1,0:T(8,128)(2,1)}, bf16[150,128]{1,0:T(8,128)(2,1)S(1)}, u32[]{:S(2)}, u32[]{:S(2)}) collective-permute-start(bf16[150,128]{1,0:T(8,128)(2,1)} %get-tuple-element.17), channel_id=1, source_target_pairs={{126,0},{127,1},{0,2},{1,3},{2,4},{3,5},{4,6},{5,7},{6,8},{7,9},{8... | collective-permute-start | bytes 115208 | tf_op jit(solution)/shard_map/ppermute | solution.py:18
  9.4 15.5 %collective-permute-start.3 = (bf16[150,128]{1,0:T(8,128)(2,1)}, bf16[150,128]{1,0:T(8,128)(2,1)S(1)}, u32[]{:S(2)}, u32[]{:S(2)}) collective-permute-start(bf16[150,128]{1,0:T(8,128)(2,1)} %get-tuple-element.18), channel_id=1, source_target_pairs={{127,0},{0,1},{1,2},{2,3},{3,4},{4,5},{5,6},{6,7},{7,8},{8,9},{9,1... | collective-permute-start | bytes 115208 | tf_op jit(solution)/shard_map/ppermute | solution.py:18
  11.6 13.3 %collective-permute-start.4 = (bf16[150,128]{1,0:T(8,128)(2,1)}, bf16[150,128]{1,0:T(8,128)(2,1)S(1)}, u32[]{:S(2)}, u32[]{:S(2)}) collective-permute-start(bf16[150,128]{1,0:T(8,128)(2,1)} %get-tuple-element.19), channel_id=1, source_target_pairs={{1,0},{2,1},{3,2},{4,3},{5,4},{6,5},{7,6},{8,7},{9,8},{10,9},{11,1... | collective-permute-start | bytes 115208 | tf_op jit(solution)/shard_map/ppermute | solution.py:18
  19.1 7.2 %copy-start.2 = (bf16[150,128]{1,0:T(8,128)(2,1)}, bf16[150,128]{1,0:T(8,128)(2,1)S(1)}, u32[]{:S(2)}) copy-start(bf16[150,128]{1,0:T(8,128)(2,1)S(1)} %collective-permute-done.refs_0_) | copy-start | bytes 115204
  19.1 5.8 %collective-permute-start.5 = (bf16[150,128]{1,0:T(8,128)(2,1)}, bf16[150,128]{1,0:T(8,128)(2,1)S(1)}, u32[]{:S(2)}, u32[]{:S(2)}) collective-permute-start(bf16[150,128]{1,0:T(8,128)(2,1)} %get-tuple-element.20), channel_id=1, source_target_pairs={{2,0},{3,1},{4,2},{5,3},{6,4},{7,5},{8,6},{9,7},{10,8},{11,9},{12,... | collective-permute-start | bytes 115208 | tf_op jit(solution)/shard_map/ppermute | solution.py:18
  19.8 6.5 %copy-start.3 = (bf16[150,128]{1,0:T(8,128)(2,1)}, bf16[150,128]{1,0:T(8,128)(2,1)S(1)}, u32[]{:S(2)}) copy-start(bf16[150,128]{1,0:T(8,128)(2,1)S(1)} %collective-permute-done.1.refs_1_) | copy-start | bytes 115204
  19.8 5.2 %collective-permute-start.6 = (bf16[150,128]{1,0:T(8,128)(2,1)}, bf16[150,128]{1,0:T(8,128)(2,1)S(1)}, u32[]{:S(2)}, u32[]{:S(2)}) collective-permute-start(bf16[150,128]{1,0:T(8,128)(2,1)} %get-tuple-element.21), channel_id=1, source_target_pairs={{3,0},{4,1},{5,2},{6,3},{7,4},{8,5},{9,6},{10,7},{11,8},{12,9},{13... | collective-permute-start | bytes 115208 | tf_op jit(solution)/shard_map/ppermute | solution.py:18
  20.1 6.2 %copy-start.4 = (bf16[150,128]{1,0:T(8,128)(2,1)}, bf16[150,128]{1,0:T(8,128)(2,1)S(1)}, u32[]{:S(2)}) copy-start(bf16[150,128]{1,0:T(8,128)(2,1)S(1)} %collective-permute-done.2.refs_2_) | copy-start | bytes 115204
  20.1 6.2 %collective-permute-start.7 = (bf16[150,128]{1,0:T(8,128)(2,1)}, bf16[150,128]{1,0:T(8,128)(2,1)S(1)}, u32[]{:S(2)}, u32[]{:S(2)}) collective-permute-start(bf16[150,128]{1,0:T(8,128)(2,1)} %get-tuple-element.22), channel_id=1, source_target_pairs={{4,0},{5,1},{6,2},{7,3},{8,4},{9,5},{10,6},{11,7},{12,8},{13,9},{1... | collective-permute-start | bytes 115208 | tf_op jit(solution)/shard_map/ppermute | solution.py:18
  24.9 1.4 %copy-start.5 = (bf16[150,128]{1,0:T(8,128)(2,1)}, bf16[150,128]{1,0:T(8,128)(2,1)S(1)}, u32[]{:S(2)}) copy-start(bf16[150,128]{1,0:T(8,128)(2,1)S(1)} %collective-permute-done.3.refs_3_) | copy-start | bytes 115204
  24.9 1.4 %copy-start.6 = (bf16[150,128]{1,0:T(8,128)(2,1)}, bf16[150,128]{1,0:T(8,128)(2,1)S(1)}, u32[]{:S(2)}) copy-start(bf16[150,128]{1,0:T(8,128)(2,1)S(1)} %collective-permute-done.4.refs_4_) | copy-start | bytes 115204
  25.0 1.4 %copy-start.7 = (bf16[150,128]{1,0:T(8,128)(2,1)}, bf16[150,128]{1,0:T(8,128)(2,1)S(1)}, u32[]{:S(2)}) copy-start(bf16[150,128]{1,0:T(8,128)(2,1)S(1)} %collective-permute-done.5.refs_5_) | copy-start | bytes 115204
  25.0 1.4 %copy-start.8 = (bf16[150,128]{1,0:T(8,128)(2,1)}, bf16[150,128]{1,0:T(8,128)(2,1)S(1)}, u32[]{:S(2)}) copy-start(bf16[150,128]{1,0:T(8,128)(2,1)S(1)} %collective-permute-done.6.refs_6_) | copy-start | bytes 115204
  26.3 0.6 copy-start.9
  33.1 15.4 %collective-permute-start.8 = (bf16[150,2048]{1,0:T(8,128)(2,1)}, bf16[150,2048]{1,0:T(8,128)(2,1)S(1)}, u32[]{:S(2)}, u32[]{:S(2)}) collective-permute-start(bf16[150,2048]{1,0:T(8,128)(2,1)} %get-tuple-element.23), channel_id=1, source_target_pairs={{127,0},{0,1},{1,2},{2,3},{3,4},{4,5},{5,6},{6,7},{7,8},{8,9},{9,1... | collective-permute-start | bytes 1843208 | tf_op jit(solution)/shard_map/ppermute | solution.py:18
  33.2 15.2 %collective-permute-start.9 = (bf16[150,2048]{1,0:T(8,128)(2,1)}, bf16[150,2048]{1,0:T(8,128)(2,1)S(1)}, u32[]{:S(2)}, u32[]{:S(2)}) collective-permute-start(bf16[150,2048]{1,0:T(8,128)(2,1)} %get-tuple-element.24), channel_id=1, source_target_pairs={{1,0},{2,1},{3,2},{4,3},{5,4},{6,5},{7,6},{8,7},{9,8},{10,9},{11,1... | collective-permute-start | bytes 1843208 | tf_op jit(solution)/shard_map/ppermute | solution.py:18
  48.5 0.8 %copy-start = (bf16[150,2048]{1,0:T(8,128)(2,1)}, bf16[150,2048]{1,0:T(8,128)(2,1)S(1)}, u32[]{:S(2)}) copy-start(bf16[150,2048]{1,0:T(8,128)(2,1)S(1)} %collective-permute-done.8.lower_hbm) | copy-start | bytes 1843204
  48.5 1.0 %copy-start.1 = (bf16[150,2048]{1,0:T(8,128)(2,1)}, bf16[150,2048]{1,0:T(8,128)(2,1)S(1)}, u32[]{:S(2)}) copy-start(bf16[150,2048]{1,0:T(8,128)(2,1)S(1)} %collective-permute-done.9.upper_hbm) | copy-start | bytes 1843204

commit v15 on v14

--- a/solution.py
+++ b/solution.py
@@ -8,7 +8,7 @@
 from jax.sharding import PartitionSpec as P
 
 HOP = 4
-TILE_BLOCKS = 16
+TILE_BLOCKS = 32
 PAD_ROWS = 160
 
 

time: 69.4 us -> 71.4 us (1.029)
  Pallas kernels: 37.5 us -> 39.7 us
    pallas_call x1, Pallas kernels: 19.2 us -> 21.4 us  [mix_react(): pl.pallas_call(kernel, grid_spec=grid_spec, out_shape=jax.ShapeDtypeStruc...]
where the time goes in v15:
time: 71.4 us; the launch traced here: 71.1 us
  Pallas kernels  39.7 us (56%)
  starting transfers between devices  24.1 us (34%)
  local copies, waits for them, and re-layouts  2.83 us (4%)
  other arithmetic  2.25 us (3%)
  waiting for transfers between devices  1.93 us (3%)
    ppermute x10, starting transfers between devices, from_behind(): return lax.ppermute(block, axis, route)  24.1 us
    pallas_call x1, Pallas kernels, mix_react(): pl.pallas_call(kernel, grid_spec=grid_spec, out_shape=jax.ShapeDtypeStruc...  21.4 us
    pallas_call x1, Pallas kernels, migrate(): pl.pallas_call(functools.partial(place_kernel, chunk, peer_count), grid=(...  6.84 us
    pallas_call x1, Pallas kernels, migrate(): pl.pallas_call(functools.partial(halo_kernel, chunk, block_size, peer_cou...  6.17 us
    pallas_call x1, Pallas kernels, migrate(): pl.pallas_call(functools.partial(pick_kernel, chunk), grid=(1,), in_specs...  5.28 us
    ppermute x10, waiting for transfers between devices, from_behind(): return lax.ppermute(block, axis, route)  1.93 us
    unnamed x28, local copies, waits for them, and re-layouts  1.92 us
  transfers between devices with their start and end apart: 10, of which 2 were waited for; matrix products, arithmetic and copies ran while one was open for 5% of the time, Pallas kernels for 10%

profile of v15, /device:TPU:0, one launch (start us, length us, event | category | flops | bytes accessed | tf_op | source)
XLA Modules:
  0.0 71.1 jit_solution(13313035945476752720)
XLA Ops:
  0.0 0.0 copy-start.12
  0.0 0.0 copy-start.11
  0.0 0.0 copy-start.10
  0.0 5.3 %shard_map.127 = (bf16[150,128]{1,0:T(8,128)(2,1)}, bf16[150,128]{1,0:T(8,128)(2,1)}, bf16[150,128]{1,0:T(8,128)(2,1)}, bf16[150,128]{1,0:T(8,128)(2,1)}, bf16[1...) custom-call(bf16[150,8192]{1,0:T(8,128)(2,1)} %mixing_ref.5, ...), custom_call_target="tpu_custom_call" | custom-call | tf_op jit(solution)/shard_map/pallas_call | solution.py:114
  5.3 3.1 %collective-permute-start = (bf16[150,128]{1,0:T(8,128)(2,1)}, bf16[150,128]{1,0:T(8,128)(2,1)S(1)}, u32[]{:S(2)}, u32[]{:S(2)}) collective-permute-start(bf16[150,128]{1,0:T(8,128)(2,1)} %get-tuple-element.15), channel_id=1, source_target_pairs={{124,0},{125,1},{126,2},{127,3},{0,4},{1,5},{2,6},{3,7},{4,8},{5,9... | collective-permute-start | bytes 115208 | tf_op jit(solution)/shard_map/ppermute | solution.py:18
  8.4 0.0 collective-permute-start.1
  8.4 1.0 %collective-permute-start.2 = (bf16[150,128]{1,0:T(8,128)(2,1)}, bf16[150,128]{1,0:T(8,128)(2,1)S(1)}, u32[]{:S(2)}, u32[]{:S(2)}) collective-permute-start(bf16[150,128]{1,0:T(8,128)(2,1)} %get-tuple-element.17), channel_id=1, source_target_pairs={{126,0},{127,1},{0,2},{1,3},{2,4},{3,5},{4,6},{5,7},{6,8},{7,9},{8... | collective-permute-start | bytes 115208 | tf_op jit(solution)/shard_map/ppermute | solution.py:18
  9.4 2.2 %collective-permute-start.3 = (bf16[150,128]{1,0:T(8,128)(2,1)}, bf16[150,128]{1,0:T(8,128)(2,1)S(1)}, u32[]{:S(2)}, u32[]{:S(2)}) collective-permute-start(bf16[150,128]{1,0:T(8,128)(2,1)} %get-tuple-element.18), channel_id=1, source_target_pairs={{127,0},{0,1},{1,2},{2,3},{3,4},{4,5},{5,6},{6,7},{7,8},{8,9},{9,1... | collective-permute-start | bytes 115208 | tf_op jit(solution)/shard_map/ppermute | solution.py:18
  11.6 5.6 %collective-permute-start.4 = (bf16[150,128]{1,0:T(8,128)(2,1)}, bf16[150,128]{1,0:T(8,128)(2,1)S(1)}, u32[]{:S(2)}, u32[]{:S(2)}) collective-permute-start(bf16[150,128]{1,0:T(8,128)(2,1)} %get-tuple-element.19), channel_id=1, source_target_pairs={{1,0},{2,1},{3,2},{4,3},{5,4},{6,5},{7,6},{8,7},{9,8},{10,9},{11,1... | collective-permute-start | bytes 115208 | tf_op jit(solution)/shard_map/ppermute | solution.py:18
  17.2 0.7 %fusion = pred[1,1,8,128]{3,2,1,0:T(8,128)(4,1)S(1)} fusion(s32[8]{0:T(128)} %bitcast.26), kind=kLoop, calls=%fused_computation.4 | loop fusion | flops 1024 | bytes 1056
  17.9 0.3 copy.17
  18.2 0.9 %copy.15 = s32[1024,1]{1,0:T(8,128)S(1)} copy(s32[1024,1]{0,1:T(1,128)} %bitcast.21) | data formatting | bytes 8192 | tf_op jit(solution)/shard_map/squeeze | solution.py:127
  19.1 0.0 collective-permute-done.refs_0_
  19.1 0.0 copy-start.2
  19.1 0.6 collective-permute-start.5
  19.8 0.0 collective-permute-done.1.refs_1_
  19.8 0.0 copy-start.3
  19.8 0.3 collective-permute-start.6
  20.1 0.0 collective-permute-done.2.refs_2_
  20.1 0.0 copy-start.4
  20.1 4.0 %collective-permute-start.7 = (bf16[150,128]{1,0:T(8,128)(2,1)}, bf16[150,128]{1,0:T(8,128)(2,1)S(1)}, u32[]{:S(2)}, u32[]{:S(2)}) collective-permute-start(bf16[150,128]{1,0:T(8,128)(2,1)} %get-tuple-element.22), channel_id=1, source_target_pairs={{4,0},{5,1},{6,2},{7,3},{8,4},{9,5},{10,6},{11,7},{12,8},{13,9},{1... | collective-permute-start | bytes 115208 | tf_op jit(solution)/shard_map/ppermute | solution.py:18
  24.1 0.8 %bitcast_select_fusion.refs_8_ = s32[1024,1]{1,0:T(8,128)} fusion(s32[1024,1]{1,0:T(8,128)S(1)} %copy.15, pred[1,1024]{0,1:T(8,128)(4,1)S(1)} %copy.17), kind=kLoop, calls=%fused_computation | loop fusion | flops 1024 | bytes 9216 | tf_op jit(solution)/shard_map/jit(_where)/select_n | solution.py:127
  24.9 0.0 collective-permute-done.3.refs_3_
  24.9 0.0 copy-start.5
  24.9 0.0 collective-permute-done.4.refs_4_
  24.9 0.0 copy-start.6
  24.9 0.0 collective-permute-done.5.refs_5_
  25.0 0.0 copy-start.7
  25.0 0.0 collective-permute-done.6.refs_6_
  25.0 0.0 copy-start.8
  25.0 1.3 %collective-permute-done.7.refs_7_ = bf16[150,128]{1,0:T(8,128)(2,1)S(1)} collective-permute-done((bf16[150,128]{1,0:T(8,128)(2,1)}, bf16[150,128]{1,0:T(8,128)(2,1)S(1)}, u32[]{:S(2)}, u32[]{:S(2)}) %collective-permute-start.7) | collective-permute-done | bytes 38432 | tf_op jit(solution)/shard_map/ppermute | solution.py:18
  26.3 0.0 copy-start.9
  26.3 0.0 copy-done.2
  26.3 0.0 copy-done.3
  26.3 0.0 copy-done.4
  26.3 0.0 copy-done.5
  26.3 0.0 copy-done.6
  26.3 0.0 copy-done.7
  26.3 0.0 copy-done.8
  26.3 0.6 copy-done.9
  26.9 6.2 %shard_map.129 = (bf16[150,2048]{1,0:T(8,128)(2,1)}, bf16[150,2048]{1,0:T(8,128)(2,1)}) custom-call(s32[2,16]{1,0:T(2,128)} %bitcast.24, bf16[150,8192]{1,0:T(8,128)(2,1)} %mixing_ref.5, bf16[150,128]{1,0:T(8,128)(2,1)} %copy-done.2, bf16[150,128]{1,0:T(8,128)(2,1)} %copy-done.3, bf16[150,128]{1,0:T(8,128)(2,1)} %copy-done.4, bf16[150,128]{1,0:T(8,128)(2,1)} %copy-done.5, ...), custom_call_target="tpu_custom_call" | custom-call | tf_op jit(solution)/shard_map/pallas_call | solution.py:139
  33.1 0.2 collective-permute-start.8
  33.2 7.1 %collective-permute-start.9 = (bf16[150,2048]{1,0:T(8,128)(2,1)}, bf16[150,2048]{1,0:T(8,128)(2,1)S(1)}, u32[]{:S(2)}, u32[]{:S(2)}) collective-permute-start(bf16[150,2048]{1,0:T(8,128)(2,1)} %get-tuple-element.24), channel_id=1, source_target_pairs={{1,0},{2,1},{3,2},{4,3},{5,4},{6,5},{7,6},{8,7},{9,8},{10,9},{11,1... | collective-permute-start | bytes 1843208 | tf_op jit(solution)/shard_map/ppermute | solution.py:18
  40.3 0.0 copy-done.12
  40.3 0.0 copy-done.11
  40.3 0.0 copy-done.10
  40.3 0.7 pad_maximum_fusion.order_ref
  41.0 6.8 %shard_map.128.own_ref.migrated_hbm = bf16[150,8192]{1,0:T(8,128)(2,1)} custom-call(bf16[150,8192]{1,0:T(8,128)(2,1)} %mixing_ref.5, bf16[150,128]{1,0:T(8,128)(2,1)} %copy-done.2, bf16[150,128]{1,0:T(8,128)(2,1)} %copy-done.3, bf16[150,128]{1,0:T(8,128)(2,1)} %copy-done.4, bf16[150,128]{1,0:T(8,128)(2,1)} %copy-done.5, bf16[150,128]{1,0:T(8,128)(2,1)} %copy-done.6, ...), custom_call_target="tpu_custom_call" | custom-call | tf_op jit(solution)/shard_map/pallas_call | solution.py:144
  47.9 0.6 collective-permute-done.8.lower_hbm
  48.5 0.0 copy-start
  48.5 0.0 collective-permute-done.9.upper_hbm
  48.5 0.0 copy-start.1
  48.5 0.8 %copy-done = bf16[150,2048]{1,0:T(8,128)(2,1)} copy-done((bf16[150,2048]{1,0:T(8,128)(2,1)}, bf16[150,2048]{1,0:T(8,128)(2,1)S(1)}, u32[]{:S(2)}) %copy-start) | copy-done | bytes 614424
  49.3 0.2 copy-done.1
  49.5 21.4 %shard_map.130 = f32[150,8192]{1,0:T(8,128)} custom-call(s32[3,64]{1,0:T(4,128)} %bitcast.23, bf16[150,8192]{1,0:T(8,128)(2,1)} %shard_map.128.own_ref.migrated_hbm, bf16[64,4,128,128]{3,2,1,0:T(8,128)(2,1)} %weight_ref.1, f32[1,8192]{1,0:T(1,128)} %bitcast.18, f32[152,256]{1,0:T(8,128)} %pad_maximum_fusion.order_ref, f32[150,256]{1,0:T(8,128)} %prod_ref.1, ...), custom_call_target="tpu_custom_call" | custom-call | tf_op jit(solution)/shard_map/pallas_call | solution.py:340
  (2 shorter events, 0.0 us)
Async XLA Ops:
  0.0 40.3 %copy-start.12 = (f32[256]{0:T(256)S(1)}, f32[256]{0:T(256)}, u32[]{:S(2)}) copy-start(f32[256]{0:T(256)} %param.23) | copy-start | bytes 3076
  0.0 40.3 %copy-start.11 = (f32[256]{0:T(256)S(1)}, f32[256]{0:T(256)}, u32[]{:S(2)}) copy-start(f32[256]{0:T(256)} %param.22) | copy-start | bytes 3076
  0.0 40.3 %copy-start.10 = (f32[256,150]{0,1:T(8,128)S(1)}, f32[256,150]{0,1:T(8,128)}, u32[]{:S(2)}) copy-start(f32[256,150]{0,1:T(8,128)} %param.21) | copy-start | bytes 460804
  5.3 13.8 %collective-permute-start = (bf16[150,128]{1,0:T(8,128)(2,1)}, bf16[150,128]{1,0:T(8,128)(2,1)S(1)}, u32[]{:S(2)}, u32[]{:S(2)}) collective-permute-start(bf16[150,128]{1,0:T(8,128)(2,1)} %get-tuple-element.15), channel_id=1, source_target_pairs={{124,0},{125,1},{126,2},{127,3},{0,4},{1,5},{2,6},{3,7},{4,8},{5,9... | collective-permute-start | bytes 115208 | tf_op jit(solution)/shard_map/ppermute | solution.py:18
  8.4 11.4 %collective-permute-start.1 = (bf16[150,128]{1,0:T(8,128)(2,1)}, bf16[150,128]{1,0:T(8,128)(2,1)S(1)}, u32[]{:S(2)}, u32[]{:S(2)}) collective-permute-start(bf16[150,128]{1,0:T(8,128)(2,1)} %get-tuple-element.16), channel_id=1, source_target_pairs={{125,0},{126,1},{127,2},{0,3},{1,4},{2,5},{3,6},{4,7},{5,8},{6,9},... | collective-permute-start | bytes 115208 | tf_op jit(solution)/shard_map/ppermute | solution.py:18
  8.4 11.7 %collective-permute-start.2 = (bf16[150,128]{1,0:T(8,128)(2,1)}, bf16[150,128]{1,0:T(8,128)(2,1)S(1)}, u32[]{:S(2)}, u32[]{:S(2)}) collective-permute-start(bf16[150,128]{1,0:T(8,128)(2,1)} %get-tuple-element.17), channel_id=1, source_target_pairs={{126,0},{127,1},{0,2},{1,3},{2,4},{3,5},{4,6},{5,7},{6,8},{7,9},{8... | collective-permute-start | bytes 115208 | tf_op jit(solution)/shard_map/ppermute | solution.py:18
  9.4 15.5 %collective-permute-start.3 = (bf16[150,128]{1,0:T(8,128)(2,1)}, bf16[150,128]{1,0:T(8,128)(2,1)S(1)}, u32[]{:S(2)}, u32[]{:S(2)}) collective-permute-start(bf16[150,128]{1,0:T(8,128)(2,1)} %get-tuple-element.18), channel_id=1, source_target_pairs={{127,0},{0,1},{1,2},{2,3},{3,4},{4,5},{5,6},{6,7},{7,8},{8,9},{9,1... | collective-permute-start | bytes 115208 | tf_op jit(solution)/shard_map/ppermute | solution.py:18
  11.6 13.3 %collective-permute-start.4 = (bf16[150,128]{1,0:T(8,128)(2,1)}, bf16[150,128]{1,0:T(8,128)(2,1)S(1)}, u32[]{:S(2)}, u32[]{:S(2)}) collective-permute-start(bf16[150,128]{1,0:T(8,128)(2,1)} %get-tuple-element.19), channel_id=1, source_target_pairs={{1,0},{2,1},{3,2},{4,3},{5,4},{6,5},{7,6},{8,7},{9,8},{10,9},{11,1... | collective-permute-start | bytes 115208 | tf_op jit(solution)/shard_map/ppermute | solution.py:18
  19.1 7.2 %copy-start.2 = (bf16[150,128]{1,0:T(8,128)(2,1)}, bf16[150,128]{1,0:T(8,128)(2,1)S(1)}, u32[]{:S(2)}) copy-start(bf16[150,128]{1,0:T(8,128)(2,1)S(1)} %collective-permute-done.refs_0_) | copy-start | bytes 115204
  19.1 5.8 %collective-permute-start.5 = (bf16[150,128]{1,0:T(8,128)(2,1)}, bf16[150,128]{1,0:T(8,128)(2,1)S(1)}, u32[]{:S(2)}, u32[]{:S(2)}) collective-permute-start(bf16[150,128]{1,0:T(8,128)(2,1)} %get-tuple-element.20), channel_id=1, source_target_pairs={{2,0},{3,1},{4,2},{5,3},{6,4},{7,5},{8,6},{9,7},{10,8},{11,9},{12,... | collective-permute-start | bytes 115208 | tf_op jit(solution)/shard_map/ppermute | solution.py:18
  19.8 6.5 %copy-start.3 = (bf16[150,128]{1,0:T(8,128)(2,1)}, bf16[150,128]{1,0:T(8,128)(2,1)S(1)}, u32[]{:S(2)}) copy-start(bf16[150,128]{1,0:T(8,128)(2,1)S(1)} %collective-permute-done.1.refs_1_) | copy-start | bytes 115204
  19.8 5.2 %collective-permute-start.6 = (bf16[150,128]{1,0:T(8,128)(2,1)}, bf16[150,128]{1,0:T(8,128)(2,1)S(1)}, u32[]{:S(2)}, u32[]{:S(2)}) collective-permute-start(bf16[150,128]{1,0:T(8,128)(2,1)} %get-tuple-element.21), channel_id=1, source_target_pairs={{3,0},{4,1},{5,2},{6,3},{7,4},{8,5},{9,6},{10,7},{11,8},{12,9},{13... | collective-permute-start | bytes 115208 | tf_op jit(solution)/shard_map/ppermute | solution.py:18
  20.1 6.2 %copy-start.4 = (bf16[150,128]{1,0:T(8,128)(2,1)}, bf16[150,128]{1,0:T(8,128)(2,1)S(1)}, u32[]{:S(2)}) copy-start(bf16[150,128]{1,0:T(8,128)(2,1)S(1)} %collective-permute-done.2.refs_2_) | copy-start | bytes 115204
  20.1 6.2 %collective-permute-start.7 = (bf16[150,128]{1,0:T(8,128)(2,1)}, bf16[150,128]{1,0:T(8,128)(2,1)S(1)}, u32[]{:S(2)}, u32[]{:S(2)}) collective-permute-start(bf16[150,128]{1,0:T(8,128)(2,1)} %get-tuple-element.22), channel_id=1, source_target_pairs={{4,0},{5,1},{6,2},{7,3},{8,4},{9,5},{10,6},{11,7},{12,8},{13,9},{1... | collective-permute-start | bytes 115208 | tf_op jit(solution)/shard_map/ppermute | solution.py:18
  24.9 1.4 %copy-start.5 = (bf16[150,128]{1,0:T(8,128)(2,1)}, bf16[150,128]{1,0:T(8,128)(2,1)S(1)}, u32[]{:S(2)}) copy-start(bf16[150,128]{1,0:T(8,128)(2,1)S(1)} %collective-permute-done.3.refs_3_) | copy-start | bytes 115204
  24.9 1.4 %copy-start.6 = (bf16[150,128]{1,0:T(8,128)(2,1)}, bf16[150,128]{1,0:T(8,128)(2,1)S(1)}, u32[]{:S(2)}) copy-start(bf16[150,128]{1,0:T(8,128)(2,1)S(1)} %collective-permute-done.4.refs_4_) | copy-start | bytes 115204
  25.0 1.4 %copy-start.7 = (bf16[150,128]{1,0:T(8,128)(2,1)}, bf16[150,128]{1,0:T(8,128)(2,1)S(1)}, u32[]{:S(2)}) copy-start(bf16[150,128]{1,0:T(8,128)(2,1)S(1)} %collective-permute-done.5.refs_5_) | copy-start | bytes 115204
  25.0 1.4 %copy-start.8 = (bf16[150,128]{1,0:T(8,128)(2,1)}, bf16[150,128]{1,0:T(8,128)(2,1)S(1)}, u32[]{:S(2)}) copy-start(bf16[150,128]{1,0:T(8,128)(2,1)S(1)} %collective-permute-done.6.refs_6_) | copy-start | bytes 115204
  26.3 0.6 copy-start.9
  33.1 15.4 %collective-permute-start.8 = (bf16[150,2048]{1,0:T(8,128)(2,1)}, bf16[150,2048]{1,0:T(8,128)(2,1)S(1)}, u32[]{:S(2)}, u32[]{:S(2)}) collective-permute-start(bf16[150,2048]{1,0:T(8,128)(2,1)} %get-tuple-element.23), channel_id=1, source_target_pairs={{127,0},{0,1},{1,2},{2,3},{3,4},{4,5},{5,6},{6,7},{7,8},{8,9},{9,1... | collective-permute-start | bytes 1843208 | tf_op jit(solution)/shard_map/ppermute | solution.py:18
  33.2 15.2 %collective-permute-start.9 = (bf16[150,2048]{1,0:T(8,128)(2,1)}, bf16[150,2048]{1,0:T(8,128)(2,1)S(1)}, u32[]{:S(2)}, u32[]{:S(2)}) collective-permute-start(bf16[150,2048]{1,0:T(8,128)(2,1)} %get-tuple-element.24), channel_id=1, source_target_pairs={{1,0},{2,1},{3,2},{4,3},{5,4},{6,5},{7,6},{8,7},{9,8},{10,9},{11,1... | collective-permute-start | bytes 1843208 | tf_op jit(solution)/shard_map/ppermute | solution.py:18
  48.5 0.8 %copy-start = (bf16[150,2048]{1,0:T(8,128)(2,1)}, bf16[150,2048]{1,0:T(8,128)(2,1)S(1)}, u32[]{:S(2)}) copy-start(bf16[150,2048]{1,0:T(8,128)(2,1)S(1)} %collective-permute-done.8.lower_hbm) | copy-start | bytes 1843204
  48.5 1.0 %copy-start.1 = (bf16[150,2048]{1,0:T(8,128)(2,1)}, bf16[150,2048]{1,0:T(8,128)(2,1)S(1)}, u32[]{:S(2)}) copy-start(bf16[150,2048]{1,0:T(8,128)(2,1)S(1)} %collective-permute-done.9.upper_hbm) | copy-start | bytes 1843204

commit v16 on v14

--- a/solution.py
+++ b/solution.py
@@ -47,18 +47,16 @@
 def place_kernel(chunk, peer_count, mixing_ref, *refs):
     received_refs = refs[:peer_count]
     slots_ref, migrated_ref = refs[peer_count:]
-    species, parcels = mixing_ref.shape
+    species = mixing_ref.shape[0]
     slots = slots_ref[...]
     marked = marked_arrivals(received_refs, slots.shape[0])
-    for part in range(parcels // chunk):
-        lanes = slice(part * chunk, (part + 1) * chunk)
-        position = lax.broadcasted_iota(jnp.int32, (slots.shape[0], chunk), 1) + part * chunk
-        place = (position == slots).astype(jnp.bfloat16)
-        placed = jnp.dot(marked, place, preferred_element_type=jnp.float32)
-        hit = placed[species:species + 1]
-        migrated_ref[:, lanes] = jnp.where(
-            hit > 0.5, placed[:species].astype(migrated_ref.dtype), mixing_ref[:, lanes]
-        )
+    position = lax.broadcasted_iota(jnp.int32, (slots.shape[0], chunk), 1)
+    place = (position + pl.program_id(0) * chunk == slots).astype(jnp.bfloat16)
+    placed = jnp.dot(marked, place, preferred_element_type=jnp.float32)
+    hit = placed[species:species + 1]
+    migrated_ref[...] = jnp.where(
+        hit > 0.5, placed[:species].astype(migrated_ref.dtype), mixing_ref[...]
+    )
 
 
 def halo_kernel(chunk, block_size, peer_count, halo_ref, mixing_ref, *refs):
@@ -143,11 +141,11 @@
     )(halo_blocks[0], mixing_ratio, *arrived, slots)
     migrated = pl.pallas_call(
         functools.partial(place_kernel, chunk, peer_count),
-        grid=(1,),
-        in_specs=[vmem_whole(mixing_ratio.shape)]
+        grid=(parcels // chunk,),
+        in_specs=[pl.BlockSpec((species, chunk), lambda i: (0, i))]
         + [vmem_whole((species, capacity))] * peer_count
         + [vmem_whole(slots.shape)],
-        out_specs=vmem_whole(mixing_ratio.shape),
+        out_specs=pl.BlockSpec((species, chunk), lambda i: (0, i)),
         out_shape=jax.ShapeDtypeStruct(mixing_ratio.shape, mixing_ratio.dtype),
     )(mixing_ratio, *arrived, slots)
     from_lower = from_behind(to_upper, "region", 1)

time: 69.4 us -> 70.8 us (1.020)
  Pallas kernels: 37.5 us -> 39.4 us
    pallas_call x1, Pallas kernels: 6.84 us -> 8.67 us  [migrate(): pl.pallas_call(functools.partial(place_kernel, chunk, peer_count), grid=(...]
  transfers between devices with their start and end apart: 10 -> 10, of which waited for: 2 -> 1; matrix products, arithmetic and copies ran while one was open for 5% -> 5% of each run, Pallas kernels for 10% -> 12%
where the time goes in v16:
time: 70.8 us; the launch traced here: 70.2 us
  Pallas kernels  39.4 us (56%)
  starting transfers between devices  24.1 us (34%)
  local copies, waits for them, and re-layouts  2.81 us (4%)
  other arithmetic  2.25 us (3%)
  waiting for transfers between devices  1.33 us (2%)
    ppermute x10, starting transfers between devices, from_behind(): return lax.ppermute(block, axis, route)  24.1 us
    pallas_call x1, Pallas kernels, mix_react(): pl.pallas_call(kernel, grid_spec=grid_spec, out_shape=jax.ShapeDtypeStruc...  19.3 us
    pallas_call x1, Pallas kernels, migrate(): pl.pallas_call(functools.partial(place_kernel, chunk, peer_count), grid=(...  8.67 us
    pallas_call x1, Pallas kernels, migrate(): pl.pallas_call(functools.partial(halo_kernel, chunk, block_size, peer_cou...  6.17 us
    pallas_call x1, Pallas kernels, migrate(): pl.pallas_call(functools.partial(pick_kernel, chunk), grid=(1,), in_specs...  5.28 us
    unnamed x28, local copies, waits for them, and re-layouts  1.91 us
  transfers between devices with their start and end apart: 10, of which 1 were waited for; matrix products, arithmetic and copies ran while one was open for 5% of the time, Pallas kernels for 12%

profile of v16, /device:TPU:0, one launch (start us, length us, event | category | flops | bytes accessed | tf_op | source)
XLA Modules:
  0.0 70.2 jit_solution(1604035952694187429)
XLA Ops:
  0.0 0.0 copy-start.12
  0.0 0.0 copy-start.11
  0.0 0.0 copy-start.10
  0.0 5.3 %shard_map.127 = (bf16[150,128]{1,0:T(8,128)(2,1)}, bf16[150,128]{1,0:T(8,128)(2,1)}, bf16[150,128]{1,0:T(8,128)(2,1)}, bf16[150,128]{1,0:T(8,128)(2,1)}, bf16[1...) custom-call(bf16[150,8192]{1,0:T(8,128)(2,1)} %mixing_ref.5, ...), custom_call_target="tpu_custom_call" | custom-call | tf_op jit(solution)/shard_map/pallas_call | solution.py:112
  5.3 3.1 %collective-permute-start = (bf16[150,128]{1,0:T(8,128)(2,1)}, bf16[150,128]{1,0:T(8,128)(2,1)S(1)}, u32[]{:S(2)}, u32[]{:S(2)}) collective-permute-start(bf16[150,128]{1,0:T(8,128)(2,1)} %get-tuple-element.15), channel_id=1, source_target_pairs={{124,0},{125,1},{126,2},{127,3},{0,4},{1,5},{2,6},{3,7},{4,8},{5,9... | collective-permute-start | bytes 115208 | tf_op jit(solution)/shard_map/ppermute | solution.py:18
  8.4 0.0 collective-permute-start.1
  8.4 1.0 %collective-permute-start.2 = (bf16[150,128]{1,0:T(8,128)(2,1)}, bf16[150,128]{1,0:T(8,128)(2,1)S(1)}, u32[]{:S(2)}, u32[]{:S(2)}) collective-permute-start(bf16[150,128]{1,0:T(8,128)(2,1)} %get-tuple-element.17), channel_id=1, source_target_pairs={{126,0},{127,1},{0,2},{1,3},{2,4},{3,5},{4,6},{5,7},{6,8},{7,9},{8... | collective-permute-start | bytes 115208 | tf_op jit(solution)/shard_map/ppermute | solution.py:18
  9.4 2.2 %collective-permute-start.3 = (bf16[150,128]{1,0:T(8,128)(2,1)}, bf16[150,128]{1,0:T(8,128)(2,1)S(1)}, u32[]{:S(2)}, u32[]{:S(2)}) collective-permute-start(bf16[150,128]{1,0:T(8,128)(2,1)} %get-tuple-element.18), channel_id=1, source_target_pairs={{127,0},{0,1},{1,2},{2,3},{3,4},{4,5},{5,6},{6,7},{7,8},{8,9},{9,1... | collective-permute-start | bytes 115208 | tf_op jit(solution)/shard_map/ppermute | solution.py:18
  11.6 5.6 %collective-permute-start.4 = (bf16[150,128]{1,0:T(8,128)(2,1)}, bf16[150,128]{1,0:T(8,128)(2,1)S(1)}, u32[]{:S(2)}, u32[]{:S(2)}) collective-permute-start(bf16[150,128]{1,0:T(8,128)(2,1)} %get-tuple-element.19), channel_id=1, source_target_pairs={{1,0},{2,1},{3,2},{4,3},{5,4},{6,5},{7,6},{8,7},{9,8},{10,9},{11,1... | collective-permute-start | bytes 115208 | tf_op jit(solution)/shard_map/ppermute | solution.py:18
  17.2 0.7 %fusion = pred[1,1,8,128]{3,2,1,0:T(8,128)(4,1)S(1)} fusion(s32[8]{0:T(128)} %bitcast.26), kind=kLoop, calls=%fused_computation.4 | loop fusion | flops 1024 | bytes 1056
  17.9 0.3 copy.17
  18.2 0.9 %copy.15 = s32[1024,1]{1,0:T(8,128)S(1)} copy(s32[1024,1]{0,1:T(1,128)} %bitcast.21) | data formatting | bytes 8192 | tf_op jit(solution)/shard_map/squeeze | solution.py:125
  19.1 0.0 collective-permute-done.refs_0_
  19.1 0.0 copy-start.2
  19.1 0.6 collective-permute-start.5
  19.8 0.0 collective-permute-done.1.refs_1_
  19.8 0.0 copy-start.3
  19.8 0.3 collective-permute-start.6
  20.1 0.0 collective-permute-done.2.refs_2_
  20.1 0.0 copy-start.4
  20.1 4.0 %collective-permute-start.7 = (bf16[150,128]{1,0:T(8,128)(2,1)}, bf16[150,128]{1,0:T(8,128)(2,1)S(1)}, u32[]{:S(2)}, u32[]{:S(2)}) collective-permute-start(bf16[150,128]{1,0:T(8,128)(2,1)} %get-tuple-element.22), channel_id=1, source_target_pairs={{4,0},{5,1},{6,2},{7,3},{8,4},{9,5},{10,6},{11,7},{12,8},{13,9},{1... | collective-permute-start | bytes 115208 | tf_op jit(solution)/shard_map/ppermute | solution.py:18
  24.1 0.8 %bitcast_select_fusion.refs_8_ = s32[1024,1]{1,0:T(8,128)} fusion(s32[1024,1]{1,0:T(8,128)S(1)} %copy.15, pred[1,1024]{0,1:T(8,128)(4,1)S(1)} %copy.17), kind=kLoop, calls=%fused_computation | loop fusion | flops 1024 | bytes 9216 | tf_op jit(solution)/shard_map/jit(_where)/select_n | solution.py:125
  24.9 0.0 collective-permute-done.3.refs_3_
  24.9 0.0 copy-start.5
  24.9 0.0 collective-permute-done.4.refs_4_
  24.9 0.0 copy-start.6
  24.9 0.0 collective-permute-done.5.refs_5_
  25.0 0.0 copy-start.7
  25.0 0.0 collective-permute-done.6.refs_6_
  25.0 0.0 copy-start.8
  25.0 1.3 %collective-permute-done.7.refs_7_ = bf16[150,128]{1,0:T(8,128)(2,1)S(1)} collective-permute-done((bf16[150,128]{1,0:T(8,128)(2,1)}, bf16[150,128]{1,0:T(8,128)(2,1)S(1)}, u32[]{:S(2)}, u32[]{:S(2)}) %collective-permute-start.7) | collective-permute-done | bytes 38432 | tf_op jit(solution)/shard_map/ppermute | solution.py:18
  26.3 0.0 copy-start.9
  26.3 0.0 copy-done.2
  26.3 0.0 copy-done.3
  26.3 0.0 copy-done.4
  26.3 0.0 copy-done.5
  26.3 0.0 copy-done.6
  26.3 0.0 copy-done.7
  26.3 0.0 copy-done.8
  26.3 0.6 copy-done.9
  26.9 6.2 %shard_map.129 = (bf16[150,2048]{1,0:T(8,128)(2,1)}, bf16[150,2048]{1,0:T(8,128)(2,1)}) custom-call(s32[2,16]{1,0:T(2,128)} %bitcast.24, bf16[150,8192]{1,0:T(8,128)(2,1)} %mixing_ref.5, bf16[150,128]{1,0:T(8,128)(2,1)} %copy-done.2, bf16[150,128]{1,0:T(8,128)(2,1)} %copy-done.3, bf16[150,128]{1,0:T(8,128)(2,1)} %copy-done.4, bf16[150,128]{1,0:T(8,128)(2,1)} %copy-done.5, ...), custom_call_target="tpu_custom_call" | custom-call | tf_op jit(solution)/shard_map/pallas_call | solution.py:137
  33.1 0.2 collective-permute-start.8
  33.2 7.1 %collective-permute-start.9 = (bf16[150,2048]{1,0:T(8,128)(2,1)}, bf16[150,2048]{1,0:T(8,128)(2,1)S(1)}, u32[]{:S(2)}, u32[]{:S(2)}) collective-permute-start(bf16[150,2048]{1,0:T(8,128)(2,1)} %get-tuple-element.24), channel_id=1, source_target_pairs={{1,0},{2,1},{3,2},{4,3},{5,4},{6,5},{7,6},{8,7},{9,8},{10,9},{11,1... | collective-permute-start | bytes 1843208 | tf_op jit(solution)/shard_map/ppermute | solution.py:18
  40.3 0.0 copy-done.12
  40.3 0.0 copy-done.11
  40.3 0.0 copy-done.10
  40.3 0.7 pad_maximum_fusion.order_ref
  41.0 8.7 %shard_map.128.own_ref.migrated_hbm = bf16[150,8192]{1,0:T(8,128)(2,1)} custom-call(bf16[150,8192]{1,0:T(8,128)(2,1)} %mixing_ref.5, bf16[150,128]{1,0:T(8,128)(2,1)} %copy-done.2, bf16[150,128]{1,0:T(8,128)(2,1)} %copy-done.3, bf16[150,128]{1,0:T(8,128)(2,1)} %copy-done.4, bf16[150,128]{1,0:T(8,128)(2,1)} %copy-done.5, bf16[150,128]{1,0:T(8,128)(2,1)} %copy-done.6, ...), custom_call_target="tpu_custom_call" | custom-call | tf_op jit(solution)/shard_map/pallas_call | solution.py:142
  49.7 0.0 collective-permute-done.8.lower_hbm
  49.7 0.0 copy-start
  49.7 0.0 collective-permute-done.9.upper_hbm
  49.7 0.0 copy-start.1
  49.7 0.8 %copy-done = bf16[150,2048]{1,0:T(8,128)(2,1)} copy-done((bf16[150,2048]{1,0:T(8,128)(2,1)}, bf16[150,2048]{1,0:T(8,128)(2,1)S(1)}, u32[]{:S(2)}) %copy-start) | copy-done | bytes 614424
  50.5 0.2 copy-done.1
  50.7 19.3 %shard_map.130 = f32[150,8192]{1,0:T(8,128)} custom-call(s32[3,64]{1,0:T(4,128)} %bitcast.23, bf16[150,8192]{1,0:T(8,128)(2,1)} %shard_map.128.own_ref.migrated_hbm, bf16[64,4,128,128]{3,2,1,0:T(8,128)(2,1)} %weight_ref.1, f32[1,8192]{1,0:T(1,128)} %bitcast.18, f32[152,256]{1,0:T(8,128)} %pad_maximum_fusion.order_ref, f32[150,256]{1,0:T(8,128)} %prod_ref.1, ...), custom_call_target="tpu_custom_call" | custom-call | tf_op jit(solution)/shard_map/pallas_call | solution.py:338
  (2 shorter events, 0.0 us)
Async XLA Ops:
  0.0 40.3 %copy-start.12 = (f32[256]{0:T(256)S(1)}, f32[256]{0:T(256)}, u32[]{:S(2)}) copy-start(f32[256]{0:T(256)} %param.23) | copy-start | bytes 3076
  0.0 40.3 %copy-start.11 = (f32[256]{0:T(256)S(1)}, f32[256]{0:T(256)}, u32[]{:S(2)}) copy-start(f32[256]{0:T(256)} %param.22) | copy-start | bytes 3076
  0.0 40.3 %copy-start.10 = (f32[256,150]{0,1:T(8,128)S(1)}, f32[256,150]{0,1:T(8,128)}, u32[]{:S(2)}) copy-start(f32[256,150]{0,1:T(8,128)} %param.21) | copy-start | bytes 460804
  5.3 13.8 %collective-permute-start = (bf16[150,128]{1,0:T(8,128)(2,1)}, bf16[150,128]{1,0:T(8,128)(2,1)S(1)}, u32[]{:S(2)}, u32[]{:S(2)}) collective-permute-start(bf16[150,128]{1,0:T(8,128)(2,1)} %get-tuple-element.15), channel_id=1, source_target_pairs={{124,0},{125,1},{126,2},{127,3},{0,4},{1,5},{2,6},{3,7},{4,8},{5,9... | collective-permute-start | bytes 115208 | tf_op jit(solution)/shard_map/ppermute | solution.py:18
  8.4 11.4 %collective-permute-start.1 = (bf16[150,128]{1,0:T(8,128)(2,1)}, bf16[150,128]{1,0:T(8,128)(2,1)S(1)}, u32[]{:S(2)}, u32[]{:S(2)}) collective-permute-start(bf16[150,128]{1,0:T(8,128)(2,1)} %get-tuple-element.16), channel_id=1, source_target_pairs={{125,0},{126,1},{127,2},{0,3},{1,4},{2,5},{3,6},{4,7},{5,8},{6,9},... | collective-permute-start | bytes 115208 | tf_op jit(solution)/shard_map/ppermute | solution.py:18
  8.4 11.7 %collective-permute-start.2 = (bf16[150,128]{1,0:T(8,128)(2,1)}, bf16[150,128]{1,0:T(8,128)(2,1)S(1)}, u32[]{:S(2)}, u32[]{:S(2)}) collective-permute-start(bf16[150,128]{1,0:T(8,128)(2,1)} %get-tuple-element.17), channel_id=1, source_target_pairs={{126,0},{127,1},{0,2},{1,3},{2,4},{3,5},{4,6},{5,7},{6,8},{7,9},{8... | collective-permute-start | bytes 115208 | tf_op jit(solution)/shard_map/ppermute | solution.py:18
  9.4 15.5 %collective-permute-start.3 = (bf16[150,128]{1,0:T(8,128)(2,1)}, bf16[150,128]{1,0:T(8,128)(2,1)S(1)}, u32[]{:S(2)}, u32[]{:S(2)}) collective-permute-start(bf16[150,128]{1,0:T(8,128)(2,1)} %get-tuple-element.18), channel_id=1, source_target_pairs={{127,0},{0,1},{1,2},{2,3},{3,4},{4,5},{5,6},{6,7},{7,8},{8,9},{9,1... | collective-permute-start | bytes 115208 | tf_op jit(solution)/shard_map/ppermute | solution.py:18
  11.6 13.3 %collective-permute-start.4 = (bf16[150,128]{1,0:T(8,128)(2,1)}, bf16[150,128]{1,0:T(8,128)(2,1)S(1)}, u32[]{:S(2)}, u32[]{:S(2)}) collective-permute-start(bf16[150,128]{1,0:T(8,128)(2,1)} %get-tuple-element.19), channel_id=1, source_target_pairs={{1,0},{2,1},{3,2},{4,3},{5,4},{6,5},{7,6},{8,7},{9,8},{10,9},{11,1... | collective-permute-start | bytes 115208 | tf_op jit(solution)/shard_map/ppermute | solution.py:18
  19.1 7.2 %copy-start.2 = (bf16[150,128]{1,0:T(8,128)(2,1)}, bf16[150,128]{1,0:T(8,128)(2,1)S(1)}, u32[]{:S(2)}) copy-start(bf16[150,128]{1,0:T(8,128)(2,1)S(1)} %collective-permute-done.refs_0_) | copy-start | bytes 115204
  19.1 5.8 %collective-permute-start.5 = (bf16[150,128]{1,0:T(8,128)(2,1)}, bf16[150,128]{1,0:T(8,128)(2,1)S(1)}, u32[]{:S(2)}, u32[]{:S(2)}) collective-permute-start(bf16[150,128]{1,0:T(8,128)(2,1)} %get-tuple-element.20), channel_id=1, source_target_pairs={{2,0},{3,1},{4,2},{5,3},{6,4},{7,5},{8,6},{9,7},{10,8},{11,9},{12,... | collective-permute-start | bytes 115208 | tf_op jit(solution)/shard_map/ppermute | solution.py:18
  19.8 6.5 %copy-start.3 = (bf16[150,128]{1,0:T(8,128)(2,1)}, bf16[150,128]{1,0:T(8,128)(2,1)S(1)}, u32[]{:S(2)}) copy-start(bf16[150,128]{1,0:T(8,128)(2,1)S(1)} %collective-permute-done.1.refs_1_) | copy-start | bytes 115204
  19.8 5.2 %collective-permute-start.6 = (bf16[150,128]{1,0:T(8,128)(2,1)}, bf16[150,128]{1,0:T(8,128)(2,1)S(1)}, u32[]{:S(2)}, u32[]{:S(2)}) collective-permute-start(bf16[150,128]{1,0:T(8,128)(2,1)} %get-tuple-element.21), channel_id=1, source_target_pairs={{3,0},{4,1},{5,2},{6,3},{7,4},{8,5},{9,6},{10,7},{11,8},{12,9},{13... | collective-permute-start | bytes 115208 | tf_op jit(solution)/shard_map/ppermute | solution.py:18
  20.1 6.2 %copy-start.4 = (bf16[150,128]{1,0:T(8,128)(2,1)}, bf16[150,128]{1,0:T(8,128)(2,1)S(1)}, u32[]{:S(2)}) copy-start(bf16[150,128]{1,0:T(8,128)(2,1)S(1)} %collective-permute-done.2.refs_2_) | copy-start | bytes 115204
  20.1 6.2 %collective-permute-start.7 = (bf16[150,128]{1,0:T(8,128)(2,1)}, bf16[150,128]{1,0:T(8,128)(2,1)S(1)}, u32[]{:S(2)}, u32[]{:S(2)}) collective-permute-start(bf16[150,128]{1,0:T(8,128)(2,1)} %get-tuple-element.22), channel_id=1, source_target_pairs={{4,0},{5,1},{6,2},{7,3},{8,4},{9,5},{10,6},{11,7},{12,8},{13,9},{1... | collective-permute-start | bytes 115208 | tf_op jit(solution)/shard_map/ppermute | solution.py:18
  24.9 1.4 %copy-start.5 = (bf16[150,128]{1,0:T(8,128)(2,1)}, bf16[150,128]{1,0:T(8,128)(2,1)S(1)}, u32[]{:S(2)}) copy-start(bf16[150,128]{1,0:T(8,128)(2,1)S(1)} %collective-permute-done.3.refs_3_) | copy-start | bytes 115204
  24.9 1.4 %copy-start.6 = (bf16[150,128]{1,0:T(8,128)(2,1)}, bf16[150,128]{1,0:T(8,128)(2,1)S(1)}, u32[]{:S(2)}) copy-start(bf16[150,128]{1,0:T(8,128)(2,1)S(1)} %collective-permute-done.4.refs_4_) | copy-start | bytes 115204
  25.0 1.4 %copy-start.7 = (bf16[150,128]{1,0:T(8,128)(2,1)}, bf16[150,128]{1,0:T(8,128)(2,1)S(1)}, u32[]{:S(2)}) copy-start(bf16[150,128]{1,0:T(8,128)(2,1)S(1)} %collective-permute-done.5.refs_5_) | copy-start | bytes 115204
  25.0 1.4 %copy-start.8 = (bf16[150,128]{1,0:T(8,128)(2,1)}, bf16[150,128]{1,0:T(8,128)(2,1)S(1)}, u32[]{:S(2)}) copy-start(bf16[150,128]{1,0:T(8,128)(2,1)S(1)} %collective-permute-done.6.refs_6_) | copy-start | bytes 115204
  26.3 0.6 copy-start.9
  33.1 16.6 %collective-permute-start.8 = (bf16[150,2048]{1,0:T(8,128)(2,1)}, bf16[150,2048]{1,0:T(8,128)(2,1)S(1)}, u32[]{:S(2)}, u32[]{:S(2)}) collective-permute-start(bf16[150,2048]{1,0:T(8,128)(2,1)} %get-tuple-element.23), channel_id=1, source_target_pairs={{127,0},{0,1},{1,2},{2,3},{3,4},{4,5},{5,6},{6,7},{7,8},{8,9},{9,1... | collective-permute-start | bytes 1843208 | tf_op jit(solution)/shard_map/ppermute | solution.py:18
  33.2 16.4 %collective-permute-start.9 = (bf16[150,2048]{1,0:T(8,128)(2,1)}, bf16[150,2048]{1,0:T(8,128)(2,1)S(1)}, u32[]{:S(2)}, u32[]{:S(2)}) collective-permute-start(bf16[150,2048]{1,0:T(8,128)(2,1)} %get-tuple-element.24), channel_id=1, source_target_pairs={{1,0},{2,1},{3,2},{4,3},{5,4},{6,5},{7,6},{8,7},{9,8},{10,9},{11,1... | collective-permute-start | bytes 1843208 | tf_op jit(solution)/shard_map/ppermute | solution.py:18
  49.7 0.8 %copy-start = (bf16[150,2048]{1,0:T(8,128)(2,1)}, bf16[150,2048]{1,0:T(8,128)(2,1)S(1)}, u32[]{:S(2)}) copy-start(bf16[150,2048]{1,0:T(8,128)(2,1)S(1)} %collective-permute-done.8.lower_hbm) | copy-start | bytes 1843204
  49.7 1.0 %copy-start.1 = (bf16[150,2048]{1,0:T(8,128)(2,1)}, bf16[150,2048]{1,0:T(8,128)(2,1)S(1)}, u32[]{:S(2)}) copy-start(bf16[150,2048]{1,0:T(8,128)(2,1)S(1)} %collective-permute-done.9.upper_hbm) | copy-start | bytes 1843204

commit v17 on v14

--- a/solution.py
+++ b/solution.py
@@ -82,8 +82,6 @@
     marked = marked_arrivals(received_refs, slots.shape[0])
     lane = lax.broadcasted_iota(jnp.int32, (1, block_size), 1)
     per_chunk = chunk // block_size
-    for copy in copies:
-        copy.wait()
     for side in range(sides):
         for part in range(listed // per_chunk):
             first = part * per_chunk
@@ -95,6 +93,9 @@
             placed = jnp.dot(marked, place, preferred_element_type=jnp.float32)
             hit = placed[species:species + 1]
             lanes = slice(first * block_size, (first + per_chunk) * block_size)
+            if side == 0 and part == 0:
+                for copy in copies:
+                    copy.wait()
             outs[side][:, lanes] = jnp.where(
                 hit > 0.5, placed[:species].astype(outs[side].dtype), outs[side][:, lanes]
             )

time: 69.4 us -> 69.4 us (level)
  no operation moved by 1% of the time
where the time goes in v17:
time: 69.4 us; the launch traced here: 68.9 us
  Pallas kernels  37.5 us (54%)
  starting transfers between devices  24.1 us (35%)
  local copies, waits for them, and re-layouts  2.83 us (4%)
  other arithmetic  2.25 us (3%)
  waiting for transfers between devices  1.92 us (3%)
    ppermute x10, starting transfers between devices, from_behind(): return lax.ppermute(block, axis, route)  24.1 us
    pallas_call x1, Pallas kernels, mix_react(): pl.pallas_call(kernel, grid_spec=grid_spec, out_shape=jax.ShapeDtypeStruc...  19.3 us
    pallas_call x1, Pallas kernels, migrate(): pl.pallas_call(functools.partial(place_kernel, chunk, peer_count), grid=(...  6.84 us
    pallas_call x1, Pallas kernels, migrate(): pl.pallas_call(functools.partial(halo_kernel, chunk, block_size, peer_cou...  6.15 us
    pallas_call x1, Pallas kernels, migrate(): pl.pallas_call(functools.partial(pick_kernel, chunk), grid=(1,), in_specs...  5.28 us
    unnamed x28, local copies, waits for them, and re-layouts  1.92 us
    ppermute x10, waiting for transfers between devices, from_behind(): return lax.ppermute(block, axis, route)  1.92 us
  transfers between devices with their start and end apart: 10, of which 2 were waited for; matrix products, arithmetic and copies ran while one was open for 5% of the time, Pallas kernels for 10%

profile of v17, /device:TPU:0, one launch (start us, length us, event | category | flops | bytes accessed | tf_op | source)
XLA Modules:
  0.0 68.9 jit_solution(5165009111459963626)
XLA Ops:
  0.0 0.0 copy-start.12
  0.0 0.0 copy-start.11
  0.0 0.0 copy-start.10
  0.0 5.3 %shard_map.127 = (bf16[150,128]{1,0:T(8,128)(2,1)}, bf16[150,128]{1,0:T(8,128)(2,1)}, bf16[150,128]{1,0:T(8,128)(2,1)}, bf16[150,128]{1,0:T(8,128)(2,1)}, bf16[1...) custom-call(bf16[150,8192]{1,0:T(8,128)(2,1)} %mixing_ref.5, ...), custom_call_target="tpu_custom_call" | custom-call | tf_op jit(solution)/shard_map/pallas_call | solution.py:115
  5.3 3.1 %collective-permute-start = (bf16[150,128]{1,0:T(8,128)(2,1)}, bf16[150,128]{1,0:T(8,128)(2,1)S(1)}, u32[]{:S(2)}, u32[]{:S(2)}) collective-permute-start(bf16[150,128]{1,0:T(8,128)(2,1)} %get-tuple-element.15), channel_id=1, source_target_pairs={{124,0},{125,1},{126,2},{127,3},{0,4},{1,5},{2,6},{3,7},{4,8},{5,9... | collective-permute-start | bytes 115208 | tf_op jit(solution)/shard_map/ppermute | solution.py:18
  8.4 0.0 collective-permute-start.1
  8.4 1.0 %collective-permute-start.2 = (bf16[150,128]{1,0:T(8,128)(2,1)}, bf16[150,128]{1,0:T(8,128)(2,1)S(1)}, u32[]{:S(2)}, u32[]{:S(2)}) collective-permute-start(bf16[150,128]{1,0:T(8,128)(2,1)} %get-tuple-element.17), channel_id=1, source_target_pairs={{126,0},{127,1},{0,2},{1,3},{2,4},{3,5},{4,6},{5,7},{6,8},{7,9},{8... | collective-permute-start | bytes 115208 | tf_op jit(solution)/shard_map/ppermute | solution.py:18
  9.4 2.2 %collective-permute-start.3 = (bf16[150,128]{1,0:T(8,128)(2,1)}, bf16[150,128]{1,0:T(8,128)(2,1)S(1)}, u32[]{:S(2)}, u32[]{:S(2)}) collective-permute-start(bf16[150,128]{1,0:T(8,128)(2,1)} %get-tuple-element.18), channel_id=1, source_target_pairs={{127,0},{0,1},{1,2},{2,3},{3,4},{4,5},{5,6},{6,7},{7,8},{8,9},{9,1... | collective-permute-start | bytes 115208 | tf_op jit(solution)/shard_map/ppermute | solution.py:18
  11.6 5.6 %collective-permute-start.4 = (bf16[150,128]{1,0:T(8,128)(2,1)}, bf16[150,128]{1,0:T(8,128)(2,1)S(1)}, u32[]{:S(2)}, u32[]{:S(2)}) collective-permute-start(bf16[150,128]{1,0:T(8,128)(2,1)} %get-tuple-element.19), channel_id=1, source_target_pairs={{1,0},{2,1},{3,2},{4,3},{5,4},{6,5},{7,6},{8,7},{9,8},{10,9},{11,1... | collective-permute-start | bytes 115208 | tf_op jit(solution)/shard_map/ppermute | solution.py:18
  17.2 0.7 %fusion = pred[1,1,8,128]{3,2,1,0:T(8,128)(4,1)S(1)} fusion(s32[8]{0:T(128)} %bitcast.26), kind=kLoop, calls=%fused_computation.4 | loop fusion | flops 1024 | bytes 1056
  17.9 0.3 copy.17
  18.2 0.9 %copy.15 = s32[1024,1]{1,0:T(8,128)S(1)} copy(s32[1024,1]{0,1:T(1,128)} %bitcast.21) | data formatting | bytes 8192 | tf_op jit(solution)/shard_map/squeeze | solution.py:128
  19.1 0.0 collective-permute-done.refs_0_
  19.1 0.0 copy-start.2
  19.1 0.6 collective-permute-start.5
  19.8 0.0 collective-permute-done.1.refs_1_
  19.8 0.0 copy-start.3
  19.8 0.3 collective-permute-start.6
  20.1 0.0 collective-permute-done.2.refs_2_
  20.1 0.0 copy-start.4
  20.1 4.0 %collective-permute-start.7 = (bf16[150,128]{1,0:T(8,128)(2,1)}, bf16[150,128]{1,0:T(8,128)(2,1)S(1)}, u32[]{:S(2)}, u32[]{:S(2)}) collective-permute-start(bf16[150,128]{1,0:T(8,128)(2,1)} %get-tuple-element.22), channel_id=1, source_target_pairs={{4,0},{5,1},{6,2},{7,3},{8,4},{9,5},{10,6},{11,7},{12,8},{13,9},{1... | collective-permute-start | bytes 115208 | tf_op jit(solution)/shard_map/ppermute | solution.py:18
  24.1 0.8 %bitcast_select_fusion.refs_8_ = s32[1024,1]{1,0:T(8,128)} fusion(s32[1024,1]{1,0:T(8,128)S(1)} %copy.15, pred[1,1024]{0,1:T(8,128)(4,1)S(1)} %copy.17), kind=kLoop, calls=%fused_computation | loop fusion | flops 1024 | bytes 9216 | tf_op jit(solution)/shard_map/jit(_where)/select_n | solution.py:128
  24.9 0.0 collective-permute-done.3.refs_3_
  24.9 0.0 copy-start.5
  24.9 0.0 collective-permute-done.4.refs_4_
  24.9 0.0 copy-start.6
  24.9 0.0 collective-permute-done.5.refs_5_
  25.0 0.0 copy-start.7
  25.0 0.0 collective-permute-done.6.refs_6_
  25.0 0.0 copy-start.8
  25.0 1.3 %collective-permute-done.7.refs_7_ = bf16[150,128]{1,0:T(8,128)(2,1)S(1)} collective-permute-done((bf16[150,128]{1,0:T(8,128)(2,1)}, bf16[150,128]{1,0:T(8,128)(2,1)S(1)}, u32[]{:S(2)}, u32[]{:S(2)}) %collective-permute-start.7) | collective-permute-done | bytes 38432 | tf_op jit(solution)/shard_map/ppermute | solution.py:18
  26.3 0.0 copy-start.9
  26.3 0.0 copy-done.2
  26.3 0.0 copy-done.3
  26.3 0.0 copy-done.4
  26.3 0.0 copy-done.5
  26.3 0.0 copy-done.6
  26.3 0.0 copy-done.7
  26.3 0.0 copy-done.8
  26.3 0.6 copy-done.9
  26.9 6.2 %shard_map.129 = (bf16[150,2048]{1,0:T(8,128)(2,1)}, bf16[150,2048]{1,0:T(8,128)(2,1)}) custom-call(s32[2,16]{1,0:T(2,128)} %bitcast.24, bf16[150,8192]{1,0:T(8,128)(2,1)} %mixing_ref.5, bf16[150,128]{1,0:T(8,128)(2,1)} %copy-done.2, bf16[150,128]{1,0:T(8,128)(2,1)} %copy-done.3, bf16[150,128]{1,0:T(8,128)(2,1)} %copy-done.4, bf16[150,128]{1,0:T(8,128)(2,1)} %copy-done.5, ...), custom_call_target="tpu_custom_call" | custom-call | tf_op jit(solution)/shard_map/pallas_call | solution.py:140
  33.1 0.2 collective-permute-start.8
  33.2 7.1 %collective-permute-start.9 = (bf16[150,2048]{1,0:T(8,128)(2,1)}, bf16[150,2048]{1,0:T(8,128)(2,1)S(1)}, u32[]{:S(2)}, u32[]{:S(2)}) collective-permute-start(bf16[150,2048]{1,0:T(8,128)(2,1)} %get-tuple-element.24), channel_id=1, source_target_pairs={{1,0},{2,1},{3,2},{4,3},{5,4},{6,5},{7,6},{8,7},{9,8},{10,9},{11,1... | collective-permute-start | bytes 1843208 | tf_op jit(solution)/shard_map/ppermute | solution.py:18
  40.3 0.0 copy-done.12
  40.3 0.0 copy-done.11
  40.3 0.0 copy-done.10
  40.3 0.7 pad_maximum_fusion.order_ref
  41.0 6.8 %shard_map.128.own_ref.migrated_hbm = bf16[150,8192]{1,0:T(8,128)(2,1)} custom-call(bf16[150,8192]{1,0:T(8,128)(2,1)} %mixing_ref.5, bf16[150,128]{1,0:T(8,128)(2,1)} %copy-done.2, bf16[150,128]{1,0:T(8,128)(2,1)} %copy-done.3, bf16[150,128]{1,0:T(8,128)(2,1)} %copy-done.4, bf16[150,128]{1,0:T(8,128)(2,1)} %copy-done.5, bf16[150,128]{1,0:T(8,128)(2,1)} %copy-done.6, ...), custom_call_target="tpu_custom_call" | custom-call | tf_op jit(solution)/shard_map/pallas_call | solution.py:145
  47.8 0.6 collective-permute-done.8.lower_hbm
  48.4 0.0 copy-start
  48.4 0.0 collective-permute-done.9.upper_hbm
  48.4 0.0 copy-start.1
  48.4 0.8 %copy-done = bf16[150,2048]{1,0:T(8,128)(2,1)} copy-done((bf16[150,2048]{1,0:T(8,128)(2,1)}, bf16[150,2048]{1,0:T(8,128)(2,1)S(1)}, u32[]{:S(2)}) %copy-start) | copy-done | bytes 614424
  49.3 0.2 copy-done.1
  49.5 19.3 %shard_map.130 = f32[150,8192]{1,0:T(8,128)} custom-call(s32[3,64]{1,0:T(4,128)} %bitcast.23, bf16[150,8192]{1,0:T(8,128)(2,1)} %shard_map.128.own_ref.migrated_hbm, bf16[64,4,128,128]{3,2,1,0:T(8,128)(2,1)} %weight_ref.1, f32[1,8192]{1,0:T(1,128)} %bitcast.18, f32[152,256]{1,0:T(8,128)} %pad_maximum_fusion.order_ref, f32[150,256]{1,0:T(8,128)} %prod_ref.1, ...), custom_call_target="tpu_custom_call" | custom-call | tf_op jit(solution)/shard_map/pallas_call | solution.py:341
  (2 shorter events, 0.0 us)
Async XLA Ops:
  0.0 40.3 %copy-start.12 = (f32[256]{0:T(256)S(1)}, f32[256]{0:T(256)}, u32[]{:S(2)}) copy-start(f32[256]{0:T(256)} %param.23) | copy-start | bytes 3076
  0.0 40.3 %copy-start.11 = (f32[256]{0:T(256)S(1)}, f32[256]{0:T(256)}, u32[]{:S(2)}) copy-start(f32[256]{0:T(256)} %param.22) | copy-start | bytes 3076
  0.0 40.3 %copy-start.10 = (f32[256,150]{0,1:T(8,128)S(1)}, f32[256,150]{0,1:T(8,128)}, u32[]{:S(2)}) copy-start(f32[256,150]{0,1:T(8,128)} %param.21) | copy-start | bytes 460804
  5.3 13.8 %collective-permute-start = (bf16[150,128]{1,0:T(8,128)(2,1)}, bf16[150,128]{1,0:T(8,128)(2,1)S(1)}, u32[]{:S(2)}, u32[]{:S(2)}) collective-permute-start(bf16[150,128]{1,0:T(8,128)(2,1)} %get-tuple-element.15), channel_id=1, source_target_pairs={{124,0},{125,1},{126,2},{127,3},{0,4},{1,5},{2,6},{3,7},{4,8},{5,9... | collective-permute-start | bytes 115208 | tf_op jit(solution)/shard_map/ppermute | solution.py:18
  8.4 11.4 %collective-permute-start.1 = (bf16[150,128]{1,0:T(8,128)(2,1)}, bf16[150,128]{1,0:T(8,128)(2,1)S(1)}, u32[]{:S(2)}, u32[]{:S(2)}) collective-permute-start(bf16[150,128]{1,0:T(8,128)(2,1)} %get-tuple-element.16), channel_id=1, source_target_pairs={{125,0},{126,1},{127,2},{0,3},{1,4},{2,5},{3,6},{4,7},{5,8},{6,9},... | collective-permute-start | bytes 115208 | tf_op jit(solution)/shard_map/ppermute | solution.py:18
  8.4 11.7 %collective-permute-start.2 = (bf16[150,128]{1,0:T(8,128)(2,1)}, bf16[150,128]{1,0:T(8,128)(2,1)S(1)}, u32[]{:S(2)}, u32[]{:S(2)}) collective-permute-start(bf16[150,128]{1,0:T(8,128)(2,1)} %get-tuple-element.17), channel_id=1, source_target_pairs={{126,0},{127,1},{0,2},{1,3},{2,4},{3,5},{4,6},{5,7},{6,8},{7,9},{8... | collective-permute-start | bytes 115208 | tf_op jit(solution)/shard_map/ppermute | solution.py:18
  9.4 15.5 %collective-permute-start.3 = (bf16[150,128]{1,0:T(8,128)(2,1)}, bf16[150,128]{1,0:T(8,128)(2,1)S(1)}, u32[]{:S(2)}, u32[]{:S(2)}) collective-permute-start(bf16[150,128]{1,0:T(8,128)(2,1)} %get-tuple-element.18), channel_id=1, source_target_pairs={{127,0},{0,1},{1,2},{2,3},{3,4},{4,5},{5,6},{6,7},{7,8},{8,9},{9,1... | collective-permute-start | bytes 115208 | tf_op jit(solution)/shard_map/ppermute | solution.py:18
  11.6 13.3 %collective-permute-start.4 = (bf16[150,128]{1,0:T(8,128)(2,1)}, bf16[150,128]{1,0:T(8,128)(2,1)S(1)}, u32[]{:S(2)}, u32[]{:S(2)}) collective-permute-start(bf16[150,128]{1,0:T(8,128)(2,1)} %get-tuple-element.19), channel_id=1, source_target_pairs={{1,0},{2,1},{3,2},{4,3},{5,4},{6,5},{7,6},{8,7},{9,8},{10,9},{11,1... | collective-permute-start | bytes 115208 | tf_op jit(solution)/shard_map/ppermute | solution.py:18
  19.1 7.2 %copy-start.2 = (bf16[150,128]{1,0:T(8,128)(2,1)}, bf16[150,128]{1,0:T(8,128)(2,1)S(1)}, u32[]{:S(2)}) copy-start(bf16[150,128]{1,0:T(8,128)(2,1)S(1)} %collective-permute-done.refs_0_) | copy-start | bytes 115204
  19.1 5.8 %collective-permute-start.5 = (bf16[150,128]{1,0:T(8,128)(2,1)}, bf16[150,128]{1,0:T(8,128)(2,1)S(1)}, u32[]{:S(2)}, u32[]{:S(2)}) collective-permute-start(bf16[150,128]{1,0:T(8,128)(2,1)} %get-tuple-element.20), channel_id=1, source_target_pairs={{2,0},{3,1},{4,2},{5,3},{6,4},{7,5},{8,6},{9,7},{10,8},{11,9},{12,... | collective-permute-start | bytes 115208 | tf_op jit(solution)/shard_map/ppermute | solution.py:18
  19.8 6.5 %copy-start.3 = (bf16[150,128]{1,0:T(8,128)(2,1)}, bf16[150,128]{1,0:T(8,128)(2,1)S(1)}, u32[]{:S(2)}) copy-start(bf16[150,128]{1,0:T(8,128)(2,1)S(1)} %collective-permute-done.1.refs_1_) | copy-start | bytes 115204
  19.8 5.2 %collective-permute-start.6 = (bf16[150,128]{1,0:T(8,128)(2,1)}, bf16[150,128]{1,0:T(8,128)(2,1)S(1)}, u32[]{:S(2)}, u32[]{:S(2)}) collective-permute-start(bf16[150,128]{1,0:T(8,128)(2,1)} %get-tuple-element.21), channel_id=1, source_target_pairs={{3,0},{4,1},{5,2},{6,3},{7,4},{8,5},{9,6},{10,7},{11,8},{12,9},{13... | collective-permute-start | bytes 115208 | tf_op jit(solution)/shard_map/ppermute | solution.py:18
  20.1 6.2 %copy-start.4 = (bf16[150,128]{1,0:T(8,128)(2,1)}, bf16[150,128]{1,0:T(8,128)(2,1)S(1)}, u32[]{:S(2)}) copy-start(bf16[150,128]{1,0:T(8,128)(2,1)S(1)} %collective-permute-done.2.refs_2_) | copy-start | bytes 115204
  20.1 6.2 %collective-permute-start.7 = (bf16[150,128]{1,0:T(8,128)(2,1)}, bf16[150,128]{1,0:T(8,128)(2,1)S(1)}, u32[]{:S(2)}, u32[]{:S(2)}) collective-permute-start(bf16[150,128]{1,0:T(8,128)(2,1)} %get-tuple-element.22), channel_id=1, source_target_pairs={{4,0},{5,1},{6,2},{7,3},{8,4},{9,5},{10,6},{11,7},{12,8},{13,9},{1... | collective-permute-start | bytes 115208 | tf_op jit(solution)/shard_map/ppermute | solution.py:18
  24.9 1.4 %copy-start.5 = (bf16[150,128]{1,0:T(8,128)(2,1)}, bf16[150,128]{1,0:T(8,128)(2,1)S(1)}, u32[]{:S(2)}) copy-start(bf16[150,128]{1,0:T(8,128)(2,1)S(1)} %collective-permute-done.3.refs_3_) | copy-start | bytes 115204
  24.9 1.4 %copy-start.6 = (bf16[150,128]{1,0:T(8,128)(2,1)}, bf16[150,128]{1,0:T(8,128)(2,1)S(1)}, u32[]{:S(2)}) copy-start(bf16[150,128]{1,0:T(8,128)(2,1)S(1)} %collective-permute-done.4.refs_4_) | copy-start | bytes 115204
  25.0 1.4 %copy-start.7 = (bf16[150,128]{1,0:T(8,128)(2,1)}, bf16[150,128]{1,0:T(8,128)(2,1)S(1)}, u32[]{:S(2)}) copy-start(bf16[150,128]{1,0:T(8,128)(2,1)S(1)} %collective-permute-done.5.refs_5_) | copy-start | bytes 115204
  25.0 1.4 %copy-start.8 = (bf16[150,128]{1,0:T(8,128)(2,1)}, bf16[150,128]{1,0:T(8,128)(2,1)S(1)}, u32[]{:S(2)}) copy-start(bf16[150,128]{1,0:T(8,128)(2,1)S(1)} %collective-permute-done.6.refs_6_) | copy-start | bytes 115204
  26.3 0.6 copy-start.9
  33.1 15.4 %collective-permute-start.8 = (bf16[150,2048]{1,0:T(8,128)(2,1)}, bf16[150,2048]{1,0:T(8,128)(2,1)S(1)}, u32[]{:S(2)}, u32[]{:S(2)}) collective-permute-start(bf16[150,2048]{1,0:T(8,128)(2,1)} %get-tuple-element.23), channel_id=1, source_target_pairs={{127,0},{0,1},{1,2},{2,3},{3,4},{4,5},{5,6},{6,7},{7,8},{8,9},{9,1... | collective-permute-start | bytes 1843208 | tf_op jit(solution)/shard_map/ppermute | solution.py:18
  33.2 15.2 %collective-permute-start.9 = (bf16[150,2048]{1,0:T(8,128)(2,1)}, bf16[150,2048]{1,0:T(8,128)(2,1)S(1)}, u32[]{:S(2)}, u32[]{:S(2)}) collective-permute-start(bf16[150,2048]{1,0:T(8,128)(2,1)} %get-tuple-element.24), channel_id=1, source_target_pairs={{1,0},{2,1},{3,2},{4,3},{5,4},{6,5},{7,6},{8,7},{9,8},{10,9},{11,1... | collective-permute-start | bytes 1843208 | tf_op jit(solution)/shard_map/ppermute | solution.py:18
  48.4 0.8 %copy-start = (bf16[150,2048]{1,0:T(8,128)(2,1)}, bf16[150,2048]{1,0:T(8,128)(2,1)S(1)}, u32[]{:S(2)}) copy-start(bf16[150,2048]{1,0:T(8,128)(2,1)S(1)} %collective-permute-done.8.lower_hbm) | copy-start | bytes 1843204
  48.4 1.0 %copy-start.1 = (bf16[150,2048]{1,0:T(8,128)(2,1)}, bf16[150,2048]{1,0:T(8,128)(2,1)S(1)}, u32[]{:S(2)}) copy-start(bf16[150,2048]{1,0:T(8,128)(2,1)S(1)} %collective-permute-done.9.upper_hbm) | copy-start | bytes 1843204

commit v18 on v14

--- a/solution.py
+++ b/solution.py
@@ -9,7 +9,7 @@
 
 HOP = 4
 TILE_BLOCKS = 16
-PAD_ROWS = 160
+PAD_ROWS = 152
 
 
 def from_behind(block, axis, distance):

time: 69.4 us -> 70.3 us (1.013)
  Pallas kernels: 37.5 us -> 38.5 us
    pallas_call x1, Pallas kernels: 19.2 us -> 20.2 us  [mix_react(): pl.pallas_call(kernel, grid_spec=grid_spec, out_shape=jax.ShapeDtypeStruc...]
where the time goes in v18:
time: 70.3 us; the launch traced here: 69.8 us
  Pallas kernels  38.5 us (55%)
  starting transfers between devices  24.1 us (34%)
  local copies, waits for them, and re-layouts  2.83 us (4%)
  other arithmetic  2.25 us (3%)
  waiting for transfers between devices  1.93 us (3%)
    ppermute x10, starting transfers between devices, from_behind(): return lax.ppermute(block, axis, route)  24.1 us
    pallas_call x1, Pallas kernels, mix_react(): pl.pallas_call(kernel, grid_spec=grid_spec, out_shape=jax.ShapeDtypeStruc...  20.2 us
    pallas_call x1, Pallas kernels, migrate(): pl.pallas_call(functools.partial(place_kernel, chunk, peer_count), grid=(...  6.84 us
    pallas_call x1, Pallas kernels, migrate(): pl.pallas_call(functools.partial(halo_kernel, chunk, block_size, peer_cou...  6.17 us
    pallas_call x1, Pallas kernels, migrate(): pl.pallas_call(functools.partial(pick_kernel, chunk), grid=(1,), in_specs...  5.28 us
    ppermute x10, waiting for transfers between devices, from_behind(): return lax.ppermute(block, axis, route)  1.93 us
    unnamed x28, local copies, waits for them, and re-layouts  1.92 us
  transfers between devices with their start and end apart: 10, of which 2 were waited for; matrix products, arithmetic and copies ran while one was open for 5% of the time, Pallas kernels for 10%

profile of v18, /device:TPU:0, one launch (start us, length us, event | category | flops | bytes accessed | tf_op | source)
XLA Modules:
  0.0 69.8 jit_solution(12668068947810783105)
XLA Ops:
  0.0 0.0 copy-start.12
  0.0 0.0 copy-start.11
  0.0 0.0 copy-start.10
  0.0 5.3 %shard_map.127 = (bf16[150,128]{1,0:T(8,128)(2,1)}, bf16[150,128]{1,0:T(8,128)(2,1)}, bf16[150,128]{1,0:T(8,128)(2,1)}, bf16[150,128]{1,0:T(8,128)(2,1)}, bf16[1...) custom-call(bf16[150,8192]{1,0:T(8,128)(2,1)} %mixing_ref.5, ...), custom_call_target="tpu_custom_call" | custom-call | tf_op jit(solution)/shard_map/pallas_call | solution.py:114
  5.3 3.1 %collective-permute-start = (bf16[150,128]{1,0:T(8,128)(2,1)}, bf16[150,128]{1,0:T(8,128)(2,1)S(1)}, u32[]{:S(2)}, u32[]{:S(2)}) collective-permute-start(bf16[150,128]{1,0:T(8,128)(2,1)} %get-tuple-element.15), channel_id=1, source_target_pairs={{124,0},{125,1},{126,2},{127,3},{0,4},{1,5},{2,6},{3,7},{4,8},{5,9... | collective-permute-start | bytes 115208 | tf_op jit(solution)/shard_map/ppermute | solution.py:18
  8.4 0.0 collective-permute-start.1
  8.4 1.0 %collective-permute-start.2 = (bf16[150,128]{1,0:T(8,128)(2,1)}, bf16[150,128]{1,0:T(8,128)(2,1)S(1)}, u32[]{:S(2)}, u32[]{:S(2)}) collective-permute-start(bf16[150,128]{1,0:T(8,128)(2,1)} %get-tuple-element.17), channel_id=1, source_target_pairs={{126,0},{127,1},{0,2},{1,3},{2,4},{3,5},{4,6},{5,7},{6,8},{7,9},{8... | collective-permute-start | bytes 115208 | tf_op jit(solution)/shard_map/ppermute | solution.py:18
  9.4 2.2 %collective-permute-start.3 = (bf16[150,128]{1,0:T(8,128)(2,1)}, bf16[150,128]{1,0:T(8,128)(2,1)S(1)}, u32[]{:S(2)}, u32[]{:S(2)}) collective-permute-start(bf16[150,128]{1,0:T(8,128)(2,1)} %get-tuple-element.18), channel_id=1, source_target_pairs={{127,0},{0,1},{1,2},{2,3},{3,4},{4,5},{5,6},{6,7},{7,8},{8,9},{9,1... | collective-permute-start | bytes 115208 | tf_op jit(solution)/shard_map/ppermute | solution.py:18
  11.6 5.6 %collective-permute-start.4 = (bf16[150,128]{1,0:T(8,128)(2,1)}, bf16[150,128]{1,0:T(8,128)(2,1)S(1)}, u32[]{:S(2)}, u32[]{:S(2)}) collective-permute-start(bf16[150,128]{1,0:T(8,128)(2,1)} %get-tuple-element.19), channel_id=1, source_target_pairs={{1,0},{2,1},{3,2},{4,3},{5,4},{6,5},{7,6},{8,7},{9,8},{10,9},{11,1... | collective-permute-start | bytes 115208 | tf_op jit(solution)/shard_map/ppermute | solution.py:18
  17.2 0.7 %fusion = pred[1,1,8,128]{3,2,1,0:T(8,128)(4,1)S(1)} fusion(s32[8]{0:T(128)} %bitcast.26), kind=kLoop, calls=%fused_computation.4 | loop fusion | flops 1024 | bytes 1056
  17.9 0.3 copy.17
  18.2 0.9 %copy.15 = s32[1024,1]{1,0:T(8,128)S(1)} copy(s32[1024,1]{0,1:T(1,128)} %bitcast.21) | data formatting | bytes 8192 | tf_op jit(solution)/shard_map/squeeze | solution.py:127
  19.1 0.0 collective-permute-done.refs_0_
  19.1 0.0 copy-start.2
  19.1 0.6 collective-permute-start.5
  19.8 0.0 collective-permute-done.1.refs_1_
  19.8 0.0 copy-start.3
  19.8 0.3 collective-permute-start.6
  20.1 0.0 collective-permute-done.2.refs_2_
  20.1 0.0 copy-start.4
  20.1 4.0 %collective-permute-start.7 = (bf16[150,128]{1,0:T(8,128)(2,1)}, bf16[150,128]{1,0:T(8,128)(2,1)S(1)}, u32[]{:S(2)}, u32[]{:S(2)}) collective-permute-start(bf16[150,128]{1,0:T(8,128)(2,1)} %get-tuple-element.22), channel_id=1, source_target_pairs={{4,0},{5,1},{6,2},{7,3},{8,4},{9,5},{10,6},{11,7},{12,8},{13,9},{1... | collective-permute-start | bytes 115208 | tf_op jit(solution)/shard_map/ppermute | solution.py:18
  24.1 0.8 %bitcast_select_fusion.refs_8_ = s32[1024,1]{1,0:T(8,128)} fusion(s32[1024,1]{1,0:T(8,128)S(1)} %copy.15, pred[1,1024]{0,1:T(8,128)(4,1)S(1)} %copy.17), kind=kLoop, calls=%fused_computation | loop fusion | flops 1024 | bytes 9216 | tf_op jit(solution)/shard_map/jit(_where)/select_n | solution.py:127
  24.9 0.0 collective-permute-done.3.refs_3_
  24.9 0.0 copy-start.5
  24.9 0.0 collective-permute-done.4.refs_4_
  24.9 0.0 copy-start.6
  24.9 0.0 collective-permute-done.5.refs_5_
  25.0 0.0 copy-start.7
  25.0 0.0 collective-permute-done.6.refs_6_
  25.0 0.0 copy-start.8
  25.0 1.3 %collective-permute-done.7.refs_7_ = bf16[150,128]{1,0:T(8,128)(2,1)S(1)} collective-permute-done((bf16[150,128]{1,0:T(8,128)(2,1)}, bf16[150,128]{1,0:T(8,128)(2,1)S(1)}, u32[]{:S(2)}, u32[]{:S(2)}) %collective-permute-start.7) | collective-permute-done | bytes 38432 | tf_op jit(solution)/shard_map/ppermute | solution.py:18
  26.3 0.0 copy-start.9
  26.3 0.0 copy-done.2
  26.3 0.0 copy-done.3
  26.3 0.0 copy-done.4
  26.3 0.0 copy-done.5
  26.3 0.0 copy-done.6
  26.3 0.0 copy-done.7
  26.3 0.0 copy-done.8
  26.3 0.6 copy-done.9
  26.9 6.2 %shard_map.129 = (bf16[150,2048]{1,0:T(8,128)(2,1)}, bf16[150,2048]{1,0:T(8,128)(2,1)}) custom-call(s32[2,16]{1,0:T(2,128)} %bitcast.24, bf16[150,8192]{1,0:T(8,128)(2,1)} %mixing_ref.5, bf16[150,128]{1,0:T(8,128)(2,1)} %copy-done.2, bf16[150,128]{1,0:T(8,128)(2,1)} %copy-done.3, bf16[150,128]{1,0:T(8,128)(2,1)} %copy-done.4, bf16[150,128]{1,0:T(8,128)(2,1)} %copy-done.5, ...), custom_call_target="tpu_custom_call" | custom-call | tf_op jit(solution)/shard_map/pallas_call | solution.py:139
  33.1 0.2 collective-permute-start.8
  33.2 7.1 %collective-permute-start.9 = (bf16[150,2048]{1,0:T(8,128)(2,1)}, bf16[150,2048]{1,0:T(8,128)(2,1)S(1)}, u32[]{:S(2)}, u32[]{:S(2)}) collective-permute-start(bf16[150,2048]{1,0:T(8,128)(2,1)} %get-tuple-element.24), channel_id=1, source_target_pairs={{1,0},{2,1},{3,2},{4,3},{5,4},{6,5},{7,6},{8,7},{9,8},{10,9},{11,1... | collective-permute-start | bytes 1843208 | tf_op jit(solution)/shard_map/ppermute | solution.py:18
  40.3 0.0 copy-done.12
  40.3 0.0 copy-done.11
  40.3 0.0 copy-done.10
  40.3 0.7 pad_maximum_fusion.order_ref
  41.0 6.8 %shard_map.128.own_ref.migrated_hbm = bf16[150,8192]{1,0:T(8,128)(2,1)} custom-call(bf16[150,8192]{1,0:T(8,128)(2,1)} %mixing_ref.5, bf16[150,128]{1,0:T(8,128)(2,1)} %copy-done.2, bf16[150,128]{1,0:T(8,128)(2,1)} %copy-done.3, bf16[150,128]{1,0:T(8,128)(2,1)} %copy-done.4, bf16[150,128]{1,0:T(8,128)(2,1)} %copy-done.5, bf16[150,128]{1,0:T(8,128)(2,1)} %copy-done.6, ...), custom_call_target="tpu_custom_call" | custom-call | tf_op jit(solution)/shard_map/pallas_call | solution.py:144
  47.9 0.6 collective-permute-done.8.lower_hbm
  48.5 0.0 copy-start
  48.5 0.0 collective-permute-done.9.upper_hbm
  48.5 0.0 copy-start.1
  48.5 0.8 %copy-done = bf16[150,2048]{1,0:T(8,128)(2,1)} copy-done((bf16[150,2048]{1,0:T(8,128)(2,1)}, bf16[150,2048]{1,0:T(8,128)(2,1)S(1)}, u32[]{:S(2)}) %copy-start) | copy-done | bytes 614424
  49.3 0.2 copy-done.1
  49.5 20.2 %shard_map.130 = f32[150,8192]{1,0:T(8,128)} custom-call(s32[3,64]{1,0:T(4,128)} %bitcast.23, bf16[150,8192]{1,0:T(8,128)(2,1)} %shard_map.128.own_ref.migrated_hbm, bf16[64,4,128,128]{3,2,1,0:T(8,128)(2,1)} %weight_ref.1, f32[1,8192]{1,0:T(1,128)} %bitcast.18, f32[152,256]{1,0:T(8,128)} %pad_maximum_fusion.order_ref, f32[150,256]{1,0:T(8,128)} %prod_ref.1, ...), custom_call_target="tpu_custom_call" | custom-call | tf_op jit(solution)/shard_map/pallas_call | solution.py:340
  (2 shorter events, 0.0 us)
Async XLA Ops:
  0.0 40.3 %copy-start.12 = (f32[256]{0:T(256)S(1)}, f32[256]{0:T(256)}, u32[]{:S(2)}) copy-start(f32[256]{0:T(256)} %param.23) | copy-start | bytes 3076
  0.0 40.3 %copy-start.11 = (f32[256]{0:T(256)S(1)}, f32[256]{0:T(256)}, u32[]{:S(2)}) copy-start(f32[256]{0:T(256)} %param.22) | copy-start | bytes 3076
  0.0 40.3 %copy-start.10 = (f32[256,150]{0,1:T(8,128)S(1)}, f32[256,150]{0,1:T(8,128)}, u32[]{:S(2)}) copy-start(f32[256,150]{0,1:T(8,128)} %param.21) | copy-start | bytes 460804
  5.3 13.8 %collective-permute-start = (bf16[150,128]{1,0:T(8,128)(2,1)}, bf16[150,128]{1,0:T(8,128)(2,1)S(1)}, u32[]{:S(2)}, u32[]{:S(2)}) collective-permute-start(bf16[150,128]{1,0:T(8,128)(2,1)} %get-tuple-element.15), channel_id=1, source_target_pairs={{124,0},{125,1},{126,2},{127,3},{0,4},{1,5},{2,6},{3,7},{4,8},{5,9... | collective-permute-start | bytes 115208 | tf_op jit(solution)/shard_map/ppermute | solution.py:18
  8.4 11.4 %collective-permute-start.1 = (bf16[150,128]{1,0:T(8,128)(2,1)}, bf16[150,128]{1,0:T(8,128)(2,1)S(1)}, u32[]{:S(2)}, u32[]{:S(2)}) collective-permute-start(bf16[150,128]{1,0:T(8,128)(2,1)} %get-tuple-element.16), channel_id=1, source_target_pairs={{125,0},{126,1},{127,2},{0,3},{1,4},{2,5},{3,6},{4,7},{5,8},{6,9},... | collective-permute-start | bytes 115208 | tf_op jit(solution)/shard_map/ppermute | solution.py:18
  8.4 11.7 %collective-permute-start.2 = (bf16[150,128]{1,0:T(8,128)(2,1)}, bf16[150,128]{1,0:T(8,128)(2,1)S(1)}, u32[]{:S(2)}, u32[]{:S(2)}) collective-permute-start(bf16[150,128]{1,0:T(8,128)(2,1)} %get-tuple-element.17), channel_id=1, source_target_pairs={{126,0},{127,1},{0,2},{1,3},{2,4},{3,5},{4,6},{5,7},{6,8},{7,9},{8... | collective-permute-start | bytes 115208 | tf_op jit(solution)/shard_map/ppermute | solution.py:18
  9.4 15.5 %collective-permute-start.3 = (bf16[150,128]{1,0:T(8,128)(2,1)}, bf16[150,128]{1,0:T(8,128)(2,1)S(1)}, u32[]{:S(2)}, u32[]{:S(2)}) collective-permute-start(bf16[150,128]{1,0:T(8,128)(2,1)} %get-tuple-element.18), channel_id=1, source_target_pairs={{127,0},{0,1},{1,2},{2,3},{3,4},{4,5},{5,6},{6,7},{7,8},{8,9},{9,1... | collective-permute-start | bytes 115208 | tf_op jit(solution)/shard_map/ppermute | solution.py:18
  11.6 13.3 %collective-permute-start.4 = (bf16[150,128]{1,0:T(8,128)(2,1)}, bf16[150,128]{1,0:T(8,128)(2,1)S(1)}, u32[]{:S(2)}, u32[]{:S(2)}) collective-permute-start(bf16[150,128]{1,0:T(8,128)(2,1)} %get-tuple-element.19), channel_id=1, source_target_pairs={{1,0},{2,1},{3,2},{4,3},{5,4},{6,5},{7,6},{8,7},{9,8},{10,9},{11,1... | collective-permute-start | bytes 115208 | tf_op jit(solution)/shard_map/ppermute | solution.py:18
  19.1 7.2 %copy-start.2 = (bf16[150,128]{1,0:T(8,128)(2,1)}, bf16[150,128]{1,0:T(8,128)(2,1)S(1)}, u32[]{:S(2)}) copy-start(bf16[150,128]{1,0:T(8,128)(2,1)S(1)} %collective-permute-done.refs_0_) | copy-start | bytes 115204
  19.1 5.8 %collective-permute-start.5 = (bf16[150,128]{1,0:T(8,128)(2,1)}, bf16[150,128]{1,0:T(8,128)(2,1)S(1)}, u32[]{:S(2)}, u32[]{:S(2)}) collective-permute-start(bf16[150,128]{1,0:T(8,128)(2,1)} %get-tuple-element.20), channel_id=1, source_target_pairs={{2,0},{3,1},{4,2},{5,3},{6,4},{7,5},{8,6},{9,7},{10,8},{11,9},{12,... | collective-permute-start | bytes 115208 | tf_op jit(solution)/shard_map/ppermute | solution.py:18
  19.8 6.5 %copy-start.3 = (bf16[150,128]{1,0:T(8,128)(2,1)}, bf16[150,128]{1,0:T(8,128)(2,1)S(1)}, u32[]{:S(2)}) copy-start(bf16[150,128]{1,0:T(8,128)(2,1)S(1)} %collective-permute-done.1.refs_1_) | copy-start | bytes 115204
  19.8 5.2 %collective-permute-start.6 = (bf16[150,128]{1,0:T(8,128)(2,1)}, bf16[150,128]{1,0:T(8,128)(2,1)S(1)}, u32[]{:S(2)}, u32[]{:S(2)}) collective-permute-start(bf16[150,128]{1,0:T(8,128)(2,1)} %get-tuple-element.21), channel_id=1, source_target_pairs={{3,0},{4,1},{5,2},{6,3},{7,4},{8,5},{9,6},{10,7},{11,8},{12,9},{13... | collective-permute-start | bytes 115208 | tf_op jit(solution)/shard_map/ppermute | solution.py:18
  20.1 6.2 %copy-start.4 = (bf16[150,128]{1,0:T(8,128)(2,1)}, bf16[150,128]{1,0:T(8,128)(2,1)S(1)}, u32[]{:S(2)}) copy-start(bf16[150,128]{1,0:T(8,128)(2,1)S(1)} %collective-permute-done.2.refs_2_) | copy-start | bytes 115204
  20.1 6.2 %collective-permute-start.7 = (bf16[150,128]{1,0:T(8,128)(2,1)}, bf16[150,128]{1,0:T(8,128)(2,1)S(1)}, u32[]{:S(2)}, u32[]{:S(2)}) collective-permute-start(bf16[150,128]{1,0:T(8,128)(2,1)} %get-tuple-element.22), channel_id=1, source_target_pairs={{4,0},{5,1},{6,2},{7,3},{8,4},{9,5},{10,6},{11,7},{12,8},{13,9},{1... | collective-permute-start | bytes 115208 | tf_op jit(solution)/shard_map/ppermute | solution.py:18
  24.9 1.4 %copy-start.5 = (bf16[150,128]{1,0:T(8,128)(2,1)}, bf16[150,128]{1,0:T(8,128)(2,1)S(1)}, u32[]{:S(2)}) copy-start(bf16[150,128]{1,0:T(8,128)(2,1)S(1)} %collective-permute-done.3.refs_3_) | copy-start | bytes 115204
  24.9 1.4 %copy-start.6 = (bf16[150,128]{1,0:T(8,128)(2,1)}, bf16[150,128]{1,0:T(8,128)(2,1)S(1)}, u32[]{:S(2)}) copy-start(bf16[150,128]{1,0:T(8,128)(2,1)S(1)} %collective-permute-done.4.refs_4_) | copy-start | bytes 115204
  25.0 1.4 %copy-start.7 = (bf16[150,128]{1,0:T(8,128)(2,1)}, bf16[150,128]{1,0:T(8,128)(2,1)S(1)}, u32[]{:S(2)}) copy-start(bf16[150,128]{1,0:T(8,128)(2,1)S(1)} %collective-permute-done.5.refs_5_) | copy-start | bytes 115204
  25.0 1.4 %copy-start.8 = (bf16[150,128]{1,0:T(8,128)(2,1)}, bf16[150,128]{1,0:T(8,128)(2,1)S(1)}, u32[]{:S(2)}) copy-start(bf16[150,128]{1,0:T(8,128)(2,1)S(1)} %collective-permute-done.6.refs_6_) | copy-start | bytes 115204
  26.3 0.6 copy-start.9
  33.1 15.4 %collective-permute-start.8 = (bf16[150,2048]{1,0:T(8,128)(2,1)}, bf16[150,2048]{1,0:T(8,128)(2,1)S(1)}, u32[]{:S(2)}, u32[]{:S(2)}) collective-permute-start(bf16[150,2048]{1,0:T(8,128)(2,1)} %get-tuple-element.23), channel_id=1, source_target_pairs={{127,0},{0,1},{1,2},{2,3},{3,4},{4,5},{5,6},{6,7},{7,8},{8,9},{9,1... | collective-permute-start | bytes 1843208 | tf_op jit(solution)/shard_map/ppermute | solution.py:18
  33.2 15.2 %collective-permute-start.9 = (bf16[150,2048]{1,0:T(8,128)(2,1)}, bf16[150,2048]{1,0:T(8,128)(2,1)S(1)}, u32[]{:S(2)}, u32[]{:S(2)}) collective-permute-start(bf16[150,2048]{1,0:T(8,128)(2,1)} %get-tuple-element.24), channel_id=1, source_target_pairs={{1,0},{2,1},{3,2},{4,3},{5,4},{6,5},{7,6},{8,7},{9,8},{10,9},{11,1... | collective-permute-start | bytes 1843208 | tf_op jit(solution)/shard_map/ppermute | solution.py:18
  48.5 0.8 %copy-start = (bf16[150,2048]{1,0:T(8,128)(2,1)}, bf16[150,2048]{1,0:T(8,128)(2,1)S(1)}, u32[]{:S(2)}) copy-start(bf16[150,2048]{1,0:T(8,128)(2,1)S(1)} %collective-permute-done.8.lower_hbm) | copy-start | bytes 1843204
  48.5 1.0 %copy-start.1 = (bf16[150,2048]{1,0:T(8,128)(2,1)}, bf16[150,2048]{1,0:T(8,128)(2,1)S(1)}, u32[]{:S(2)}) copy-start(bf16[150,2048]{1,0:T(8,128)(2,1)S(1)} %collective-permute-done.9.upper_hbm) | copy-start | bytes 1843204
